TPU v7x, 32 devices: a whole 2x2x4 slice. The times are simulated.
32 devices in a mesh: chan: 16 (over z, y, core), tm: 2 (over x).
Axes of the slice: x: 2, y: 2, z: 4, core: 2. Of those that a mesh axis runs over, the one named last changes fastest.
Arguments:
- record: bfloat16 [2, 256, 1536], P('tm', 'chan'), may hold values from -6 to 6
- pairs: int32 [32, 256], P('chan'), may hold values from 0 to 255, as said below
- stretch_index: int32 [4, 1024], replicated, may hold values from 0 to 1023, as said below
Outputs:
- coherence: float32 [2, 4, 32, 256], P('tm', None, 'chan')
Inputs may be any that keep to these rules, and one draw needn't show every extreme that they name: `pairs`: row j lists the receivers of the virtual source at channel 8 j. With channel blocks of 16 channels, B = 16 of them, and b the block of channel 8 j: the first 128 receivers lie in blocks b - 1 to b + 1, and the others, across the fold of the fibre, in blocks B - 2 - b to B - b. `stretch_index`: row s is a stretch of the lag axis about lag index 512, rounded down and clipped to the lag range; row 0 reads every lag itself.
All inputs are finite; a program needn't handle non-finite values.
Results may differ from a plain program's by a relative error of at most 0.00074.
Values may be sent and summed in bfloat16 or wider, within the bound.
No kernel may reach another device: no remote copies, remote signals or barrier semaphores. Data moves between devices by JAX's collectives and lax.ppermute only.
A program may use at most 64 MiB of HBM per device.

v0:
```python
import math

import jax
import jax.numpy as jnp
from jax import lax
from jax.sharding import PartitionSpec as P

NT = 1536
LAGS = 1024
NF = 768


epsilon = 1e-05


def padded(value, sides, width):
    for axis, dim in sides:
        size, length = (lax.axis_size(axis), value.shape[dim])
        up = [(i, (i + 1) % size) for i in range(size - 1)]
        down = [(j, i) for i, j in up]
        last = lax.slice_in_dim(value, length - width, length, axis=dim)
        leading = lax.slice_in_dim(value, 0, width, axis=dim)
        before = lax.ppermute(last, axis, up)
        after = lax.ppermute(leading, axis, down)
        value = jnp.concatenate([before, value, after], axis=dim)
    return value


def from_partner(value, axis, distance):
    mask = 2**distance
    pairs = [(source, source ^ mask) for source in range(lax.axis_size(axis))]
    return lax.ppermute(value, axis, pairs)


def forward_table(first_bin, bin_count):
    sample_index = jnp.arange(NT, dtype=jnp.int32)[:, None]
    bin_index = (first_bin + jnp.arange(bin_count, dtype=jnp.int32))[None, :]
    phase_angle = (sample_index * bin_index % NT).astype(jnp.float32) * (2.0 * math.pi / NT)
    return jnp.concatenate([jnp.cos(phase_angle), -jnp.sin(phase_angle)], axis=1).astype(
        jnp.bfloat16
    )


def inverse_table():
    bin_index = jnp.arange(NF, dtype=jnp.int32)[:, None]
    lag_offset = jnp.arange(LAGS, dtype=jnp.int32)[None, :] - LAGS // 2
    phase_angle = (bin_index * lag_offset % NT).astype(jnp.float32) * (2.0 * math.pi / NT)
    bin_weight = jnp.where(bin_index == 0, 1.0, 2.0).astype(jnp.float32)
    return jnp.concatenate(
        [bin_weight * jnp.cos(phase_angle), -bin_weight * jnp.sin(phase_angle)], axis=0
    ).astype(jnp.bfloat16)


def whiten(spectrum):
    power = jnp.mean(spectrum * spectrum, axis=-1, keepdims=True)
    return (spectrum / jnp.sqrt(power + epsilon)).astype(jnp.bfloat16)


def cross_spectrum(source_row, receivers):
    half_width = receivers.shape[-1] // 2
    source_vals = source_row.astype(jnp.float32)
    receiver_vals = receivers.astype(jnp.float32)
    src_re = source_vals[..., :half_width]
    src_im = source_vals[..., half_width:]
    rec_re = receiver_vals[..., :half_width]
    rec_im = receiver_vals[..., half_width:]
    real_part = src_re * rec_re + src_im * rec_im
    imag_part = src_re * rec_im - src_im * rec_re
    return jnp.concatenate([real_part, imag_part], axis=-1).astype(jnp.bfloat16)


def curves(current, stacked, stretch_index):
    current_power = jnp.mean(current * current, axis=-1)
    columns = []
    for stretch in range(stretch_index.shape[0]):
        shifted = jnp.take(stacked, stretch_index[stretch], axis=1, mode="clip")
        numerator = jnp.mean(current * shifted[None], axis=-1)
        shifted_power = jnp.mean(shifted * shifted, axis=-1)[None]
        columns.append(numerator / jnp.sqrt((current_power + epsilon) * (shifted_power + epsilon)))
    return jnp.stack(columns, axis=1)


def body(record, pairs, stretch_index):
    block_rows = record.shape[1]
    samples = record[0]
    bin_block = min(128, NF)
    real_parts = []
    imag_parts = []
    for first_bin in range(0, NF, bin_block):
        product = jnp.dot(
            samples, forward_table(first_bin, bin_block), preferred_element_type=jnp.float32
        )
        real_parts.append(product[:, :bin_block])
        imag_parts.append(product[:, bin_block:])
    spectrum = jnp.concatenate(real_parts + imag_parts, axis=1)
    whitened = whiten(spectrum)
    near_rows = padded(whitened, (("chan", 0),), block_rows)
    position = lax.axis_index("chan")
    axis_count = lax.axis_size("chan")
    bit_count = axis_count.bit_length() - 1
    far_rows = whitened
    for bit_number in range(bit_count):
        far_rows = from_partner(far_rows, "chan", bit_number)
    far_rows = padded(far_rows, (("chan", 0),), block_rows)
    far_slot = (axis_count - position - pairs // block_rows) * block_rows + pairs % block_rows
    candidates = jnp.concatenate([near_rows, far_rows], axis=0)
    near_start = (position - 1) * block_rows
    column_index = jnp.arange(pairs.shape[1], dtype=jnp.int32)[None, :]
    is_near = column_index < pairs.shape[1] // 2
    slot_index = jnp.where(is_near, pairs - near_start, 3 * block_rows + far_slot)
    sources = whitened[::8]
    inverse = inverse_table()
    source_count = slot_index.shape[0]
    recv_count = slot_index.shape[1]
    receivers = jnp.take(candidates, slot_index.reshape(-1), axis=0, mode="clip")
    receivers = receivers.reshape(source_count, recv_count, receivers.shape[-1])
    crossed = cross_spectrum(sources[:, None, :], receivers).reshape(source_count * recv_count, -1)
    correlation = jnp.dot(crossed, inverse, preferred_element_type=jnp.float32)
    pair_count = source_count * recv_count
    flattened = correlation.reshape(1, pair_count, correlation.shape[1])
    stacked = lax.psum(flattened[0], "tm")
    result = curves(flattened, stacked, stretch_index)
    return result.reshape(1, result.shape[1], source_count, recv_count)


def solution(mesh):
    return jax.shard_map(
        body,
        mesh=mesh,
        in_specs=(P("tm", "chan", None), P("chan", None), P()),
        out_specs=P("tm", None, "chan", None),
        check_vma=False,
    )
```

profile of v0, /device:TPU:1, one launch (start us, length us, event | category | flops | bytes accessed | tf_op | source)
XLA Modules:
  0.0 187.7 jit_solution(14236996720502922308)
XLA Ops:
  6.5 0.0 copy-start
  6.5 0.0 all-reduce.2.cloned.1.call-start
  6.6 3.4 %negate_convert_fusion.5 = (bf16[1536,128]{1,0:T(8,128)(2,1)S(1)}, bf16[1536,128]{1,0:T(8,128)(2,1)S(1)}) fusion(), kind=kLoop, calls=%fused_computation.107 | loop fusion | flops 2359296 | bytes 786432 | tf_op jit(solution)/shard_map/convert.19
  10.0 3.4 %cosine_convert_fusion = (bf16[1536,128]{1,0:T(8,128)(2,1)S(1)}, bf16[1536,128]{1,0:T(8,128)(2,1)S(1)}) fusion(s32[128]{0:T(128)S(1)} %iota_add_fusion.1), kind=kLoop, calls=%fused_computation.83 | loop fusion | flops 2359296 | bytes 786944 | tf_op jit(solution)/shard_map/convert.8
  13.4 3.4 %cosine_convert_fusion.1 = (bf16[1536,128]{1,0:T(8,128)(2,1)S(1)}, bf16[1536,128]{1,0:T(8,128)(2,1)S(1)}) fusion(s32[128]{0:T(128)S(1)} %iota_add_fusion.2), kind=kLoop, calls=%fused_computation.88 | loop fusion | flops 2359296 | bytes 786944 | tf_op jit(solution)/shard_map/convert.10
  16.8 3.4 %cosine_convert_fusion.2 = (bf16[1536,128]{1,0:T(8,128)(2,1)S(1)}, bf16[1536,128]{1,0:T(8,128)(2,1)S(1)}) fusion(s32[128]{0:T(128)S(1)} %iota_add_fusion.3), kind=kLoop, calls=%fused_computation.93 | loop fusion | flops 2359296 | bytes 786944 | tf_op jit(solution)/shard_map/convert.12
  20.3 3.4 %cosine_convert_fusion.3 = (bf16[1536,128]{1,0:T(8,128)(2,1)S(1)}, bf16[1536,128]{1,0:T(8,128)(2,1)S(1)}) fusion(s32[128]{0:T(128)S(1)} %iota_add_fusion.4), kind=kLoop, calls=%fused_computation.98 | loop fusion | flops 2359296 | bytes 786944 | tf_op jit(solution)/shard_map/convert.14
  23.7 3.4 %cosine_convert_fusion.4 = (bf16[1536,128]{1,0:T(8,128)(2,1)S(1)}, bf16[1536,128]{1,0:T(8,128)(2,1)S(1)}) fusion(s32[128]{0:T(128)S(1)} %iota_add_fusion.5), kind=kLoop, calls=%fused_computation.103 | loop fusion | flops 2359296 | bytes 786944 | tf_op jit(solution)/shard_map/convert.16
  27.1 0.0 copy-done
  27.1 0.2 convolution_bitcast_fusion.5
  27.4 0.2 convolution_bitcast_fusion
  27.6 0.2 convolution_bitcast_fusion.1
  27.8 0.2 convolution_bitcast_fusion.2
  28.0 0.2 convolution_bitcast_fusion.3
  28.2 0.2 convolution_bitcast_fusion.4
  28.5 0.0 copy-start.4
  28.6 0.1 multiply_reduce_fusion.1
  28.7 0.1 divide_convert_fusion
  28.8 0.1 collective-permute-start.2
  28.9 2.3 %collective-permute-start.1 = (bf16[16,1536]{1,0:T(8,128)(2,1)S(1)}, bf16[16,1536]{1,0:T(8,128)(2,1)S(1)}, u32[]{:S(2)}, u32[]{:S(2)}) collective-permute-start(bf16[16,1536]{1,0:T(8,128)(2,1)S(1)} %divide_convert_fusion), channel_id=1, source_target_pairs={{2,0},{4,2},{6,4},{8,6},{10,8},{12,10},{14,12},{16,14},{18,16},{20... | collective-permute-start | bytes 147464 | tf_op jit(solution)/shard_map/ppermute | solution.py:24
  31.3 4.1 %collective-permute-start = (bf16[16,1536]{1,0:T(8,128)(2,1)S(1)}, bf16[16,1536]{1,0:T(8,128)(2,1)S(1)}, u32[]{:S(2)}, u32[]{:S(2)}) collective-permute-start(bf16[16,1536]{1,0:T(8,128)(2,1)S(1)} %divide_convert_fusion), channel_id=1, source_target_pairs={{0,2},{2,4},{4,6},{6,8},{8,10},{10,12},{12,14},{14,16},{16,18},{18... | collective-permute-start | bytes 147464 | tf_op jit(solution)/shard_map/ppermute | solution.py:23
  35.4 14.1 %multiply_convert_fusion.1 = (bf16[768,1024]{1,0:T(8,128)(2,1)S(1)}, bf16[768,1024]{1,0:T(8,128)(2,1)}) fusion(s32[1024]{0:T(1024)S(1)} %iota_add_fusion, f32[768]{0:T(1024)S(1)} %get-tuple-element.38, f32[768]{0:T(1024)S(1)} %get-tuple-element.39), kind=kLoop, calls=%fused_computation.13 | loop fusion | flops 10223616 | bytes 3155968 | tf_op jit(solution)/shard_map/convert.2
  49.5 0.0 copy-done.4
  49.6 0.0 collective-permute-done.2
  49.6 2.8 %collective-permute-start.3 = (bf16[16,1536]{1,0:T(8,128)(2,1)S(1)}, bf16[16,1536]{1,0:T(8,128)(2,1)S(1)}, u32[]{:S(2)}, u32[]{:S(2)}) collective-permute-start(bf16[16,1536]{1,0:T(8,128)(2,1)S(1)} %collective-permute-done.2), channel_id=1, source_target_pairs={{0,4},{2,6},{4,0},{6,2},{8,12},{10,14},{12,8},{14,10},{16,20},{18,... | collective-permute-start | bytes 147464 | tf_op jit(solution)/shard_map/ppermute | solution.py:32
  52.4 1.5 collective-permute-done.3
  53.9 1.4 collective-permute-start.4
  55.2 0.0 collective-permute-done
  55.3 2.0 %collective-permute-done.4 = bf16[16,1536]{1,0:T(8,128)(2,1)S(1)} collective-permute-done((bf16[16,1536]{1,0:T(8,128)(2,1)S(1)}, bf16[16,1536]{1,0:T(8,128)(2,1)S(1)}, u32[]{:S(2)}, u32[]{:S(2)}) %collective-permute-start.4) | collective-permute-done | bytes 49184 | tf_op jit(solution)/shard_map/ppermute | solution.py:32
  57.2 1.9 %collective-permute-start.5 = (bf16[16,1536]{1,0:T(8,128)(2,1)S(1)}, bf16[16,1536]{1,0:T(8,128)(2,1)S(1)}, u32[]{:S(2)}, u32[]{:S(2)}) collective-permute-start(bf16[16,1536]{1,0:T(8,128)(2,1)S(1)} %collective-permute-done.4), channel_id=1, source_target_pairs={{0,16},{2,18},{4,20},{6,22},{8,24},{10,26},{12,28},{14,30},{16,0},... | collective-permute-start | bytes 147464 | tf_op jit(solution)/shard_map/ppermute | solution.py:32
  59.2 0.1 constant_dynamic-update-slice_fusion.16
  59.3 1.8 collective-permute-done.5
  61.1 4.7 %collective-permute-start.6 = (bf16[16,1536]{1,0:T(8,128)(2,1)S(1)}, bf16[16,1536]{1,0:T(8,128)(2,1)S(1)}, u32[]{:S(2)}, u32[]{:S(2)}) collective-permute-start(bf16[16,1536]{1,0:T(8,128)(2,1)S(1)} %collective-permute-done.5), channel_id=1, source_target_pairs={{0,2},{2,4},{4,6},{6,8},{8,10},{10,12},{12,14},{14,16},{16,18},{18... | collective-permute-start | bytes 147464 | tf_op jit(solution)/shard_map/ppermute | solution.py:23
  65.8 0.0 collective-permute-done.1
  65.9 2.1 %collective-permute-start.7 = (bf16[16,1536]{1,0:T(8,128)(2,1)S(1)}, bf16[16,1536]{1,0:T(8,128)(2,1)S(1)}, u32[]{:S(2)}, u32[]{:S(2)}) collective-permute-start(bf16[16,1536]{1,0:T(8,128)(2,1)S(1)} %collective-permute-done.5), channel_id=1, source_target_pairs={{2,0},{4,2},{6,4},{8,6},{10,8},{12,10},{14,12},{16,14},{18,16},{20... | collective-permute-start | bytes 147464 | tf_op jit(solution)/shard_map/ppermute | solution.py:24
  68.0 0.0 collective-permute-done.6
  68.0 3.3 %collective-permute-done.7 = bf16[16,1536]{1,0:T(8,128)(2,1)S(1)} collective-permute-done((bf16[16,1536]{1,0:T(8,128)(2,1)S(1)}, bf16[16,1536]{1,0:T(8,128)(2,1)S(1)}, u32[]{:S(2)}, u32[]{:S(2)}) %collective-permute-start.7) | collective-permute-done | bytes 49184 | tf_op jit(solution)/shard_map/ppermute | solution.py:24
  71.3 2.1 %gather_fusion = bf16[512,1536]{1,0:T(8,128)(2,1)S(1)} fusion(bf16[96,1536]{1,0:T(8,128)(2,1)S(1)} %constant_dynamic-update-slice_fusion.12, s32[1024]{0:T(1024)S(1)} %pad_clamp_fusion), kind=kCustom, calls=%fused_computation | custom fusion | bytes 3147776 | tf_op jit(solution)/shard_map/jit(_take)/gather | solution.py:115
  73.4 0.4 convert.69
  73.8 0.0 copy-start.2
  73.8 0.5 add_convert_fusion
  74.3 0.9 copy-done.2
  75.2 3.2 %fusion.2 = f32[512,1024]{1,0:T(8,128)} fusion(bf16[768,1024]{1,0:T(8,128)(2,1)S(1)} %copy-done.2, bf16[768,1024]{1,0:T(8,128)(2,1)S(1)} %get-tuple-element.22, bf16[512,768]{1,0:T(8,128)(2,1)S(1)} %bitcast.73, bf16[512,768]{1,0:T(8,128)(2,1)S(1)} %bitcast.72), kind=kOutput, calls=%fused_computation.8 | convolution fusion | flops 1620049920 | bytes 6815744 | tf_op jit(solution)/shard_map/dot_general | solution.py:118
  78.4 0.0 copy-start.3
  78.4 0.0 all-reduce.2.cloned.1.call-update
  78.4 0.7 copy-done.3
  79.2 63.9 %all-reduce.2.cloned.1.call-done = f32[512,1024]{1,0:T(8,128)} async-done(((f32[512,1024]{1,0:T(8,128)}), f32[512,1024]{1,0:T(8,128)}) %all-reduce.2.cloned.1.call-update) | async-done | bytes 2097168 | tf_op jit(solution)/shard_map/psum | solution.py:121
  143.1 1.9 %copy.4 = f32[512,1024]{0,1:T(8,128)S(1)} copy(f32[512,1024]{1,0:T(8,128)} %all-reduce.2.cloned.1.call-done) | data formatting | bytes 4194304 | tf_op jit(solution)/shard_map/psum | solution.py:121
  145.0 4.9 %gather_fusion.4 = f32[1024,512]{1,0:T(8,128)} fusion(f32[512,1024]{0,1:T(8,128)S(1)} %copy.4, s32[1024]{0:T(1024)S(1)} %get-tuple-element.42), kind=kCustom, calls=%fused_computation.4 | custom fusion | bytes 4198400 | tf_op jit(solution)/shard_map/jit(_take)/gather | solution.py:76
  149.9 2.9 %copy.11 = f32[1024,512]{0,1:T(8,128)} copy(f32[1024,512]{1,0:T(8,128)} %gather_fusion.4) | data formatting | bytes 4194304 | tf_op jit(solution)/shard_map/jit(_take)/gather | solution.py:76
  152.8 4.9 %gather_fusion.3 = f32[1024,512]{1,0:T(8,128)} fusion(f32[512,1024]{0,1:T(8,128)S(1)} %copy.4, s32[1024]{0:T(1024)S(1)} %get-tuple-element.43), kind=kCustom, calls=%fused_computation.3 | custom fusion | bytes 4198400 | tf_op jit(solution)/shard_map/jit(_take)/gather | solution.py:76
  157.7 2.9 %copy.9 = f32[1024,512]{0,1:T(8,128)} copy(f32[1024,512]{1,0:T(8,128)} %gather_fusion.3) | data formatting | bytes 4194304 | tf_op jit(solution)/shard_map/jit(_take)/gather | solution.py:76
  160.6 4.9 %gather_fusion.2 = f32[1024,512]{1,0:T(8,128)} fusion(f32[512,1024]{0,1:T(8,128)S(1)} %copy.4, s32[1024]{0:T(1024)S(1)} %get-tuple-element.44), kind=kCustom, calls=%fused_computation.2 | custom fusion | bytes 4198400 | tf_op jit(solution)/shard_map/jit(_take)/gather | solution.py:76
  165.5 4.9 %gather_fusion.1 = f32[1024,512]{1,0:T(8,128)} fusion(f32[512,1024]{0,1:T(8,128)S(1)} %copy.4, s32[1024]{0:T(1024)S(1)} %get-tuple-element.45), kind=kCustom, calls=%fused_computation.1 | custom fusion | bytes 4198400 | tf_op jit(solution)/shard_map/jit(_take)/gather | solution.py:76
  170.4 0.0 copy-start.1
  170.4 3.1 %copy.5 = f32[1024,512]{0,1:T(8,128)} copy(f32[1024,512]{1,0:T(8,128)} %gather_fusion.1) | data formatting | bytes 4194304 | tf_op jit(solution)/shard_map/jit(_take)/gather | solution.py:76
  173.5 0.0 copy-done.1
  173.5 1.9 %copy.7 = f32[1024,512]{0,1:T(8,128)} copy(f32[1024,512]{1,0:T(8,128)S(1)} %copy-done.1) | data formatting | bytes 4194304 | tf_op jit(solution)/shard_map/jit(_take)/gather | solution.py:76
  175.4 4.8 %fusion.16 = (f32[512]{0:T(512)S(1)}, f32[512]{0:T(512)S(1)}, f32[512]{0:T(512)S(1)}, f32[512]{0:T(512)S(1)}, f32[512]{0:T(512)S(1)}, /*index=5*/f32[512]{0:T(51...) fusion(f32[512,1024]{1,0:T(8,128)} %fusion.2, f32[1024,512]{0,1:T(8,128)} %copy.5, f32[1024,512]{0,1:T(8,128)} %copy.11, ...), kind=kLoop, calls=%fused_computation.33 | loop fusion | flops 9432576 | bytes 10504192 | tf_op jit(solution)/shard_map/reduce_sum | solution.py:77
  180.2 0.6 pad_maximum_fusion
  (40 shorter events, 0.3 us)
Async XLA Ops:
  6.5 20.6 %copy-start = (bf16[1,16,1536]{2,1,0:T(8,128)(2,1)S(1)}, bf16[1,16,1536]{2,1,0:T(8,128)(2,1)}, u32[]{:S(2)}) copy-start(bf16[1,16,1536]{2,1,0:T(8,128)(2,1)} %param.3) | copy-start | bytes 147460
  6.5 136.5 %all-reduce.2.cloned.1.call-start = ((), (), s32[]{:S(2)}) async-start(), calls=%async_computation | async-start | bytes 4194304 | tf_op jit(solution)/shard_map/psum | solution.py:121
  28.5 21.1 %copy-start.4 = (s32[2,256]{1,0:T(2,128)S(1)}, s32[2,256]{1,0:T(2,128)}, u32[]{:S(2)}) copy-start(s32[2,256]{1,0:T(2,128)} %param.4) | copy-start | bytes 6148
  28.8 20.8 %collective-permute-start.2 = (bf16[16,1536]{1,0:T(8,128)(2,1)S(1)}, bf16[16,1536]{1,0:T(8,128)(2,1)S(1)}, u32[]{:S(2)}, u32[]{:S(2)}) collective-permute-start(bf16[16,1536]{1,0:T(8,128)(2,1)S(1)} %divide_convert_fusion), channel_id=1, source_target_pairs={{0,2},{2,0},{4,6},{6,4},{8,10},{10,8},{12,14},{14,12},{16,18},{18,... | collective-permute-start | bytes 147464 | tf_op jit(solution)/shard_map/ppermute | solution.py:32
  28.9 36.9 %collective-permute-start.1 = (bf16[16,1536]{1,0:T(8,128)(2,1)S(1)}, bf16[16,1536]{1,0:T(8,128)(2,1)S(1)}, u32[]{:S(2)}, u32[]{:S(2)}) collective-permute-start(bf16[16,1536]{1,0:T(8,128)(2,1)S(1)} %divide_convert_fusion), channel_id=1, source_target_pairs={{2,0},{4,2},{6,4},{8,6},{10,8},{12,10},{14,12},{16,14},{18,16},{20... | collective-permute-start | bytes 147464 | tf_op jit(solution)/shard_map/ppermute | solution.py:24
  31.3 24.0 %collective-permute-start = (bf16[16,1536]{1,0:T(8,128)(2,1)S(1)}, bf16[16,1536]{1,0:T(8,128)(2,1)S(1)}, u32[]{:S(2)}, u32[]{:S(2)}) collective-permute-start(bf16[16,1536]{1,0:T(8,128)(2,1)S(1)} %divide_convert_fusion), channel_id=1, source_target_pairs={{0,2},{2,4},{4,6},{6,8},{8,10},{10,12},{12,14},{14,16},{16,18},{18... | collective-permute-start | bytes 147464 | tf_op jit(solution)/shard_map/ppermute | solution.py:23
  49.6 4.3 %collective-permute-start.3 = (bf16[16,1536]{1,0:T(8,128)(2,1)S(1)}, bf16[16,1536]{1,0:T(8,128)(2,1)S(1)}, u32[]{:S(2)}, u32[]{:S(2)}) collective-permute-start(bf16[16,1536]{1,0:T(8,128)(2,1)S(1)} %collective-permute-done.2), channel_id=1, source_target_pairs={{0,4},{2,6},{4,0},{6,2},{8,12},{10,14},{12,8},{14,10},{16,20},{18,... | collective-permute-start | bytes 147464 | tf_op jit(solution)/shard_map/ppermute | solution.py:32
  53.9 3.4 %collective-permute-start.4 = (bf16[16,1536]{1,0:T(8,128)(2,1)S(1)}, bf16[16,1536]{1,0:T(8,128)(2,1)S(1)}, u32[]{:S(2)}, u32[]{:S(2)}) collective-permute-start(bf16[16,1536]{1,0:T(8,128)(2,1)S(1)} %collective-permute-done.3), channel_id=1, source_target_pairs={{0,8},{2,10},{4,12},{6,14},{8,0},{10,2},{12,4},{14,6},{16,24},{18,... | collective-permute-start | bytes 147464 | tf_op jit(solution)/shard_map/ppermute | solution.py:32
  57.2 3.8 %collective-permute-start.5 = (bf16[16,1536]{1,0:T(8,128)(2,1)S(1)}, bf16[16,1536]{1,0:T(8,128)(2,1)S(1)}, u32[]{:S(2)}, u32[]{:S(2)}) collective-permute-start(bf16[16,1536]{1,0:T(8,128)(2,1)S(1)} %collective-permute-done.4), channel_id=1, source_target_pairs={{0,16},{2,18},{4,20},{6,22},{8,24},{10,26},{12,28},{14,30},{16,0},... | collective-permute-start | bytes 147464 | tf_op jit(solution)/shard_map/ppermute | solution.py:32
  61.1 6.9 %collective-permute-start.6 = (bf16[16,1536]{1,0:T(8,128)(2,1)S(1)}, bf16[16,1536]{1,0:T(8,128)(2,1)S(1)}, u32[]{:S(2)}, u32[]{:S(2)}) collective-permute-start(bf16[16,1536]{1,0:T(8,128)(2,1)S(1)} %collective-permute-done.5), channel_id=1, source_target_pairs={{0,2},{2,4},{4,6},{6,8},{8,10},{10,12},{12,14},{14,16},{16,18},{18... | collective-permute-start | bytes 147464 | tf_op jit(solution)/shard_map/ppermute | solution.py:23
  65.9 5.4 %collective-permute-start.7 = (bf16[16,1536]{1,0:T(8,128)(2,1)S(1)}, bf16[16,1536]{1,0:T(8,128)(2,1)S(1)}, u32[]{:S(2)}, u32[]{:S(2)}) collective-permute-start(bf16[16,1536]{1,0:T(8,128)(2,1)S(1)} %collective-permute-done.5), channel_id=1, source_target_pairs={{2,0},{4,2},{6,4},{8,6},{10,8},{12,10},{14,12},{16,14},{18,16},{20... | collective-permute-start | bytes 147464 | tf_op jit(solution)/shard_map/ppermute | solution.py:24
  73.8 1.4 copy-start.2
  78.4 0.7 copy-start.3
  170.4 3.1 %copy-start.1 = (f32[1024,512]{1,0:T(8,128)S(1)}, f32[1024,512]{1,0:T(8,128)}, u32[]{:S(2)}) copy-start(f32[1024,512]{1,0:T(8,128)} %gather_fusion.2) | copy-start | bytes 6291460
Sparse Core Ops, SparseCore 0:
  78.5 64.4 all-reduce.1
where the time goes:
time: 189 us; the launch traced here: 188 us
  waiting for transfers between devices  72.5 us (38%)
  other arithmetic  41.2 us (22%)
  local copies, waits for them, and re-layouts  36.2 us (19%)
  starting transfers between devices  19.5 us (10%)
  between operations  13.8 us (7%)
  matrix products  4.48 us (2%)
    psum x1, waiting for transfers between devices, body(): stacked = lax.psum(flattened[0], 'tm')  63.9 us
    another operation x8, other arithmetic  35 us
    gather x8, local copies, waits for them, and re-layouts, curves(): shifted = jnp.take(stacked, stretch_index[stretch], axis=1, mode='clip')  30.4 us
    ppermute x2, starting transfers between devices, padded(): before = lax.ppermute(last, axis, up)  8.81 us
    ppermute x4, starting transfers between devices, from_partner(): return lax.ppermute(value, axis, pairs)  6.25 us
    ppermute x4, waiting for transfers between devices, from_partner(): return lax.ppermute(value, axis, pairs)  5.28 us
    reduce_sum x1, other arithmetic, curves(): numerator = jnp.mean(current * shifted[None], axis=-1)  4.77 us
    ppermute x2, starting transfers between devices, padded(): after = lax.ppermute(leading, axis, down)  4.45 us
  transfers between devices with their start and end apart: 9, of which 5 were waited for; matrix products, arithmetic and copies ran while one was open for 8% of the time, Pallas kernels for 0%

commit v1 on v0

v1 whole, which is shorter than its diff:
```python
import math

import jax
import jax.numpy as jnp
from jax import lax
from jax.sharding import PartitionSpec as P

NT = 1536
LAGS = 1024
NF = 768

epsilon = 1e-05


def unit_angles(numerators, period):
    phase = (numerators % period).astype(jnp.float32) * (2.0 * math.pi / period)
    return jnp.cos(phase), jnp.sin(phase)


def forward_table():
    coarse = NT // 64
    bins = jnp.arange(NF, dtype=jnp.int32)[None, :]
    cos_a, sin_a = unit_angles(jnp.arange(coarse, dtype=jnp.int32)[:, None] * bins, coarse)
    cos_c, sin_c = unit_angles(jnp.arange(64, dtype=jnp.int32)[:, None] * bins, NT)
    cos_t = cos_a[:, None, :] * cos_c[None] - sin_a[:, None, :] * sin_c[None]
    sin_t = sin_a[:, None, :] * cos_c[None] + cos_a[:, None, :] * sin_c[None]
    table = jnp.concatenate([cos_t, -sin_t], axis=-1).astype(jnp.bfloat16)
    return table.reshape(NT, 2 * NF)


def inverse_table():
    coarse = NT // 64
    groups = LAGS // 64
    bins = jnp.arange(NF, dtype=jnp.int32)[:, None]
    cos_a, sin_a = unit_angles(bins * (jnp.arange(groups, dtype=jnp.int32)[None, :] - groups // 2), coarse)
    cos_c, sin_c = unit_angles(bins * jnp.arange(64, dtype=jnp.int32)[None, :], NT)
    cos_t = cos_a[:, :, None] * cos_c[:, None, :] - sin_a[:, :, None] * sin_c[:, None, :]
    sin_t = sin_a[:, :, None] * cos_c[:, None, :] + cos_a[:, :, None] * sin_c[:, None, :]
    weight = jnp.where(bins == 0, 1.0, 2.0).astype(jnp.float32)[:, :, None]
    table = jnp.concatenate([weight * cos_t, -weight * sin_t], axis=0).astype(jnp.bfloat16)
    return table.reshape(2 * NF, LAGS)


def whiten(spectrum):
    power = jnp.mean(spectrum * spectrum, axis=-1, keepdims=True)
    return (spectrum / jnp.sqrt(power + epsilon)).astype(jnp.bfloat16)


def cross_spectrum(source_row, receivers):
    half_width = receivers.shape[-1] // 2
    source_vals = source_row.astype(jnp.float32)
    receiver_vals = receivers.astype(jnp.float32)
    src_re = source_vals[..., :half_width]
    src_im = source_vals[..., half_width:]
    rec_re = receiver_vals[..., :half_width]
    rec_im = receiver_vals[..., half_width:]
    real_part = src_re * rec_re + src_im * rec_im
    imag_part = src_re * rec_im - src_im * rec_re
    return jnp.concatenate([real_part, imag_part], axis=-1).astype(jnp.bfloat16)


def body(record, pairs, stretch_index):
    block_rows = record.shape[1]
    minutes = lax.axis_size("tm")
    blocks = lax.axis_size("chan")
    parts = [record]
    for shift in range(1, minutes):
        parts.append(
            lax.ppermute(record, "tm", [(i, (i + shift) % minutes) for i in range(minutes)])
        )
    own_block = jnp.concatenate(parts, axis=0)
    below = lax.ppermute(own_block, "chan", [(s, s + 1) for s in range(blocks - 1)])
    above = lax.ppermute(own_block, "chan", [(s, s - 1) for s in range(1, blocks)])
    far_low = lax.ppermute(own_block, "chan", [(s, blocks - 2 - s) for s in range(blocks - 1)])
    far_mid = lax.ppermute(own_block, "chan", [(s, blocks - 1 - s) for s in range(blocks)])
    far_high = lax.ppermute(own_block, "chan", [(s, blocks - s) for s in range(1, blocks)])
    candidates = jnp.concatenate([below, own_block, above, far_low, far_mid, far_high], axis=1)
    slot_rows = candidates.shape[1]
    spectrum = jnp.dot(
        candidates.reshape(minutes * slot_rows, NT), forward_table(),
        preferred_element_type=jnp.float32,
    )
    whitened = whiten(spectrum).reshape(minutes, slot_rows, 2 * NF)

    position = lax.axis_index("chan")
    column_index = jnp.arange(pairs.shape[1], dtype=jnp.int32)[None, :]
    is_near = column_index < pairs.shape[1] // 2
    near_slot = pairs - (position - 1) * block_rows
    far_slot = pairs - (blocks - 2 - position) * block_rows + 3 * block_rows
    slot_index = jnp.where(is_near, near_slot, far_slot)
    source_count, recv_count = slot_index.shape
    sources = whitened[:, block_rows:2 * block_rows:8]
    receivers = jnp.take(whitened, slot_index.reshape(-1), axis=1, mode="clip")
    receivers = receivers.reshape(minutes, source_count, recv_count, 2 * NF)
    crossed = cross_spectrum(sources[:, :, None, :], receivers)
    pair_count = source_count * recv_count
    crossed = crossed.reshape(minutes, pair_count, 2 * NF)
    correlation = jnp.einsum(
        "mpk,kl->mlp", crossed, inverse_table(), preferred_element_type=jnp.float32
    )
    current = correlation[0]
    stacked = jnp.sum(correlation, axis=0)
    current_power = jnp.mean(current * current, axis=0)
    stretch_count = stretch_index.shape[0]
    shifted = jnp.take(stacked, stretch_index.reshape(-1), axis=0, mode="clip")
    shifted = shifted.reshape(stretch_count, LAGS, pair_count)
    numerator = jnp.mean(current[None] * shifted, axis=1)
    shifted_power = jnp.mean(shifted * shifted, axis=1)
    result = numerator / jnp.sqrt((current_power[None] + epsilon) * (shifted_power + epsilon))
    return result.reshape(1, stretch_count, source_count, recv_count)


def solution(mesh):
    return jax.shard_map(
        body,
        mesh=mesh,
        in_specs=(P("tm", "chan", None), P("chan", None), P()),
        out_specs=P("tm", None, "chan", None),
        check_vma=False,
    )
```

time: 189 us -> 90.4 us (0.48)
  waiting for transfers between devices: 72.5 us -> 4.68 us
  other arithmetic: 41.2 us -> 19.5 us
  between operations: 13.8 us -> 0.33 us
  local copies, waits for them, and re-layouts: 36.2 us -> 42.3 us
    psum x1 -> x0, waiting for transfers between devices: 63.9 us -> none  [body(): stacked = lax.psum(flattened[0], 'tm')]
    another operation x9 -> x3, other arithmetic: 35.7 us -> 4.61 us
    ppermute x8 -> x6, waiting for transfers between devices: 8.55 us -> 4.68 us  [the longest x1 4.66 us: body(): lax.ppermute(own_block, 'chan', [(s, s - 1) for s in range(1, blocks)])]
    convert_element_type x1, other arithmetic: 0.39 us -> 4.05 us  [cross_spectrum(): receiver_vals = receivers.astype(jnp.float32)]
    gather x9 -> x2, local copies, waits for them, and re-layouts: 32.5 us -> 36 us  [the longest x1 19.2 us: body(): receivers = jnp.take(whitened, slot_index.reshape(-1), axis=1, mode='clip')]
    slice x2, local copies, waits for them, and re-layouts: 0.05 us -> 2.2 us  [the longest x1 2.16 us: cross_spectrum(): rec_re = receiver_vals[..., :half_width]]
    psum x1 -> x0, local copies, waits for them, and re-layouts: 1.92 us -> none  [body(): stacked = lax.psum(flattened[0], 'tm')]
    ppermute x8 -> x6, starting transfers between devices: 19.5 us -> 18.6 us  [the longest x1 5.22 us: body(): lax.ppermute(own_block, 'chan', [(s, blocks - 2 - s) for s in range(block...]
  transfers between devices with their start and end apart: 9 -> 6, of which waited for: 5 -> 1; matrix products, arithmetic and copies ran while one was open for 8% -> 10% of each run, Pallas kernels for 0% -> 0%
where the time goes in v1:
time: 90.4 us; the launch traced here: 90 us
  local copies, waits for them, and re-layouts  42.3 us (47%)
  other arithmetic  19.5 us (22%)
  starting transfers between devices  18.6 us (21%)
  waiting for transfers between devices  4.68 us (5%)
  matrix products  4.62 us (5%)
    gather x1, local copies, waits for them, and re-layouts, body(): receivers = jnp.take(whitened, slot_index.reshape(-1), axis=1, mode='clip')  19.2 us
    gather x1, local copies, waits for them, and re-layouts, body(): shifted = jnp.take(stacked, stretch_index.reshape(-1), axis=0, mode='clip')  16.7 us
    reduce_sum x1, other arithmetic, body(): shifted_power = jnp.mean(shifted * shifted, axis=1)  5.35 us
    ppermute x1, starting transfers between devices, body(): lax.ppermute(own_block, 'chan', [(s, blocks - 2 - s) for s in range(block...  5.22 us
    ppermute x1, waiting for transfers between devices, body(): lax.ppermute(own_block, 'chan', [(s, s - 1) for s in range(1, blocks)])  4.66 us
    another operation x3, other arithmetic  4.61 us
    convert_element_type x1, other arithmetic, cross_spectrum(): receiver_vals = receivers.astype(jnp.float32)  4.05 us
    ppermute x1, starting transfers between devices, body(): lax.ppermute(own_block, 'chan', [(s, s + 1) for s in range(blocks - 1)])  3.99 us
  transfers between devices with their start and end apart: 6, of which 1 were waited for; matrix products, arithmetic and copies ran while one was open for 10% of the time, Pallas kernels for 0%

profile of v1, /device:TPU:1, one launch (start us, length us, event | category | flops | bytes accessed | tf_op | source)
XLA Modules:
  0.0 90.0 jit_solution(11183597370489004223)
XLA Ops:
  0.0 2.0 %collective-permute-start = (bf16[1,16,1536]{2,1,0:T(8,128)(2,1)}, bf16[1,16,1536]{2,1,0:T(8,128)(2,1)S(1)}, u32[]{:S(2)}, u32[]{:S(2)}) collective-permute-start(bf16[1,16,1536]{2,1,0:T(8,128)(2,1)} %param.3), channel_id=1, source_target_pairs={{0,1},{1,0},{2,3},{3,2},{4,5},{5,4},{6,7},{7,6},{8,9},{9,8},{10,11... | collective-permute-start | bytes 147464 | tf_op jit(solution)/shard_map/ppermute | solution.py:69
  2.1 0.8 constant_dynamic-update-slice_fusion.1
  2.9 0.3 fusion.33
  3.2 0.7 fusion.26
  3.9 0.8 fusion.25
  4.7 0.8 fusion.21
  5.5 0.7 bitcast_clamp_fusion
  6.2 0.3 fusion.41
  6.5 1.6 %subtract_convert_fusion = (bf16[24,64,768]{2,1,0:T(8,128)(2,1)S(1)}, bf16[24,64,768]{2,1,0:T(8,128)(2,1)S(1)}) fusion(f32[64,768]{1,0:T(8,128)S(1)} %get-tuple-element.23, f32[24,768]{1,0:T(8,128)S(1)} %get-tuple-element.25, f32[64,768]{1,0:T(8,128)S(1)} %get-tuple-element.24, f32[24,768]{1,0:T(8,128)S(1)} %get-tuple-element.26), kind=kLoop, calls=%fused_computation.9 | loop fusion | flops 10616832 | bytes 5259264 | tf_op jit(solution)/shard_map/convert.9
  8.1 0.9 multiply_subtract_fusion
  9.0 0.0 copy-start.3
  9.0 0.0 copy-start.2
  9.0 2.2 %fusion.10 = (bf16[768,1024]{0,1:T(8,128)(2,1)}, bf16[768,1024]{0,1:T(8,128)(2,1)}) fusion(f32[768,16,64]{0,2,1:T(8,128)S(1)} %get-tuple-element.14, f32[768]{0:T(1024)S(1)} %fusion.44, f32[768,16,64]{0,2,1:T(8,128)S(1)} %get-tuple-element.13, f32[768]{0:T(1024)S(1)} %fusion.43), kind=kLoop, calls=%fused_computation.18 | loop fusion | flops 3145728 | bytes 9443328 | tf_op jit(solution)/shard_map/convert.11
  11.2 0.0 copy-done.3
  11.3 0.0 collective-permute-done
  11.3 4.0 %collective-permute-start.1 = (bf16[2,16,1536]{2,1,0:T(8,128)(2,1)S(1)}, bf16[2,16,1536]{2,1,0:T(8,128)(2,1)S(1)}, u32[]{:S(2)}, u32[]{:S(2)}) collective-permute-start(bf16[2,16,1536]{2,1,0:T(8,128)(2,1)S(1)} %constant_dynamic-update-slice_fusion), channel_id=1, source_target_pairs={{0,2},{2,4},{4,6},{6,8},{8,10},{10,12},{12,14},{14,16},{16,18},{18... | collective-permute-start | bytes 294920 | tf_op jit(solution)/shard_map/ppermute | solution.py:72
  15.3 3.5 %collective-permute-start.5 = (bf16[2,16,1536]{2,1,0:T(8,128)(2,1)S(1)}, bf16[2,16,1536]{2,1,0:T(8,128)(2,1)S(1)}, u32[]{:S(2)}, u32[]{:S(2)}) collective-permute-start(bf16[2,16,1536]{2,1,0:T(8,128)(2,1)S(1)} %constant_dynamic-update-slice_fusion), channel_id=1, source_target_pairs={{2,30},{4,28},{6,26},{8,24},{10,22},{12,20},{14,18},{16,16},{18,14... | collective-permute-start | bytes 294920 | tf_op jit(solution)/shard_map/ppermute | solution.py:76
  18.8 1.8 %collective-permute-start.4 = (bf16[2,16,1536]{2,1,0:T(8,128)(2,1)S(1)}, bf16[2,16,1536]{2,1,0:T(8,128)(2,1)S(1)}, u32[]{:S(2)}, u32[]{:S(2)}) collective-permute-start(bf16[2,16,1536]{2,1,0:T(8,128)(2,1)S(1)} %constant_dynamic-update-slice_fusion), channel_id=1, source_target_pairs={{0,30},{2,28},{4,26},{6,24},{8,22},{10,20},{12,18},{14,16},{16,14}... | collective-permute-start | bytes 294920 | tf_op jit(solution)/shard_map/ppermute | solution.py:75
  20.5 5.2 %collective-permute-start.3 = (bf16[2,16,1536]{2,1,0:T(8,128)(2,1)S(1)}, bf16[2,16,1536]{2,1,0:T(8,128)(2,1)S(1)}, u32[]{:S(2)}, u32[]{:S(2)}) collective-permute-start(bf16[2,16,1536]{2,1,0:T(8,128)(2,1)S(1)} %constant_dynamic-update-slice_fusion), channel_id=1, source_target_pairs={{0,28},{2,26},{4,24},{6,22},{8,20},{10,18},{12,16},{14,14},{16,12}... | collective-permute-start | bytes 294920 | tf_op jit(solution)/shard_map/ppermute | solution.py:74
  25.8 2.1 %collective-permute-start.2 = (bf16[2,16,1536]{2,1,0:T(8,128)(2,1)S(1)}, bf16[2,16,1536]{2,1,0:T(8,128)(2,1)S(1)}, u32[]{:S(2)}, u32[]{:S(2)}) collective-permute-start(bf16[2,16,1536]{2,1,0:T(8,128)(2,1)S(1)} %constant_dynamic-update-slice_fusion), channel_id=1, source_target_pairs={{2,0},{4,2},{6,4},{8,6},{10,8},{12,10},{14,12},{16,14},{18,16},{20... | collective-permute-start | bytes 294920 | tf_op jit(solution)/shard_map/ppermute | solution.py:73
  27.9 0.0 collective-permute-done.1
  27.9 0.0 copy-done.2
  27.9 4.7 %collective-permute-done.2 = bf16[2,16,1536]{2,1,0:T(8,128)(2,1)S(1)} collective-permute-done((bf16[2,16,1536]{2,1,0:T(8,128)(2,1)S(1)}, bf16[2,16,1536]{2,1,0:T(8,128)(2,1)S(1)}, u32[]{:S(2)}, u32[]{:S(2)}) %collective-permute-start.2) | collective-permute-done | bytes 98336 | tf_op jit(solution)/shard_map/ppermute | solution.py:73
  32.6 0.0 collective-permute-done.3
  32.6 0.0 collective-permute-done.4
  32.7 0.0 collective-permute-done.5
  32.7 1.2 %multiply_reduce_fusion.3 = (f32[192]{0:T(256)S(1)}, f32[192,1536]{1,0:T(8,128)S(1)}) fusion(bf16[192,1536]{1,0:T(8,128)(2,1)S(1)} %bitcast.61, bf16[1536,768]{1,0:T(8,128)(2,1)S(1)} %bitcast.55, bf16[1536,768]{1,0:T(8,128)(2,1)S(1)} %bitcast.54), kind=kOutput, calls=%fused_computation.29 | convolution fusion | flops 915996480 | bytes 6488832 | tf_op jit(solution)/shard_map/dot_general | solution.py:79
  33.9 0.2 divide_convert_fusion
  34.1 0.6 copy.4
  34.8 19.2 %gather_fusion = bf16[512,2,1536]{2,1,0:T(2,128)(2,1)} fusion(bf16[2,96,1536]{2,0,1:T(2,128)(2,1)S(1)} %copy.4, s32[1024]{0:T(1024)S(1)} %pad_clamp_fusion), kind=kCustom, calls=%fused_computation | custom fusion | bytes 6293504 | tf_op jit(solution)/shard_map/jit(_take)/gather | solution.py:93
  54.0 4.0 %convert_element_type.80 = f32[512,2,1536]{2,1,0:T(2,128)S(1)} convert(bf16[512,2,1536]{2,1,0:T(2,128)(2,1)} %gather_fusion) | non-fusion elementwise | flops 1572864 | bytes 9437184 | tf_op jit(solution)/shard_map/convert_element_type | solution.py:52
  58.1 2.2 %fusion.47 = (f32[2,2,256,768]{3,0,2,1:T(2,128)S(1)}, f32[2,2,256,768]{3,0,2,1:T(2,128)S(1)}) fusion(f32[2,2,256,1536]{3,0,2,1:T(2,128)S(1)} %bitcast.51), kind=kLoop, calls=%fused_computation.93 | loop fusion | bytes 12582912 | tf_op jit(solution)/shard_map/slice | solution.py:55
  60.2 0.0 copy-start
  60.2 0.0 copy-start.1
  60.2 0.8 add_convert_fusion
  61.0 0.6 copy-done
  61.6 0.5 copy-done.1
  62.1 3.4 %fusion.48 = (f32[1024,512]{1,0:T(8,128)S(1)}, f32[2,1024,512]{2,1,0:T(8,128)S(1)}) fusion(bf16[2,512,768]{2,1,0:T(8,128)(2,1)S(1)} %bitcast.57, bf16[2,512,768]{2,1,0:T(8,128)(2,1)S(1)} %bitcast.56, bf16[768,1024]{0,1:T(8,128)(2,1)S(1)} %copy-done, bf16[768,1024]{0,1:T(8,128)(2,1)S(1)} %copy-done.1), kind=kOutput, calls=%fused_computation.94 | convolution fusion | flops 3234332672 | bytes 12582912 | tf_op jit(solution)/shard_map/mpk,kl->mlp/dot_general | solution.py:98
  65.5 0.2 multiply_reduce_fusion.2
  65.8 1.5 %slice_bitcast_fusion = f32[1024,512]{1,0:T(8,128)} fusion(f32[2,1024,512]{2,1,0:T(8,128)S(1)} %get-tuple-element.22), kind=kLoop, calls=%fused_computation.26 | loop fusion | bytes 4194304 | tf_op jit(solution)/shard_map/mul | solution.py:107
  67.3 16.7 %gather_fusion.1 = f32[4096,512]{1,0:T(8,128)} fusion(f32[1024,512]{1,0:T(8,128)S(1)} %get-tuple-element.21, s32[4096]{0:T(1024)S(1)} %bitcast_clamp_fusion), kind=kCustom, calls=%fused_computation.1 | custom fusion | bytes 16793600 | tf_op jit(solution)/shard_map/jit(_take)/gather | solution.py:105
  84.0 5.3 %multiply_reduce_fusion = (f32[4,512]{1,0:T(4,128)S(1)}, f32[4,512]{1,0:T(4,128)S(1)}) fusion(f32[4096,512]{1,0:T(8,128)} %gather_fusion.1, f32[1024,512]{1,0:T(8,128)} %slice_bitcast_fusion), kind=kLoop, calls=%fused_computation.2 | loop fusion | flops 8384512 | bytes 10502144 | tf_op jit(solution)/shard_map/reduce_sum | solution.py:108
  89.4 0.6 rsqrt_multiply_fusion
  (26 shorter events, 0.2 us)
Async XLA Ops:
  0.0 11.3 %collective-permute-start = (bf16[1,16,1536]{2,1,0:T(8,128)(2,1)}, bf16[1,16,1536]{2,1,0:T(8,128)(2,1)S(1)}, u32[]{:S(2)}, u32[]{:S(2)}) collective-permute-start(bf16[1,16,1536]{2,1,0:T(8,128)(2,1)} %param.3), channel_id=1, source_target_pairs={{0,1},{1,0},{2,3},{3,2},{4,5},{5,4},{6,7},{7,6},{8,9},{9,8},{10,11... | collective-permute-start | bytes 147464 | tf_op jit(solution)/shard_map/ppermute | solution.py:69
  9.0 2.3 %copy-start.3 = (s32[2,256]{1,0:T(2,128)S(1)}, s32[2,256]{1,0:T(2,128)}, u32[]{:S(2)}) copy-start(s32[2,256]{1,0:T(2,128)} %param.4) | copy-start | bytes 6148
  9.0 18.9 %copy-start.2 = (bf16[1,16,1536]{2,1,0:T(8,128)(2,1)S(1)}, bf16[1,16,1536]{2,1,0:T(8,128)(2,1)}, u32[]{:S(2)}) copy-start(bf16[1,16,1536]{2,1,0:T(8,128)(2,1)} %param.3) | copy-start | bytes 147460
  11.3 16.6 %collective-permute-start.1 = (bf16[2,16,1536]{2,1,0:T(8,128)(2,1)S(1)}, bf16[2,16,1536]{2,1,0:T(8,128)(2,1)S(1)}, u32[]{:S(2)}, u32[]{:S(2)}) collective-permute-start(bf16[2,16,1536]{2,1,0:T(8,128)(2,1)S(1)} %constant_dynamic-update-slice_fusion), channel_id=1, source_target_pairs={{0,2},{2,4},{4,6},{6,8},{8,10},{10,12},{12,14},{14,16},{16,18},{18... | collective-permute-start | bytes 294920 | tf_op jit(solution)/shard_map/ppermute | solution.py:72
  15.3 17.4 %collective-permute-start.5 = (bf16[2,16,1536]{2,1,0:T(8,128)(2,1)S(1)}, bf16[2,16,1536]{2,1,0:T(8,128)(2,1)S(1)}, u32[]{:S(2)}, u32[]{:S(2)}) collective-permute-start(bf16[2,16,1536]{2,1,0:T(8,128)(2,1)S(1)} %constant_dynamic-update-slice_fusion), channel_id=1, source_target_pairs={{2,30},{4,28},{6,26},{8,24},{10,22},{12,20},{14,18},{16,16},{18,14... | collective-permute-start | bytes 294920 | tf_op jit(solution)/shard_map/ppermute | solution.py:76
  18.8 13.9 %collective-permute-start.4 = (bf16[2,16,1536]{2,1,0:T(8,128)(2,1)S(1)}, bf16[2,16,1536]{2,1,0:T(8,128)(2,1)S(1)}, u32[]{:S(2)}, u32[]{:S(2)}) collective-permute-start(bf16[2,16,1536]{2,1,0:T(8,128)(2,1)S(1)} %constant_dynamic-update-slice_fusion), channel_id=1, source_target_pairs={{0,30},{2,28},{4,26},{6,24},{8,22},{10,20},{12,18},{14,16},{16,14}... | collective-permute-start | bytes 294920 | tf_op jit(solution)/shard_map/ppermute | solution.py:75
  20.5 12.1 %collective-permute-start.3 = (bf16[2,16,1536]{2,1,0:T(8,128)(2,1)S(1)}, bf16[2,16,1536]{2,1,0:T(8,128)(2,1)S(1)}, u32[]{:S(2)}, u32[]{:S(2)}) collective-permute-start(bf16[2,16,1536]{2,1,0:T(8,128)(2,1)S(1)} %constant_dynamic-update-slice_fusion), channel_id=1, source_target_pairs={{0,28},{2,26},{4,24},{6,22},{8,20},{10,18},{12,16},{14,14},{16,12}... | collective-permute-start | bytes 294920 | tf_op jit(solution)/shard_map/ppermute | solution.py:74
  25.8 6.8 %collective-permute-start.2 = (bf16[2,16,1536]{2,1,0:T(8,128)(2,1)S(1)}, bf16[2,16,1536]{2,1,0:T(8,128)(2,1)S(1)}, u32[]{:S(2)}, u32[]{:S(2)}) collective-permute-start(bf16[2,16,1536]{2,1,0:T(8,128)(2,1)S(1)} %constant_dynamic-update-slice_fusion), channel_id=1, source_target_pairs={{2,0},{4,2},{6,4},{8,6},{10,8},{12,10},{14,12},{16,14},{18,16},{20... | collective-permute-start | bytes 294920 | tf_op jit(solution)/shard_map/ppermute | solution.py:73
  60.2 1.4 %copy-start = (bf16[768,1024]{0,1:T(8,128)(2,1)S(1)}, bf16[768,1024]{0,1:T(8,128)(2,1)}, u32[]{:S(2)}) copy-start(bf16[768,1024]{0,1:T(8,128)(2,1)} %get-tuple-element.27) | copy-start | bytes 4718596
  60.2 1.9 %copy-start.1 = (bf16[768,1024]{0,1:T(8,128)(2,1)S(1)}, bf16[768,1024]{0,1:T(8,128)(2,1)}, u32[]{:S(2)}) copy-start(bf16[768,1024]{0,1:T(8,128)(2,1)} %get-tuple-element.28) | copy-start | bytes 4718596

commit v2 on v1

--- a/solution.py
+++ b/solution.py
@@ -89,24 +89,39 @@
     far_slot = pairs - (blocks - 2 - position) * block_rows + 3 * block_rows
     slot_index = jnp.where(is_near, near_slot, far_slot)
     source_count, recv_count = slot_index.shape
+    pair_count = source_count * recv_count
     sources = whitened[:, block_rows:2 * block_rows:8]
-    receivers = jnp.take(whitened, slot_index.reshape(-1), axis=1, mode="clip")
+    selector = (
+        slot_index.reshape(pair_count, 1) == jnp.arange(slot_rows, dtype=jnp.int32)[None, :]
+    ).astype(jnp.bfloat16)
+    receivers = jnp.einsum(
+        "pq,mqk->mpk", selector, whitened, preferred_element_type=jnp.float32
+    )
     receivers = receivers.reshape(minutes, source_count, recv_count, 2 * NF)
     crossed = cross_spectrum(sources[:, :, None, :], receivers)
-    pair_count = source_count * recv_count
     crossed = crossed.reshape(minutes, pair_count, 2 * NF)
     correlation = jnp.einsum(
-        "mpk,kl->mlp", crossed, inverse_table(), preferred_element_type=jnp.float32
+        "mpk,kl->mpl", crossed, inverse_table(), preferred_element_type=jnp.float32
     )
     current = correlation[0]
     stacked = jnp.sum(correlation, axis=0)
-    current_power = jnp.mean(current * current, axis=0)
+    current_power = jnp.mean(current * current, axis=-1)
     stretch_count = stretch_index.shape[0]
-    shifted = jnp.take(stacked, stretch_index.reshape(-1), axis=0, mode="clip")
-    shifted = shifted.reshape(stretch_count, LAGS, pair_count)
-    numerator = jnp.mean(current[None] * shifted, axis=1)
-    shifted_power = jnp.mean(shifted * shifted, axis=1)
-    result = numerator / jnp.sqrt((current_power[None] + epsilon) * (shifted_power + epsilon))
+    picks = (
+        jnp.arange(LAGS, dtype=jnp.int32)[:, None, None] == stretch_index[None, 1:, :]
+    ).astype(jnp.bfloat16).reshape(LAGS, (stretch_count - 1) * LAGS)
+    stacked_high = stacked.astype(jnp.bfloat16)
+    stacked_low = (stacked - stacked_high.astype(jnp.float32)).astype(jnp.bfloat16)
+    moved = jnp.dot(
+        jnp.concatenate([stacked_high, stacked_low], axis=0), picks,
+        preferred_element_type=jnp.float32,
+    )
+    moved = (moved[:pair_count] + moved[pair_count:]).reshape(pair_count, stretch_count - 1, LAGS)
+    shifted = jnp.concatenate([stacked[:, None, :], moved], axis=1)
+    numerator = jnp.mean(current[:, None, :] * shifted, axis=-1)
+    shifted_power = jnp.mean(shifted * shifted, axis=-1)
+    result = numerator / jnp.sqrt((current_power[:, None] + epsilon) * (shifted_power + epsilon))
+    result = result.T
     return result.reshape(1, stretch_count, source_count, recv_count)
 
 

time: 90.4 us -> 89.7 us (level)
  local copies, waits for them, and re-layouts: 42.3 us -> 23.5 us
  matrix products: 4.62 us -> 16.8 us
  other arithmetic: 19.5 us -> 26.1 us
    gather x2 -> x0, local copies, waits for them, and re-layouts: 36 us -> none  [the longest x1 19.2 us: body(): receivers = jnp.take(whitened, slot_index.reshape(-1), axis=1, mode='clip')]
    dot_general x1 -> x3, matrix products: 3.43 us -> 13.9 us  [the longest x1 8.18 us: body(): jnp.dot(jnp.concatenate([stacked_high, stacked_low], axis=0), picks, pref...]
    add x2, local copies, waits for them, and re-layouts: 0.03 us -> 8.94 us  [the longest x1 6.57 us: body(): moved[:pair_count] + moved[pair_count:]]
    another operation x3 -> x4, other arithmetic: 4.61 us -> 8.66 us
    add x2, other arithmetic: 0.01 us -> 3.77 us  [the longest x1 3.77 us: body(): moved[:pair_count] + moved[pair_count:]]
    sub x0 -> x1, local copies, waits for them, and re-layouts: none -> 3.51 us  [inverse_table(): cos_a[:, :, None] * cos_c[:, None, :]]
    broadcast_in_dim x0 -> x1, local copies, waits for them, and re-layouts: none -> 2.88 us  [body(): shifted = jnp.concatenate([stacked[:, None, :], moved], axis=1)]
    slice x1, local copies, waits for them, and re-layouts: 2.16 us -> 0.01 us  [body(): stretch_index[None, 1:, :]]
  transfers between devices with their start and end apart: 6 -> 6, of which waited for: 1 -> 1; matrix products, arithmetic and copies ran while one was open for 10% -> 24% of each run, Pallas kernels for 0% -> 0%
where the time goes in v2:
time: 89.7 us; the launch traced here: 89.1 us
  other arithmetic  26.1 us (29%)
  local copies, waits for them, and re-layouts  23.5 us (26%)
  starting transfers between devices  18.6 us (21%)
  matrix products  16.8 us (19%)
  waiting for transfers between devices  3.88 us (4%)
    another operation x4, other arithmetic  8.66 us
    dot_general x1, matrix products, body(): jnp.dot(jnp.concatenate([stacked_high, stacked_low], axis=0), picks, pref...  8.18 us
    add x1, local copies, waits for them, and re-layouts, body(): moved[:pair_count] + moved[pair_count:]  6.57 us
    ppermute x1, starting transfers between devices, body(): lax.ppermute(own_block, 'chan', [(s, blocks - 2 - s) for s in range(block...  5.22 us
    dot_general x1, matrix products, body(): jnp.einsum('mpk,kl->mpl', crossed, inverse_table(), preferred_element_typ...  4.74 us
    reduce_sum x1, other arithmetic, body(): numerator = jnp.mean(current[:, None, :] * shifted, axis=-1)  4.05 us
    ppermute x1, starting transfers between devices, body(): lax.ppermute(own_block, 'chan', [(s, s + 1) for s in range(blocks - 1)])  3.98 us
    ppermute x1, waiting for transfers between devices, body(): lax.ppermute(own_block, 'chan', [(s, s - 1) for s in range(1, blocks)])  3.87 us
  transfers between devices with their start and end apart: 6, of which 1 were waited for; matrix products, arithmetic and copies ran while one was open for 24% of the time, Pallas kernels for 0%

profile of v2, /device:TPU:1, one launch (start us, length us, event | category | flops | bytes accessed | tf_op | source)
XLA Modules:
  0.0 89.1 jit_solution(9354552635042839307)
XLA Ops:
  0.0 2.0 %collective-permute-start = (bf16[1,16,1536]{2,1,0:T(8,128)(2,1)}, bf16[1,16,1536]{2,1,0:T(8,128)(2,1)}, u32[]{:S(2)}, u32[]{:S(2)}) collective-permute-start(bf16[1,16,1536]{2,1,0:T(8,128)(2,1)} %param.3), channel_id=1, source_target_pairs={{0,1},{1,0},{2,3},{3,2},{4,5},{5,4},{6,7},{7,6},{8,9},{9,8},{10,11... | collective-permute-start | bytes 147464 | tf_op jit(solution)/shard_map/ppermute | solution.py:69
  2.1 1.4 %constant_dynamic-update-slice_fusion.1 = bf16[2,16,1536]{2,1,0:T(8,128)(2,1)} fusion(bf16[1,16,1536]{2,1,0:T(8,128)(2,1)} %param.3), kind=kLoop, calls=%fused_computation.75 | loop fusion | bytes 98304
  3.5 1.0 %fusion.37 = (f32[24,768]{1,0:T(8,128)}, f32[24,768]{1,0:T(8,128)}) fusion(), kind=kLoop, calls=%fused_computation.63 | loop fusion | flops 165888 | bytes 147456 | tf_op jit(solution)/shard_map/sin | solution.py:17
  4.5 0.8 fusion.25
  5.3 0.8 fusion.21
  6.1 0.3 fusion.45
  6.4 2.5 %multiply_subtract_fusion = (f32[768,16,64]{0,2,1:T(8,128)}, f32[768,16,64]{0,2,1:T(8,128)S(1)}) fusion(f32[768,64]{0,1:T(8,128)S(1)} %get-tuple-element.23, f32[768,16]{0,1:T(8,128)S(1)} %get-tuple-element.18, f32[768,64]{0,1:T(8,128)S(1)} %get-tuple-element.24, f32[768,16]{0,1:T(8,128)S(1)} %get-tuple-element.17), kind=kLoop, calls=%fused_computation.23 | loop fusion | flops 4718592 | bytes 6782976 | tf_op jit(solution)/shard_map/sub | solution.py:37
  8.9 3.5 %copy.8 = f32[768,1024]{1,0:T(8,128)} copy(f32[768,1024]{0,1:T(8,128)} %bitcast.42) | data formatting | bytes 6291456 | tf_op jit(solution)/shard_map/sub | solution.py:37
  12.4 2.4 %copy.9 = f32[768,1024]{1,0:T(8,128)} copy(f32[768,1024]{0,1:T(8,128)S(1)} %bitcast.41) | data formatting | bytes 6291456 | tf_op jit(solution)/shard_map/add | solution.py:38
  14.8 0.0 copy-start
  14.8 3.4 %multiply_convert_fusion.1 = bf16[768,1024]{1,0:T(8,128)(2,1)} fusion(f32[768,1024]{1,0:T(8,128)} %copy.8, f32[768]{0:T(1024)S(1)} %fusion.47), kind=kLoop, calls=%fused_computation.22 | loop fusion | flops 1572864 | bytes 4721664 | tf_op jit(solution)/shard_map/convert.1
  18.2 0.0 copy-done
  18.2 0.0 copy-start.3
  18.2 0.0 copy-start.4
  18.2 1.4 %multiply_convert_fusion = bf16[768,1024]{1,0:T(8,128)(2,1)} fusion(f32[768,1024]{1,0:T(8,128)S(1)} %copy-done, f32[768]{0:T(1024)S(1)} %fusion.48), kind=kLoop, calls=%fused_computation.20 | loop fusion | flops 1572864 | bytes 4721664 | tf_op jit(solution)/shard_map/convert.2
  19.6 0.0 copy-start.6
  19.6 0.0 copy-start.8
  19.6 0.0 copy-start.7
  19.6 0.0 copy-start.5
  19.6 0.0 copy-done.3
  19.6 0.0 copy-done.4
  19.6 2.9 %subtract_convert_fusion = (bf16[24,64,768]{2,1,0:T(8,128)(2,1)S(1)}, bf16[24,64,768]{2,1,0:T(8,128)(2,1)}) fusion(f32[64,768]{1,0:T(8,128)S(1)} %get-tuple-element.25, f32[24,768]{1,0:T(8,128)S(1)} %copy-done.3, f32[64,768]{1,0:T(8,128)S(1)} %get-tuple-element.26, f32[24,768]{1,0:T(8,128)S(1)} %copy-done.4), kind=kLoop, calls=%fused_computation.12 | loop fusion | flops 10616832 | bytes 5259264 | tf_op jit(solution)/shard_map/convert.10
  22.6 0.0 collective-permute-done
  22.6 0.0 copy-done.6
  22.6 0.8 constant_dynamic-update-slice_fusion
  23.4 4.0 %collective-permute-start.1 = (bf16[2,16,1536]{2,1,0:T(8,128)(2,1)S(1)}, bf16[2,16,1536]{2,1,0:T(8,128)(2,1)S(1)}, u32[]{:S(2)}, u32[]{:S(2)}) collective-permute-start(bf16[2,16,1536]{2,1,0:T(8,128)(2,1)S(1)} %constant_dynamic-update-slice_fusion), channel_id=1, source_target_pairs={{0,2},{2,4},{4,6},{6,8},{8,10},{10,12},{12,14},{14,16},{16,18},{18... | collective-permute-start | bytes 294920 | tf_op jit(solution)/shard_map/ppermute | solution.py:72
  27.4 0.0 copy-done.8
  27.4 0.0 copy-done.7
  27.5 3.5 %collective-permute-start.5 = (bf16[2,16,1536]{2,1,0:T(8,128)(2,1)S(1)}, bf16[2,16,1536]{2,1,0:T(8,128)(2,1)S(1)}, u32[]{:S(2)}, u32[]{:S(2)}) collective-permute-start(bf16[2,16,1536]{2,1,0:T(8,128)(2,1)S(1)} %constant_dynamic-update-slice_fusion), channel_id=1, source_target_pairs={{2,30},{4,28},{6,26},{8,24},{10,22},{12,20},{14,18},{16,16},{18,14... | collective-permute-start | bytes 294920 | tf_op jit(solution)/shard_map/ppermute | solution.py:76
  30.9 1.8 %collective-permute-start.4 = (bf16[2,16,1536]{2,1,0:T(8,128)(2,1)S(1)}, bf16[2,16,1536]{2,1,0:T(8,128)(2,1)S(1)}, u32[]{:S(2)}, u32[]{:S(2)}) collective-permute-start(bf16[2,16,1536]{2,1,0:T(8,128)(2,1)S(1)} %constant_dynamic-update-slice_fusion), channel_id=1, source_target_pairs={{0,30},{2,28},{4,26},{6,24},{8,22},{10,20},{12,18},{14,16},{16,14}... | collective-permute-start | bytes 294920 | tf_op jit(solution)/shard_map/ppermute | solution.py:75
  32.7 5.2 %collective-permute-start.3 = (bf16[2,16,1536]{2,1,0:T(8,128)(2,1)S(1)}, bf16[2,16,1536]{2,1,0:T(8,128)(2,1)S(1)}, u32[]{:S(2)}, u32[]{:S(2)}) collective-permute-start(bf16[2,16,1536]{2,1,0:T(8,128)(2,1)S(1)} %constant_dynamic-update-slice_fusion), channel_id=1, source_target_pairs={{0,28},{2,26},{4,24},{6,22},{8,20},{10,18},{12,16},{14,14},{16,12}... | collective-permute-start | bytes 294920 | tf_op jit(solution)/shard_map/ppermute | solution.py:74
  37.9 2.1 %collective-permute-start.2 = (bf16[2,16,1536]{2,1,0:T(8,128)(2,1)S(1)}, bf16[2,16,1536]{2,1,0:T(8,128)(2,1)S(1)}, u32[]{:S(2)}, u32[]{:S(2)}) collective-permute-start(bf16[2,16,1536]{2,1,0:T(8,128)(2,1)S(1)} %constant_dynamic-update-slice_fusion), channel_id=1, source_target_pairs={{2,0},{4,2},{6,4},{8,6},{10,8},{12,10},{14,12},{16,14},{18,16},{20... | collective-permute-start | bytes 294920 | tf_op jit(solution)/shard_map/ppermute | solution.py:73
  40.0 0.0 collective-permute-done.1
  40.1 0.0 copy-done.5
  40.1 0.8 constant_dynamic-update-slice_fusion.6
  40.9 3.9 %collective-permute-done.2 = bf16[2,16,1536]{2,1,0:T(8,128)(2,1)S(1)} collective-permute-done((bf16[2,16,1536]{2,1,0:T(8,128)(2,1)S(1)}, bf16[2,16,1536]{2,1,0:T(8,128)(2,1)S(1)}, u32[]{:S(2)}, u32[]{:S(2)}) %collective-permute-start.2) | collective-permute-done | bytes 98336 | tf_op jit(solution)/shard_map/ppermute | solution.py:73
  44.8 0.0 collective-permute-done.3
  44.8 0.0 collective-permute-done.4
  44.8 0.0 collective-permute-done.5
  44.9 2.9 %multiply_reduce_fusion.3 = (f32[192]{0:T(256)S(1)}, f32[192,1536]{1,0:T(8,128)S(1)}) fusion(bf16[192,1536]{1,0:T(8,128)(2,1)S(1)} %bitcast.50, bf16[1536,768]{1,0:T(8,128)(2,1)} %bitcast.47, bf16[1536,768]{1,0:T(8,128)(2,1)S(1)} %bitcast.46), kind=kOutput, calls=%fused_computation.33 | convolution fusion | flops 915996480 | bytes 6488832 | tf_op jit(solution)/shard_map/dot_general | solution.py:79
  47.7 0.2 divide_convert_fusion
  48.0 1.0 %fusion.30 = f32[2,1536,512]{1,2,0:T(8,128)S(1)} fusion(bf16[2,96,1536]{2,1,0:T(8,128)(2,1)S(1)} %bitcast.45, s32[512]{0:T(512)S(1)} %bitcast.51), kind=kOutput, calls=%fused_computation.54 | convolution fusion | flops 302039040 | bytes 6883328 | tf_op jit(solution)/shard_map/pq,mqk->mpk/dot_general | solution.py:97
  49.0 0.0 copy-start.1
  49.0 0.0 copy-start.2
  49.0 0.9 %add_convert_fusion = (bf16[2,2,256,768]{3,2,1,0:T(8,128)(2,1)S(1)}, bf16[2,2,256,768]{3,2,1,0:T(8,128)(2,1)S(1)}) fusion(f32[2,2,256,1536]{3,2,1,0:T(8,128)S(1)} %bitcast.40, f32[2,2,768]{2,1,0:T(2,128)S(1)} %get-tuple-element.16, f32[2,2,768]{2,1,0:T(2,128)S(1)} %get-tuple-element.15), kind=kLoop, calls=%fused_computation.25 | loop fusion | flops 6291456 | bytes 9461760 | tf_op jit(solution)/shard_map/convert.6
  49.9 0.5 copy-done.1
  50.4 0.5 copy-done.2
  50.9 4.7 %fusion.52 = (f32[512,1024]{1,0:T(8,128)}, f32[2,512,1024]{2,1,0:T(8,128)S(1)}) fusion(bf16[768,1024]{1,0:T(8,128)(2,1)S(1)} %copy-done.2, bf16[768,1024]{1,0:T(8,128)(2,1)S(1)} %copy-done.1, bf16[2,512,768]{2,1,0:T(8,128)(2,1)S(1)} %bitcast.49, bf16[2,512,768]{2,1,0:T(8,128)(2,1)S(1)} %bitcast.48), kind=kOutput, calls=%fused_computation.98 | convolution fusion | flops 3234332672 | bytes 12582912 | tf_op jit(solution)/shard_map/mpk,kl->mpl/dot_general | solution.py:103
  55.6 0.2 multiply_reduce_fusion.2
  55.8 1.5 %slice_bitcast_fusion = f32[512,1024]{1,0:T(8,128)} fusion(f32[2,512,1024]{2,1,0:T(8,128)S(1)} %get-tuple-element.22), kind=kLoop, calls=%fused_computation.26 | loop fusion | bytes 4194304 | tf_op jit(solution)/shard_map/mul | solution.py:121
  57.3 1.9 %copy.10 = f32[512,1024]{0,1:T(8,128)S(1)} copy(f32[512,1024]{1,0:T(8,128)} %slice_bitcast_fusion) | data formatting | bytes 4194304 | tf_op jit(solution)/shard_map/mul | solution.py:121
  59.2 3.8 %subtract_convert_fusion.2 = (bf16[512,1024]{1,0:T(8,128)(2,1)S(1)}, bf16[512,1024]{1,0:T(8,128)(2,1)}) fusion(f32[512,1024]{1,0:T(8,128)} %get-tuple-element.21), kind=kLoop, calls=%fused_computation.31 | loop fusion | flops 2097152 | bytes 4194304 | tf_op jit(solution)/shard_map/convert_element_type | solution.py:114
  63.0 2.9 %copy.12 = f32[512,1,1024]{0,2,1:T(8,128)} copy(f32[512,1,1024]{2,0,1:T(8,128)} %bitcast.43) | data formatting | bytes 4194304 | tf_op jit(solution)/shard_map/broadcast_in_dim | solution.py:120
  65.9 8.2 %fusion = f32[1024,3072]{1,0:T(8,128)S(1)} fusion(s32[3072]{0:T(1024)S(1)} %eq.64, bf16[512,1024]{1,0:T(8,128)(2,1)S(1)} %get-tuple-element.7, bf16[512,1024]{1,0:T(8,128)(2,1)} %get-tuple-element.8), kind=kOutput, calls=%fused_computation.1 | convolution fusion | flops 6449790976 | bytes 14692352 | tf_op jit(solution)/shard_map/dot_general | solution.py:115
  74.1 3.8 %slice_add_fusion = f32[512,3072]{1,0:T(8,128)} fusion(f32[1024,3072]{1,0:T(8,128)S(1)} %fusion), kind=kLoop, calls=%fused_computation.5 | loop fusion | flops 1572864 | bytes 18874368 | tf_op jit(solution)/shard_map/add | solution.py:119
  77.9 6.6 %copy.11 = f32[512,3072]{0,1:T(8,128)} copy(f32[512,3072]{1,0:T(8,128)} %slice_add_fusion) | data formatting | bytes 12582912 | tf_op jit(solution)/shard_map/add | solution.py:119
  84.4 4.0 %multiply_reduce_fusion.1 = (f32[512,4]{0,1:T(4,128)S(1)}, f32[512,4]{0,1:T(4,128)S(1)}) fusion(f32[512,3,1024]{0,2,1:T(8,128)} %bitcast.39, f32[512,1,1024]{0,2,1:T(8,128)} %copy.12, f32[512,1024]{0,1:T(8,128)S(1)} %copy.10), kind=kLoop, calls=%fused_computation.4 | loop fusion | flops 10481664 | bytes 10502144 | tf_op jit(solution)/shard_map/reduce_sum | solution.py:121
  88.5 0.6 reshape.242
  (20 shorter events, 0.2 us)
Async XLA Ops:
  0.0 22.6 %collective-permute-start = (bf16[1,16,1536]{2,1,0:T(8,128)(2,1)}, bf16[1,16,1536]{2,1,0:T(8,128)(2,1)}, u32[]{:S(2)}, u32[]{:S(2)}) collective-permute-start(bf16[1,16,1536]{2,1,0:T(8,128)(2,1)} %param.3), channel_id=1, source_target_pairs={{0,1},{1,0},{2,3},{3,2},{4,5},{5,4},{6,7},{7,6},{8,9},{9,8},{10,11... | collective-permute-start | bytes 147464 | tf_op jit(solution)/shard_map/ppermute | solution.py:69
  14.8 3.4 %copy-start = (f32[768,1024]{1,0:T(8,128)S(1)}, f32[768,1024]{1,0:T(8,128)}, u32[]{:S(2)}) copy-start(f32[768,1024]{1,0:T(8,128)} %copy.9) | copy-start | bytes 9437188
  18.2 1.4 %copy-start.3 = (f32[24,768]{1,0:T(8,128)S(1)}, f32[24,768]{1,0:T(8,128)}, u32[]{:S(2)}) copy-start(f32[24,768]{1,0:T(8,128)} %get-tuple-element.27) | copy-start | bytes 221188
  18.2 1.4 %copy-start.4 = (f32[24,768]{1,0:T(8,128)S(1)}, f32[24,768]{1,0:T(8,128)}, u32[]{:S(2)}) copy-start(f32[24,768]{1,0:T(8,128)} %get-tuple-element.28) | copy-start | bytes 221188
  19.6 3.0 %copy-start.6 = (bf16[2,16,1536]{2,1,0:T(8,128)(2,1)S(1)}, bf16[2,16,1536]{2,1,0:T(8,128)(2,1)}, u32[]{:S(2)}) copy-start(bf16[2,16,1536]{2,1,0:T(8,128)(2,1)} %constant_dynamic-update-slice_fusion.1) | copy-start | bytes 294916
  19.6 7.8 %copy-start.8 = (s32[2,256]{1,0:T(2,128)S(1)}, s32[2,256]{1,0:T(2,128)}, u32[]{:S(2)}) copy-start(s32[2,256]{1,0:T(2,128)} %param.4) | copy-start | bytes 6148
  19.6 7.8 %copy-start.7 = (s32[4,1024]{1,0:T(4,128)S(1)}, s32[4,1024]{1,0:T(4,128)}, u32[]{:S(2)}) copy-start(s32[4,1024]{1,0:T(4,128)} %param.5) | copy-start | bytes 49156
  19.6 20.5 %copy-start.5 = (bf16[1,16,1536]{2,1,0:T(8,128)(2,1)S(1)}, bf16[1,16,1536]{2,1,0:T(8,128)(2,1)}, u32[]{:S(2)}) copy-start(bf16[1,16,1536]{2,1,0:T(8,128)(2,1)} %param.3) | copy-start | bytes 147460
  23.4 16.7 %collective-permute-start.1 = (bf16[2,16,1536]{2,1,0:T(8,128)(2,1)S(1)}, bf16[2,16,1536]{2,1,0:T(8,128)(2,1)S(1)}, u32[]{:S(2)}, u32[]{:S(2)}) collective-permute-start(bf16[2,16,1536]{2,1,0:T(8,128)(2,1)S(1)} %constant_dynamic-update-slice_fusion), channel_id=1, source_target_pairs={{0,2},{2,4},{4,6},{6,8},{8,10},{10,12},{12,14},{14,16},{16,18},{18... | collective-permute-start | bytes 294920 | tf_op jit(solution)/shard_map/ppermute | solution.py:72
  27.5 17.4 %collective-permute-start.5 = (bf16[2,16,1536]{2,1,0:T(8,128)(2,1)S(1)}, bf16[2,16,1536]{2,1,0:T(8,128)(2,1)S(1)}, u32[]{:S(2)}, u32[]{:S(2)}) collective-permute-start(bf16[2,16,1536]{2,1,0:T(8,128)(2,1)S(1)} %constant_dynamic-update-slice_fusion), channel_id=1, source_target_pairs={{2,30},{4,28},{6,26},{8,24},{10,22},{12,20},{14,18},{16,16},{18,14... | collective-permute-start | bytes 294920 | tf_op jit(solution)/shard_map/ppermute | solution.py:76
  30.9 13.9 %collective-permute-start.4 = (bf16[2,16,1536]{2,1,0:T(8,128)(2,1)S(1)}, bf16[2,16,1536]{2,1,0:T(8,128)(2,1)S(1)}, u32[]{:S(2)}, u32[]{:S(2)}) collective-permute-start(bf16[2,16,1536]{2,1,0:T(8,128)(2,1)S(1)} %constant_dynamic-update-slice_fusion), channel_id=1, source_target_pairs={{0,30},{2,28},{4,26},{6,24},{8,22},{10,20},{12,18},{14,16},{16,14}... | collective-permute-start | bytes 294920 | tf_op jit(solution)/shard_map/ppermute | solution.py:75
  32.7 12.1 %collective-permute-start.3 = (bf16[2,16,1536]{2,1,0:T(8,128)(2,1)S(1)}, bf16[2,16,1536]{2,1,0:T(8,128)(2,1)S(1)}, u32[]{:S(2)}, u32[]{:S(2)}) collective-permute-start(bf16[2,16,1536]{2,1,0:T(8,128)(2,1)S(1)} %constant_dynamic-update-slice_fusion), channel_id=1, source_target_pairs={{0,28},{2,26},{4,24},{6,22},{8,20},{10,18},{12,16},{14,14},{16,12}... | collective-permute-start | bytes 294920 | tf_op jit(solution)/shard_map/ppermute | solution.py:74
  37.9 6.8 %collective-permute-start.2 = (bf16[2,16,1536]{2,1,0:T(8,128)(2,1)S(1)}, bf16[2,16,1536]{2,1,0:T(8,128)(2,1)S(1)}, u32[]{:S(2)}, u32[]{:S(2)}) collective-permute-start(bf16[2,16,1536]{2,1,0:T(8,128)(2,1)S(1)} %constant_dynamic-update-slice_fusion), channel_id=1, source_target_pairs={{2,0},{4,2},{6,4},{8,6},{10,8},{12,10},{14,12},{16,14},{18,16},{20... | collective-permute-start | bytes 294920 | tf_op jit(solution)/shard_map/ppermute | solution.py:73
  49.0 1.4 %copy-start.1 = (bf16[768,1024]{1,0:T(8,128)(2,1)S(1)}, bf16[768,1024]{1,0:T(8,128)(2,1)}, u32[]{:S(2)}) copy-start(bf16[768,1024]{1,0:T(8,128)(2,1)} %multiply_convert_fusion.1) | copy-start | bytes 4718596
  49.0 1.9 %copy-start.2 = (bf16[768,1024]{1,0:T(8,128)(2,1)S(1)}, bf16[768,1024]{1,0:T(8,128)(2,1)}, u32[]{:S(2)}) copy-start(bf16[768,1024]{1,0:T(8,128)(2,1)} %multiply_convert_fusion) | copy-start | bytes 4718596

commit v3 on v2

--- a/solution.py
+++ b/solution.py
@@ -1,3 +1,4 @@
+import functools
 import math
 
 import jax
@@ -18,10 +19,10 @@
 
 
 def forward_table():
-    coarse = NT // 64
+    coarse = NT // 128
     bins = jnp.arange(NF, dtype=jnp.int32)[None, :]
     cos_a, sin_a = unit_angles(jnp.arange(coarse, dtype=jnp.int32)[:, None] * bins, coarse)
-    cos_c, sin_c = unit_angles(jnp.arange(64, dtype=jnp.int32)[:, None] * bins, NT)
+    cos_c, sin_c = unit_angles(jnp.arange(128, dtype=jnp.int32)[:, None] * bins, NT)
     cos_t = cos_a[:, None, :] * cos_c[None] - sin_a[:, None, :] * sin_c[None]
     sin_t = sin_a[:, None, :] * cos_c[None] + cos_a[:, None, :] * sin_c[None]
     table = jnp.concatenate([cos_t, -sin_t], axis=-1).astype(jnp.bfloat16)
@@ -29,11 +30,11 @@
 
 
 def inverse_table():
-    coarse = NT // 64
-    groups = LAGS // 64
+    coarse = NT // 128
+    groups = LAGS // 128
     bins = jnp.arange(NF, dtype=jnp.int32)[:, None]
     cos_a, sin_a = unit_angles(bins * (jnp.arange(groups, dtype=jnp.int32)[None, :] - groups // 2), coarse)
-    cos_c, sin_c = unit_angles(bins * jnp.arange(64, dtype=jnp.int32)[None, :], NT)
+    cos_c, sin_c = unit_angles(bins * jnp.arange(128, dtype=jnp.int32)[None, :], NT)
     cos_t = cos_a[:, :, None] * cos_c[:, None, :] - sin_a[:, :, None] * sin_c[:, None, :]
     sin_t = sin_a[:, :, None] * cos_c[:, None, :] + cos_a[:, :, None] * sin_c[:, None, :]
     weight = jnp.where(bins == 0, 1.0, 2.0).astype(jnp.float32)[:, :, None]
@@ -59,22 +60,38 @@
     return jnp.concatenate([real_part, imag_part], axis=-1).astype(jnp.bfloat16)
 
 
-def body(record, pairs, stretch_index):
+def body(axis_order, record, pairs, stretch_index):
     block_rows = record.shape[1]
     minutes = lax.axis_size("tm")
     blocks = lax.axis_size("chan")
-    parts = [record]
-    for shift in range(1, minutes):
-        parts.append(
-            lax.ppermute(record, "tm", [(i, (i + shift) % minutes) for i in range(minutes)])
-        )
-    own_block = jnp.concatenate(parts, axis=0)
-    below = lax.ppermute(own_block, "chan", [(s, s + 1) for s in range(blocks - 1)])
-    above = lax.ppermute(own_block, "chan", [(s, s - 1) for s in range(1, blocks)])
-    far_low = lax.ppermute(own_block, "chan", [(s, blocks - 2 - s) for s in range(blocks - 1)])
-    far_mid = lax.ppermute(own_block, "chan", [(s, blocks - 1 - s) for s in range(blocks)])
-    far_high = lax.ppermute(own_block, "chan", [(s, blocks - s) for s in range(1, blocks)])
-    candidates = jnp.concatenate([below, own_block, above, far_low, far_mid, far_high], axis=1)
+
+    def linear(t, b):
+        return t * blocks + b if axis_order[0] == "tm" else b * minutes + t
+
+    slot_maps = (
+        lambda b: b + 1,
+        lambda b: b,
+        lambda b: b - 1,
+        lambda b: blocks - 2 - b,
+        lambda b: blocks - 1 - b,
+        lambda b: blocks - b,
+    )
+    minute_rows = []
+    for shift in range(minutes):
+        slots = []
+        for slot, target in enumerate(slot_maps):
+            if shift == 0 and slot == 1:
+                slots.append(record)
+                continue
+            route = [
+                (linear(t, b), linear((t + shift) % minutes, target(b)))
+                for t in range(minutes)
+                for b in range(blocks)
+                if 0 <= target(b) < blocks
+            ]
+            slots.append(lax.ppermute(record, axis_order, route))
+        minute_rows.append(jnp.concatenate(slots, axis=1))
+    candidates = jnp.concatenate(minute_rows, axis=0)
     slot_rows = candidates.shape[1]
     spectrum = jnp.dot(
         candidates.reshape(minutes * slot_rows, NT), forward_table(),
@@ -110,8 +127,9 @@
     picks = (
         jnp.arange(LAGS, dtype=jnp.int32)[:, None, None] == stretch_index[None, 1:, :]
     ).astype(jnp.bfloat16).reshape(LAGS, (stretch_count - 1) * LAGS)
-    stacked_high = stacked.astype(jnp.bfloat16)
-    stacked_low = (stacked - stacked_high.astype(jnp.float32)).astype(jnp.bfloat16)
+    stacked_round = lax.reduce_precision(stacked, exponent_bits=8, mantissa_bits=7)
+    stacked_high = stacked_round.astype(jnp.bfloat16)
+    stacked_low = (stacked - stacked_round).astype(jnp.bfloat16)
     moved = jnp.dot(
         jnp.concatenate([stacked_high, stacked_low], axis=0), picks,
         preferred_element_type=jnp.float32,
@@ -126,8 +144,9 @@
 
 
 def solution(mesh):
+    axis_order = tuple(name for name in mesh.axis_names if name in ("tm", "chan"))
     return jax.shard_map(
-        body,
+        functools.partial(body, axis_order),
         mesh=mesh,
         in_specs=(P("tm", "chan", None), P("chan", None), P()),
         out_specs=P("tm", None, "chan", None),

time: 89.7 us -> 107 us (1.19)
  the two profiles are of different devices: /device:TPU:1 before, /device:TPU:4 now
where the time goes in v3:
time: 107 us; the launch traced here: 106 us
  starting transfers between devices  33.1 us (31%)
  other arithmetic  23.9 us (22%)
  waiting for transfers between devices  17.1 us (16%)
  matrix products  16.8 us (16%)
  local copies, waits for them, and re-layouts  14.8 us (14%)
    ppermute x11, starting transfers between devices, body(): slots.append(lax.ppermute(record, axis_order, route))  33.1 us
    ppermute x11, waiting for transfers between devices, body(): slots.append(lax.ppermute(record, axis_order, route))  17.1 us
    dot_general x1, matrix products, body(): jnp.dot(jnp.concatenate([stacked_high, stacked_low], axis=0), picks, pref...  8.19 us
    another operation x4, other arithmetic  7.19 us
    add x1, local copies, waits for them, and re-layouts, body(): moved[:pair_count] + moved[pair_count:]  6.57 us
    dot_general x1, matrix products, body(): jnp.einsum('mpk,kl->mpl', crossed, inverse_table(), preferred_element_typ...  4.74 us
    reduce_sum x1, other arithmetic, body(): numerator = jnp.mean(current[:, None, :] * shifted, axis=-1)  4.05 us
    add x1, other arithmetic, body(): moved[:pair_count] + moved[pair_count:]  3.76 us
  transfers between devices with their start and end apart: 11, of which 4 were waited for; matrix products, arithmetic and copies ran while one was open for 11% of the time, Pallas kernels for 0%

profile of v3, /device:TPU:4, one launch (start us, length us, event | category | flops | bytes accessed | tf_op | source)
XLA Modules:
  0.0 106.1 jit_solution(13716189374562942790)
XLA Ops:
  0.0 6.4 %collective-permute-start.8 = (bf16[1,16,1536]{2,1,0:T(8,128)(2,1)}, bf16[1,16,1536]{2,1,0:T(8,128)(2,1)S(1)}, u32[]{:S(2)}, u32[]{:S(2)}) collective-permute-start(bf16[1,16,1536]{2,1,0:T(8,128)(2,1)} %param.3), channel_id=1, source_target_pairs={{0,29},{2,27},{4,25},{6,23},{8,21},{10,19},{12,17},{14,15},{16,13}... | collective-permute-start | bytes 147464 | tf_op jit(solution)/shard_map/ppermute | solution.py:92
  6.4 1.9 %collective-permute-start.7 = (bf16[1,16,1536]{2,1,0:T(8,128)(2,1)}, bf16[1,16,1536]{2,1,0:T(8,128)(2,1)S(1)}, u32[]{:S(2)}, u32[]{:S(2)}) collective-permute-start(bf16[1,16,1536]{2,1,0:T(8,128)(2,1)} %param.3), channel_id=1, source_target_pairs={{2,1},{4,3},{6,5},{8,7},{10,9},{12,11},{14,13},{16,15},{18,17},{20... | collective-permute-start | bytes 147464 | tf_op jit(solution)/shard_map/ppermute | solution.py:92
  8.3 1.2 %collective-permute-start.6 = (bf16[1,16,1536]{2,1,0:T(8,128)(2,1)}, bf16[1,16,1536]{2,1,0:T(8,128)(2,1)S(1)}, u32[]{:S(2)}, u32[]{:S(2)}) collective-permute-start(bf16[1,16,1536]{2,1,0:T(8,128)(2,1)} %param.3), channel_id=1, source_target_pairs={{0,1},{2,3},{4,5},{6,7},{8,9},{10,11},{12,13},{14,15},{16,17},{18,... | collective-permute-start | bytes 147464 | tf_op jit(solution)/shard_map/ppermute | solution.py:92
  9.5 2.7 %collective-permute-start.5 = (bf16[1,16,1536]{2,1,0:T(8,128)(2,1)}, bf16[1,16,1536]{2,1,0:T(8,128)(2,1)S(1)}, u32[]{:S(2)}, u32[]{:S(2)}) collective-permute-start(bf16[1,16,1536]{2,1,0:T(8,128)(2,1)} %param.3), channel_id=1, source_target_pairs={{0,3},{2,5},{4,7},{6,9},{8,11},{10,13},{12,15},{14,17},{16,19},{18... | collective-permute-start | bytes 147464 | tf_op jit(solution)/shard_map/ppermute | solution.py:92
  12.3 2.6 %collective-permute-start = (bf16[1,16,1536]{2,1,0:T(8,128)(2,1)}, bf16[1,16,1536]{2,1,0:T(8,128)(2,1)S(1)}, u32[]{:S(2)}, u32[]{:S(2)}) collective-permute-start(bf16[1,16,1536]{2,1,0:T(8,128)(2,1)} %param.3), channel_id=1, source_target_pairs={{0,2},{2,4},{4,6},{6,8},{8,10},{10,12},{12,14},{14,16},{16,18},{18... | collective-permute-start | bytes 147464 | tf_op jit(solution)/shard_map/ppermute | solution.py:92
  14.9 0.2 fusion.40
  15.1 1.6 %fusion.28 = (f32[128,768]{1,0:T(8,128)S(1)}, f32[128,768]{1,0:T(8,128)S(1)}) fusion(), kind=kLoop, calls=%fused_computation.53 | loop fusion | flops 884736 | bytes 786432 | tf_op jit(solution)/shard_map/sin | solution.py:18
  16.7 1.6 %fusion.24 = (f32[768,128]{1,0:T(8,128)S(1)}, f32[768,128]{1,0:T(8,128)S(1)}) fusion(), kind=kLoop, calls=%fused_computation.48 | loop fusion | flops 884736 | bytes 786432 | tf_op jit(solution)/shard_map/sin | solution.py:18
  18.3 0.2 fusion.48
  18.5 0.2 copy.9
  18.7 0.2 copy.10
  18.9 1.8 %multiply_subtract_fusion = (f32[768,8,128]{2,1,0:T(8,128)S(1)}, f32[768,8,128]{2,1,0:T(8,128)S(1)}) fusion(f32[768,128]{1,0:T(8,128)S(1)} %get-tuple-element.23, f32[768,8]{1,0:T(8,128)S(1)} %copy.10, f32[768,128]{1,0:T(8,128)S(1)} %get-tuple-element.24, f32[768,8]{1,0:T(8,128)S(1)} %copy.9), kind=kLoop, calls=%fused_computation.25 | loop fusion | flops 4718592 | bytes 7127040 | tf_op jit(solution)/shard_map/sub | solution.py:38
  20.7 1.7 %fusion.7 = bf16[768,1024]{1,0:T(8,128)(2,1)} fusion(f32[96,8,8,128]{3,2,1,0:T(8,128)S(1)} %bitcast.50, f32[768]{0:T(1024)S(1)} %fusion.50), kind=kLoop, calls=%fused_computation.16 | loop fusion | flops 1572864 | bytes 4721664 | tf_op jit(solution)/shard_map/convert.1
  22.4 1.7 %fusion.6 = bf16[768,1024]{1,0:T(8,128)(2,1)} fusion(f32[96,8,8,128]{3,2,1,0:T(8,128)S(1)} %bitcast.49, f32[768]{0:T(1024)S(1)} %fusion.51), kind=kLoop, calls=%fused_computation.14 | loop fusion | flops 1572864 | bytes 4721664 | tf_op jit(solution)/shard_map/convert.2
  24.1 0.0 copy-start.4
  24.1 0.0 copy-start.3
  24.1 0.0 copy-start.2
  24.1 2.8 %subtract_convert_fusion = (bf16[12,128,768]{2,1,0:T(8,128)(2,1)S(1)}, bf16[12,128,768]{2,1,0:T(8,128)(2,1)}) fusion(f32[128,768]{1,0:T(8,128)S(1)} %get-tuple-element.25, f32[12,768]{1,0:T(8,128)S(1)} %get-tuple-element.27, f32[128,768]{1,0:T(8,128)S(1)} %get-tuple-element.26, f32[12,768]{1,0:T(8,128)S(1)} %get-tuple-element.28), kind=kLoop, calls=%fused_computation.12 | loop fusion | flops 10616832 | bytes 5578752 | tf_op jit(solution)/shard_map/convert.10
  26.9 0.0 copy-done.4
  26.9 0.0 copy-done.3
  27.0 0.0 collective-permute-done
  27.0 0.0 copy-done.2
  27.0 1.9 %collective-permute-start.4 = (bf16[1,16,1536]{2,1,0:T(8,128)(2,1)S(1)}, bf16[1,16,1536]{2,1,0:T(8,128)(2,1)S(1)}, u32[]{:S(2)}, u32[]{:S(2)}) collective-permute-start(bf16[1,16,1536]{2,1,0:T(8,128)(2,1)S(1)} %copy-done.2), channel_id=1, source_target_pairs={{2,30},{4,28},{6,26},{8,24},{10,22},{12,20},{14,18},{16,16},{18,14... | collective-permute-start | bytes 147464 | tf_op jit(solution)/shard_map/ppermute | solution.py:92
  29.0 0.0 collective-permute-done.5
  29.0 3.0 %collective-permute-start.1 = (bf16[1,16,1536]{2,1,0:T(8,128)(2,1)S(1)}, bf16[1,16,1536]{2,1,0:T(8,128)(2,1)S(1)}, u32[]{:S(2)}, u32[]{:S(2)}) collective-permute-start(bf16[1,16,1536]{2,1,0:T(8,128)(2,1)S(1)} %copy-done.2), channel_id=1, source_target_pairs={{2,0},{4,2},{6,4},{8,6},{10,8},{12,10},{14,12},{16,14},{18,16},{20... | collective-permute-start | bytes 147464 | tf_op jit(solution)/shard_map/ppermute | solution.py:92
  32.0 1.9 %collective-permute-done.1 = bf16[1,16,1536]{2,1,0:T(8,128)(2,1)S(1)} collective-permute-done((bf16[1,16,1536]{2,1,0:T(8,128)(2,1)S(1)}, bf16[1,16,1536]{2,1,0:T(8,128)(2,1)S(1)}, u32[]{:S(2)}, u32[]{:S(2)}) %collective-permute-start.1) | collective-permute-done | bytes 49184 | tf_op jit(solution)/shard_map/ppermute | solution.py:92
  33.8 4.3 %collective-permute-start.2 = (bf16[1,16,1536]{2,1,0:T(8,128)(2,1)S(1)}, bf16[1,16,1536]{2,1,0:T(8,128)(2,1)S(1)}, u32[]{:S(2)}, u32[]{:S(2)}) collective-permute-start(bf16[1,16,1536]{2,1,0:T(8,128)(2,1)S(1)} %copy-done.2), channel_id=1, source_target_pairs={{0,28},{2,26},{4,24},{6,22},{8,20},{10,18},{12,16},{14,14},{16,12}... | collective-permute-start | bytes 147464 | tf_op jit(solution)/shard_map/ppermute | solution.py:92
  38.1 4.9 %collective-permute-done.2 = bf16[1,16,1536]{2,1,0:T(8,128)(2,1)S(1)} collective-permute-done((bf16[1,16,1536]{2,1,0:T(8,128)(2,1)S(1)}, bf16[1,16,1536]{2,1,0:T(8,128)(2,1)S(1)}, u32[]{:S(2)}, u32[]{:S(2)}) %collective-permute-start.2) | collective-permute-done | bytes 49184 | tf_op jit(solution)/shard_map/ppermute | solution.py:92
  43.0 2.3 %collective-permute-start.3 = (bf16[1,16,1536]{2,1,0:T(8,128)(2,1)S(1)}, bf16[1,16,1536]{2,1,0:T(8,128)(2,1)S(1)}, u32[]{:S(2)}, u32[]{:S(2)}) collective-permute-start(bf16[1,16,1536]{2,1,0:T(8,128)(2,1)S(1)} %copy-done.2), channel_id=1, source_target_pairs={{0,30},{2,28},{4,26},{6,24},{8,22},{10,20},{12,18},{14,16},{16,14}... | collective-permute-start | bytes 147464 | tf_op jit(solution)/shard_map/ppermute | solution.py:92
  45.3 4.0 %collective-permute-done.3 = bf16[1,16,1536]{2,1,0:T(8,128)(2,1)S(1)} collective-permute-done((bf16[1,16,1536]{2,1,0:T(8,128)(2,1)S(1)}, bf16[1,16,1536]{2,1,0:T(8,128)(2,1)S(1)}, u32[]{:S(2)}, u32[]{:S(2)}) %collective-permute-start.3) | collective-permute-done | bytes 49184 | tf_op jit(solution)/shard_map/ppermute | solution.py:92
  49.3 6.1 %collective-permute-start.10 = (bf16[1,16,1536]{2,1,0:T(8,128)(2,1)S(1)}, bf16[1,16,1536]{2,1,0:T(8,128)(2,1)S(1)}, u32[]{:S(2)}, u32[]{:S(2)}) collective-permute-start(bf16[1,16,1536]{2,1,0:T(8,128)(2,1)S(1)} %copy-done.2), channel_id=1, source_target_pairs={{2,31},{4,29},{6,27},{8,25},{10,23},{12,21},{14,19},{16,17},{18,15... | collective-permute-start | bytes 147464 | tf_op jit(solution)/shard_map/ppermute | solution.py:92
  55.4 0.0 collective-permute-done.4
  55.4 0.8 collective-permute-start.9
  56.2 0.0 collective-permute-done.6
  56.2 0.0 collective-permute-done.7
  56.2 0.0 collective-permute-done.8
  56.2 6.4 %collective-permute-done.9 = bf16[1,16,1536]{2,1,0:T(8,128)(2,1)S(1)} collective-permute-done((bf16[1,16,1536]{2,1,0:T(8,128)(2,1)S(1)}, bf16[1,16,1536]{2,1,0:T(8,128)(2,1)S(1)}, u32[]{:S(2)}, u32[]{:S(2)}) %collective-permute-start.9) | collective-permute-done | bytes 49184 | tf_op jit(solution)/shard_map/ppermute | solution.py:92
  62.6 0.0 collective-permute-done.10
  62.6 0.1 pad_maximum_fusion.1
  62.7 2.9 %multiply_reduce_fusion.3 = (f32[192]{0:T(256)S(1)}, f32[192,1536]{1,0:T(8,128)S(1)}) fusion(bf16[192,1536]{1,0:T(8,128)(2,1)S(1)} %bitcast.58, bf16[1536,768]{1,0:T(8,128)(2,1)} %bitcast.55, bf16[1536,768]{1,0:T(8,128)(2,1)S(1)} %bitcast.54), kind=kOutput, calls=%fused_computation.37 | convolution fusion | flops 915996480 | bytes 6488832 | tf_op jit(solution)/shard_map/dot_general | solution.py:96
  65.5 0.2 divide_convert_fusion
  65.8 1.0 fusion.33
  66.8 0.0 copy-start
  66.8 0.0 copy-start.1
  66.8 0.9 add_convert_fusion
  67.8 0.5 copy-done
  68.2 0.5 copy-done.1
  68.7 4.7 %fusion.55 = (f32[512,1024]{1,0:T(8,128)}, f32[2,512,1024]{2,1,0:T(8,128)S(1)}) fusion(bf16[768,1024]{1,0:T(8,128)(2,1)S(1)} %copy-done.1, bf16[768,1024]{1,0:T(8,128)(2,1)S(1)} %copy-done, bf16[2,512,768]{2,1,0:T(8,128)(2,1)S(1)} %bitcast.57, bf16[2,512,768]{2,1,0:T(8,128)(2,1)S(1)} %bitcast.56), kind=kOutput, calls=%fused_computation.106 | convolution fusion | flops 3234332672 | bytes 12582912 | tf_op jit(solution)/shard_map/mpk,kl->mpl/dot_general | solution.py:120
  73.4 0.2 multiply_reduce_fusion.2
  73.6 1.4 %slice_bitcast_fusion = f32[512,1024]{1,0:T(8,128)} fusion(f32[2,512,1024]{2,1,0:T(8,128)S(1)} %get-tuple-element.22), kind=kLoop, calls=%fused_computation.31 | loop fusion | bytes 4194304 | tf_op jit(solution)/shard_map/mul | solution.py:139
  75.1 1.9 %copy.11 = f32[512,1024]{0,1:T(8,128)S(1)} copy(f32[512,1024]{1,0:T(8,128)} %slice_bitcast_fusion) | data formatting | bytes 4194304 | tf_op jit(solution)/shard_map/mul | solution.py:139
  77.0 3.0 %reduce-precision_convert_fusion = (bf16[512,1024]{1,0:T(8,128)(2,1)S(1)}, bf16[512,1024]{1,0:T(8,128)(2,1)}) fusion(f32[512,1024]{1,0:T(8,128)} %get-tuple-element.21), kind=kLoop, calls=%fused_computation.29 | loop fusion | flops 2097152 | bytes 4194304 | tf_op jit(solution)/shard_map/convert_element_type | solution.py:131
  80.0 2.9 %copy.13 = f32[512,1,1024]{0,2,1:T(8,128)} copy(f32[512,1,1024]{2,0,1:T(8,128)} %bitcast.51) | data formatting | bytes 4194304 | tf_op jit(solution)/shard_map/broadcast_in_dim | solution.py:138
  82.9 8.2 %fusion = f32[1024,3072]{1,0:T(8,128)S(1)} fusion(s32[3072]{0:T(1024)S(1)} %eq.64, bf16[512,1024]{1,0:T(8,128)(2,1)} %get-tuple-element.10, bf16[512,1024]{1,0:T(8,128)(2,1)S(1)} %get-tuple-element.9), kind=kOutput, calls=%fused_computation.1 | convolution fusion | flops 6449790976 | bytes 14692352 | tf_op jit(solution)/shard_map/dot_general | solution.py:133
  91.1 3.8 %slice_add_fusion = f32[512,3072]{1,0:T(8,128)} fusion(f32[1024,3072]{1,0:T(8,128)S(1)} %fusion), kind=kLoop, calls=%fused_computation.5 | loop fusion | flops 1572864 | bytes 18874368 | tf_op jit(solution)/shard_map/add | solution.py:137
  94.9 6.6 %copy.12 = f32[512,3072]{0,1:T(8,128)} copy(f32[512,3072]{1,0:T(8,128)} %slice_add_fusion) | data formatting | bytes 12582912 | tf_op jit(solution)/shard_map/add | solution.py:137
  101.5 4.0 %multiply_reduce_fusion.1 = (f32[512,4]{0,1:T(4,128)S(1)}, f32[512,4]{0,1:T(4,128)S(1)}) fusion(f32[512,3,1024]{0,2,1:T(8,128)} %bitcast.47, f32[512,1,1024]{0,2,1:T(8,128)} %copy.13, f32[512,1024]{0,1:T(8,128)S(1)} %copy.11), kind=kLoop, calls=%fused_computation.4 | loop fusion | flops 10481664 | bytes 10502144 | tf_op jit(solution)/shard_map/reduce_sum | solution.py:139
  105.5 0.6 reshape.242
  (26 shorter events, 0.2 us)
Async XLA Ops:
  0.0 56.2 %collective-permute-start.8 = (bf16[1,16,1536]{2,1,0:T(8,128)(2,1)}, bf16[1,16,1536]{2,1,0:T(8,128)(2,1)S(1)}, u32[]{:S(2)}, u32[]{:S(2)}) collective-permute-start(bf16[1,16,1536]{2,1,0:T(8,128)(2,1)} %param.3), channel_id=1, source_target_pairs={{0,29},{2,27},{4,25},{6,23},{8,21},{10,19},{12,17},{14,15},{16,13}... | collective-permute-start | bytes 147464 | tf_op jit(solution)/shard_map/ppermute | solution.py:92
  6.4 49.8 %collective-permute-start.7 = (bf16[1,16,1536]{2,1,0:T(8,128)(2,1)}, bf16[1,16,1536]{2,1,0:T(8,128)(2,1)S(1)}, u32[]{:S(2)}, u32[]{:S(2)}) collective-permute-start(bf16[1,16,1536]{2,1,0:T(8,128)(2,1)} %param.3), channel_id=1, source_target_pairs={{2,1},{4,3},{6,5},{8,7},{10,9},{12,11},{14,13},{16,15},{18,17},{20... | collective-permute-start | bytes 147464 | tf_op jit(solution)/shard_map/ppermute | solution.py:92
  8.3 47.9 %collective-permute-start.6 = (bf16[1,16,1536]{2,1,0:T(8,128)(2,1)}, bf16[1,16,1536]{2,1,0:T(8,128)(2,1)S(1)}, u32[]{:S(2)}, u32[]{:S(2)}) collective-permute-start(bf16[1,16,1536]{2,1,0:T(8,128)(2,1)} %param.3), channel_id=1, source_target_pairs={{0,1},{2,3},{4,5},{6,7},{8,9},{10,11},{12,13},{14,15},{16,17},{18,... | collective-permute-start | bytes 147464 | tf_op jit(solution)/shard_map/ppermute | solution.py:92
  9.5 19.4 %collective-permute-start.5 = (bf16[1,16,1536]{2,1,0:T(8,128)(2,1)}, bf16[1,16,1536]{2,1,0:T(8,128)(2,1)S(1)}, u32[]{:S(2)}, u32[]{:S(2)}) collective-permute-start(bf16[1,16,1536]{2,1,0:T(8,128)(2,1)} %param.3), channel_id=1, source_target_pairs={{0,3},{2,5},{4,7},{6,9},{8,11},{10,13},{12,15},{14,17},{16,19},{18... | collective-permute-start | bytes 147464 | tf_op jit(solution)/shard_map/ppermute | solution.py:92
  12.3 14.7 %collective-permute-start = (bf16[1,16,1536]{2,1,0:T(8,128)(2,1)}, bf16[1,16,1536]{2,1,0:T(8,128)(2,1)S(1)}, u32[]{:S(2)}, u32[]{:S(2)}) collective-permute-start(bf16[1,16,1536]{2,1,0:T(8,128)(2,1)} %param.3), channel_id=1, source_target_pairs={{0,2},{2,4},{4,6},{6,8},{8,10},{10,12},{12,14},{14,16},{16,18},{18... | collective-permute-start | bytes 147464 | tf_op jit(solution)/shard_map/ppermute | solution.py:92
  24.1 2.8 %copy-start.4 = (s32[2,256]{1,0:T(2,128)S(1)}, s32[2,256]{1,0:T(2,128)}, u32[]{:S(2)}) copy-start(s32[2,256]{1,0:T(2,128)} %param.4) | copy-start | bytes 6148
  24.1 2.8 %copy-start.3 = (s32[4,1024]{1,0:T(4,128)S(1)}, s32[4,1024]{1,0:T(4,128)}, u32[]{:S(2)}) copy-start(s32[4,1024]{1,0:T(4,128)} %param.5) | copy-start | bytes 49156
  24.1 2.9 %copy-start.2 = (bf16[1,16,1536]{2,1,0:T(8,128)(2,1)S(1)}, bf16[1,16,1536]{2,1,0:T(8,128)(2,1)}, u32[]{:S(2)}) copy-start(bf16[1,16,1536]{2,1,0:T(8,128)(2,1)} %param.3) | copy-start | bytes 147460
  27.0 28.4 %collective-permute-start.4 = (bf16[1,16,1536]{2,1,0:T(8,128)(2,1)S(1)}, bf16[1,16,1536]{2,1,0:T(8,128)(2,1)S(1)}, u32[]{:S(2)}, u32[]{:S(2)}) collective-permute-start(bf16[1,16,1536]{2,1,0:T(8,128)(2,1)S(1)} %copy-done.2), channel_id=1, source_target_pairs={{2,30},{4,28},{6,26},{8,24},{10,22},{12,20},{14,18},{16,16},{18,14... | collective-permute-start | bytes 147464 | tf_op jit(solution)/shard_map/ppermute | solution.py:92
  29.0 4.9 %collective-permute-start.1 = (bf16[1,16,1536]{2,1,0:T(8,128)(2,1)S(1)}, bf16[1,16,1536]{2,1,0:T(8,128)(2,1)S(1)}, u32[]{:S(2)}, u32[]{:S(2)}) collective-permute-start(bf16[1,16,1536]{2,1,0:T(8,128)(2,1)S(1)} %copy-done.2), channel_id=1, source_target_pairs={{2,0},{4,2},{6,4},{8,6},{10,8},{12,10},{14,12},{16,14},{18,16},{20... | collective-permute-start | bytes 147464 | tf_op jit(solution)/shard_map/ppermute | solution.py:92
  33.8 9.2 %collective-permute-start.2 = (bf16[1,16,1536]{2,1,0:T(8,128)(2,1)S(1)}, bf16[1,16,1536]{2,1,0:T(8,128)(2,1)S(1)}, u32[]{:S(2)}, u32[]{:S(2)}) collective-permute-start(bf16[1,16,1536]{2,1,0:T(8,128)(2,1)S(1)} %copy-done.2), channel_id=1, source_target_pairs={{0,28},{2,26},{4,24},{6,22},{8,20},{10,18},{12,16},{14,14},{16,12}... | collective-permute-start | bytes 147464 | tf_op jit(solution)/shard_map/ppermute | solution.py:92
  43.0 6.3 %collective-permute-start.3 = (bf16[1,16,1536]{2,1,0:T(8,128)(2,1)S(1)}, bf16[1,16,1536]{2,1,0:T(8,128)(2,1)S(1)}, u32[]{:S(2)}, u32[]{:S(2)}) collective-permute-start(bf16[1,16,1536]{2,1,0:T(8,128)(2,1)S(1)} %copy-done.2), channel_id=1, source_target_pairs={{0,30},{2,28},{4,26},{6,24},{8,22},{10,20},{12,18},{14,16},{16,14}... | collective-permute-start | bytes 147464 | tf_op jit(solution)/shard_map/ppermute | solution.py:92
  49.3 13.3 %collective-permute-start.10 = (bf16[1,16,1536]{2,1,0:T(8,128)(2,1)S(1)}, bf16[1,16,1536]{2,1,0:T(8,128)(2,1)S(1)}, u32[]{:S(2)}, u32[]{:S(2)}) collective-permute-start(bf16[1,16,1536]{2,1,0:T(8,128)(2,1)S(1)} %copy-done.2), channel_id=1, source_target_pairs={{2,31},{4,29},{6,27},{8,25},{10,23},{12,21},{14,19},{16,17},{18,15... | collective-permute-start | bytes 147464 | tf_op jit(solution)/shard_map/ppermute | solution.py:92
  55.4 7.2 %collective-permute-start.9 = (bf16[1,16,1536]{2,1,0:T(8,128)(2,1)S(1)}, bf16[1,16,1536]{2,1,0:T(8,128)(2,1)S(1)}, u32[]{:S(2)}, u32[]{:S(2)}) collective-permute-start(bf16[1,16,1536]{2,1,0:T(8,128)(2,1)S(1)} %copy-done.2), channel_id=1, source_target_pairs={{0,31},{2,29},{4,27},{6,25},{8,23},{10,21},{12,19},{14,17},{16,15}... | collective-permute-start | bytes 147464 | tf_op jit(solution)/shard_map/ppermute | solution.py:92
  66.8 1.4 %copy-start = (bf16[768,1024]{1,0:T(8,128)(2,1)S(1)}, bf16[768,1024]{1,0:T(8,128)(2,1)}, u32[]{:S(2)}) copy-start(bf16[768,1024]{1,0:T(8,128)(2,1)} %fusion.7) | copy-start | bytes 4718596
  66.8 1.9 %copy-start.1 = (bf16[768,1024]{1,0:T(8,128)(2,1)S(1)}, bf16[768,1024]{1,0:T(8,128)(2,1)}, u32[]{:S(2)}) copy-start(bf16[768,1024]{1,0:T(8,128)(2,1)} %fusion.6) | copy-start | bytes 4718596

commit v4 on v3

--- a/solution.py
+++ b/solution.py
@@ -11,6 +11,7 @@
 NF = 768
 
 epsilon = 1e-05
+GATHER_BYTES = 4 << 20
 
 
 def unit_angles(numerators, period):
@@ -65,33 +66,34 @@
     minutes = lax.axis_size("tm")
     blocks = lax.axis_size("chan")
 
-    def linear(t, b):
-        return t * blocks + b if axis_order[0] == "tm" else b * minutes + t
 
-    slot_maps = (
-        lambda b: b + 1,
-        lambda b: b,
-        lambda b: b - 1,
-        lambda b: blocks - 2 - b,
-        lambda b: blocks - 1 - b,
-        lambda b: blocks - b,
-    )
-    minute_rows = []
-    for shift in range(minutes):
-        slots = []
-        for slot, target in enumerate(slot_maps):
-            if shift == 0 and slot == 1:
-                slots.append(record)
-                continue
-            route = [
-                (linear(t, b), linear((t + shift) % minutes, target(b)))
-                for t in range(minutes)
-                for b in range(blocks)
-                if 0 <= target(b) < blocks
-            ]
-            slots.append(lax.ppermute(record, axis_order, route))
-        minute_rows.append(jnp.concatenate(slots, axis=1))
-    candidates = jnp.concatenate(minute_rows, axis=0)
+    position = lax.axis_index("chan")
+    gathered_bytes = record.size * record.dtype.itemsize * minutes * blocks
+    if gathered_bytes <= GATHER_BYTES:
+        everything = lax.all_gather(record[0], axis_order, axis=0)
+        if axis_order[0] == "tm":
+            everything = everything.reshape(minutes, blocks, block_rows, NT)
+        else:
+            everything = everything.reshape(blocks, minutes, block_rows, NT).transpose(1, 0, 2, 3)
+        everything = jnp.pad(everything, ((0, 0), (1, 1), (0, 0), (0, 0)))
+        near = lax.dynamic_slice_in_dim(everything, position, 3, axis=1)
+        far = lax.dynamic_slice_in_dim(everything, blocks - 1 - position, 3, axis=1)
+        candidates = jnp.concatenate([near, far], axis=1).reshape(minutes, 6 * block_rows, NT)
+        own_minute = lax.axis_index("tm")
+    else:
+        parts = [record]
+        for shift in range(1, minutes):
+            parts.append(
+                lax.ppermute(record, "tm", [(i, (i + shift) % minutes) for i in range(minutes)])
+            )
+        own_block = jnp.concatenate(parts, axis=0)
+        below = lax.ppermute(own_block, "chan", [(s, s + 1) for s in range(blocks - 1)])
+        above = lax.ppermute(own_block, "chan", [(s, s - 1) for s in range(1, blocks)])
+        far_low = lax.ppermute(own_block, "chan", [(s, blocks - 2 - s) for s in range(blocks - 1)])
+        far_mid = lax.ppermute(own_block, "chan", [(s, blocks - 1 - s) for s in range(blocks)])
+        far_high = lax.ppermute(own_block, "chan", [(s, blocks - s) for s in range(1, blocks)])
+        candidates = jnp.concatenate([below, own_block, above, far_low, far_mid, far_high], axis=1)
+        own_minute = 0
     slot_rows = candidates.shape[1]
     spectrum = jnp.dot(
         candidates.reshape(minutes * slot_rows, NT), forward_table(),
@@ -99,7 +101,6 @@
     )
     whitened = whiten(spectrum).reshape(minutes, slot_rows, 2 * NF)
 
-    position = lax.axis_index("chan")
     column_index = jnp.arange(pairs.shape[1], dtype=jnp.int32)[None, :]
     is_near = column_index < pairs.shape[1] // 2
     near_slot = pairs - (position - 1) * block_rows
@@ -120,7 +121,7 @@
     correlation = jnp.einsum(
         "mpk,kl->mpl", crossed, inverse_table(), preferred_element_type=jnp.float32
     )
-    current = correlation[0]
+    current = lax.dynamic_index_in_dim(correlation, own_minute, axis=0, keepdims=False)
     stacked = jnp.sum(correlation, axis=0)
     current_power = jnp.mean(current * current, axis=-1)
     stretch_count = stretch_index.shape[0]

time: 107 us -> 116 us (1.084)
  the two profiles are of different devices: /device:TPU:4 before, /device:TPU:1 now
where the time goes in v4:
time: 116 us; the launch traced here: 115 us
  waiting for transfers between devices  47.6 us (41%)
  other arithmetic  24.6 us (21%)
  local copies, waits for them, and re-layouts  15.8 us (14%)
  matrix products  13.8 us (12%)
  between operations  13.6 us (12%)
    all_gather x1, waiting for transfers between devices, body(): everything = lax.all_gather(record[0], axis_order, axis=0)  46.9 us
    dot_general x1, matrix products, body(): jnp.dot(jnp.concatenate([stacked_high, stacked_low], axis=0), picks, pref...  8.19 us
    another operation x4, other arithmetic  7.21 us
    add x1, local copies, waits for them, and re-layouts, body(): moved[:pair_count] + moved[pair_count:]  6.58 us
    reduce_sum x1, other arithmetic, body(): numerator = jnp.mean(current[:, None, :] * shifted, axis=-1)  4.01 us
    add x1, other arithmetic, body(): moved[:pair_count] + moved[pair_count:]  3.77 us
    dot_general x1, matrix products, body(): jnp.einsum('mpk,kl->mpl', crossed, inverse_table(), preferred_element_typ...  3.41 us
    sin x3, other arithmetic, unit_angles(): return (jnp.cos(phase), jnp.sin(phase))  3.4 us
  transfers between devices with their start and end apart: 1, of which 1 were waited for; matrix products, arithmetic and copies ran while one was open for 12% of the time, Pallas kernels for 0%

profile of v4, /device:TPU:1, one launch (start us, length us, event | category | flops | bytes accessed | tf_op | source)
XLA Modules:
  0.0 115.5 jit_solution(6622145435714009252)
XLA Ops:
  6.5 0.0 all-gather.2.cloned.1.call-start
  6.5 0.7 all-gather.2.cloned.1.call-update
  7.3 0.7 select_bitcast_fusion
  8.0 0.7 slice.29
  8.7 0.2 fusion.48
  8.9 0.2 copy.15
  9.1 0.2 copy.16
  9.3 0.2 fusion.40
  9.5 1.6 %fusion.28 = (f32[128,768]{1,0:T(8,128)S(1)}, f32[128,768]{1,0:T(8,128)S(1)}) fusion(), kind=kLoop, calls=%fused_computation.55 | loop fusion | flops 884736 | bytes 786432 | tf_op jit(solution)/shard_map/sin | solution.py:19
  11.1 1.6 %fusion.24 = (f32[768,128]{1,0:T(8,128)S(1)}, f32[768,128]{1,0:T(8,128)S(1)}) fusion(), kind=kLoop, calls=%fused_computation.50 | loop fusion | flops 884736 | bytes 786432 | tf_op jit(solution)/shard_map/sin | solution.py:19
  12.7 2.0 %multiply_subtract_fusion = (f32[768,8,128]{2,1,0:T(8,128)S(1)}, f32[768,8,128]{2,1,0:T(8,128)S(1)}) fusion(f32[768,128]{1,0:T(8,128)S(1)} %get-tuple-element.27, f32[768,8]{1,0:T(8,128)S(1)} %copy.16, f32[768,128]{1,0:T(8,128)S(1)} %get-tuple-element.28, f32[768,8]{1,0:T(8,128)S(1)} %copy.15), kind=kLoop, calls=%fused_computation.25 | loop fusion | flops 4718592 | bytes 7127040 | tf_op jit(solution)/shard_map/sub | solution.py:39
  14.7 1.7 %fusion.7 = bf16[768,1024]{1,0:T(8,128)(2,1)} fusion(f32[96,8,8,128]{3,2,1,0:T(8,128)S(1)} %bitcast.52, f32[768]{0:T(1024)S(1)} %fusion.50), kind=kLoop, calls=%fused_computation.16 | loop fusion | flops 1572864 | bytes 4721664 | tf_op jit(solution)/shard_map/convert.1
  16.4 1.7 %fusion.6 = bf16[768,1024]{1,0:T(8,128)(2,1)} fusion(f32[96,8,8,128]{3,2,1,0:T(8,128)S(1)} %bitcast.51, f32[768]{0:T(1024)S(1)} %fusion.51), kind=kLoop, calls=%fused_computation.14 | loop fusion | flops 1572864 | bytes 4721664 | tf_op jit(solution)/shard_map/convert.2
  18.1 2.8 %subtract_convert_fusion = (bf16[12,128,768]{2,1,0:T(8,128)(2,1)S(1)}, bf16[12,128,768]{2,1,0:T(8,128)(2,1)}) fusion(f32[128,768]{1,0:T(8,128)S(1)} %get-tuple-element.29, f32[12,768]{1,0:T(8,128)S(1)} %get-tuple-element.31, f32[128,768]{1,0:T(8,128)S(1)} %get-tuple-element.30, f32[12,768]{1,0:T(8,128)S(1)} %get-tuple-element.32), kind=kLoop, calls=%fused_computation.12 | loop fusion | flops 10616832 | bytes 5578752 | tf_op jit(solution)/shard_map/convert.10
  20.9 46.9 %all-gather.2.cloned.1.call-done = bf16[32,16,1536]{2,1,0:T(8,128)(2,1)} async-done(((bf16[1,16,1536]{2,1,0:T(8,128)(2,1)}), bf16[32,16,1536]{2,1,0:T(8,128)(2,1)}) %all-gather.2.cloned.1.call-update) | async-done | bytes 1572880 | tf_op jit(solution)/shard_map/all_gather | solution.py:73
  67.9 0.0 copy-start.1
  67.9 1.3 %pad_dynamic-slice_fusion.1 = (bf16[2,3,16,1536]{3,2,0,1:T(8,128)(2,1)S(1)}, bf16[2,3,16,1536]{3,2,0,1:T(8,128)(2,1)S(1)}) fusion(s32[]{:T(128)S(6)} %select_n.91, bf16[2,16,16,1536]{3,2,0,1:T(8,128)(2,1)} %bitcast.58, s32[]{:T(128)S(6)} %select_n.92), kind=kLoop, calls=%fused_computation.37 | loop fusion | bytes 2162696 | tf_op jit(solution)/shard_map/dynamic_slice | solution.py:79
  69.1 0.1 pad_maximum_fusion.1
  69.3 0.5 copy-done.1
  69.7 1.2 %multiply_reduce_fusion.3 = (f32[192]{0:T(256)S(1)}, f32[192,1536]{1,0:T(8,128)S(1)}) fusion(bf16[192,1536]{1,0:T(8,128)(2,1)S(1)} %bitcast.61, bf16[1536,768]{1,0:T(8,128)(2,1)S(1)} %bitcast.57, bf16[1536,768]{1,0:T(8,128)(2,1)S(1)} %bitcast.56), kind=kOutput, calls=%fused_computation.39 | convolution fusion | flops 915996480 | bytes 6488832 | tf_op jit(solution)/shard_map/dot_general | solution.py:98
  70.9 0.2 divide_convert_fusion
  71.2 1.0 fusion.33
  72.2 0.0 copy-start.2
  72.2 0.0 copy-start.3
  72.2 0.9 add_convert_fusion
  73.1 0.5 copy-done.2
  73.6 0.5 copy-done.3
  74.1 3.4 %fusion.55 = (f32[512,1024]{1,0:T(8,128)S(1)}, f32[2,512,1024]{2,1,0:T(8,128)S(1)}) fusion(bf16[768,1024]{1,0:T(8,128)(2,1)S(1)} %copy-done.3, bf16[768,1024]{1,0:T(8,128)(2,1)S(1)} %copy-done.2, bf16[2,512,768]{2,1,0:T(8,128)(2,1)S(1)} %bitcast.60, bf16[2,512,768]{2,1,0:T(8,128)(2,1)S(1)} %bitcast.59), kind=kOutput, calls=%fused_computation.96 | convolution fusion | flops 3234332672 | bytes 12582912 | tf_op jit(solution)/shard_map/mpk,kl->mpl/dot_general | solution.py:121
  77.5 0.0 copy-start
  77.5 1.7 %multiply_reduce_fusion.2 = (f32[512]{0:T(512)S(1)}, f32[512,1024]{1,0:T(8,128)}) fusion(f32[2,512,1024]{2,1,0:T(8,128)S(1)} %get-tuple-element.26, s32[]{:T(128)S(6)} %select_n.99), kind=kLoop, calls=%fused_computation.34 | loop fusion | flops 1048064 | bytes 4196356 | tf_op jit(solution)/shard_map/reduce_sum | solution.py:126
  79.2 1.4 %reduce-precision_convert_fusion = (bf16[512,1024]{1,0:T(8,128)(2,1)S(1)}, bf16[512,1024]{1,0:T(8,128)(2,1)}) fusion(f32[512,1024]{1,0:T(8,128)S(1)} %get-tuple-element.25), kind=kLoop, calls=%fused_computation.29 | loop fusion | flops 2097152 | bytes 4194304 | tf_op jit(solution)/shard_map/convert_element_type | solution.py:132
  80.6 0.0 copy-done
  80.6 1.9 %copy.19 = f32[512,1,1024]{0,2,1:T(8,128)S(1)} copy(f32[512,1,1024]{2,0,1:T(8,128)} %bitcast.53) | data formatting | bytes 4194304 | tf_op jit(solution)/shard_map/broadcast_in_dim | solution.py:139
  82.5 2.9 %copy.17 = f32[512,1024]{0,1:T(8,128)} copy(f32[512,1024]{1,0:T(8,128)} %get-tuple-element.8) | data formatting | bytes 4194304 | tf_op jit(solution)/shard_map/mul | solution.py:140
  85.4 8.2 %fusion = f32[1024,3072]{1,0:T(8,128)S(1)} fusion(s32[3072]{0:T(1024)S(1)} %eq.64, bf16[512,1024]{1,0:T(8,128)(2,1)} %get-tuple-element.12, bf16[512,1024]{1,0:T(8,128)(2,1)S(1)} %get-tuple-element.11), kind=kOutput, calls=%fused_computation.1 | convolution fusion | flops 6449790976 | bytes 14692352 | tf_op jit(solution)/shard_map/dot_general | solution.py:134
  93.6 3.8 %slice_add_fusion = f32[512,3072]{1,0:T(8,128)} fusion(f32[1024,3072]{1,0:T(8,128)S(1)} %fusion), kind=kLoop, calls=%fused_computation.5 | loop fusion | flops 1572864 | bytes 18874368 | tf_op jit(solution)/shard_map/add | solution.py:138
  97.4 6.6 %copy.18 = f32[512,3072]{0,1:T(8,128)} copy(f32[512,3072]{1,0:T(8,128)} %slice_add_fusion) | data formatting | bytes 12582912 | tf_op jit(solution)/shard_map/add | solution.py:138
  104.0 4.0 %multiply_reduce_fusion.1 = (f32[512,4]{0,1:T(4,128)S(1)}, f32[512,4]{0,1:T(4,128)S(1)}) fusion(f32[512,3,1024]{0,2,1:T(8,128)} %bitcast.49, f32[512,1,1024]{0,2,1:T(8,128)S(1)} %copy.19, f32[512,1024]{0,1:T(8,128)} %copy.17), kind=kLoop, calls=%fused_computation.4 | loop fusion | flops 10481664 | bytes 10502144 | tf_op jit(solution)/shard_map/reduce_sum | solution.py:140
  108.0 0.6 reshape.243
  (13 shorter events, 0.2 us)
Async XLA Ops:
  6.5 61.3 %all-gather.2.cloned.1.call-start = ((), (), s32[]{:S(2)}) async-start(), calls=%async_computation | async-start | bytes 1622016 | tf_op jit(solution)/shard_map/all_gather | solution.py:73
  67.9 1.8 %copy-start.1 = (bf16[12,128,768]{2,1,0:T(8,128)(2,1)S(1)}, bf16[12,128,768]{2,1,0:T(8,128)(2,1)}, u32[]{:S(2)}) copy-start(bf16[12,128,768]{2,1,0:T(8,128)(2,1)} %get-tuple-element.18) | copy-start | bytes 7077892
  72.2 1.4 %copy-start.2 = (bf16[768,1024]{1,0:T(8,128)(2,1)S(1)}, bf16[768,1024]{1,0:T(8,128)(2,1)}, u32[]{:S(2)}) copy-start(bf16[768,1024]{1,0:T(8,128)(2,1)} %fusion.7) | copy-start | bytes 4718596
  72.2 1.9 %copy-start.3 = (bf16[768,1024]{1,0:T(8,128)(2,1)S(1)}, bf16[768,1024]{1,0:T(8,128)(2,1)}, u32[]{:S(2)}) copy-start(bf16[768,1024]{1,0:T(8,128)(2,1)} %fusion.6) | copy-start | bytes 4718596
  77.5 3.1 %copy-start = (f32[512,1024]{1,0:T(8,128)}, f32[512,1024]{1,0:T(8,128)S(1)}, u32[]{:S(2)}) copy-start(f32[512,1024]{1,0:T(8,128)S(1)} %get-tuple-element.25) | copy-start | bytes 6291460
Sparse Core Ops, SparseCore 0:
  10.2 57.5 all-gather.1

commit v5 on v1

--- a/solution.py
+++ b/solution.py
@@ -3,6 +3,8 @@
 import jax
 import jax.numpy as jnp
 from jax import lax
+from jax.experimental import pallas as pl
+from jax.experimental.pallas import tpu as pltpu
 from jax.sharding import PartitionSpec as P
 
 NT = 1536
@@ -18,10 +20,10 @@
 
 
 def forward_table():
-    coarse = NT // 64
+    coarse = NT // 128
     bins = jnp.arange(NF, dtype=jnp.int32)[None, :]
     cos_a, sin_a = unit_angles(jnp.arange(coarse, dtype=jnp.int32)[:, None] * bins, coarse)
-    cos_c, sin_c = unit_angles(jnp.arange(64, dtype=jnp.int32)[:, None] * bins, NT)
+    cos_c, sin_c = unit_angles(jnp.arange(128, dtype=jnp.int32)[:, None] * bins, NT)
     cos_t = cos_a[:, None, :] * cos_c[None] - sin_a[:, None, :] * sin_c[None]
     sin_t = sin_a[:, None, :] * cos_c[None] + cos_a[:, None, :] * sin_c[None]
     table = jnp.concatenate([cos_t, -sin_t], axis=-1).astype(jnp.bfloat16)
@@ -29,11 +31,11 @@
 
 
 def inverse_table():
-    coarse = NT // 64
-    groups = LAGS // 64
+    coarse = NT // 128
+    groups = LAGS // 128
     bins = jnp.arange(NF, dtype=jnp.int32)[:, None]
     cos_a, sin_a = unit_angles(bins * (jnp.arange(groups, dtype=jnp.int32)[None, :] - groups // 2), coarse)
-    cos_c, sin_c = unit_angles(bins * jnp.arange(64, dtype=jnp.int32)[None, :], NT)
+    cos_c, sin_c = unit_angles(bins * jnp.arange(128, dtype=jnp.int32)[None, :], NT)
     cos_t = cos_a[:, :, None] * cos_c[:, None, :] - sin_a[:, :, None] * sin_c[:, None, :]
     sin_t = sin_a[:, :, None] * cos_c[:, None, :] + cos_a[:, :, None] * sin_c[:, None, :]
     weight = jnp.where(bins == 0, 1.0, 2.0).astype(jnp.float32)[:, :, None]
@@ -57,6 +59,79 @@
     real_part = src_re * rec_re + src_im * rec_im
     imag_part = src_re * rec_im - src_im * rec_re
     return jnp.concatenate([real_part, imag_part], axis=-1).astype(jnp.bfloat16)
+
+
+PAIR_BLOCK = 128
+
+
+def coherence_kernel(own_ref, stretch_ref, crossed_ref, inverse_ref, out_ref, picks_ref):
+    minutes = crossed_ref.shape[0]
+    moves = stretch_ref.shape[0] - 1
+
+    @pl.when(pl.program_id(0) == 0)
+    def _():
+        rows = lax.broadcasted_iota(jnp.int32, (LAGS, LAGS), 0)
+        for move in range(moves):
+            picks_ref[:, move * LAGS:(move + 1) * LAGS] = (
+                rows == stretch_ref[move + 1:move + 2, :]
+            ).astype(jnp.bfloat16)
+
+    inverse = inverse_ref[...]
+    own = own_ref[0]
+    stacked = None
+    current = None
+    for minute in range(minutes):
+        correlation = jnp.dot(crossed_ref[minute], inverse, preferred_element_type=jnp.float32)
+        if stacked is None:
+            stacked, current = correlation, correlation
+        else:
+            stacked = stacked + correlation
+            current = jnp.where(own == minute, correlation, current)
+    high = stacked.astype(jnp.bfloat16)
+    low = (stacked - high.astype(jnp.float32)).astype(jnp.bfloat16)
+    picks = picks_ref[...]
+    moved = jnp.dot(high, picks, preferred_element_type=jnp.float32) + jnp.dot(
+        low, picks, preferred_element_type=jnp.float32
+    )
+    scale = 1.0 / LAGS
+    current_power = jnp.sum(current * current, axis=1, keepdims=True) * scale
+    lanes = lax.broadcasted_iota(jnp.int32, out_ref.shape, 1)
+    result = jnp.zeros(out_ref.shape, jnp.float32)
+    for stretch in range(moves + 1):
+        if stretch == 0:
+            shifted = stacked
+        else:
+            shifted = moved[:, (stretch - 1) * LAGS:stretch * LAGS]
+        numerator = jnp.sum(current * shifted, axis=1, keepdims=True) * scale
+        shifted_power = jnp.sum(shifted * shifted, axis=1, keepdims=True) * scale
+        value = numerator / jnp.sqrt((current_power + epsilon) * (shifted_power + epsilon))
+        result = jnp.where(lanes == stretch, value, result)
+    out_ref[...] = result
+
+
+def coherence(own_minute, stretch_index, crossed, inverse):
+    minutes, pair_count, width = crossed.shape
+    stretch_count = stretch_index.shape[0]
+    own = jnp.reshape(own_minute, (1,)).astype(jnp.int32)
+    out = pl.pallas_call(
+        coherence_kernel,
+        grid_spec=pltpu.PrefetchScalarGridSpec(
+            num_scalar_prefetch=1,
+            grid=(pair_count // PAIR_BLOCK,),
+            in_specs=[
+                pl.BlockSpec(stretch_index.shape, lambda i, own: (0, 0)),
+                pl.BlockSpec((minutes, PAIR_BLOCK, width), lambda i, own: (0, i, 0)),
+                pl.BlockSpec(inverse.shape, lambda i, own: (0, 0)),
+            ],
+            out_specs=pl.BlockSpec((PAIR_BLOCK, 128), lambda i, own: (i, 0)),
+            scratch_shapes=[pltpu.VMEM((LAGS, (stretch_count - 1) * LAGS), jnp.bfloat16)],
+        ),
+        out_shape=jax.ShapeDtypeStruct((pair_count, 128), jnp.float32),
+        compiler_params=pltpu.CompilerParams(
+            dimension_semantics=("arbitrary",), vmem_limit_bytes=48 << 20
+        ),
+    )(own, stretch_index, crossed, inverse)
+    return out[:, :stretch_count].T
 
 
 def body(record, pairs, stretch_index):
@@ -89,24 +164,19 @@
     far_slot = pairs - (blocks - 2 - position) * block_rows + 3 * block_rows
     slot_index = jnp.where(is_near, near_slot, far_slot)
     source_count, recv_count = slot_index.shape
+    pair_count = source_count * recv_count
     sources = whitened[:, block_rows:2 * block_rows:8]
-    receivers = jnp.take(whitened, slot_index.reshape(-1), axis=1, mode="clip")
+    selector = (
+        slot_index.reshape(pair_count, 1) == jnp.arange(slot_rows, dtype=jnp.int32)[None, :]
+    ).astype(jnp.bfloat16)
+    receivers = jnp.einsum(
+        "pq,mqk->mpk", selector, whitened, preferred_element_type=jnp.float32
+    )
     receivers = receivers.reshape(minutes, source_count, recv_count, 2 * NF)
     crossed = cross_spectrum(sources[:, :, None, :], receivers)
-    pair_count = source_count * recv_count
     crossed = crossed.reshape(minutes, pair_count, 2 * NF)
-    correlation = jnp.einsum(
-        "mpk,kl->mlp", crossed, inverse_table(), preferred_element_type=jnp.float32
-    )
-    current = correlation[0]
-    stacked = jnp.sum(correlation, axis=0)
-    current_power = jnp.mean(current * current, axis=0)
+    result = coherence(0, stretch_index, crossed, inverse_table())
     stretch_count = stretch_index.shape[0]
-    shifted = jnp.take(stacked, stretch_index.reshape(-1), axis=0, mode="clip")
-    shifted = shifted.reshape(stretch_count, LAGS, pair_count)
-    numerator = jnp.mean(current[None] * shifted, axis=1)
-    shifted_power = jnp.mean(shifted * shifted, axis=1)
-    result = numerator / jnp.sqrt((current_power[None] + epsilon) * (shifted_power + epsilon))
     return result.reshape(1, stretch_count, source_count, recv_count)
 
 

time: 90.4 us -> 58.4 us (0.65)
  local copies, waits for them, and re-layouts: 42.3 us -> 2.45 us
  Pallas kernels: 0 us -> 14.9 us
  other arithmetic: 19.5 us -> 12.7 us
  starting transfers between devices: 18.6 us -> 21.2 us
  waiting for transfers between devices: 4.68 us -> 2.36 us
    gather x2 -> x0, local copies, waits for them, and re-layouts: 36 us -> none  [the longest x1 19.2 us: body(): receivers = jnp.take(whitened, slot_index.reshape(-1), axis=1, mode='clip')]
    pallas_call x0 -> x1, Pallas kernels: none -> 14.9 us  [coherence(): pl.pallas_call(coherence_kernel, grid_spec=pltpu.PrefetchScalarGridSpec(n...]
    reduce_sum x2 -> x0, other arithmetic: 5.56 us -> none  [the longest x1 5.35 us: body(): shifted_power = jnp.mean(shifted * shifted, axis=1)]
    ppermute x1, waiting for transfers between devices: 4.66 us -> 0.01 us  [body(): lax.ppermute(own_block, 'chan', [(s, s - 1) for s in range(1, blocks)])]
    convert_element_type x1 -> x0, other arithmetic: 4.05 us -> none  [cross_spectrum(): receiver_vals = receivers.astype(jnp.float32)]
    ppermute x1, starting transfers between devices: 3.49 us -> 6.51 us  [body(): lax.ppermute(own_block, 'chan', [(s, blocks - s) for s in range(1, blocks)])]
    dot_general x1, matrix products: 3.43 us -> 1.03 us  [body(): jnp.einsum('pq,mqk->mpk', selector, whitened, preferred_element_type=jnp....]
    ppermute x1, waiting for transfers between devices: 0.01 us -> 2.35 us  [body(): lax.ppermute(own_block, 'chan', [(s, blocks - s) for s in range(1, blocks)])]
  transfers between devices with their start and end apart: 6 -> 6, of which waited for: 1 -> 1; matrix products, arithmetic and copies ran while one was open for 10% -> 22% of each run, Pallas kernels for 0% -> 0%
where the time goes in v5:
time: 58.4 us; the launch traced here: 57.8 us
  starting transfers between devices  21.2 us (36%)
  Pallas kernels  14.9 us (26%)
  other arithmetic  12.7 us (22%)
  matrix products  3.88 us (7%)
  local copies, waits for them, and re-layouts  2.45 us (4%)
  waiting for transfers between devices  2.36 us (4%)
    pallas_call x1, Pallas kernels, coherence(): pl.pallas_call(coherence_kernel, grid_spec=pltpu.PrefetchScalarGridSpec(n...  14.9 us
    ppermute x1, starting transfers between devices, body(): lax.ppermute(own_block, 'chan', [(s, blocks - s) for s in range(1, blocks)])  6.51 us
    ppermute x1, starting transfers between devices, body(): lax.ppermute(own_block, 'chan', [(s, blocks - 2 - s) for s in range(block...  5.23 us
    another operation x4, other arithmetic  4.93 us
    ppermute x1, starting transfers between devices, body(): lax.ppermute(own_block, 'chan', [(s, s + 1) for s in range(blocks - 1)])  3.99 us
    sin x3, other arithmetic, unit_angles(): return (jnp.cos(phase), jnp.sin(phase))  3.4 us
    dot_general x1, matrix products, body(): jnp.dot(candidates.reshape(minutes * slot_rows, NT), forward_table(), pre...  2.86 us
    ppermute x1, waiting for transfers between devices, body(): lax.ppermute(own_block, 'chan', [(s, blocks - s) for s in range(1, blocks)])  2.35 us
  transfers between devices with their start and end apart: 6, of which 1 were waited for; matrix products, arithmetic and copies ran while one was open for 22% of the time, Pallas kernels for 0%

profile of v5, /device:TPU:1, one launch (start us, length us, event | category | flops | bytes accessed | tf_op | source)
XLA Modules:
  0.0 57.8 jit_solution(11189957998998430959)
XLA Ops:
  0.0 2.0 %collective-permute-start = (bf16[1,16,1536]{2,1,0:T(8,128)(2,1)}, bf16[1,16,1536]{2,1,0:T(8,128)(2,1)S(1)}, u32[]{:S(2)}, u32[]{:S(2)}) collective-permute-start(bf16[1,16,1536]{2,1,0:T(8,128)(2,1)} %param.3), channel_id=1, source_target_pairs={{0,1},{1,0},{2,3},{3,2},{4,5},{5,4},{6,7},{7,6},{8,9},{9,8},{10,11... | collective-permute-start | bytes 147464 | tf_op jit(solution)/shard_map/ppermute | solution.py:144
  2.0 0.8 %constant_dynamic-update-slice_fusion.1 = bf16[2,16,1536]{2,1,0:T(8,128)(2,1)S(1)} fusion(bf16[1,16,1536]{2,1,0:T(8,128)(2,1)} %param.3), kind=kLoop, calls=%fused_computation.59 | loop fusion | bytes 98304
  2.9 1.6 %fusion.16 = (f32[128,768]{1,0:T(8,128)S(1)}, f32[128,768]{1,0:T(8,128)S(1)}) fusion(), kind=kLoop, calls=%fused_computation.32 | loop fusion | flops 884736 | bytes 786432 | tf_op jit(solution)/shard_map/sin | solution.py:19
  4.5 0.2 fusion.28
  4.7 1.6 %fusion.12 = (f32[768,128]{1,0:T(8,128)S(1)}, f32[768,128]{1,0:T(8,128)S(1)}) fusion(), kind=kLoop, calls=%fused_computation.27 | loop fusion | flops 884736 | bytes 786432 | tf_op jit(solution)/shard_map/sin | solution.py:19
  6.3 0.2 fusion.36
  6.5 0.2 copy.5
  6.7 0.2 copy.6
  6.8 1.8 %multiply_subtract_fusion = (f32[768,8,128]{2,1,0:T(8,128)S(1)}, f32[768,8,128]{2,1,0:T(8,128)S(1)}) fusion(f32[768,128]{1,0:T(8,128)S(1)} %get-tuple-element.21, f32[768,8]{1,0:T(8,128)S(1)} %copy.6, f32[768,128]{1,0:T(8,128)S(1)} %get-tuple-element.22, f32[768,8]{1,0:T(8,128)S(1)} %copy.5), kind=kLoop, calls=%fused_computation.13 | loop fusion | flops 4718592 | bytes 7127040 | tf_op jit(solution)/shard_map/sub | solution.py:39
  8.6 0.6 fusion.4
  9.2 0.6 fusion.5
  9.8 1.9 %pad_maximum_fusion.1.inverse_ref = bf16[1536,1024]{1,0:T(8,128)(2,1)} fusion(bf16[768,1024]{1,0:T(8,128)(2,1)S(1)} %fusion.4, bf16[768,1024]{1,0:T(8,128)(2,1)S(1)} %fusion.5), kind=kLoop, calls=%fused_computation.11 | loop fusion | flops 6291456 | bytes 6291456 | tf_op jit(solution)/shard_map/concatenate | solution.py:42
  11.8 0.0 copy-start.2
  11.8 0.0 copy-start.1
  11.8 2.9 %subtract_convert_fusion = (bf16[12,128,768]{2,1,0:T(8,128)(2,1)S(1)}, bf16[12,128,768]{2,1,0:T(8,128)(2,1)}) fusion(f32[128,768]{1,0:T(8,128)S(1)} %get-tuple-element.17, f32[12,768]{1,0:T(8,128)S(1)} %get-tuple-element.19, f32[128,768]{1,0:T(8,128)S(1)} %get-tuple-element.18, f32[12,768]{1,0:T(8,128)S(1)} %get-tuple-element.20), kind=kLoop, calls=%fused_computation.5 | loop fusion | flops 10616832 | bytes 5578752 | tf_op jit(solution)/shard_map/convert.10
  14.6 0.0 collective-permute-done
  14.6 4.0 %collective-permute-start.1 = (bf16[2,16,1536]{2,1,0:T(8,128)(2,1)S(1)}, bf16[2,16,1536]{2,1,0:T(8,128)(2,1)S(1)}, u32[]{:S(2)}, u32[]{:S(2)}) collective-permute-start(bf16[2,16,1536]{2,1,0:T(8,128)(2,1)S(1)} %constant_dynamic-update-slice_fusion), channel_id=1, source_target_pairs={{0,2},{2,4},{4,6},{6,8},{8,10},{10,12},{12,14},{14,16},{16,18},{18... | collective-permute-start | bytes 294920 | tf_op jit(solution)/shard_map/ppermute | solution.py:147
  18.6 0.0 copy-done.2
  18.7 1.9 %collective-permute-start.2 = (bf16[2,16,1536]{2,1,0:T(8,128)(2,1)S(1)}, bf16[2,16,1536]{2,1,0:T(8,128)(2,1)S(1)}, u32[]{:S(2)}, u32[]{:S(2)}) collective-permute-start(bf16[2,16,1536]{2,1,0:T(8,128)(2,1)S(1)} %constant_dynamic-update-slice_fusion), channel_id=1, source_target_pairs={{2,0},{4,2},{6,4},{8,6},{10,8},{12,10},{14,12},{16,14},{18,16},{20... | collective-permute-start | bytes 294920 | tf_op jit(solution)/shard_map/ppermute | solution.py:148
  20.6 5.2 %collective-permute-start.3 = (bf16[2,16,1536]{2,1,0:T(8,128)(2,1)S(1)}, bf16[2,16,1536]{2,1,0:T(8,128)(2,1)S(1)}, u32[]{:S(2)}, u32[]{:S(2)}) collective-permute-start(bf16[2,16,1536]{2,1,0:T(8,128)(2,1)S(1)} %constant_dynamic-update-slice_fusion), channel_id=1, source_target_pairs={{0,28},{2,26},{4,24},{6,22},{8,20},{10,18},{12,16},{14,14},{16,12}... | collective-permute-start | bytes 294920 | tf_op jit(solution)/shard_map/ppermute | solution.py:149
  25.8 1.5 %collective-permute-start.4 = (bf16[2,16,1536]{2,1,0:T(8,128)(2,1)S(1)}, bf16[2,16,1536]{2,1,0:T(8,128)(2,1)S(1)}, u32[]{:S(2)}, u32[]{:S(2)}) collective-permute-start(bf16[2,16,1536]{2,1,0:T(8,128)(2,1)S(1)} %constant_dynamic-update-slice_fusion), channel_id=1, source_target_pairs={{0,30},{2,28},{4,26},{6,24},{8,22},{10,20},{12,18},{14,16},{16,14}... | collective-permute-start | bytes 294920 | tf_op jit(solution)/shard_map/ppermute | solution.py:150
  27.4 6.5 %collective-permute-start.5 = (bf16[2,16,1536]{2,1,0:T(8,128)(2,1)S(1)}, bf16[2,16,1536]{2,1,0:T(8,128)(2,1)S(1)}, u32[]{:S(2)}, u32[]{:S(2)}) collective-permute-start(bf16[2,16,1536]{2,1,0:T(8,128)(2,1)S(1)} %constant_dynamic-update-slice_fusion), channel_id=1, source_target_pairs={{2,30},{4,28},{6,26},{8,24},{10,22},{12,20},{14,18},{16,16},{18,14... | collective-permute-start | bytes 294920 | tf_op jit(solution)/shard_map/ppermute | solution.py:151
  33.9 0.0 collective-permute-done.1
  33.9 0.0 copy-done.1
  33.9 0.0 collective-permute-done.2
  34.0 0.0 collective-permute-done.3
  34.0 0.0 collective-permute-done.4
  34.0 2.4 %collective-permute-done.5 = bf16[2,16,1536]{2,1,0:T(8,128)(2,1)S(1)} collective-permute-done((bf16[2,16,1536]{2,1,0:T(8,128)(2,1)S(1)}, bf16[2,16,1536]{2,1,0:T(8,128)(2,1)S(1)}, u32[]{:S(2)}, u32[]{:S(2)}) %collective-permute-start.5) | collective-permute-done | bytes 98336 | tf_op jit(solution)/shard_map/ppermute | solution.py:151
  36.4 2.9 %multiply_reduce_fusion = (f32[192]{0:T(256)S(1)}, f32[192,1536]{1,0:T(8,128)S(1)}) fusion(bf16[192,1536]{1,0:T(8,128)(2,1)S(1)} %bitcast.48, bf16[1536,768]{1,0:T(8,128)(2,1)} %bitcast.47, bf16[1536,768]{1,0:T(8,128)(2,1)S(1)} %bitcast.46), kind=kOutput, calls=%fused_computation.17 | convolution fusion | flops 915996480 | bytes 6488832 | tf_op jit(solution)/shard_map/dot_general | solution.py:154
  39.3 0.2 divide_convert_fusion
  39.5 1.0 %fusion.21 = f32[2,1536,512]{1,2,0:T(8,128)S(1)} fusion(bf16[2,96,1536]{2,1,0:T(8,128)(2,1)S(1)} %bitcast.45, s32[512]{0:T(512)S(1)} %bitcast.49), kind=kOutput, calls=%fused_computation.38 | convolution fusion | flops 302039040 | bytes 6883328 | tf_op jit(solution)/shard_map/pq,mqk->mpk/dot_general | solution.py:172
  40.5 0.9 %add_convert_fusion = (bf16[2,2,256,768]{3,2,1,0:T(8,128)(2,1)S(1)}, bf16[2,2,256,768]{3,2,1,0:T(8,128)(2,1)S(1)}) fusion(f32[2,2,256,1536]{3,2,1,0:T(8,128)S(1)} %bitcast.39, f32[2,2,768]{2,1,0:T(2,128)S(1)} %get-tuple-element.12, f32[2,2,768]{2,1,0:T(2,128)S(1)} %get-tuple-element.11), kind=kLoop, calls=%fused_computation.15 | loop fusion | flops 6291456 | bytes 9461760 | tf_op jit(solution)/shard_map/convert.6
  41.4 0.0 copy-start
  41.5 0.2 pad_maximum_fusion.crossed_ref
  41.7 0.5 copy-done
  42.2 14.9 %shard_map.37 = f32[512,128]{1,0:T(8,128)S(1)} custom-call(s32[1]{0:T(128)} %constant.23.clone.1.own_ref, s32[4,1024]{1,0:T(4,128)S(1)} %copy-done, bf16[2,512,1536]{2,1,0:T(8,128)(2,1)S(1)} %pad_maximum_fusion.crossed_ref, bf16[1536,1024]{1,0:T(8,128)(2,1)} %pad_maximum_fusion.1.inverse_ref), custom_call_target="tpu_custom_call" | custom-call | tf_op jit(solution)/shard_map/pallas_call | solution.py:116
  57.1 0.7 %copy.7 = f32[1,4,2,256]{3,2,1,0:T(2,128)} copy(f32[1,4,2,256]{1,3,2,0:T(8,128)S(1)} %bitcast.38) | data formatting | bytes 16384 | tf_op jit(solution)/shard_map/reshape | solution.py:180
  (18 shorter events, 0.2 us)
Async XLA Ops:
  0.0 14.6 %collective-permute-start = (bf16[1,16,1536]{2,1,0:T(8,128)(2,1)}, bf16[1,16,1536]{2,1,0:T(8,128)(2,1)S(1)}, u32[]{:S(2)}, u32[]{:S(2)}) collective-permute-start(bf16[1,16,1536]{2,1,0:T(8,128)(2,1)} %param.3), channel_id=1, source_target_pairs={{0,1},{1,0},{2,3},{3,2},{4,5},{5,4},{6,7},{7,6},{8,9},{9,8},{10,11... | collective-permute-start | bytes 147464 | tf_op jit(solution)/shard_map/ppermute | solution.py:144
  11.8 6.9 %copy-start.2 = (s32[2,256]{1,0:T(2,128)S(1)}, s32[2,256]{1,0:T(2,128)}, u32[]{:S(2)}) copy-start(s32[2,256]{1,0:T(2,128)} %param.4) | copy-start | bytes 6148
  11.8 22.1 %copy-start.1 = (bf16[1,16,1536]{2,1,0:T(8,128)(2,1)S(1)}, bf16[1,16,1536]{2,1,0:T(8,128)(2,1)}, u32[]{:S(2)}) copy-start(bf16[1,16,1536]{2,1,0:T(8,128)(2,1)} %param.3) | copy-start | bytes 147460
  14.6 19.2 %collective-permute-start.1 = (bf16[2,16,1536]{2,1,0:T(8,128)(2,1)S(1)}, bf16[2,16,1536]{2,1,0:T(8,128)(2,1)S(1)}, u32[]{:S(2)}, u32[]{:S(2)}) collective-permute-start(bf16[2,16,1536]{2,1,0:T(8,128)(2,1)S(1)} %constant_dynamic-update-slice_fusion), channel_id=1, source_target_pairs={{0,2},{2,4},{4,6},{6,8},{8,10},{10,12},{12,14},{14,16},{16,18},{18... | collective-permute-start | bytes 294920 | tf_op jit(solution)/shard_map/ppermute | solution.py:147
  18.7 15.3 %collective-permute-start.2 = (bf16[2,16,1536]{2,1,0:T(8,128)(2,1)S(1)}, bf16[2,16,1536]{2,1,0:T(8,128)(2,1)S(1)}, u32[]{:S(2)}, u32[]{:S(2)}) collective-permute-start(bf16[2,16,1536]{2,1,0:T(8,128)(2,1)S(1)} %constant_dynamic-update-slice_fusion), channel_id=1, source_target_pairs={{2,0},{4,2},{6,4},{8,6},{10,8},{12,10},{14,12},{16,14},{18,16},{20... | collective-permute-start | bytes 294920 | tf_op jit(solution)/shard_map/ppermute | solution.py:148
  20.6 13.4 %collective-permute-start.3 = (bf16[2,16,1536]{2,1,0:T(8,128)(2,1)S(1)}, bf16[2,16,1536]{2,1,0:T(8,128)(2,1)S(1)}, u32[]{:S(2)}, u32[]{:S(2)}) collective-permute-start(bf16[2,16,1536]{2,1,0:T(8,128)(2,1)S(1)} %constant_dynamic-update-slice_fusion), channel_id=1, source_target_pairs={{0,28},{2,26},{4,24},{6,22},{8,20},{10,18},{12,16},{14,14},{16,12}... | collective-permute-start | bytes 294920 | tf_op jit(solution)/shard_map/ppermute | solution.py:149
  25.8 8.2 %collective-permute-start.4 = (bf16[2,16,1536]{2,1,0:T(8,128)(2,1)S(1)}, bf16[2,16,1536]{2,1,0:T(8,128)(2,1)S(1)}, u32[]{:S(2)}, u32[]{:S(2)}) collective-permute-start(bf16[2,16,1536]{2,1,0:T(8,128)(2,1)S(1)} %constant_dynamic-update-slice_fusion), channel_id=1, source_target_pairs={{0,30},{2,28},{4,26},{6,24},{8,22},{10,20},{12,18},{14,16},{16,14}... | collective-permute-start | bytes 294920 | tf_op jit(solution)/shard_map/ppermute | solution.py:150
  27.4 9.0 %collective-permute-start.5 = (bf16[2,16,1536]{2,1,0:T(8,128)(2,1)S(1)}, bf16[2,16,1536]{2,1,0:T(8,128)(2,1)S(1)}, u32[]{:S(2)}, u32[]{:S(2)}) collective-permute-start(bf16[2,16,1536]{2,1,0:T(8,128)(2,1)S(1)} %constant_dynamic-update-slice_fusion), channel_id=1, source_target_pairs={{2,30},{4,28},{6,26},{8,24},{10,22},{12,20},{14,18},{16,16},{18,14... | collective-permute-start | bytes 294920 | tf_op jit(solution)/shard_map/ppermute | solution.py:151
  41.4 0.7 %copy-start = (s32[4,1024]{1,0:T(4,128)S(1)}, s32[4,1024]{1,0:T(4,128)}, u32[]{:S(2)}) copy-start(s32[4,1024]{1,0:T(4,128)} %stretch_ref.1) | copy-start | bytes 49156

commit v6 on v5

--- a/solution.py
+++ b/solution.py
@@ -146,36 +146,41 @@
     own_block = jnp.concatenate(parts, axis=0)
     below = lax.ppermute(own_block, "chan", [(s, s + 1) for s in range(blocks - 1)])
     above = lax.ppermute(own_block, "chan", [(s, s - 1) for s in range(1, blocks)])
-    far_low = lax.ppermute(own_block, "chan", [(s, blocks - 2 - s) for s in range(blocks - 1)])
-    far_mid = lax.ppermute(own_block, "chan", [(s, blocks - 1 - s) for s in range(blocks)])
-    far_high = lax.ppermute(own_block, "chan", [(s, blocks - s) for s in range(1, blocks)])
-    candidates = jnp.concatenate([below, own_block, above, far_low, far_mid, far_high], axis=1)
-    slot_rows = candidates.shape[1]
-    spectrum = jnp.dot(
-        candidates.reshape(minutes * slot_rows, NT), forward_table(),
-        preferred_element_type=jnp.float32,
-    )
-    whitened = whiten(spectrum).reshape(minutes, slot_rows, 2 * NF)
+    near = jnp.concatenate([below, own_block, above], axis=1)
+    far = lax.ppermute(near, "chan", [(s, blocks - 1 - s) for s in range(blocks)])
+    forward = forward_table()
+    inverse = inverse_table()
+    slot_rows = near.shape[1]
+
+    def spectra(rows):
+        spectrum = jnp.dot(
+            rows.reshape(minutes * slot_rows, NT), forward, preferred_element_type=jnp.float32
+        )
+        return whiten(spectrum).reshape(minutes, slot_rows, 2 * NF)
 
     position = lax.axis_index("chan")
-    column_index = jnp.arange(pairs.shape[1], dtype=jnp.int32)[None, :]
-    is_near = column_index < pairs.shape[1] // 2
-    near_slot = pairs - (position - 1) * block_rows
-    far_slot = pairs - (blocks - 2 - position) * block_rows + 3 * block_rows
-    slot_index = jnp.where(is_near, near_slot, far_slot)
-    source_count, recv_count = slot_index.shape
-    pair_count = source_count * recv_count
-    sources = whitened[:, block_rows:2 * block_rows:8]
-    selector = (
-        slot_index.reshape(pair_count, 1) == jnp.arange(slot_rows, dtype=jnp.int32)[None, :]
-    ).astype(jnp.bfloat16)
-    receivers = jnp.einsum(
-        "pq,mqk->mpk", selector, whitened, preferred_element_type=jnp.float32
-    )
-    receivers = receivers.reshape(minutes, source_count, recv_count, 2 * NF)
-    crossed = cross_spectrum(sources[:, :, None, :], receivers)
-    crossed = crossed.reshape(minutes, pair_count, 2 * NF)
-    result = coherence(0, stretch_index, crossed, inverse_table())
+    source_count, recv_count = pairs.shape
+    half = recv_count // 2
+    whitened_near = spectra(near)
+    sources = whitened_near[:, block_rows:2 * block_rows:8]
+
+    def half_coherence(whitened, receiver_ids, first_block):
+        slot_index = (receiver_ids - first_block * block_rows).reshape(-1, 1)
+        selector = (slot_index == jnp.arange(slot_rows, dtype=jnp.int32)[None, :]).astype(
+            jnp.bfloat16
+        )
+        receivers = jnp.einsum(
+            "pq,mqk->mpk", selector, whitened, preferred_element_type=jnp.float32
+        )
+        receivers = receivers.reshape(minutes, source_count, half, 2 * NF)
+        crossed = cross_spectrum(sources[:, :, None, :], receivers)
+        crossed = crossed.reshape(minutes, source_count * half, 2 * NF)
+        result = coherence(0, stretch_index, crossed, inverse)
+        return result.reshape(-1, source_count, half)
+
+    near_result = half_coherence(whitened_near, pairs[:, :half], position - 1)
+    far_result = half_coherence(spectra(far), pairs[:, half:], blocks - 2 - position)
+    result = jnp.concatenate([near_result, far_result], axis=2)
     stretch_count = stretch_index.shape[0]
     return result.reshape(1, stretch_count, source_count, recv_count)
 

time: 58.4 us -> 68.5 us (1.17)
  the two profiles are of different devices: /device:TPU:1 before, /device:TPU:17 now
where the time goes in v6:
time: 68.5 us; the launch traced here: 68.1 us
  other arithmetic  19.3 us (28%)
  waiting for transfers between devices  15.4 us (22%)
  Pallas kernels  14.3 us (21%)
  matrix products  7.44 us (11%)
  starting transfers between devices  7.29 us (11%)
  local copies, waits for them, and re-layouts  4.11 us (6%)
    pallas_call x2, Pallas kernels, coherence(): pl.pallas_call(coherence_kernel, grid_spec=pltpu.PrefetchScalarGridSpec(n...  14.3 us
    ppermute x1, waiting for transfers between devices, body(): lax.ppermute(near, 'chan', [(s, blocks - 1 - s) for s in range(blocks)])  11.6 us
    another operation x4, other arithmetic  6.79 us
    dot_general x2, matrix products, spectra(): jnp.dot(rows.reshape(minutes * slot_rows, NT), forward, preferred_element...  6.23 us
    sin x3, other arithmetic, unit_angles(): return (jnp.cos(phase), jnp.sin(phase))  5.82 us
    ppermute x1, starting transfers between devices, body(): lax.ppermute(own_block, 'chan', [(s, s + 1) for s in range(blocks - 1)])  3.98 us
    ppermute x1, waiting for transfers between devices, body(): lax.ppermute(own_block, 'chan', [(s, s - 1) for s in range(1, blocks)])  3.79 us
    sub x1, other arithmetic, inverse_table(): cos_a[:, :, None] * cos_c[:, None, :]  3.01 us
  transfers between devices with their start and end apart: 4, of which 2 were waited for; matrix products, arithmetic and copies ran while one was open for 30% of the time, Pallas kernels for 0%

profile of v6, /device:TPU:17, one launch (start us, length us, event | category | flops | bytes accessed | tf_op | source)
XLA Modules:
  0.0 68.1 jit_solution(8348054060419920482)
XLA Ops:
  0.0 1.2 %collective-permute-start = (bf16[1,16,1536]{2,1,0:T(8,128)(2,1)}, bf16[1,16,1536]{2,1,0:T(8,128)(2,1)}, u32[]{:S(2)}, u32[]{:S(2)}) collective-permute-start(bf16[1,16,1536]{2,1,0:T(8,128)(2,1)} %param.3), channel_id=1, source_target_pairs={{0,1},{1,0},{2,3},{3,2},{4,5},{5,4},{6,7},{7,6},{8,9},{9,8},{10,11... | collective-permute-start | bytes 147464 | tf_op jit(solution)/shard_map/ppermute | solution.py:144
  1.2 2.4 %fusion.14 = (f32[128,768]{1,0:T(8,128)S(1)}, f32[128,768]{1,0:T(8,128)}) fusion(), kind=kLoop, calls=%fused_computation.36 | loop fusion | flops 884736 | bytes 786432 | tf_op jit(solution)/shard_map/sin | solution.py:19
  3.7 0.9 %fusion.22 = (f32[12,768]{1,0:T(8,128)}, f32[12,768]{1,0:T(8,128)}) fusion(), kind=kLoop, calls=%fused_computation.49 | loop fusion | flops 82944 | bytes 73728 | tf_op jit(solution)/shard_map/sin | solution.py:19
  4.5 2.5 %fusion.10 = (f32[768,128]{1,0:T(8,128)}, f32[768,128]{1,0:T(8,128)}) fusion(), kind=kLoop, calls=%fused_computation.31 | loop fusion | flops 884736 | bytes 786432 | tf_op jit(solution)/shard_map/sin | solution.py:19
  7.0 0.2 fusion.37
  7.2 0.9 %copy.6 = f32[768,8]{1,0:T(8,128)} copy(f32[768,8]{0,1:T(8,128)S(1)} %get-tuple-element.19) | data formatting | bytes 49152 | tf_op jit(solution)/shard_map/cos | solution.py:19
  8.2 0.9 %copy.7 = f32[768,8]{1,0:T(8,128)} copy(f32[768,8]{0,1:T(8,128)S(1)} %get-tuple-element.20) | data formatting | bytes 49152 | tf_op jit(solution)/shard_map/sin | solution.py:19
  9.1 3.0 %multiply_subtract_fusion = (f32[768,8,128]{2,1,0:T(8,128)S(1)}, f32[768,8,128]{2,1,0:T(8,128)S(1)}) fusion(f32[768,128]{1,0:T(8,128)} %get-tuple-element.29, f32[768,8]{1,0:T(8,128)} %copy.7, f32[768,128]{1,0:T(8,128)} %get-tuple-element.30, f32[768,8]{1,0:T(8,128)} %copy.6), kind=kLoop, calls=%fused_computation.9 | loop fusion | flops 4718592 | bytes 7127040 | tf_op jit(solution)/shard_map/sub | solution.py:39
  12.1 0.6 fusion
  12.7 0.6 fusion.1
  13.3 0.0 copy-start.2
  13.3 0.0 copy-start.3
  13.3 0.0 copy-start.4
  13.3 0.3 pad_maximum_fusion.1.inverse_ref
  13.6 0.0 copy-start.5
  13.6 0.0 copy-start.6
  13.6 0.6 copy-done.2
  14.3 0.0 copy-done.3
  14.3 0.0 copy-done.4
  14.3 3.6 %subtract_convert_fusion = (bf16[12,128,768]{2,1,0:T(8,128)(2,1)}, bf16[12,128,768]{2,1,0:T(8,128)(2,1)}) fusion(f32[128,768]{1,0:T(8,128)S(1)} %get-tuple-element.25, f32[12,768]{1,0:T(8,128)S(1)} %copy-done.3, f32[128,768]{1,0:T(8,128)S(1)} %copy-done.2, f32[12,768]{1,0:T(8,128)S(1)} %copy-done.4), kind=kLoop, calls=%fused_computation.2 | loop fusion | flops 10616832 | bytes 5578752 | tf_op jit(solution)/shard_map/convert.14
  17.8 0.0 copy-done.5
  17.8 0.0 collective-permute-done
  17.8 0.8 %constant_dynamic-update-slice_fusion = bf16[2,16,1536]{2,1,0:T(8,128)(2,1)S(1)} fusion(bf16[2,16,1536]{2,1,0:T(8,128)(2,1)S(1)} %constant_dynamic-update-slice_fusion.1, bf16[1,16,1536]{2,1,0:T(8,128)(2,1)} %collective-permute-done), kind=kLoop, calls=%fused_computation.71 | loop fusion | bytes 98304 | tf_op jit(solution)/shard_map/concatenate | solution.py:146
  18.6 4.0 %collective-permute-start.1 = (bf16[2,16,1536]{2,1,0:T(8,128)(2,1)S(1)}, bf16[2,16,1536]{2,1,0:T(8,128)(2,1)S(1)}, u32[]{:S(2)}, u32[]{:S(2)}) collective-permute-start(bf16[2,16,1536]{2,1,0:T(8,128)(2,1)S(1)} %constant_dynamic-update-slice_fusion), channel_id=1, source_target_pairs={{0,2},{2,4},{4,6},{6,8},{8,10},{10,12},{12,14},{14,16},{16,18},{18... | collective-permute-start | bytes 294920 | tf_op jit(solution)/shard_map/ppermute | solution.py:147
  22.6 2.1 %collective-permute-start.2 = (bf16[2,16,1536]{2,1,0:T(8,128)(2,1)S(1)}, bf16[2,16,1536]{2,1,0:T(8,128)(2,1)S(1)}, u32[]{:S(2)}, u32[]{:S(2)}) collective-permute-start(bf16[2,16,1536]{2,1,0:T(8,128)(2,1)S(1)} %constant_dynamic-update-slice_fusion), channel_id=1, source_target_pairs={{2,0},{4,2},{6,4},{8,6},{10,8},{12,10},{14,12},{16,14},{18,16},{20... | collective-permute-start | bytes 294920 | tf_op jit(solution)/shard_map/ppermute | solution.py:148
  24.7 0.0 copy-done.6
  24.8 0.0 collective-permute-done.1
  24.8 3.8 %collective-permute-done.2 = bf16[2,16,1536]{2,1,0:T(8,128)(2,1)S(1)} collective-permute-done((bf16[2,16,1536]{2,1,0:T(8,128)(2,1)S(1)}, bf16[2,16,1536]{2,1,0:T(8,128)(2,1)S(1)}, u32[]{:S(2)}, u32[]{:S(2)}) %collective-permute-start.2) | collective-permute-done | bytes 98336 | tf_op jit(solution)/shard_map/ppermute | solution.py:148
  28.6 0.7 %pad_maximum_fusion.6 = bf16[2,48,1536]{2,1,0:T(8,128)(2,1)} fusion(bf16[2,16,1536]{2,1,0:T(8,128)(2,1)S(1)} %collective-permute-done.2, bf16[2,16,1536]{2,1,0:T(8,128)(2,1)S(1)} %constant_dynamic-update-slice_fusion, bf16[2,16,1536]{2,1,0:T(8,128)(2,1)S(1)} %collective-permute-done.1), kind=kLoop, calls=%fused_computation.40 | loop fusion | flops 884736 | bytes 589824 | tf_op jit(solution)/shard_map/concatenate | solution.py:149
  29.3 0.0 collective-permute-start.3
  29.3 3.5 %multiply_reduce_fusion.1 = (f32[96]{0:T(128)S(1)}, f32[96,1536]{1,0:T(8,128)S(1)}) fusion(bf16[96,1536]{1,0:T(8,128)(2,1)} %bitcast, bf16[1536,768]{1,0:T(8,128)(2,1)} %bitcast.69, bf16[1536,768]{1,0:T(8,128)(2,1)} %bitcast.67), kind=kOutput, calls=%fused_computation.23 | convolution fusion | flops 462716832 | bytes 5603712 | tf_op jit(solution)/shard_map/dot_general | solution.py:156
  32.8 0.1 divide_convert_fusion.1
  33.0 0.0 copy-start.1
  33.0 0.6 fusion.26
  33.6 11.6 %collective-permute-done.3 = bf16[2,48,1536]{2,1,0:T(8,128)(2,1)} collective-permute-done((bf16[2,48,1536]{2,1,0:T(8,128)(2,1)}, bf16[2,48,1536]{2,1,0:T(8,128)(2,1)}, u32[]{:S(2)}, u32[]{:S(2)}) %collective-permute-start.3) | collective-permute-done | bytes 294944 | tf_op jit(solution)/shard_map/ppermute | solution.py:150
  45.2 0.0 copy-done.1
  45.2 2.8 %multiply_reduce_fusion = (f32[96]{0:T(128)S(1)}, f32[96,1536]{1,0:T(8,128)S(1)}) fusion(bf16[96,1536]{1,0:T(8,128)(2,1)} %bitcast.17, bf16[1536,768]{1,0:T(8,128)(2,1)} %bitcast.70, bf16[1536,768]{1,0:T(8,128)(2,1)S(1)} %bitcast.68), kind=kOutput, calls=%fused_computation.21 | convolution fusion | flops 462716832 | bytes 5603712 | tf_op jit(solution)/shard_map/dot_general | solution.py:156
  48.0 0.1 divide_convert_fusion
  48.1 0.6 fusion.29
  48.7 2.1 %add_convert_fusion.1 = (bf16[2,2,128,768]{3,2,1,0:T(8,128)(2,1)S(1)}, bf16[2,2,128,768]{3,2,1,0:T(8,128)(2,1)S(1)}, bf16[2,2,128,768]{3,2,1,0:T(8,128)(2,1)}, bf16[2,2,128,768]{3,2,1,0:T(8,128)(2,1)}) fusion(f32[2,2,128,1536]{3,2,1,0:T(8,128)S(1)} %bitcast.59, f32[2,2,768]{2,1,0:T(2,128)S(1)} %get-tuple-element.16, f32[2,2,768]{2,1,0:T(2,128)S(1)} %get-tuple-element.15, ...), kind=kLoop, calls=%fused_computation.17 | loop fusion | flops 6291456 | bytes 9461760 | tf_op jit(solution)/shard_map/convert.10
  50.8 0.0 copy-start
  50.8 0.1 pad_maximum_fusion.4.crossed_ref
  51.0 0.6 copy-done
  51.5 7.1 %shard_map.37 = f32[256,128]{1,0:T(8,128)S(1)} custom-call(s32[1]{0:T(128)} %constant.27.clone.1.own_ref, s32[4,1024]{1,0:T(4,128)S(1)} %copy-done, bf16[2,256,1536]{2,1,0:T(8,128)(2,1)S(1)} %pad_maximum_fusion.4.crossed_ref, bf16[1536,1024]{1,0:T(8,128)(2,1)S(1)} %pad_maximum_fusion.1.inverse_ref), custom_call_target="tpu_custom_call" | custom-call | tf_op jit(solution)/shard_map/pallas_call | solution.py:116
  58.7 0.1 copy.8
  58.8 1.5 %pad_maximum_fusion.5.crossed_ref = bf16[2,256,1536]{2,1,0:T(8,128)(2,1)S(1)} fusion(bf16[2,256,768]{2,1,0:T(8,128)(2,1)} %bitcast.63, bf16[2,256,768]{2,1,0:T(8,128)(2,1)} %bitcast.64), kind=kLoop, calls=%fused_computation.13 | loop fusion | flops 3145728 | bytes 3145728 | tf_op jit(solution)/shard_map/concatenate | solution.py:61
  60.3 7.2 %shard_map.38 = f32[256,128]{1,0:T(8,128)S(1)} custom-call(s32[1]{0:T(128)} %constant.27.clone.1.own_ref, s32[4,1024]{1,0:T(4,128)S(1)} %copy-done, bf16[2,256,1536]{2,1,0:T(8,128)(2,1)S(1)} %pad_maximum_fusion.5.crossed_ref, bf16[1536,1024]{1,0:T(8,128)(2,1)S(1)} %pad_maximum_fusion.1.inverse_ref), custom_call_target="tpu_custom_call" | custom-call | tf_op jit(solution)/shard_map/pallas_call | solution.py:116
  67.4 0.1 copy.9
  67.5 0.6 maximum_bitcast_fusion
  (10 shorter events, 0.1 us)
Async XLA Ops:
  0.0 17.8 %collective-permute-start = (bf16[1,16,1536]{2,1,0:T(8,128)(2,1)}, bf16[1,16,1536]{2,1,0:T(8,128)(2,1)}, u32[]{:S(2)}, u32[]{:S(2)}) collective-permute-start(bf16[1,16,1536]{2,1,0:T(8,128)(2,1)} %param.3), channel_id=1, source_target_pairs={{0,1},{1,0},{2,3},{3,2},{4,5},{5,4},{6,7},{7,6},{8,9},{9,8},{10,11... | collective-permute-start | bytes 147464 | tf_op jit(solution)/shard_map/ppermute | solution.py:144
  13.3 1.0 %copy-start.2 = (f32[128,768]{1,0:T(8,128)S(1)}, f32[128,768]{1,0:T(8,128)}, u32[]{:S(2)}) copy-start(f32[128,768]{1,0:T(8,128)} %get-tuple-element.26) | copy-start | bytes 1179652
  13.3 1.0 %copy-start.3 = (f32[12,768]{1,0:T(8,128)S(1)}, f32[12,768]{1,0:T(8,128)}, u32[]{:S(2)}) copy-start(f32[12,768]{1,0:T(8,128)} %get-tuple-element.27) | copy-start | bytes 110596
  13.3 1.0 %copy-start.4 = (f32[12,768]{1,0:T(8,128)S(1)}, f32[12,768]{1,0:T(8,128)}, u32[]{:S(2)}) copy-start(f32[12,768]{1,0:T(8,128)} %get-tuple-element.28) | copy-start | bytes 110596
  13.6 4.2 %copy-start.5 = (bf16[1,16,1536]{2,1,0:T(8,128)(2,1)S(1)}, bf16[1,16,1536]{2,1,0:T(8,128)(2,1)}, u32[]{:S(2)}) copy-start(bf16[1,16,1536]{2,1,0:T(8,128)(2,1)} %param.3) | copy-start | bytes 147460
  13.6 11.1 %copy-start.6 = (s32[2,256]{1,0:T(2,128)S(1)}, s32[2,256]{1,0:T(2,128)}, u32[]{:S(2)}) copy-start(s32[2,256]{1,0:T(2,128)} %param.4) | copy-start | bytes 6148
  18.6 6.1 %collective-permute-start.1 = (bf16[2,16,1536]{2,1,0:T(8,128)(2,1)S(1)}, bf16[2,16,1536]{2,1,0:T(8,128)(2,1)S(1)}, u32[]{:S(2)}, u32[]{:S(2)}) collective-permute-start(bf16[2,16,1536]{2,1,0:T(8,128)(2,1)S(1)} %constant_dynamic-update-slice_fusion), channel_id=1, source_target_pairs={{0,2},{2,4},{4,6},{6,8},{8,10},{10,12},{12,14},{14,16},{16,18},{18... | collective-permute-start | bytes 294920 | tf_op jit(solution)/shard_map/ppermute | solution.py:147
  22.6 5.9 %collective-permute-start.2 = (bf16[2,16,1536]{2,1,0:T(8,128)(2,1)S(1)}, bf16[2,16,1536]{2,1,0:T(8,128)(2,1)S(1)}, u32[]{:S(2)}, u32[]{:S(2)}) collective-permute-start(bf16[2,16,1536]{2,1,0:T(8,128)(2,1)S(1)} %constant_dynamic-update-slice_fusion), channel_id=1, source_target_pairs={{2,0},{4,2},{6,4},{8,6},{10,8},{12,10},{14,12},{16,14},{18,16},{20... | collective-permute-start | bytes 294920 | tf_op jit(solution)/shard_map/ppermute | solution.py:148
  29.3 15.9 %collective-permute-start.3 = (bf16[2,48,1536]{2,1,0:T(8,128)(2,1)}, bf16[2,48,1536]{2,1,0:T(8,128)(2,1)}, u32[]{:S(2)}, u32[]{:S(2)}) collective-permute-start(bf16[2,48,1536]{2,1,0:T(8,128)(2,1)} %pad_maximum_fusion.6), channel_id=1, source_target_pairs={{0,30},{2,28},{4,26},{6,24},{8,22},{10,20},{12,18},{14,16},{16,14}... | collective-permute-start | bytes 884744 | tf_op jit(solution)/shard_map/ppermute | solution.py:150
  33.0 12.3 %copy-start.1 = (bf16[12,128,768]{2,1,0:T(8,128)(2,1)S(1)}, bf16[12,128,768]{2,1,0:T(8,128)(2,1)}, u32[]{:S(2)}) copy-start(bf16[12,128,768]{2,1,0:T(8,128)(2,1)} %get-tuple-element.11) | copy-start | bytes 7077892
  50.8 0.7 %copy-start = (s32[4,1024]{1,0:T(4,128)S(1)}, s32[4,1024]{1,0:T(4,128)}, u32[]{:S(2)}) copy-start(s32[4,1024]{1,0:T(4,128)} %stretch_ref.3) | copy-start | bytes 49156

commit v7 on v5

--- a/solution.py
+++ b/solution.py
@@ -1,3 +1,4 @@
+import functools
 import math
 
 import jax
@@ -12,6 +13,7 @@
 NF = 768
 
 epsilon = 1e-05
+EXCHANGE_BYTES = 4 << 20
 
 
 def unit_angles(numerators, period):
@@ -134,22 +136,49 @@
     return out[:, :stretch_count].T
 
 
-def body(record, pairs, stretch_index):
+def body(axis_order, record, pairs, stretch_index):
     block_rows = record.shape[1]
     minutes = lax.axis_size("tm")
     blocks = lax.axis_size("chan")
-    parts = [record]
-    for shift in range(1, minutes):
-        parts.append(
-            lax.ppermute(record, "tm", [(i, (i + shift) % minutes) for i in range(minutes)])
+    position = lax.axis_index("chan")
+    minute = lax.axis_index("tm")
+    devices = minutes * blocks
+    if devices * record.size * record.dtype.itemsize <= EXCHANGE_BYTES:
+        targets = jnp.arange(devices, dtype=jnp.int32)
+        if axis_order[0] == "tm":
+            target_block = targets % blocks
+        else:
+            target_block = targets // minutes
+        offset = position - target_block
+        readers = (jnp.abs(offset) <= 1) | (jnp.abs(position + target_block - (blocks - 1)) <= 1)
+        outgoing = jnp.where(readers[:, None, None], record, jnp.zeros_like(record))
+        incoming = lax.all_to_all(outgoing, axis_order, 0, 0, tiled=True)
+        slot_blocks = jnp.stack(
+            [position - 1, position, position + 1,
+             blocks - 2 - position, blocks - 1 - position, blocks - position]
         )
-    own_block = jnp.concatenate(parts, axis=0)
-    below = lax.ppermute(own_block, "chan", [(s, s + 1) for s in range(blocks - 1)])
-    above = lax.ppermute(own_block, "chan", [(s, s - 1) for s in range(1, blocks)])
-    far_low = lax.ppermute(own_block, "chan", [(s, blocks - 2 - s) for s in range(blocks - 1)])
-    far_mid = lax.ppermute(own_block, "chan", [(s, blocks - 1 - s) for s in range(blocks)])
-    far_high = lax.ppermute(own_block, "chan", [(s, blocks - s) for s in range(1, blocks)])
-    candidates = jnp.concatenate([below, own_block, above, far_low, far_mid, far_high], axis=1)
+        slot_blocks = jnp.clip(slot_blocks, 0, blocks - 1)
+        shifts = jnp.arange(minutes, dtype=jnp.int32)
+        slot_minutes = (minute + shifts) % minutes
+        if axis_order[0] == "tm":
+            sources_at = slot_minutes[:, None] * blocks + slot_blocks[None, :]
+        else:
+            sources_at = slot_blocks[None, :] * minutes + slot_minutes[:, None]
+        candidates = jnp.take(incoming, sources_at.reshape(-1), axis=0)
+        candidates = candidates.reshape(minutes, 6 * block_rows, NT)
+    else:
+        parts = [record]
+        for shift in range(1, minutes):
+            parts.append(
+                lax.ppermute(record, "tm", [(i, (i + shift) % minutes) for i in range(minutes)])
+            )
+        own_block = jnp.concatenate(parts, axis=0)
+        below = lax.ppermute(own_block, "chan", [(s, s + 1) for s in range(blocks - 1)])
+        above = lax.ppermute(own_block, "chan", [(s, s - 1) for s in range(1, blocks)])
+        far_low = lax.ppermute(own_block, "chan", [(s, blocks - 2 - s) for s in range(blocks - 1)])
+        far_mid = lax.ppermute(own_block, "chan", [(s, blocks - 1 - s) for s in range(blocks)])
+        far_high = lax.ppermute(own_block, "chan", [(s, blocks - s) for s in range(1, blocks)])
+        candidates = jnp.concatenate([below, own_block, above, far_low, far_mid, far_high], axis=1)
     slot_rows = candidates.shape[1]
     spectrum = jnp.dot(
         candidates.reshape(minutes * slot_rows, NT), forward_table(),
@@ -157,7 +186,6 @@
     )
     whitened = whiten(spectrum).reshape(minutes, slot_rows, 2 * NF)
 
-    position = lax.axis_index("chan")
     column_index = jnp.arange(pairs.shape[1], dtype=jnp.int32)[None, :]
     is_near = column_index < pairs.shape[1] // 2
     near_slot = pairs - (position - 1) * block_rows
@@ -181,8 +209,9 @@
 
 
 def solution(mesh):
+    axis_order = tuple(name for name in mesh.axis_names if name in ("tm", "chan"))
     return jax.shard_map(
-        body,
+        functools.partial(body, axis_order),
         mesh=mesh,
         in_specs=(P("tm", "chan", None), P("chan", None), P()),
         out_specs=P("tm", None, "chan", None),

time: 58.4 us -> 70.2 us (1.20)
  waiting for transfers between devices: 2.36 us -> 23.8 us
  starting transfers between devices: 21.2 us -> 7.1 us
  other arithmetic: 12.7 us -> 15.9 us
    all_to_all x0 -> x1, waiting for transfers between devices: none -> 23.8 us  [body(): incoming = lax.all_to_all(outgoing, axis_order, 0, 0, tiled=True)]
    ppermute x6 -> x0, starting transfers between devices: 21.2 us -> none  [the longest x1 6.51 us: body(): lax.ppermute(own_block, 'chan', [(s, blocks - s) for s in range(1, blocks)])]
    all_to_all x0 -> x1, starting transfers between devices: none -> 7.1 us  [body(): incoming = lax.all_to_all(outgoing, axis_order, 0, 0, tiled=True)]
    select_n x0 -> x4, other arithmetic: none -> 2.37 us  [the longest x1 2.22 us: body(): outgoing = jnp.where(readers[:, None, None], record, jnp.zeros_like(record))]
    ppermute x6 -> x0, waiting for transfers between devices: 2.36 us -> none  [the longest x1 2.35 us: body(): lax.ppermute(own_block, 'chan', [(s, blocks - s) for s in range(1, blocks)])]
    unnamed x14 -> x5, local copies, waits for them, and re-layouts: 1.36 us -> 0.47 us
    another operation x4, other arithmetic: 4.93 us -> 5.63 us
  transfers between devices with their start and end apart: 6 -> 1, of which waited for: 1 -> 1; matrix products, arithmetic and copies ran while one was open for 22% -> 19% of each run, Pallas kernels for 0% -> 0%
where the time goes in v7:
time: 70.2 us; the launch traced here: 69 us
  waiting for transfers between devices  23.8 us (34%)
  other arithmetic  15.9 us (23%)
  Pallas kernels  14.9 us (21%)
  starting transfers between devices  7.1 us (10%)
  matrix products  4.58 us (7%)
  local copies, waits for them, and re-layouts  2.55 us (4%)
    all_to_all x1, waiting for transfers between devices, body(): incoming = lax.all_to_all(outgoing, axis_order, 0, 0, tiled=True)  23.8 us
    pallas_call x1, Pallas kernels, coherence(): pl.pallas_call(coherence_kernel, grid_spec=pltpu.PrefetchScalarGridSpec(n...  14.9 us
    all_to_all x1, starting transfers between devices, body(): incoming = lax.all_to_all(outgoing, axis_order, 0, 0, tiled=True)  7.1 us
    another operation x4, other arithmetic  5.63 us
    dot_general x1, matrix products, body(): jnp.dot(candidates.reshape(minutes * slot_rows, NT), forward_table(), pre...  3.56 us
    sin x3, other arithmetic, unit_angles(): return (jnp.cos(phase), jnp.sin(phase))  3.4 us
    select_n x1, other arithmetic, body(): outgoing = jnp.where(readers[:, None, None], record, jnp.zeros_like(record))  2.22 us
    concatenate x1, other arithmetic, inverse_table(): jnp.concatenate([weight * cos_t, -weight * sin_t], axis=0)  1.94 us
  transfers between devices with their start and end apart: 1, of which 1 were waited for; matrix products, arithmetic and copies ran while one was open for 19% of the time, Pallas kernels for 0%

profile of v7, /device:TPU:1, one launch (start us, length us, event | category | flops | bytes accessed | tf_op | source)
XLA Modules:
  0.0 69.0 jit_solution(5985451655430574959)
XLA Ops:
  0.0 0.0 copy-start.1
  0.0 2.2 %broadcast_select_fusion = bf16[32,16,1536]{2,1,0:T(8,128)(2,1)} fusion(pred[32]{0:T(512)(128)(4,1)S(1)} %compare_or_fusion, bf16[16,1536]{1,0:T(8,128)(2,1)} %bitcast.58), kind=kLoop, calls=%fused_computation.17 | loop fusion | flops 786432 | bytes 1622048 | tf_op jit(solution)/shard_map/jit(_where)/select_n | solution.py:154
  2.2 7.1 %all-to-all-start = ((bf16[32,16,1536]{2,1,0:T(8,128)(2,1)}), bf16[32,16,1536]{2,1,0:T(8,128)(2,1)S(1)}, u32[]{:S(2)}, u32[]{:S(2)}) async-start(bf16[32,16,1536]{2,1,0:T(8,128)(2,1)} %broadcast_select_fusion), calls=%async_computation | async-start | bytes 3145728 | tf_op jit(solution)/shard_map/all_to_all | solution.py:155
  9.4 0.1 stack.27
  9.5 0.1 broadcast_add_fusion
  9.5 0.1 add.191
  9.6 0.0 copy-done.1
  9.7 0.1 add.194
  9.7 0.1 broadcast_in_dim.54
  9.8 0.1 broadcast_in_dim.55
  9.9 0.2 fusion.36
  10.1 0.2 copy.5
  10.3 0.2 copy.6
  10.5 0.2 fusion.28
  10.7 1.6 %fusion.16 = (f32[128,768]{1,0:T(8,128)S(1)}, f32[128,768]{1,0:T(8,128)S(1)}) fusion(), kind=kLoop, calls=%fused_computation.35 | loop fusion | flops 884736 | bytes 786432 | tf_op jit(solution)/shard_map/sin | solution.py:21
  12.3 1.6 %fusion.12 = (f32[768,128]{1,0:T(8,128)S(1)}, f32[768,128]{1,0:T(8,128)S(1)}) fusion(), kind=kLoop, calls=%fused_computation.30 | loop fusion | flops 884736 | bytes 786432 | tf_op jit(solution)/shard_map/sin | solution.py:21
  13.9 1.8 %multiply_subtract_fusion = (f32[768,8,128]{2,1,0:T(8,128)S(1)}, f32[768,8,128]{2,1,0:T(8,128)S(1)}) fusion(f32[768,128]{1,0:T(8,128)S(1)} %get-tuple-element.21, f32[768,8]{1,0:T(8,128)S(1)} %copy.6, f32[768,128]{1,0:T(8,128)S(1)} %get-tuple-element.22, f32[768,8]{1,0:T(8,128)S(1)} %copy.5), kind=kLoop, calls=%fused_computation.14 | loop fusion | flops 4718592 | bytes 7127040 | tf_op jit(solution)/shard_map/sub | solution.py:41
  15.7 0.6 fusion.4
  16.3 0.6 fusion.5
  16.9 1.9 %pad_maximum_fusion.1.inverse_ref = bf16[1536,1024]{1,0:T(8,128)(2,1)} fusion(bf16[768,1024]{1,0:T(8,128)(2,1)S(1)} %fusion.4, bf16[768,1024]{1,0:T(8,128)(2,1)S(1)} %fusion.5), kind=kLoop, calls=%fused_computation.12 | loop fusion | flops 6291456 | bytes 6291456 | tf_op jit(solution)/shard_map/concatenate | solution.py:44
  18.8 3.6 %subtract_convert_fusion = (bf16[12,128,768]{2,1,0:T(8,128)(2,1)}, bf16[12,128,768]{2,1,0:T(8,128)(2,1)}) fusion(f32[128,768]{1,0:T(8,128)S(1)} %get-tuple-element.17, f32[12,768]{1,0:T(8,128)S(1)} %get-tuple-element.19, f32[128,768]{1,0:T(8,128)S(1)} %get-tuple-element.18, f32[12,768]{1,0:T(8,128)S(1)} %get-tuple-element.20), kind=kLoop, calls=%fused_computation.6 | loop fusion | flops 10616832 | bytes 5578752 | tf_op jit(solution)/shard_map/convert.10
  22.4 23.8 %all-to-all-done = bf16[32,16,1536]{2,1,0:T(8,128)(2,1)S(1)} async-done(((bf16[32,16,1536]{2,1,0:T(8,128)(2,1)}), bf16[32,16,1536]{2,1,0:T(8,128)(2,1)S(1)}, u32[]{:S(2)}, u32[]{:S(2)}) %all-to-all-start) | async-done | bytes 1572896 | tf_op jit(solution)/shard_map/all_to_all | solution.py:155
  46.2 0.6 gather_fusion
  46.8 0.1 bitcast_select_fusion
  46.9 3.6 %multiply_reduce_fusion = (f32[192]{0:T(256)S(1)}, f32[192,1536]{1,0:T(8,128)S(1)}) fusion(bf16[192,1536]{1,0:T(8,128)(2,1)S(1)} %bitcast_select_fusion, bf16[1536,768]{1,0:T(8,128)(2,1)} %bitcast.57, bf16[1536,768]{1,0:T(8,128)(2,1)} %bitcast.56), kind=kOutput, calls=%fused_computation.19 | convolution fusion | flops 915996480 | bytes 6488832 | tf_op jit(solution)/shard_map/dot_general | solution.py:183
  50.5 0.2 divide_convert_fusion
  50.7 1.0 %fusion.21 = f32[2,1536,512]{1,2,0:T(8,128)S(1)} fusion(bf16[2,96,1536]{2,1,0:T(8,128)(2,1)S(1)} %bitcast.55, s32[512]{0:T(512)S(1)} %bitcast.59), kind=kOutput, calls=%fused_computation.41 | convolution fusion | flops 302039040 | bytes 6883328 | tf_op jit(solution)/shard_map/pq,mqk->mpk/dot_general | solution.py:200
  51.8 0.9 %add_convert_fusion = (bf16[2,2,256,768]{3,2,1,0:T(8,128)(2,1)S(1)}, bf16[2,2,256,768]{3,2,1,0:T(8,128)(2,1)S(1)}) fusion(f32[2,2,256,1536]{3,2,1,0:T(8,128)S(1)} %bitcast.49, f32[2,2,768]{2,1,0:T(2,128)S(1)} %get-tuple-element.12, f32[2,2,768]{2,1,0:T(2,128)S(1)} %get-tuple-element.11), kind=kLoop, calls=%fused_computation.16 | loop fusion | flops 6291456 | bytes 9461760 | tf_op jit(solution)/shard_map/convert.6
  52.7 0.0 copy-start
  52.7 0.2 pad_maximum_fusion.crossed_ref
  53.0 0.5 copy-done
  53.4 14.9 %shard_map.37 = f32[512,128]{1,0:T(8,128)S(1)} custom-call(s32[1]{0:T(128)} %constant.69.clone.1.own_ref, s32[4,1024]{1,0:T(4,128)S(1)} %copy-done, bf16[2,512,1536]{2,1,0:T(8,128)(2,1)S(1)} %pad_maximum_fusion.crossed_ref, bf16[1536,1024]{1,0:T(8,128)(2,1)} %pad_maximum_fusion.1.inverse_ref), custom_call_target="tpu_custom_call" | custom-call | tf_op jit(solution)/shard_map/pallas_call | solution.py:118
  68.3 0.7 %copy.7 = f32[1,4,2,256]{3,2,1,0:T(2,128)} copy(f32[1,4,2,256]{1,3,2,0:T(8,128)S(1)} %bitcast.48) | data formatting | bytes 16384 | tf_op jit(solution)/shard_map/reshape | solution.py:208
  (16 shorter events, 0.1 us)
Async XLA Ops:
  0.0 9.6 %copy-start.1 = (s32[2,256]{1,0:T(2,128)S(1)}, s32[2,256]{1,0:T(2,128)}, u32[]{:S(2)}) copy-start(s32[2,256]{1,0:T(2,128)} %param.4) | copy-start | bytes 6148
  2.2 44.0 %all-to-all-start = ((bf16[32,16,1536]{2,1,0:T(8,128)(2,1)}), bf16[32,16,1536]{2,1,0:T(8,128)(2,1)S(1)}, u32[]{:S(2)}, u32[]{:S(2)}) async-start(bf16[32,16,1536]{2,1,0:T(8,128)(2,1)} %broadcast_select_fusion), calls=%async_computation | async-start | bytes 3145728 | tf_op jit(solution)/shard_map/all_to_all | solution.py:155
  52.7 0.7 %copy-start = (s32[4,1024]{1,0:T(4,128)S(1)}, s32[4,1024]{1,0:T(4,128)}, u32[]{:S(2)}) copy-start(s32[4,1024]{1,0:T(4,128)} %stretch_ref.1) | copy-start | bytes 49156

commit v8 on v5

--- a/solution.py
+++ b/solution.py
@@ -146,10 +146,9 @@
     own_block = jnp.concatenate(parts, axis=0)
     below = lax.ppermute(own_block, "chan", [(s, s + 1) for s in range(blocks - 1)])
     above = lax.ppermute(own_block, "chan", [(s, s - 1) for s in range(1, blocks)])
-    far_low = lax.ppermute(own_block, "chan", [(s, blocks - 2 - s) for s in range(blocks - 1)])
-    far_mid = lax.ppermute(own_block, "chan", [(s, blocks - 1 - s) for s in range(blocks)])
-    far_high = lax.ppermute(own_block, "chan", [(s, blocks - s) for s in range(1, blocks)])
-    candidates = jnp.concatenate([below, own_block, above, far_low, far_mid, far_high], axis=1)
+    near = jnp.concatenate([below, own_block, above], axis=1)
+    far = lax.ppermute(near, "chan", [(s, blocks - 1 - s) for s in range(blocks)])
+    candidates = jnp.concatenate([near, far], axis=1)
     slot_rows = candidates.shape[1]
     spectrum = jnp.dot(
         candidates.reshape(minutes * slot_rows, NT), forward_table(),

time: 58.4 us -> 63.4 us (1.086)
  the two profiles are of different devices: /device:TPU:1 before, /device:TPU:17 now
where the time goes in v8:
time: 63.4 us; the launch traced here: 63 us
  waiting for transfers between devices  17.7 us (28%)
  other arithmetic  15.8 us (25%)
  Pallas kernels  14.9 us (24%)
  starting transfers between devices  7.36 us (12%)
  local copies, waits for them, and re-layouts  4.82 us (8%)
  matrix products  2.21 us (3%)
    pallas_call x1, Pallas kernels, coherence(): pl.pallas_call(coherence_kernel, grid_spec=pltpu.PrefetchScalarGridSpec(n...  14.9 us
    ppermute x1, waiting for transfers between devices, body(): lax.ppermute(near, 'chan', [(s, blocks - 1 - s) for s in range(blocks)])  13.7 us
    another operation x4, other arithmetic  5.57 us
    sin x3, other arithmetic, unit_angles(): return (jnp.cos(phase), jnp.sin(phase))  4.88 us
    ppermute x1, waiting for transfers between devices, body(): lax.ppermute(own_block, 'chan', [(s, s - 1) for s in range(1, blocks)])  3.99 us
    ppermute x1, starting transfers between devices, body(): lax.ppermute(own_block, 'chan', [(s, s + 1) for s in range(blocks - 1)])  3.98 us
    unnamed x18, local copies, waits for them, and re-layouts  2.32 us
    ppermute x1, starting transfers between devices, body(): lax.ppermute(own_block, 'chan', [(s, s - 1) for s in range(1, blocks)])  2.1 us
  transfers between devices with their start and end apart: 4, of which 2 were waited for; matrix products, arithmetic and copies ran while one was open for 24% of the time, Pallas kernels for 0%

profile of v8, /device:TPU:17, one launch (start us, length us, event | category | flops | bytes accessed | tf_op | source)
XLA Modules:
  0.0 63.0 jit_solution(3893661235071169172)
XLA Ops:
  0.0 1.2 %collective-permute-start = (bf16[1,16,1536]{2,1,0:T(8,128)(2,1)}, bf16[1,16,1536]{2,1,0:T(8,128)(2,1)}, u32[]{:S(2)}, u32[]{:S(2)}) collective-permute-start(bf16[1,16,1536]{2,1,0:T(8,128)(2,1)} %param.3), channel_id=1, source_target_pairs={{0,1},{1,0},{2,3},{3,2},{4,5},{5,4},{6,7},{7,6},{8,9},{9,8},{10,11... | collective-permute-start | bytes 147464 | tf_op jit(solution)/shard_map/ppermute | solution.py:144
  1.2 1.4 %constant_dynamic-update-slice_fusion.1 = bf16[2,16,1536]{2,1,0:T(8,128)(2,1)} fusion(bf16[1,16,1536]{2,1,0:T(8,128)(2,1)} %param.3), kind=kLoop, calls=%fused_computation.64 | loop fusion | bytes 98304
  2.7 2.4 %fusion.16 = (f32[128,768]{1,0:T(8,128)S(1)}, f32[128,768]{1,0:T(8,128)}) fusion(), kind=kLoop, calls=%fused_computation.33 | loop fusion | flops 884736 | bytes 786432 | tf_op jit(solution)/shard_map/sin | solution.py:19
  5.1 0.8 %fusion.28 = (f32[12,768]{1,0:T(8,128)}, f32[12,768]{1,0:T(8,128)}) fusion(), kind=kLoop, calls=%fused_computation.48 | loop fusion | flops 82944 | bytes 73728 | tf_op jit(solution)/shard_map/sin | solution.py:19
  5.9 1.6 %fusion.12 = (f32[768,128]{1,0:T(8,128)S(1)}, f32[768,128]{1,0:T(8,128)S(1)}) fusion(), kind=kLoop, calls=%fused_computation.28 | loop fusion | flops 884736 | bytes 786432 | tf_op jit(solution)/shard_map/sin | solution.py:19
  7.6 0.2 fusion.36
  7.8 0.2 copy.5
  7.9 0.2 copy.6
  8.1 1.8 %multiply_subtract_fusion = (f32[768,8,128]{2,1,0:T(8,128)S(1)}, f32[768,8,128]{2,1,0:T(8,128)S(1)}) fusion(f32[768,128]{1,0:T(8,128)S(1)} %get-tuple-element.21, f32[768,8]{1,0:T(8,128)S(1)} %copy.6, f32[768,128]{1,0:T(8,128)S(1)} %get-tuple-element.22, f32[768,8]{1,0:T(8,128)S(1)} %copy.5), kind=kLoop, calls=%fused_computation.13 | loop fusion | flops 4718592 | bytes 7127040 | tf_op jit(solution)/shard_map/sub | solution.py:39
  9.9 0.6 fusion.4
  10.5 0.0 copy-start.3
  10.5 0.0 copy-start.5
  10.5 0.0 copy-start.6
  10.5 0.6 fusion.5
  11.1 0.0 copy-start.7
  11.1 0.4 copy-done.3
  11.5 0.0 copy-done.5
  11.5 0.0 copy-done.6
  11.5 3.5 %subtract_convert_fusion = (bf16[12,128,768]{2,1,0:T(8,128)(2,1)}, bf16[12,128,768]{2,1,0:T(8,128)(2,1)}) fusion(f32[128,768]{1,0:T(8,128)S(1)} %get-tuple-element.17, f32[12,768]{1,0:T(8,128)S(1)} %copy-done.5, f32[128,768]{1,0:T(8,128)S(1)} %copy-done.3, f32[12,768]{1,0:T(8,128)S(1)} %copy-done.6), kind=kLoop, calls=%fused_computation.5 | loop fusion | flops 10616832 | bytes 5578752 | tf_op jit(solution)/shard_map/convert.10
  15.0 0.0 collective-permute-done
  15.0 1.4 %constant_dynamic-update-slice_fusion = bf16[2,16,1536]{2,1,0:T(8,128)(2,1)} fusion(bf16[2,16,1536]{2,1,0:T(8,128)(2,1)} %constant_dynamic-update-slice_fusion.1, bf16[1,16,1536]{2,1,0:T(8,128)(2,1)} %collective-permute-done), kind=kLoop, calls=%fused_computation.63 | loop fusion | bytes 98304 | tf_op jit(solution)/shard_map/concatenate | solution.py:146
  16.4 4.0 %collective-permute-start.1 = (bf16[2,16,1536]{2,1,0:T(8,128)(2,1)}, bf16[2,16,1536]{2,1,0:T(8,128)(2,1)S(1)}, u32[]{:S(2)}, u32[]{:S(2)}) collective-permute-start(bf16[2,16,1536]{2,1,0:T(8,128)(2,1)} %constant_dynamic-update-slice_fusion), channel_id=1, source_target_pairs={{0,2},{2,4},{4,6},{6,8},{8,10},{10,12},{12,14},{14,16},{16,18},{18... | collective-permute-start | bytes 294920 | tf_op jit(solution)/shard_map/ppermute | solution.py:147
  20.4 2.1 %collective-permute-start.2 = (bf16[2,16,1536]{2,1,0:T(8,128)(2,1)}, bf16[2,16,1536]{2,1,0:T(8,128)(2,1)S(1)}, u32[]{:S(2)}, u32[]{:S(2)}) collective-permute-start(bf16[2,16,1536]{2,1,0:T(8,128)(2,1)} %constant_dynamic-update-slice_fusion), channel_id=1, source_target_pairs={{2,0},{4,2},{6,4},{8,6},{10,8},{12,10},{14,12},{16,14},{18,16},{20... | collective-permute-start | bytes 294920 | tf_op jit(solution)/shard_map/ppermute | solution.py:148
  22.5 0.0 copy-done.7
  22.5 0.0 collective-permute-done.1
  22.5 4.0 %collective-permute-done.2 = bf16[2,16,1536]{2,1,0:T(8,128)(2,1)S(1)} collective-permute-done((bf16[2,16,1536]{2,1,0:T(8,128)(2,1)}, bf16[2,16,1536]{2,1,0:T(8,128)(2,1)S(1)}, u32[]{:S(2)}, u32[]{:S(2)}) %collective-permute-start.2) | collective-permute-done | bytes 98336 | tf_op jit(solution)/shard_map/ppermute | solution.py:148
  26.5 0.9 %pad_maximum_fusion.3 = bf16[2,48,1536]{2,1,0:T(8,128)(2,1)S(1)} fusion(bf16[2,16,1536]{2,1,0:T(8,128)(2,1)S(1)} %collective-permute-done.2, bf16[2,16,1536]{2,1,0:T(8,128)(2,1)} %constant_dynamic-update-slice_fusion, bf16[2,16,1536]{2,1,0:T(8,128)(2,1)S(1)} %collective-permute-done.1), kind=kLoop, calls=%fused_computation.37 | loop fusion | flops 884736 | bytes 589824 | tf_op jit(solution)/shard_map/concatenate | solution.py:149
  27.4 0.0 copy-start.4
  27.5 0.0 copy-start.1
  27.5 0.0 copy-start.2
  27.5 0.1 collective-permute-start.3
  27.6 2.0 %pad_maximum_fusion.1.inverse_ref = bf16[1536,1024]{1,0:T(8,128)(2,1)} fusion(bf16[768,1024]{1,0:T(8,128)(2,1)S(1)} %fusion.4, bf16[768,1024]{1,0:T(8,128)(2,1)S(1)} %fusion.5), kind=kLoop, calls=%fused_computation.11 | loop fusion | flops 6291456 | bytes 6291456 | tf_op jit(solution)/shard_map/concatenate | solution.py:42
  29.5 13.7 %collective-permute-done.3 = bf16[2,48,1536]{2,1,0:T(8,128)(2,1)S(1)} collective-permute-done((bf16[2,48,1536]{2,1,0:T(8,128)(2,1)S(1)}, bf16[2,48,1536]{2,1,0:T(8,128)(2,1)S(1)}, u32[]{:S(2)}, u32[]{:S(2)}) %collective-permute-start.3) | collective-permute-done | bytes 294944 | tf_op jit(solution)/shard_map/ppermute | solution.py:150
  43.2 0.0 copy-done.4
  43.2 0.0 copy-done.1
  43.2 0.0 copy-done.2
  43.2 1.2 %multiply_reduce_fusion = (f32[192]{0:T(256)S(1)}, f32[192,1536]{1,0:T(8,128)S(1)}) fusion(bf16[192,1536]{1,0:T(8,128)(2,1)S(1)} %bitcast.48, bf16[1536,768]{1,0:T(8,128)(2,1)S(1)} %bitcast.47, bf16[1536,768]{1,0:T(8,128)(2,1)S(1)} %bitcast.46), kind=kOutput, calls=%fused_computation.17 | convolution fusion | flops 915996480 | bytes 6488832 | tf_op jit(solution)/shard_map/dot_general | solution.py:153
  44.4 0.2 divide_convert_fusion
  44.6 1.0 %fusion.21 = f32[2,1536,512]{1,2,0:T(8,128)S(1)} fusion(bf16[2,96,1536]{2,1,0:T(8,128)(2,1)S(1)} %bitcast.45, s32[512]{0:T(512)S(1)} %bitcast.49), kind=kOutput, calls=%fused_computation.40 | convolution fusion | flops 302039040 | bytes 6883328 | tf_op jit(solution)/shard_map/pq,mqk->mpk/dot_general | solution.py:171
  45.7 0.9 %add_convert_fusion = (bf16[2,2,256,768]{3,2,1,0:T(8,128)(2,1)S(1)}, bf16[2,2,256,768]{3,2,1,0:T(8,128)(2,1)S(1)}) fusion(f32[2,2,256,1536]{3,2,1,0:T(8,128)S(1)} %bitcast.39, f32[2,2,768]{2,1,0:T(2,128)S(1)} %get-tuple-element.12, f32[2,2,768]{2,1,0:T(2,128)S(1)} %get-tuple-element.11), kind=kLoop, calls=%fused_computation.15 | loop fusion | flops 6291456 | bytes 9461760 | tf_op jit(solution)/shard_map/convert.6
  46.6 0.0 copy-start
  46.6 0.2 pad_maximum_fusion.crossed_ref
  46.9 0.5 copy-done
  47.4 14.9 %shard_map.37 = f32[512,128]{1,0:T(8,128)S(1)} custom-call(s32[1]{0:T(128)} %constant.23.clone.1.own_ref, s32[4,1024]{1,0:T(4,128)S(1)} %copy-done, bf16[2,512,1536]{2,1,0:T(8,128)(2,1)S(1)} %pad_maximum_fusion.crossed_ref, bf16[1536,1024]{1,0:T(8,128)(2,1)} %pad_maximum_fusion.1.inverse_ref), custom_call_target="tpu_custom_call" | custom-call | tf_op jit(solution)/shard_map/pallas_call | solution.py:116
  62.2 0.7 %copy.7 = f32[1,4,2,256]{3,2,1,0:T(2,128)} copy(f32[1,4,2,256]{1,3,2,0:T(8,128)S(1)} %bitcast.38) | data formatting | bytes 16384 | tf_op jit(solution)/shard_map/reshape | solution.py:179
  (11 shorter events, 0.1 us)
Async XLA Ops:
  0.0 15.0 %collective-permute-start = (bf16[1,16,1536]{2,1,0:T(8,128)(2,1)}, bf16[1,16,1536]{2,1,0:T(8,128)(2,1)}, u32[]{:S(2)}, u32[]{:S(2)}) collective-permute-start(bf16[1,16,1536]{2,1,0:T(8,128)(2,1)} %param.3), channel_id=1, source_target_pairs={{0,1},{1,0},{2,3},{3,2},{4,5},{5,4},{6,7},{7,6},{8,9},{9,8},{10,11... | collective-permute-start | bytes 147464 | tf_op jit(solution)/shard_map/ppermute | solution.py:144
  10.5 1.0 %copy-start.3 = (f32[128,768]{1,0:T(8,128)S(1)}, f32[128,768]{1,0:T(8,128)}, u32[]{:S(2)}) copy-start(f32[128,768]{1,0:T(8,128)} %get-tuple-element.18) | copy-start | bytes 1179652
  10.5 1.0 %copy-start.5 = (f32[12,768]{1,0:T(8,128)S(1)}, f32[12,768]{1,0:T(8,128)}, u32[]{:S(2)}) copy-start(f32[12,768]{1,0:T(8,128)} %get-tuple-element.19) | copy-start | bytes 110596
  10.5 1.0 %copy-start.6 = (f32[12,768]{1,0:T(8,128)S(1)}, f32[12,768]{1,0:T(8,128)}, u32[]{:S(2)}) copy-start(f32[12,768]{1,0:T(8,128)} %get-tuple-element.20) | copy-start | bytes 110596
  11.1 11.4 %copy-start.7 = (s32[2,256]{1,0:T(2,128)S(1)}, s32[2,256]{1,0:T(2,128)}, u32[]{:S(2)}) copy-start(s32[2,256]{1,0:T(2,128)} %param.4) | copy-start | bytes 6148
  16.4 6.1 %collective-permute-start.1 = (bf16[2,16,1536]{2,1,0:T(8,128)(2,1)}, bf16[2,16,1536]{2,1,0:T(8,128)(2,1)S(1)}, u32[]{:S(2)}, u32[]{:S(2)}) collective-permute-start(bf16[2,16,1536]{2,1,0:T(8,128)(2,1)} %constant_dynamic-update-slice_fusion), channel_id=1, source_target_pairs={{0,2},{2,4},{4,6},{6,8},{8,10},{10,12},{12,14},{14,16},{16,18},{18... | collective-permute-start | bytes 294920 | tf_op jit(solution)/shard_map/ppermute | solution.py:147
  20.4 6.1 %collective-permute-start.2 = (bf16[2,16,1536]{2,1,0:T(8,128)(2,1)}, bf16[2,16,1536]{2,1,0:T(8,128)(2,1)S(1)}, u32[]{:S(2)}, u32[]{:S(2)}) collective-permute-start(bf16[2,16,1536]{2,1,0:T(8,128)(2,1)} %constant_dynamic-update-slice_fusion), channel_id=1, source_target_pairs={{2,0},{4,2},{6,4},{8,6},{10,8},{12,10},{14,12},{16,14},{18,16},{20... | collective-permute-start | bytes 294920 | tf_op jit(solution)/shard_map/ppermute | solution.py:148
  27.4 15.7 %copy-start.4 = (bf16[2,16,1536]{2,1,0:T(8,128)(2,1)S(1)}, bf16[2,16,1536]{2,1,0:T(8,128)(2,1)}, u32[]{:S(2)}) copy-start(bf16[2,16,1536]{2,1,0:T(8,128)(2,1)} %constant_dynamic-update-slice_fusion) | copy-start | bytes 294916
  27.5 15.8 %copy-start.1 = (bf16[12,128,768]{2,1,0:T(8,128)(2,1)S(1)}, bf16[12,128,768]{2,1,0:T(8,128)(2,1)}, u32[]{:S(2)}) copy-start(bf16[12,128,768]{2,1,0:T(8,128)(2,1)} %get-tuple-element.9) | copy-start | bytes 7077892
  27.5 15.8 %copy-start.2 = (bf16[12,128,768]{2,1,0:T(8,128)(2,1)S(1)}, bf16[12,128,768]{2,1,0:T(8,128)(2,1)}, u32[]{:S(2)}) copy-start(bf16[12,128,768]{2,1,0:T(8,128)(2,1)} %get-tuple-element.10) | copy-start | bytes 7077892
  27.5 15.7 %collective-permute-start.3 = (bf16[2,48,1536]{2,1,0:T(8,128)(2,1)S(1)}, bf16[2,48,1536]{2,1,0:T(8,128)(2,1)S(1)}, u32[]{:S(2)}, u32[]{:S(2)}) collective-permute-start(bf16[2,48,1536]{2,1,0:T(8,128)(2,1)S(1)} %pad_maximum_fusion.3), channel_id=1, source_target_pairs={{0,30},{2,28},{4,26},{6,24},{8,22},{10,20},{12,18},{14,16},{16,14}... | collective-permute-start | bytes 884744 | tf_op jit(solution)/shard_map/ppermute | solution.py:150
  46.6 0.7 %copy-start = (s32[4,1024]{1,0:T(4,128)S(1)}, s32[4,1024]{1,0:T(4,128)}, u32[]{:S(2)}) copy-start(s32[4,1024]{1,0:T(4,128)} %stretch_ref.1) | copy-start | bytes 49156

commit v9 on v8

--- a/solution.py
+++ b/solution.py
@@ -144,11 +144,21 @@
             lax.ppermute(record, "tm", [(i, (i + shift) % minutes) for i in range(minutes)])
         )
     own_block = jnp.concatenate(parts, axis=0)
-    below = lax.ppermute(own_block, "chan", [(s, s + 1) for s in range(blocks - 1)])
-    above = lax.ppermute(own_block, "chan", [(s, s - 1) for s in range(1, blocks)])
-    near = jnp.concatenate([below, own_block, above], axis=1)
-    far = lax.ppermute(near, "chan", [(s, blocks - 1 - s) for s in range(blocks)])
-    candidates = jnp.concatenate([near, far], axis=1)
+    mirrored = lax.ppermute(own_block, "chan", [(s, blocks - 1 - s) for s in range(blocks)])
+    bundle = jnp.concatenate([own_block, mirrored], axis=1)
+    from_below = lax.ppermute(bundle, "chan", [(s, s + 1) for s in range(blocks - 1)])
+    from_above = lax.ppermute(bundle, "chan", [(s, s - 1) for s in range(1, blocks)])
+    candidates = jnp.concatenate(
+        [
+            from_below[:, :block_rows],
+            own_block,
+            from_above[:, :block_rows],
+            from_above[:, block_rows:],
+            mirrored,
+            from_below[:, block_rows:],
+        ],
+        axis=1,
+    )
     slot_rows = candidates.shape[1]
     spectrum = jnp.dot(
         candidates.reshape(minutes * slot_rows, NT), forward_table(),

time: 63.4 us -> 59.8 us (0.943)
  the two profiles are of different devices: /device:TPU:17 before, /device:TPU:1 now
where the time goes in v9:
time: 59.8 us; the launch traced here: 59 us
  other arithmetic  15.7 us (26%)
  Pallas kernels  14.9 us (25%)
  starting transfers between devices  13 us (22%)
  waiting for transfers between devices  7.27 us (12%)
  local copies, waits for them, and re-layouts  5.68 us (9%)
  matrix products  2.21 us (4%)
    pallas_call x1, Pallas kernels, coherence(): pl.pallas_call(coherence_kernel, grid_spec=pltpu.PrefetchScalarGridSpec(n...  14.9 us
    another operation x4, other arithmetic  5.57 us
    ppermute x1, starting transfers between devices, body(): lax.ppermute(own_block, 'chan', [(s, blocks - 1 - s) for s in range(block...  5.12 us
    sin x3, other arithmetic, unit_angles(): return (jnp.cos(phase), jnp.sin(phase))  4.88 us
    ppermute x1, waiting for transfers between devices, body(): lax.ppermute(bundle, 'chan', [(s, s - 1) for s in range(1, blocks)])  4.03 us
    ppermute x1, starting transfers between devices, body(): lax.ppermute(bundle, 'chan', [(s, s + 1) for s in range(blocks - 1)])  3.72 us
    ppermute x1, waiting for transfers between devices, body(): lax.ppermute(own_block, 'chan', [(s, blocks - 1 - s) for s in range(block...  3.24 us
    unnamed x23, local copies, waits for them, and re-layouts  3.18 us
  transfers between devices with their start and end apart: 4, of which 2 were waited for; matrix products, arithmetic and copies ran while one was open for 27% of the time, Pallas kernels for 0%

profile of v9, /device:TPU:1, one launch (start us, length us, event | category | flops | bytes accessed | tf_op | source)
XLA Modules:
  0.0 59.0 jit_solution(18087157201407133170)
XLA Ops:
  0.0 2.0 %collective-permute-start = (bf16[1,16,1536]{2,1,0:T(8,128)(2,1)}, bf16[1,16,1536]{2,1,0:T(8,128)(2,1)}, u32[]{:S(2)}, u32[]{:S(2)}) collective-permute-start(bf16[1,16,1536]{2,1,0:T(8,128)(2,1)} %param.3), channel_id=1, source_target_pairs={{0,1},{1,0},{2,3},{3,2},{4,5},{5,4},{6,7},{7,6},{8,9},{9,8},{10,11... | collective-permute-start | bytes 147464 | tf_op jit(solution)/shard_map/ppermute | solution.py:144
  2.0 1.5 %constant_dynamic-update-slice_fusion.1 = bf16[2,16,1536]{2,1,0:T(8,128)(2,1)} fusion(bf16[1,16,1536]{2,1,0:T(8,128)(2,1)} %param.3), kind=kLoop, calls=%fused_computation.62 | loop fusion | bytes 98304
  3.5 2.4 %fusion.16 = (f32[128,768]{1,0:T(8,128)S(1)}, f32[128,768]{1,0:T(8,128)}) fusion(), kind=kLoop, calls=%fused_computation.32 | loop fusion | flops 884736 | bytes 786432 | tf_op jit(solution)/shard_map/sin | solution.py:19
  5.9 0.9 %fusion.28 = (f32[12,768]{1,0:T(8,128)}, f32[12,768]{1,0:T(8,128)}) fusion(), kind=kLoop, calls=%fused_computation.49 | loop fusion | flops 82944 | bytes 73728 | tf_op jit(solution)/shard_map/sin | solution.py:19
  6.8 1.6 %fusion.12 = (f32[768,128]{1,0:T(8,128)S(1)}, f32[768,128]{1,0:T(8,128)S(1)}) fusion(), kind=kLoop, calls=%fused_computation.27 | loop fusion | flops 884736 | bytes 786432 | tf_op jit(solution)/shard_map/sin | solution.py:19
  8.4 0.2 fusion.36
  8.6 0.2 copy.5
  8.8 0.2 copy.6
  8.9 1.8 %multiply_subtract_fusion = (f32[768,8,128]{2,1,0:T(8,128)S(1)}, f32[768,8,128]{2,1,0:T(8,128)S(1)}) fusion(f32[768,128]{1,0:T(8,128)S(1)} %get-tuple-element.21, f32[768,8]{1,0:T(8,128)S(1)} %copy.6, f32[768,128]{1,0:T(8,128)S(1)} %get-tuple-element.22, f32[768,8]{1,0:T(8,128)S(1)} %copy.5), kind=kLoop, calls=%fused_computation.13 | loop fusion | flops 4718592 | bytes 7127040 | tf_op jit(solution)/shard_map/sub | solution.py:39
  10.7 0.6 fusion.4
  11.3 0.0 copy-start.3
  11.3 0.0 copy-start.4
  11.3 0.0 copy-start.5
  11.3 0.6 fusion.5
  11.9 0.0 copy-start.7
  11.9 0.4 copy-done.3
  12.3 0.0 copy-done.4
  12.3 0.0 copy-done.5
  12.3 3.5 %subtract_convert_fusion = (bf16[12,128,768]{2,1,0:T(8,128)(2,1)}, bf16[12,128,768]{2,1,0:T(8,128)(2,1)}) fusion(f32[128,768]{1,0:T(8,128)S(1)} %get-tuple-element.17, f32[12,768]{1,0:T(8,128)S(1)} %copy-done.4, f32[128,768]{1,0:T(8,128)S(1)} %copy-done.3, f32[12,768]{1,0:T(8,128)S(1)} %copy-done.5), kind=kLoop, calls=%fused_computation.5 | loop fusion | flops 10616832 | bytes 5578752 | tf_op jit(solution)/shard_map/convert.10
  15.8 0.0 collective-permute-done
  15.8 1.4 %constant_dynamic-update-slice_fusion = bf16[2,16,1536]{2,1,0:T(8,128)(2,1)} fusion(bf16[2,16,1536]{2,1,0:T(8,128)(2,1)} %constant_dynamic-update-slice_fusion.1, bf16[1,16,1536]{2,1,0:T(8,128)(2,1)} %collective-permute-done), kind=kLoop, calls=%fused_computation.61 | loop fusion | bytes 98304 | tf_op jit(solution)/shard_map/concatenate | solution.py:146
  17.2 5.1 %collective-permute-start.1 = (bf16[2,16,1536]{2,1,0:T(8,128)(2,1)}, bf16[2,16,1536]{2,1,0:T(8,128)(2,1)S(1)}, u32[]{:S(2)}, u32[]{:S(2)}) collective-permute-start(bf16[2,16,1536]{2,1,0:T(8,128)(2,1)} %constant_dynamic-update-slice_fusion), channel_id=1, source_target_pairs={{0,30},{2,28},{4,26},{6,24},{8,22},{10,20},{12,18},{14,16},{16,14}... | collective-permute-start | bytes 294920 | tf_op jit(solution)/shard_map/ppermute | solution.py:147
  22.4 0.0 copy-done.7
  22.4 3.2 %collective-permute-done.1 = bf16[2,16,1536]{2,1,0:T(8,128)(2,1)S(1)} collective-permute-done((bf16[2,16,1536]{2,1,0:T(8,128)(2,1)}, bf16[2,16,1536]{2,1,0:T(8,128)(2,1)S(1)}, u32[]{:S(2)}, u32[]{:S(2)}) %collective-permute-start.1) | collective-permute-done | bytes 98336 | tf_op jit(solution)/shard_map/ppermute | solution.py:147
  25.6 0.9 %pad_maximum_fusion.2 = bf16[2,32,1536]{2,1,0:T(8,128)(2,1)S(1)} fusion(bf16[2,16,1536]{2,1,0:T(8,128)(2,1)S(1)} %collective-permute-done.1, bf16[2,16,1536]{2,1,0:T(8,128)(2,1)} %constant_dynamic-update-slice_fusion), kind=kLoop, calls=%fused_computation.36 | loop fusion | flops 393216 | bytes 393216 | tf_op jit(solution)/shard_map/concatenate | solution.py:148
  26.5 0.0 copy-start.6
  26.5 0.0 copy-start.1
  26.6 0.0 copy-start.2
  26.6 3.7 %collective-permute-start.2 = (bf16[2,32,1536]{2,1,0:T(8,128)(2,1)S(1)}, bf16[2,32,1536]{2,1,0:T(8,128)(2,1)S(1)}, u32[]{:S(2)}, u32[]{:S(2)}) collective-permute-start(bf16[2,32,1536]{2,1,0:T(8,128)(2,1)S(1)} %pad_maximum_fusion.2), channel_id=1, source_target_pairs={{0,2},{2,4},{4,6},{6,8},{8,10},{10,12},{12,14},{14,16},{16,18},{18... | collective-permute-start | bytes 589832 | tf_op jit(solution)/shard_map/ppermute | solution.py:149
  30.3 2.0 %pad_maximum_fusion.1.inverse_ref = bf16[1536,1024]{1,0:T(8,128)(2,1)} fusion(bf16[768,1024]{1,0:T(8,128)(2,1)S(1)} %fusion.4, bf16[768,1024]{1,0:T(8,128)(2,1)S(1)} %fusion.5), kind=kLoop, calls=%fused_computation.11 | loop fusion | flops 6291456 | bytes 6291456 | tf_op jit(solution)/shard_map/concatenate | solution.py:42
  32.2 2.1 %collective-permute-start.3 = (bf16[2,32,1536]{2,1,0:T(8,128)(2,1)S(1)}, bf16[2,32,1536]{2,1,0:T(8,128)(2,1)S(1)}, u32[]{:S(2)}, u32[]{:S(2)}) collective-permute-start(bf16[2,32,1536]{2,1,0:T(8,128)(2,1)S(1)} %pad_maximum_fusion.2), channel_id=1, source_target_pairs={{2,0},{4,2},{6,4},{8,6},{10,8},{12,10},{14,12},{16,14},{18,16},{20... | collective-permute-start | bytes 589832 | tf_op jit(solution)/shard_map/ppermute | solution.py:150
  34.3 0.0 collective-permute-done.2
  34.4 0.0 copy-done.6
  34.4 0.8 %constant_dynamic-update-slice_fusion.4 = bf16[2,96,1536]{2,1,0:T(8,128)(2,1)S(1)} fusion(bf16[2,96,1536]{2,1,0:T(8,128)(2,1)S(1)} %constant_dynamic-update-slice_fusion.5, bf16[1,16,1536]{2,1,0:T(8,128)(2,1)} %collective-permute-done), kind=kLoop, calls=%fused_computation.65 | loop fusion | bytes 98304
  35.2 4.0 %collective-permute-done.3 = bf16[2,32,1536]{2,1,0:T(8,128)(2,1)S(1)} collective-permute-done((bf16[2,32,1536]{2,1,0:T(8,128)(2,1)S(1)}, bf16[2,32,1536]{2,1,0:T(8,128)(2,1)S(1)}, u32[]{:S(2)}, u32[]{:S(2)}) %collective-permute-start.3) | collective-permute-done | bytes 196640 | tf_op jit(solution)/shard_map/ppermute | solution.py:150
  39.3 0.0 copy-done.1
  39.3 0.0 copy-done.2
  39.3 1.2 %multiply_reduce_fusion = (f32[192]{0:T(256)S(1)}, f32[192,1536]{1,0:T(8,128)S(1)}) fusion(bf16[192,1536]{1,0:T(8,128)(2,1)S(1)} %bitcast.48, bf16[1536,768]{1,0:T(8,128)(2,1)S(1)} %bitcast.47, bf16[1536,768]{1,0:T(8,128)(2,1)S(1)} %bitcast.46), kind=kOutput, calls=%fused_computation.17 | convolution fusion | flops 915996480 | bytes 6488832 | tf_op jit(solution)/shard_map/dot_general | solution.py:163
  40.5 0.2 divide_convert_fusion
  40.7 1.0 %fusion.21 = f32[2,1536,512]{1,2,0:T(8,128)S(1)} fusion(bf16[2,96,1536]{2,1,0:T(8,128)(2,1)S(1)} %bitcast.45, s32[512]{0:T(512)S(1)} %bitcast.49), kind=kOutput, calls=%fused_computation.39 | convolution fusion | flops 302039040 | bytes 6883328 | tf_op jit(solution)/shard_map/pq,mqk->mpk/dot_general | solution.py:181
  41.8 0.9 %add_convert_fusion = (bf16[2,2,256,768]{3,2,1,0:T(8,128)(2,1)S(1)}, bf16[2,2,256,768]{3,2,1,0:T(8,128)(2,1)S(1)}) fusion(f32[2,2,256,1536]{3,2,1,0:T(8,128)S(1)} %bitcast.39, f32[2,2,768]{2,1,0:T(2,128)S(1)} %get-tuple-element.12, f32[2,2,768]{2,1,0:T(2,128)S(1)} %get-tuple-element.11), kind=kLoop, calls=%fused_computation.15 | loop fusion | flops 6291456 | bytes 9461760 | tf_op jit(solution)/shard_map/convert.6
  42.7 0.0 copy-start
  42.7 0.2 pad_maximum_fusion.crossed_ref
  42.9 0.5 copy-done
  43.4 14.9 %shard_map.37 = f32[512,128]{1,0:T(8,128)S(1)} custom-call(s32[1]{0:T(128)} %constant.23.clone.1.own_ref, s32[4,1024]{1,0:T(4,128)S(1)} %copy-done, bf16[2,512,1536]{2,1,0:T(8,128)(2,1)S(1)} %pad_maximum_fusion.crossed_ref, bf16[1536,1024]{1,0:T(8,128)(2,1)} %pad_maximum_fusion.1.inverse_ref), custom_call_target="tpu_custom_call" | custom-call | tf_op jit(solution)/shard_map/pallas_call | solution.py:116
  58.3 0.7 %copy.7 = f32[1,4,2,256]{3,2,1,0:T(2,128)} copy(f32[1,4,2,256]{1,3,2,0:T(8,128)S(1)} %bitcast.38) | data formatting | bytes 16384 | tf_op jit(solution)/shard_map/reshape | solution.py:189
  (15 shorter events, 0.1 us)
Async XLA Ops:
  0.0 15.8 %collective-permute-start = (bf16[1,16,1536]{2,1,0:T(8,128)(2,1)}, bf16[1,16,1536]{2,1,0:T(8,128)(2,1)}, u32[]{:S(2)}, u32[]{:S(2)}) collective-permute-start(bf16[1,16,1536]{2,1,0:T(8,128)(2,1)} %param.3), channel_id=1, source_target_pairs={{0,1},{1,0},{2,3},{3,2},{4,5},{5,4},{6,7},{7,6},{8,9},{9,8},{10,11... | collective-permute-start | bytes 147464 | tf_op jit(solution)/shard_map/ppermute | solution.py:144
  11.3 1.0 %copy-start.3 = (f32[128,768]{1,0:T(8,128)S(1)}, f32[128,768]{1,0:T(8,128)}, u32[]{:S(2)}) copy-start(f32[128,768]{1,0:T(8,128)} %get-tuple-element.18) | copy-start | bytes 1179652
  11.3 1.0 %copy-start.4 = (f32[12,768]{1,0:T(8,128)S(1)}, f32[12,768]{1,0:T(8,128)}, u32[]{:S(2)}) copy-start(f32[12,768]{1,0:T(8,128)} %get-tuple-element.19) | copy-start | bytes 110596
  11.3 1.0 %copy-start.5 = (f32[12,768]{1,0:T(8,128)S(1)}, f32[12,768]{1,0:T(8,128)}, u32[]{:S(2)}) copy-start(f32[12,768]{1,0:T(8,128)} %get-tuple-element.20) | copy-start | bytes 110596
  11.9 10.4 %copy-start.7 = (s32[2,256]{1,0:T(2,128)S(1)}, s32[2,256]{1,0:T(2,128)}, u32[]{:S(2)}) copy-start(s32[2,256]{1,0:T(2,128)} %param.4) | copy-start | bytes 6148
  17.2 8.4 %collective-permute-start.1 = (bf16[2,16,1536]{2,1,0:T(8,128)(2,1)}, bf16[2,16,1536]{2,1,0:T(8,128)(2,1)S(1)}, u32[]{:S(2)}, u32[]{:S(2)}) collective-permute-start(bf16[2,16,1536]{2,1,0:T(8,128)(2,1)} %constant_dynamic-update-slice_fusion), channel_id=1, source_target_pairs={{0,30},{2,28},{4,26},{6,24},{8,22},{10,20},{12,18},{14,16},{16,14}... | collective-permute-start | bytes 294920 | tf_op jit(solution)/shard_map/ppermute | solution.py:147
  26.5 7.8 %copy-start.6 = (bf16[1,16,1536]{2,1,0:T(8,128)(2,1)S(1)}, bf16[1,16,1536]{2,1,0:T(8,128)(2,1)}, u32[]{:S(2)}) copy-start(bf16[1,16,1536]{2,1,0:T(8,128)(2,1)} %param.3) | copy-start | bytes 147460
  26.5 12.7 %copy-start.1 = (bf16[12,128,768]{2,1,0:T(8,128)(2,1)S(1)}, bf16[12,128,768]{2,1,0:T(8,128)(2,1)}, u32[]{:S(2)}) copy-start(bf16[12,128,768]{2,1,0:T(8,128)(2,1)} %get-tuple-element.9) | copy-start | bytes 7077892
  26.6 12.7 %copy-start.2 = (bf16[12,128,768]{2,1,0:T(8,128)(2,1)S(1)}, bf16[12,128,768]{2,1,0:T(8,128)(2,1)}, u32[]{:S(2)}) copy-start(bf16[12,128,768]{2,1,0:T(8,128)(2,1)} %get-tuple-element.10) | copy-start | bytes 7077892
  26.6 7.8 %collective-permute-start.2 = (bf16[2,32,1536]{2,1,0:T(8,128)(2,1)S(1)}, bf16[2,32,1536]{2,1,0:T(8,128)(2,1)S(1)}, u32[]{:S(2)}, u32[]{:S(2)}) collective-permute-start(bf16[2,32,1536]{2,1,0:T(8,128)(2,1)S(1)} %pad_maximum_fusion.2), channel_id=1, source_target_pairs={{0,2},{2,4},{4,6},{6,8},{8,10},{10,12},{12,14},{14,16},{16,18},{18... | collective-permute-start | bytes 589832 | tf_op jit(solution)/shard_map/ppermute | solution.py:149
  32.2 7.0 %collective-permute-start.3 = (bf16[2,32,1536]{2,1,0:T(8,128)(2,1)S(1)}, bf16[2,32,1536]{2,1,0:T(8,128)(2,1)S(1)}, u32[]{:S(2)}, u32[]{:S(2)}) collective-permute-start(bf16[2,32,1536]{2,1,0:T(8,128)(2,1)S(1)} %pad_maximum_fusion.2), channel_id=1, source_target_pairs={{2,0},{4,2},{6,4},{8,6},{10,8},{12,10},{14,12},{16,14},{18,16},{20... | collective-permute-start | bytes 589832 | tf_op jit(solution)/shard_map/ppermute | solution.py:150
  42.7 0.7 %copy-start = (s32[4,1024]{1,0:T(4,128)S(1)}, s32[4,1024]{1,0:T(4,128)}, u32[]{:S(2)}) copy-start(s32[4,1024]{1,0:T(4,128)} %stretch_ref.1) | copy-start | bytes 49156

commit v10 on v5

--- a/solution.py
+++ b/solution.py
@@ -19,28 +19,39 @@
     return jnp.cos(phase), jnp.sin(phase)
 
 
-def forward_table():
+def fine_angles():
+    bins = jnp.arange(NF, dtype=jnp.int32)[None, :]
+    cos_1, sin_1 = unit_angles(jnp.arange(16, dtype=jnp.int32)[:, None] * bins, NT // 8)
+    cos_2, sin_2 = unit_angles(jnp.arange(8, dtype=jnp.int32)[:, None] * bins, NT)
+    cos_c = cos_1[:, None] * cos_2[None] - sin_1[:, None] * sin_2[None]
+    sin_c = sin_1[:, None] * cos_2[None] + cos_1[:, None] * sin_2[None]
+    return cos_c.reshape(128, NF), sin_c.reshape(128, NF)
+
+
+def forward_table(cos_c, sin_c):
     coarse = NT // 128
     bins = jnp.arange(NF, dtype=jnp.int32)[None, :]
     cos_a, sin_a = unit_angles(jnp.arange(coarse, dtype=jnp.int32)[:, None] * bins, coarse)
-    cos_c, sin_c = unit_angles(jnp.arange(128, dtype=jnp.int32)[:, None] * bins, NT)
-    cos_t = cos_a[:, None, :] * cos_c[None] - sin_a[:, None, :] * sin_c[None]
-    sin_t = sin_a[:, None, :] * cos_c[None] + cos_a[:, None, :] * sin_c[None]
-    table = jnp.concatenate([cos_t, -sin_t], axis=-1).astype(jnp.bfloat16)
-    return table.reshape(NT, 2 * NF)
-
-
-def inverse_table():
+    first = jnp.concatenate([cos_a, -sin_a], axis=1)
+    second = jnp.concatenate([-sin_a, -cos_a], axis=1)
+    fine_cos = jnp.concatenate([cos_c, cos_c], axis=1)
+    fine_sin = jnp.concatenate([sin_c, sin_c], axis=1)
+    table = first[:, None, :] * fine_cos[None] + second[:, None, :] * fine_sin[None]
+    return table.astype(jnp.bfloat16).reshape(NT, 2 * NF)
+
+
+def inverse_table(cos_c, sin_c):
     coarse = NT // 128
     groups = LAGS // 128
     bins = jnp.arange(NF, dtype=jnp.int32)[:, None]
     cos_a, sin_a = unit_angles(bins * (jnp.arange(groups, dtype=jnp.int32)[None, :] - groups // 2), coarse)
-    cos_c, sin_c = unit_angles(bins * jnp.arange(128, dtype=jnp.int32)[None, :], NT)
-    cos_t = cos_a[:, :, None] * cos_c[:, None, :] - sin_a[:, :, None] * sin_c[:, None, :]
-    sin_t = sin_a[:, :, None] * cos_c[:, None, :] + cos_a[:, :, None] * sin_c[:, None, :]
-    weight = jnp.where(bins == 0, 1.0, 2.0).astype(jnp.float32)[:, :, None]
-    table = jnp.concatenate([weight * cos_t, -weight * sin_t], axis=0).astype(jnp.bfloat16)
-    return table.reshape(2 * NF, LAGS)
+    weight = jnp.where(bins == 0, 1.0, 2.0).astype(jnp.float32)
+    first = jnp.concatenate([weight * cos_a, -weight * sin_a], axis=0)
+    second = jnp.concatenate([-weight * sin_a, -weight * cos_a], axis=0)
+    fine_cos = jnp.concatenate([cos_c.T, cos_c.T], axis=0)
+    fine_sin = jnp.concatenate([sin_c.T, sin_c.T], axis=0)
+    table = first[:, :, None] * fine_cos[:, None, :] + second[:, :, None] * fine_sin[:, None, :]
+    return table.astype(jnp.bfloat16).reshape(2 * NF, LAGS)
 
 
 def whiten(spectrum):
@@ -151,8 +162,9 @@
     far_high = lax.ppermute(own_block, "chan", [(s, blocks - s) for s in range(1, blocks)])
     candidates = jnp.concatenate([below, own_block, above, far_low, far_mid, far_high], axis=1)
     slot_rows = candidates.shape[1]
+    cos_c, sin_c = fine_angles()
     spectrum = jnp.dot(
-        candidates.reshape(minutes * slot_rows, NT), forward_table(),
+        candidates.reshape(minutes * slot_rows, NT), forward_table(cos_c, sin_c),
         preferred_element_type=jnp.float32,
     )
     whitened = whiten(spectrum).reshape(minutes, slot_rows, 2 * NF)
@@ -175,7 +187,7 @@
     receivers = receivers.reshape(minutes, source_count, recv_count, 2 * NF)
     crossed = cross_spectrum(sources[:, :, None, :], receivers)
     crossed = crossed.reshape(minutes, pair_count, 2 * NF)
-    result = coherence(0, stretch_index, crossed, inverse_table())
+    result = coherence(0, stretch_index, crossed, inverse_table(cos_c, sin_c))
     stretch_count = stretch_index.shape[0]
     return result.reshape(1, stretch_count, source_count, recv_count)
 

time: 58.4 us -> 61.3 us (1.050)
  local copies, waits for them, and re-layouts: 2.45 us -> 9.31 us
  other arithmetic: 12.7 us -> 10.2 us
  matrix products: 3.88 us -> 2.22 us
    convert_element_type x0 -> x2, other arithmetic: none -> 7.24 us  [the longest x1 3.83 us: inverse_table(): return table.astype(jnp.bfloat16).reshape(2 * NF, LAGS)]
    concatenate x0 -> x4, local copies, waits for them, and re-layouts: none -> 4.66 us  [the longest x1 1.18 us: inverse_table(): fine_cos = jnp.concatenate([cos_c.T, cos_c.T], axis=0)]
    another operation x4 -> x1, other arithmetic: 4.93 us -> 0.92 us
    sin x3 -> x2, other arithmetic: 3.4 us -> 0.32 us  [unit_angles(): return (jnp.cos(phase), jnp.sin(phase))]
    unnamed x14 -> x25, local copies, waits for them, and re-layouts: 1.36 us -> 3.88 us
    sub x1 -> x0, other arithmetic: 1.79 us -> none  [inverse_table(): cos_a[:, :, None] * cos_c[:, None, :]]
    concatenate x1 -> x4, other arithmetic: 1.95 us -> 0.26 us  [the longest x1 0.12 us: forward_table(): fine_cos = jnp.concatenate([cos_c, cos_c], axis=1)]
    dot_general x1, matrix products: 2.86 us -> 1.19 us  [body(): jnp.dot(candidates.reshape(minutes * slot_rows, NT), forward_table(cos_c,...]
  transfers between devices with their start and end apart: 6 -> 6, of which waited for: 1 -> 1; matrix products, arithmetic and copies ran while one was open for 22% -> 28% of each run, Pallas kernels for 0% -> 0%
where the time goes in v10:
time: 61.3 us; the launch traced here: 60.7 us
  starting transfers between devices  21.3 us (35%)
  Pallas kernels  14.9 us (24%)
  other arithmetic  10.2 us (17%)
  local copies, waits for them, and re-layouts  9.31 us (15%)
  waiting for transfers between devices  2.36 us (4%)
  matrix products  2.22 us (4%)
    pallas_call x1, Pallas kernels, coherence(): pl.pallas_call(coherence_kernel, grid_spec=pltpu.PrefetchScalarGridSpec(n...  14.9 us
    ppermute x1, starting transfers between devices, body(): lax.ppermute(own_block, 'chan', [(s, blocks - s) for s in range(1, blocks)])  6.51 us
    ppermute x1, starting transfers between devices, body(): lax.ppermute(own_block, 'chan', [(s, blocks - 2 - s) for s in range(block...  5.23 us
    ppermute x1, starting transfers between devices, body(): lax.ppermute(own_block, 'chan', [(s, s + 1) for s in range(blocks - 1)])  3.99 us
    unnamed x25, local copies, waits for them, and re-layouts  3.88 us
    convert_element_type x1, other arithmetic, inverse_table(): return table.astype(jnp.bfloat16).reshape(2 * NF, LAGS)  3.83 us
    convert_element_type x1, other arithmetic, forward_table(): return table.astype(jnp.bfloat16).reshape(NT, 2 * NF)  3.41 us
    ppermute x1, waiting for transfers between devices, body(): lax.ppermute(own_block, 'chan', [(s, blocks - s) for s in range(1, blocks)])  2.35 us
  transfers between devices with their start and end apart: 6, of which 1 were waited for; matrix products, arithmetic and copies ran while one was open for 28% of the time, Pallas kernels for 0%

profile of v10, /device:TPU:1, one launch (start us, length us, event | category | flops | bytes accessed | tf_op | source)
XLA Modules:
  0.0 60.7 jit_solution(4798242994870241969)
XLA Ops:
  0.0 2.0 %collective-permute-start = (bf16[1,16,1536]{2,1,0:T(8,128)(2,1)}, bf16[1,16,1536]{2,1,0:T(8,128)(2,1)S(1)}, u32[]{:S(2)}, u32[]{:S(2)}) collective-permute-start(bf16[1,16,1536]{2,1,0:T(8,128)(2,1)} %param.3), channel_id=1, source_target_pairs={{0,1},{1,0},{2,3},{3,2},{4,5},{5,4},{6,7},{7,6},{8,9},{9,8},{10,11... | collective-permute-start | bytes 147464 | tf_op jit(solution)/shard_map/ppermute | solution.py:155
  2.0 0.8 %constant_dynamic-update-slice_fusion.1 = bf16[2,16,1536]{2,1,0:T(8,128)(2,1)S(1)} fusion(bf16[1,16,1536]{2,1,0:T(8,128)(2,1)} %param.3), kind=kLoop, calls=%fused_computation.66 | loop fusion | bytes 98304
  2.9 0.2 fusion.14
  3.1 0.2 fusion.15
  3.3 0.1 fusion.32
  3.4 0.1 fusion.33
  3.5 0.2 sine_negate_fusion
  3.8 0.2 fusion.36
  4.0 0.2 sine_multiply_fusion
  4.2 1.2 %copy.10 = f32[1536,8]{1,0:T(8,128)} copy(f32[1536,8]{0,1:T(8,128)S(1)} %get-tuple-element.13) | data formatting | bytes 98304 | tf_op jit(solution)/shard_map/concatenate | solution.py:49
  5.4 1.2 %copy.12 = f32[1536,8]{1,0:T(8,128)} copy(f32[1536,8]{0,1:T(8,128)S(1)} %get-tuple-element.14) | data formatting | bytes 98304 | tf_op jit(solution)/shard_map/concatenate | solution.py:50
  6.5 0.1 fusion.2
  6.6 0.1 pad_maximum_fusion.3
  6.8 1.2 %copy.11 = f32[1536,128]{1,0:T(8,128)} copy(f32[1536,128]{0,1:T(8,128)S(1)} %get-tuple-element.24) | data formatting | bytes 1572864 | tf_op jit(solution)/shard_map/concatenate | solution.py:51
  7.9 1.2 %copy.13 = f32[1536,128]{1,0:T(8,128)} copy(f32[1536,128]{0,1:T(8,128)S(1)} %get-tuple-element.25) | data formatting | bytes 1572864 | tf_op jit(solution)/shard_map/concatenate | solution.py:52
  9.1 0.1 pad_maximum_fusion.1
  9.3 0.0 copy-start.2
  9.3 0.0 copy-start.3
  9.3 0.0 copy-start.4
  9.3 0.0 copy-start.5
  9.3 3.4 %add_convert_fusion = bf16[12,128,1536]{2,1,0:T(8,128)(2,1)} fusion(f32[128,1536]{1,0:T(8,128)S(1)} %get-tuple-element.23, f32[12,1536]{1,0:T(8,128)S(1)} %get-tuple-element.12, f32[128,1536]{1,0:T(8,128)S(1)} %get-tuple-element.22, f32[12,1536]{1,0:T(8,128)S(1)} %get-tuple-element.11), kind=kLoop, calls=%fused_computation | loop fusion | flops 9437184 | bytes 6438912 | tf_op jit(solution)/shard_map/convert_element_type | solution.py:40
  12.7 0.0 copy-done.2
  12.7 0.0 copy-done.3
  12.7 0.0 copy-done.4
  12.7 0.0 copy-done.5
  12.7 0.0 copy-start.7
  12.7 3.8 %add_convert_fusion.1 = bf16[1536,8,128]{2,1,0:T(8,128)(2,1)S(1)} fusion(f32[1536,128]{1,0:T(8,128)S(1)} %copy-done.5, f32[1536,8]{1,0:T(8,128)S(1)} %copy-done.3, f32[1536,128]{1,0:T(8,128)S(1)} %copy-done.4, f32[1536,8]{1,0:T(8,128)S(1)} %copy-done.2), kind=kLoop, calls=%fused_computation.1 | loop fusion | flops 6291456 | bytes 4816896 | tf_op jit(solution)/shard_map/convert_element_type | solution.py:54
  16.6 0.0 collective-permute-done
  16.6 4.0 %collective-permute-start.1 = (bf16[2,16,1536]{2,1,0:T(8,128)(2,1)S(1)}, bf16[2,16,1536]{2,1,0:T(8,128)(2,1)S(1)}, u32[]{:S(2)}, u32[]{:S(2)}) collective-permute-start(bf16[2,16,1536]{2,1,0:T(8,128)(2,1)S(1)} %constant_dynamic-update-slice_fusion), channel_id=1, source_target_pairs={{0,2},{2,4},{4,6},{6,8},{8,10},{10,12},{12,14},{14,16},{16,18},{18... | collective-permute-start | bytes 294920 | tf_op jit(solution)/shard_map/ppermute | solution.py:158
  20.6 0.0 copy-done.7
  20.6 0.0 copy-start.6
  20.7 0.0 copy-start.1
  20.7 2.5 %copy.18 = bf16[192,8,8,128]{3,1,2,0:T(8,128)(2,1)} copy(bf16[192,8,8,128]{3,2,1,0:T(8,128)(2,1)S(1)} %bitcast.45) | data formatting | bytes 6291456
  23.2 2.0 %collective-permute-start.2 = (bf16[2,16,1536]{2,1,0:T(8,128)(2,1)S(1)}, bf16[2,16,1536]{2,1,0:T(8,128)(2,1)S(1)}, u32[]{:S(2)}, u32[]{:S(2)}) collective-permute-start(bf16[2,16,1536]{2,1,0:T(8,128)(2,1)S(1)} %constant_dynamic-update-slice_fusion), channel_id=1, source_target_pairs={{2,0},{4,2},{6,4},{8,6},{10,8},{12,10},{14,12},{16,14},{18,16},{20... | collective-permute-start | bytes 294920 | tf_op jit(solution)/shard_map/ppermute | solution.py:159
  25.2 5.2 %collective-permute-start.3 = (bf16[2,16,1536]{2,1,0:T(8,128)(2,1)S(1)}, bf16[2,16,1536]{2,1,0:T(8,128)(2,1)S(1)}, u32[]{:S(2)}, u32[]{:S(2)}) collective-permute-start(bf16[2,16,1536]{2,1,0:T(8,128)(2,1)S(1)} %constant_dynamic-update-slice_fusion), channel_id=1, source_target_pairs={{0,28},{2,26},{4,24},{6,22},{8,20},{10,18},{12,16},{14,14},{16,12}... | collective-permute-start | bytes 294920 | tf_op jit(solution)/shard_map/ppermute | solution.py:160
  30.5 1.5 %collective-permute-start.4 = (bf16[2,16,1536]{2,1,0:T(8,128)(2,1)S(1)}, bf16[2,16,1536]{2,1,0:T(8,128)(2,1)S(1)}, u32[]{:S(2)}, u32[]{:S(2)}) collective-permute-start(bf16[2,16,1536]{2,1,0:T(8,128)(2,1)S(1)} %constant_dynamic-update-slice_fusion), channel_id=1, source_target_pairs={{0,30},{2,28},{4,26},{6,24},{8,22},{10,20},{12,18},{14,16},{16,14}... | collective-permute-start | bytes 294920 | tf_op jit(solution)/shard_map/ppermute | solution.py:161
  32.0 6.5 %collective-permute-start.5 = (bf16[2,16,1536]{2,1,0:T(8,128)(2,1)S(1)}, bf16[2,16,1536]{2,1,0:T(8,128)(2,1)S(1)}, u32[]{:S(2)}, u32[]{:S(2)}) collective-permute-start(bf16[2,16,1536]{2,1,0:T(8,128)(2,1)S(1)} %constant_dynamic-update-slice_fusion), channel_id=1, source_target_pairs={{2,30},{4,28},{6,26},{8,24},{10,22},{12,20},{14,18},{16,16},{18,14... | collective-permute-start | bytes 294920 | tf_op jit(solution)/shard_map/ppermute | solution.py:162
  38.5 0.0 collective-permute-done.1
  38.5 0.0 copy-done.6
  38.6 0.0 collective-permute-done.2
  38.6 0.0 collective-permute-done.3
  38.6 0.0 collective-permute-done.4
  38.6 2.4 %collective-permute-done.5 = bf16[2,16,1536]{2,1,0:T(8,128)(2,1)S(1)} collective-permute-done((bf16[2,16,1536]{2,1,0:T(8,128)(2,1)S(1)}, bf16[2,16,1536]{2,1,0:T(8,128)(2,1)S(1)}, u32[]{:S(2)}, u32[]{:S(2)}) %collective-permute-start.5) | collective-permute-done | bytes 98336 | tf_op jit(solution)/shard_map/ppermute | solution.py:162
  41.0 0.0 copy-done.1
  41.0 1.2 %multiply_reduce_fusion = (f32[192]{0:T(256)S(1)}, f32[192,1536]{1,0:T(8,128)S(1)}) fusion(bf16[192,1536]{1,0:T(8,128)(2,1)S(1)} %bitcast.51, bf16[1536,1536]{1,0:T(8,128)(2,1)S(1)} %bitcast.44), kind=kOutput, calls=%fused_computation.7 | convolution fusion | flops 906559296 | bytes 6488832 | tf_op jit(solution)/shard_map/dot_general | solution.py:166
  42.2 0.2 divide_convert_fusion
  42.4 1.0 %fusion.5 = f32[2,1536,512]{1,2,0:T(8,128)S(1)} fusion(bf16[2,96,1536]{2,1,0:T(8,128)(2,1)S(1)} %bitcast.50, s32[512]{0:T(512)S(1)} %bitcast.52), kind=kOutput, calls=%fused_computation.20 | convolution fusion | flops 302039040 | bytes 6883328 | tf_op jit(solution)/shard_map/pq,mqk->mpk/dot_general | solution.py:184
  43.5 0.9 %add_convert_fusion.2 = (bf16[2,2,256,768]{3,2,1,0:T(8,128)(2,1)S(1)}, bf16[2,2,256,768]{3,2,1,0:T(8,128)(2,1)S(1)}) fusion(f32[2,2,256,1536]{3,2,1,0:T(8,128)S(1)} %bitcast.43, f32[2,2,768]{2,1,0:T(2,128)S(1)} %get-tuple-element.16, f32[2,2,768]{2,1,0:T(2,128)S(1)} %get-tuple-element.15), kind=kLoop, calls=%fused_computation.5 | loop fusion | flops 6291456 | bytes 9461760 | tf_op jit(solution)/shard_map/convert.4
  44.4 0.0 copy-start
  44.4 0.2 pad_maximum_fusion.crossed_ref
  44.7 0.5 copy-done
  45.1 14.9 %shard_map.37 = f32[512,128]{1,0:T(8,128)S(1)} custom-call(s32[1]{0:T(128)} %constant.29.clone.1.own_ref, s32[4,1024]{1,0:T(4,128)S(1)} %copy-done, bf16[2,512,1536]{2,1,0:T(8,128)(2,1)S(1)} %pad_maximum_fusion.crossed_ref, bf16[1536,1024]{1,0:T(8,128)(2,1)} %bitcast.46), custom_call_target="tpu_custom_call" | custom-call | tf_op jit(solution)/shard_map/pallas_call | solution.py:127
  60.0 0.7 %copy.14 = f32[1,4,2,256]{3,2,1,0:T(2,128)} copy(f32[1,4,2,256]{1,3,2,0:T(8,128)S(1)} %bitcast.42) | data formatting | bytes 16384 | tf_op jit(solution)/shard_map/reshape | solution.py:192
  (19 shorter events, 0.2 us)
Async XLA Ops:
  0.0 16.6 %collective-permute-start = (bf16[1,16,1536]{2,1,0:T(8,128)(2,1)}, bf16[1,16,1536]{2,1,0:T(8,128)(2,1)S(1)}, u32[]{:S(2)}, u32[]{:S(2)}) collective-permute-start(bf16[1,16,1536]{2,1,0:T(8,128)(2,1)} %param.3), channel_id=1, source_target_pairs={{0,1},{1,0},{2,3},{3,2},{4,5},{5,4},{6,7},{7,6},{8,9},{9,8},{10,11... | collective-permute-start | bytes 147464 | tf_op jit(solution)/shard_map/ppermute | solution.py:155
  9.3 3.5 %copy-start.2 = (f32[1536,8]{1,0:T(8,128)S(1)}, f32[1536,8]{1,0:T(8,128)}, u32[]{:S(2)}) copy-start(f32[1536,8]{1,0:T(8,128)} %copy.10) | copy-start | bytes 147460
  9.3 3.4 %copy-start.3 = (f32[1536,8]{1,0:T(8,128)S(1)}, f32[1536,8]{1,0:T(8,128)}, u32[]{:S(2)}) copy-start(f32[1536,8]{1,0:T(8,128)} %copy.12) | copy-start | bytes 147460
  9.3 3.4 %copy-start.4 = (f32[1536,128]{1,0:T(8,128)S(1)}, f32[1536,128]{1,0:T(8,128)}, u32[]{:S(2)}) copy-start(f32[1536,128]{1,0:T(8,128)} %copy.11) | copy-start | bytes 2359300
  9.3 3.4 %copy-start.5 = (f32[1536,128]{1,0:T(8,128)S(1)}, f32[1536,128]{1,0:T(8,128)}, u32[]{:S(2)}) copy-start(f32[1536,128]{1,0:T(8,128)} %copy.13) | copy-start | bytes 2359300
  12.7 7.9 %copy-start.7 = (s32[2,256]{1,0:T(2,128)S(1)}, s32[2,256]{1,0:T(2,128)}, u32[]{:S(2)}) copy-start(s32[2,256]{1,0:T(2,128)} %param.4) | copy-start | bytes 6148
  16.6 21.9 %collective-permute-start.1 = (bf16[2,16,1536]{2,1,0:T(8,128)(2,1)S(1)}, bf16[2,16,1536]{2,1,0:T(8,128)(2,1)S(1)}, u32[]{:S(2)}, u32[]{:S(2)}) collective-permute-start(bf16[2,16,1536]{2,1,0:T(8,128)(2,1)S(1)} %constant_dynamic-update-slice_fusion), channel_id=1, source_target_pairs={{0,2},{2,4},{4,6},{6,8},{8,10},{10,12},{12,14},{14,16},{16,18},{18... | collective-permute-start | bytes 294920 | tf_op jit(solution)/shard_map/ppermute | solution.py:158
  20.6 17.9 %copy-start.6 = (bf16[1,16,1536]{2,1,0:T(8,128)(2,1)S(1)}, bf16[1,16,1536]{2,1,0:T(8,128)(2,1)}, u32[]{:S(2)}) copy-start(bf16[1,16,1536]{2,1,0:T(8,128)(2,1)} %param.3) | copy-start | bytes 147460
  20.7 20.3 %copy-start.1 = (bf16[12,128,1536]{2,1,0:T(8,128)(2,1)S(1)}, bf16[12,128,1536]{2,1,0:T(8,128)(2,1)}, u32[]{:S(2)}) copy-start(bf16[12,128,1536]{2,1,0:T(8,128)(2,1)} %add_convert_fusion) | copy-start | bytes 14155780
  23.2 15.4 %collective-permute-start.2 = (bf16[2,16,1536]{2,1,0:T(8,128)(2,1)S(1)}, bf16[2,16,1536]{2,1,0:T(8,128)(2,1)S(1)}, u32[]{:S(2)}, u32[]{:S(2)}) collective-permute-start(bf16[2,16,1536]{2,1,0:T(8,128)(2,1)S(1)} %constant_dynamic-update-slice_fusion), channel_id=1, source_target_pairs={{2,0},{4,2},{6,4},{8,6},{10,8},{12,10},{14,12},{16,14},{18,16},{20... | collective-permute-start | bytes 294920 | tf_op jit(solution)/shard_map/ppermute | solution.py:159
  25.2 13.4 %collective-permute-start.3 = (bf16[2,16,1536]{2,1,0:T(8,128)(2,1)S(1)}, bf16[2,16,1536]{2,1,0:T(8,128)(2,1)S(1)}, u32[]{:S(2)}, u32[]{:S(2)}) collective-permute-start(bf16[2,16,1536]{2,1,0:T(8,128)(2,1)S(1)} %constant_dynamic-update-slice_fusion), channel_id=1, source_target_pairs={{0,28},{2,26},{4,24},{6,22},{8,20},{10,18},{12,16},{14,14},{16,12}... | collective-permute-start | bytes 294920 | tf_op jit(solution)/shard_map/ppermute | solution.py:160
  30.5 8.2 %collective-permute-start.4 = (bf16[2,16,1536]{2,1,0:T(8,128)(2,1)S(1)}, bf16[2,16,1536]{2,1,0:T(8,128)(2,1)S(1)}, u32[]{:S(2)}, u32[]{:S(2)}) collective-permute-start(bf16[2,16,1536]{2,1,0:T(8,128)(2,1)S(1)} %constant_dynamic-update-slice_fusion), channel_id=1, source_target_pairs={{0,30},{2,28},{4,26},{6,24},{8,22},{10,20},{12,18},{14,16},{16,14}... | collective-permute-start | bytes 294920 | tf_op jit(solution)/shard_map/ppermute | solution.py:161
  32.0 9.0 %collective-permute-start.5 = (bf16[2,16,1536]{2,1,0:T(8,128)(2,1)S(1)}, bf16[2,16,1536]{2,1,0:T(8,128)(2,1)S(1)}, u32[]{:S(2)}, u32[]{:S(2)}) collective-permute-start(bf16[2,16,1536]{2,1,0:T(8,128)(2,1)S(1)} %constant_dynamic-update-slice_fusion), channel_id=1, source_target_pairs={{2,30},{4,28},{6,26},{8,24},{10,22},{12,20},{14,18},{16,16},{18,14... | collective-permute-start | bytes 294920 | tf_op jit(solution)/shard_map/ppermute | solution.py:162
  44.4 0.7 %copy-start = (s32[4,1024]{1,0:T(4,128)S(1)}, s32[4,1024]{1,0:T(4,128)}, u32[]{:S(2)}) copy-start(s32[4,1024]{1,0:T(4,128)} %stretch_ref.1) | copy-start | bytes 49156

commit v11 on v5

--- a/solution.py
+++ b/solution.py
@@ -30,17 +30,14 @@
     return table.reshape(NT, 2 * NF)
 
 
-def inverse_table():
+def inverse_factors():
     coarse = NT // 128
     groups = LAGS // 128
     bins = jnp.arange(NF, dtype=jnp.int32)[:, None]
     cos_a, sin_a = unit_angles(bins * (jnp.arange(groups, dtype=jnp.int32)[None, :] - groups // 2), coarse)
     cos_c, sin_c = unit_angles(bins * jnp.arange(128, dtype=jnp.int32)[None, :], NT)
-    cos_t = cos_a[:, :, None] * cos_c[:, None, :] - sin_a[:, :, None] * sin_c[:, None, :]
-    sin_t = sin_a[:, :, None] * cos_c[:, None, :] + cos_a[:, :, None] * sin_c[:, None, :]
-    weight = jnp.where(bins == 0, 1.0, 2.0).astype(jnp.float32)[:, :, None]
-    table = jnp.concatenate([weight * cos_t, -weight * sin_t], axis=0).astype(jnp.bfloat16)
-    return table.reshape(2 * NF, LAGS)
+    weight = jnp.where(bins == 0, 1.0, 2.0).astype(jnp.float32)
+    return weight * cos_a, weight * sin_a, cos_c, sin_c
 
 
 def whiten(spectrum):
@@ -64,9 +61,29 @@
 PAIR_BLOCK = 128
 
 
-def coherence_kernel(own_ref, stretch_ref, crossed_ref, inverse_ref, out_ref, picks_ref):
+def coherence_kernel(
+    own_ref, stretch_ref, crossed_ref, wcos_ref, wsin_ref, fcos_ref, fsin_ref,
+    out_ref, picks_ref, inverse_ref,
+):
     minutes = crossed_ref.shape[0]
     moves = stretch_ref.shape[0] - 1
+    groups = wcos_ref.shape[1]
+    fine = fcos_ref.shape[1]
+
+    @pl.when(pl.program_id(0) == 0)
+    def _():
+        fine_cos = fcos_ref[...]
+        fine_sin = fsin_ref[...]
+        for group in range(groups):
+            coarse_cos = wcos_ref[:, group:group + 1]
+            coarse_sin = wsin_ref[:, group:group + 1]
+            lags = slice(group * fine, (group + 1) * fine)
+            inverse_ref[:NF, lags] = (coarse_cos * fine_cos - coarse_sin * fine_sin).astype(
+                jnp.bfloat16
+            )
+            inverse_ref[NF:, lags] = (-(coarse_sin * fine_cos + coarse_cos * fine_sin)).astype(
+                jnp.bfloat16
+            )
 
     @pl.when(pl.program_id(0) == 0)
     def _():
@@ -109,7 +126,7 @@
     out_ref[...] = result
 
 
-def coherence(own_minute, stretch_index, crossed, inverse):
+def coherence(own_minute, stretch_index, crossed, factors):
     minutes, pair_count, width = crossed.shape
     stretch_count = stretch_index.shape[0]
     own = jnp.reshape(own_minute, (1,)).astype(jnp.int32)
@@ -121,16 +138,18 @@
             in_specs=[
                 pl.BlockSpec(stretch_index.shape, lambda i, own: (0, 0)),
                 pl.BlockSpec((minutes, PAIR_BLOCK, width), lambda i, own: (0, i, 0)),
-                pl.BlockSpec(inverse.shape, lambda i, own: (0, 0)),
+            ] + [pl.BlockSpec(factor.shape, lambda i, own: (0, 0)) for factor in factors],
+            out_specs=pl.BlockSpec((PAIR_BLOCK, 128), lambda i, own: (i, 0)),
+            scratch_shapes=[
+                pltpu.VMEM((LAGS, (stretch_count - 1) * LAGS), jnp.bfloat16),
+                pltpu.VMEM((width, LAGS), jnp.bfloat16),
             ],
-            out_specs=pl.BlockSpec((PAIR_BLOCK, 128), lambda i, own: (i, 0)),
-            scratch_shapes=[pltpu.VMEM((LAGS, (stretch_count - 1) * LAGS), jnp.bfloat16)],
         ),
         out_shape=jax.ShapeDtypeStruct((pair_count, 128), jnp.float32),
         compiler_params=pltpu.CompilerParams(
             dimension_semantics=("arbitrary",), vmem_limit_bytes=48 << 20
         ),
-    )(own, stretch_index, crossed, inverse)
+    )(own, stretch_index, crossed, *factors)
     return out[:, :stretch_count].T
 
 
@@ -175,7 +194,7 @@
     receivers = receivers.reshape(minutes, source_count, recv_count, 2 * NF)
     crossed = cross_spectrum(sources[:, :, None, :], receivers)
     crossed = crossed.reshape(minutes, pair_count, 2 * NF)
-    result = coherence(0, stretch_index, crossed, inverse_table())
+    result = coherence(0, stretch_index, crossed, inverse_factors())
     stretch_count = stretch_index.shape[0]
     return result.reshape(1, stretch_count, source_count, recv_count)
 

time: 58.4 us -> 53.2 us (0.911)
  other arithmetic: 12.7 us -> 7.8 us
  Pallas kernels: 14.9 us -> 16.7 us
  matrix products: 3.88 us -> 2.21 us
    another operation x4 -> x2, other arithmetic: 4.93 us -> 2.33 us
    concatenate x1 -> x0, other arithmetic: 1.95 us -> none  [inverse_table(): jnp.concatenate([weight * cos_t, -weight * sin_t], axis=0)]
    sub x2 -> x1, other arithmetic: 1.79 us -> 0.01 us  [inverse_factors(): jnp.arange(groups, dtype=jnp.int32)[None, :] - groups // 2]
    pallas_call x1, Pallas kernels: 14.9 us -> 16.7 us  [coherence(): pl.pallas_call(coherence_kernel, grid_spec=pltpu.PrefetchScalarGridSpec(n...]
    dot_general x1, matrix products: 2.86 us -> 1.19 us  [body(): jnp.dot(candidates.reshape(minutes * slot_rows, NT), forward_table(), pre...]
    mul x0 -> x1, other arithmetic: none -> 1.63 us  [inverse_factors(): return (weight * cos_a, weight * sin_a, cos_c, sin_c)]
  transfers between devices with their start and end apart: 6 -> 6, of which waited for: 1 -> 1; matrix products, arithmetic and copies ran while one was open for 22% -> 14% of each run, Pallas kernels for 0% -> 0%
where the time goes in v11:
time: 53.2 us; the launch traced here: 52.7 us
  starting transfers between devices  21.2 us (40%)
  Pallas kernels  16.7 us (31%)
  other arithmetic  7.8 us (15%)
  waiting for transfers between devices  2.36 us (4%)
  matrix products  2.21 us (4%)
  local copies, waits for them, and re-layouts  2.13 us (4%)
    pallas_call x1, Pallas kernels, coherence(): pl.pallas_call(coherence_kernel, grid_spec=pltpu.PrefetchScalarGridSpec(n...  16.7 us
    ppermute x1, starting transfers between devices, body(): lax.ppermute(own_block, 'chan', [(s, blocks - s) for s in range(1, blocks)])  6.51 us
    ppermute x1, starting transfers between devices, body(): lax.ppermute(own_block, 'chan', [(s, blocks - 2 - s) for s in range(block...  5.23 us
    ppermute x1, starting transfers between devices, body(): lax.ppermute(own_block, 'chan', [(s, s + 1) for s in range(blocks - 1)])  3.99 us
    sin x3, other arithmetic, unit_angles(): return (jnp.cos(phase), jnp.sin(phase))  3.4 us
    ppermute x1, waiting for transfers between devices, body(): lax.ppermute(own_block, 'chan', [(s, blocks - s) for s in range(1, blocks)])  2.35 us
    another operation x2, other arithmetic  2.33 us
    ppermute x1, starting transfers between devices, body(): lax.ppermute(record, 'tm', [(i, (i + shift) % minutes) for i in range(min...  2.04 us
  transfers between devices with their start and end apart: 6, of which 1 were waited for; matrix products, arithmetic and copies ran while one was open for 14% of the time, Pallas kernels for 0%

profile of v11, /device:TPU:1, one launch (start us, length us, event | category | flops | bytes accessed | tf_op | source)
XLA Modules:
  0.0 52.7 jit_solution(11963447460471384133)
XLA Ops:
  0.0 2.0 %collective-permute-start = (bf16[1,16,1536]{2,1,0:T(8,128)(2,1)}, bf16[1,16,1536]{2,1,0:T(8,128)(2,1)S(1)}, u32[]{:S(2)}, u32[]{:S(2)}) collective-permute-start(bf16[1,16,1536]{2,1,0:T(8,128)(2,1)} %param.3), channel_id=1, source_target_pairs={{0,1},{1,0},{2,3},{3,2},{4,5},{5,4},{6,7},{7,6},{8,9},{9,8},{10,11... | collective-permute-start | bytes 147464 | tf_op jit(solution)/shard_map/ppermute | solution.py:163
  2.0 0.8 %constant_dynamic-update-slice_fusion.1 = bf16[2,16,1536]{2,1,0:T(8,128)(2,1)S(1)} fusion(bf16[1,16,1536]{2,1,0:T(8,128)(2,1)} %param.3), kind=kLoop, calls=%fused_computation.52 | loop fusion | bytes 98304
  2.9 1.6 %fusion.18 = (f32[128,768]{1,0:T(8,128)S(1)}, f32[128,768]{1,0:T(8,128)S(1)}) fusion(), kind=kLoop, calls=%fused_computation.33 | loop fusion | flops 884736 | bytes 786432 | tf_op jit(solution)/shard_map/sin | solution.py:19
  4.5 0.2 fusion.31
  4.7 0.0 copy-start.2
  4.7 1.6 %sine_multiply_fusion = (f32[768,8]{1,0:T(8,128)S(1)}, f32[768,8]{1,0:T(8,128)S(1)}) fusion(f32[768]{0:T(1024)S(1)} %fusion.34, s32[8]{0:T(128)S(1)} %iota_add_fusion), kind=kLoop, calls=%fused_computation.25 | loop fusion | flops 67584 | bytes 52256 | tf_op jit(solution)/shard_map/mul | solution.py:40
  6.4 0.0 copy-start.1
  6.4 1.4 %subtract_convert_fusion = (bf16[12,128,768]{2,1,0:T(8,128)(2,1)S(1)}, bf16[12,128,768]{2,1,0:T(8,128)(2,1)S(1)}) fusion(f32[128,768]{1,0:T(8,128)S(1)} %get-tuple-element.15, f32[12,768]{1,0:T(8,128)S(1)} %get-tuple-element.17, f32[128,768]{1,0:T(8,128)S(1)} %get-tuple-element.16, f32[12,768]{1,0:T(8,128)S(1)} %get-tuple-element.18), kind=kLoop, calls=%fused_computation.5 | loop fusion | flops 10616832 | bytes 5578752 | tf_op jit(solution)/shard_map/convert.8
  7.8 0.0 copy-done.2
  7.8 0.0 collective-permute-done
  7.9 4.0 %collective-permute-start.1 = (bf16[2,16,1536]{2,1,0:T(8,128)(2,1)S(1)}, bf16[2,16,1536]{2,1,0:T(8,128)(2,1)S(1)}, u32[]{:S(2)}, u32[]{:S(2)}) collective-permute-start(bf16[2,16,1536]{2,1,0:T(8,128)(2,1)S(1)} %constant_dynamic-update-slice_fusion), channel_id=1, source_target_pairs={{0,2},{2,4},{4,6},{6,8},{8,10},{10,12},{12,14},{14,16},{16,18},{18... | collective-permute-start | bytes 294920 | tf_op jit(solution)/shard_map/ppermute | solution.py:166
  11.9 1.6 %fusion.12 = (f32[768,128]{1,0:T(8,128)S(1)}, f32[768,128]{1,0:T(8,128)S(1)}) fusion(), kind=kLoop, calls=%fused_computation.23 | loop fusion | flops 884736 | bytes 786432 | tf_op jit(solution)/shard_map/sin | solution.py:19
  13.5 1.9 %collective-permute-start.2 = (bf16[2,16,1536]{2,1,0:T(8,128)(2,1)S(1)}, bf16[2,16,1536]{2,1,0:T(8,128)(2,1)S(1)}, u32[]{:S(2)}, u32[]{:S(2)}) collective-permute-start(bf16[2,16,1536]{2,1,0:T(8,128)(2,1)S(1)} %constant_dynamic-update-slice_fusion), channel_id=1, source_target_pairs={{2,0},{4,2},{6,4},{8,6},{10,8},{12,10},{14,12},{16,14},{18,16},{20... | collective-permute-start | bytes 294920 | tf_op jit(solution)/shard_map/ppermute | solution.py:167
  15.4 5.2 %collective-permute-start.3 = (bf16[2,16,1536]{2,1,0:T(8,128)(2,1)S(1)}, bf16[2,16,1536]{2,1,0:T(8,128)(2,1)S(1)}, u32[]{:S(2)}, u32[]{:S(2)}) collective-permute-start(bf16[2,16,1536]{2,1,0:T(8,128)(2,1)S(1)} %constant_dynamic-update-slice_fusion), channel_id=1, source_target_pairs={{0,28},{2,26},{4,24},{6,22},{8,20},{10,18},{12,16},{14,14},{16,12}... | collective-permute-start | bytes 294920 | tf_op jit(solution)/shard_map/ppermute | solution.py:168
  20.6 1.5 %collective-permute-start.4 = (bf16[2,16,1536]{2,1,0:T(8,128)(2,1)S(1)}, bf16[2,16,1536]{2,1,0:T(8,128)(2,1)S(1)}, u32[]{:S(2)}, u32[]{:S(2)}) collective-permute-start(bf16[2,16,1536]{2,1,0:T(8,128)(2,1)S(1)} %constant_dynamic-update-slice_fusion), channel_id=1, source_target_pairs={{0,30},{2,28},{4,26},{6,24},{8,22},{10,20},{12,18},{14,16},{16,14}... | collective-permute-start | bytes 294920 | tf_op jit(solution)/shard_map/ppermute | solution.py:169
  22.2 6.5 %collective-permute-start.5 = (bf16[2,16,1536]{2,1,0:T(8,128)(2,1)S(1)}, bf16[2,16,1536]{2,1,0:T(8,128)(2,1)S(1)}, u32[]{:S(2)}, u32[]{:S(2)}) collective-permute-start(bf16[2,16,1536]{2,1,0:T(8,128)(2,1)S(1)} %constant_dynamic-update-slice_fusion), channel_id=1, source_target_pairs={{2,30},{4,28},{6,26},{8,24},{10,22},{12,20},{14,18},{16,16},{18,14... | collective-permute-start | bytes 294920 | tf_op jit(solution)/shard_map/ppermute | solution.py:170
  28.7 0.0 collective-permute-done.1
  28.7 0.0 copy-done.1
  28.7 0.0 collective-permute-done.2
  28.8 0.0 collective-permute-done.3
  28.8 0.0 collective-permute-done.4
  28.8 2.4 %collective-permute-done.5 = bf16[2,16,1536]{2,1,0:T(8,128)(2,1)S(1)} collective-permute-done((bf16[2,16,1536]{2,1,0:T(8,128)(2,1)S(1)}, bf16[2,16,1536]{2,1,0:T(8,128)(2,1)S(1)}, u32[]{:S(2)}, u32[]{:S(2)}) %collective-permute-start.5) | collective-permute-done | bytes 98336 | tf_op jit(solution)/shard_map/ppermute | solution.py:170
  31.2 1.2 %multiply_reduce_fusion = (f32[192]{0:T(256)S(1)}, f32[192,1536]{1,0:T(8,128)S(1)}) fusion(bf16[192,1536]{1,0:T(8,128)(2,1)S(1)} %bitcast.36, bf16[1536,768]{1,0:T(8,128)(2,1)S(1)} %bitcast.35, bf16[1536,768]{1,0:T(8,128)(2,1)S(1)} %bitcast.34), kind=kOutput, calls=%fused_computation.10 | convolution fusion | flops 915996480 | bytes 6488832 | tf_op jit(solution)/shard_map/dot_general | solution.py:173
  32.4 0.2 divide_convert_fusion
  32.6 1.0 %fusion.24 = f32[2,1536,512]{1,2,0:T(8,128)S(1)} fusion(bf16[2,96,1536]{2,1,0:T(8,128)(2,1)S(1)} %bitcast.33, s32[512]{0:T(512)S(1)} %bitcast.37), kind=kOutput, calls=%fused_computation.40 | convolution fusion | flops 302039040 | bytes 6883328 | tf_op jit(solution)/shard_map/pq,mqk->mpk/dot_general | solution.py:191
  33.6 0.9 %add_convert_fusion = (bf16[2,2,256,768]{3,2,1,0:T(8,128)(2,1)S(1)}, bf16[2,2,256,768]{3,2,1,0:T(8,128)(2,1)S(1)}) fusion(f32[2,2,256,1536]{3,2,1,0:T(8,128)S(1)} %bitcast.29, f32[2,2,768]{2,1,0:T(2,128)S(1)} %get-tuple-element.10, f32[2,2,768]{2,1,0:T(2,128)S(1)} %get-tuple-element.9), kind=kLoop, calls=%fused_computation.8 | loop fusion | flops 6291456 | bytes 9461760 | tf_op jit(solution)/shard_map/convert.4
  34.6 0.0 copy-start
  34.6 0.2 pad_maximum_fusion.crossed_ref
  34.8 0.5 copy-done
  35.3 16.7 %shard_map.37 = f32[512,128]{1,0:T(8,128)S(1)} custom-call(s32[1]{0:T(128)} %constant.23.clone.1.own_ref, s32[4,1024]{1,0:T(4,128)S(1)} %copy-done, bf16[2,512,1536]{2,1,0:T(8,128)(2,1)S(1)} %pad_maximum_fusion.crossed_ref, f32[768,8]{1,0:T(8,128)S(1)} %get-tuple-element.12.wcos_ref, f32[768,8]{1,0:T(8,128)S(1)} %get-tuple-element.11.wsin_ref, ...), custom_call_target="tpu_custom_call" | custom-call | tf_op jit(solution)/shard_map/pallas_call | solution.py:133
  52.0 0.7 %copy.7 = f32[1,4,2,256]{3,2,1,0:T(2,128)} copy(f32[1,4,2,256]{1,3,2,0:T(8,128)S(1)} %bitcast.28) | data formatting | bytes 16384 | tf_op jit(solution)/shard_map/reshape | solution.py:199
  (17 shorter events, 0.2 us)
Async XLA Ops:
  0.0 7.8 %collective-permute-start = (bf16[1,16,1536]{2,1,0:T(8,128)(2,1)}, bf16[1,16,1536]{2,1,0:T(8,128)(2,1)S(1)}, u32[]{:S(2)}, u32[]{:S(2)}) collective-permute-start(bf16[1,16,1536]{2,1,0:T(8,128)(2,1)} %param.3), channel_id=1, source_target_pairs={{0,1},{1,0},{2,3},{3,2},{4,5},{5,4},{6,7},{7,6},{8,9},{9,8},{10,11... | collective-permute-start | bytes 147464 | tf_op jit(solution)/shard_map/ppermute | solution.py:163
  4.7 3.1 %copy-start.2 = (s32[2,256]{1,0:T(2,128)S(1)}, s32[2,256]{1,0:T(2,128)}, u32[]{:S(2)}) copy-start(s32[2,256]{1,0:T(2,128)} %param.4) | copy-start | bytes 6148
  6.4 22.3 %copy-start.1 = (bf16[1,16,1536]{2,1,0:T(8,128)(2,1)S(1)}, bf16[1,16,1536]{2,1,0:T(8,128)(2,1)}, u32[]{:S(2)}) copy-start(bf16[1,16,1536]{2,1,0:T(8,128)(2,1)} %param.3) | copy-start | bytes 147460
  7.9 20.8 %collective-permute-start.1 = (bf16[2,16,1536]{2,1,0:T(8,128)(2,1)S(1)}, bf16[2,16,1536]{2,1,0:T(8,128)(2,1)S(1)}, u32[]{:S(2)}, u32[]{:S(2)}) collective-permute-start(bf16[2,16,1536]{2,1,0:T(8,128)(2,1)S(1)} %constant_dynamic-update-slice_fusion), channel_id=1, source_target_pairs={{0,2},{2,4},{4,6},{6,8},{8,10},{10,12},{12,14},{14,16},{16,18},{18... | collective-permute-start | bytes 294920 | tf_op jit(solution)/shard_map/ppermute | solution.py:166
  13.5 15.3 %collective-permute-start.2 = (bf16[2,16,1536]{2,1,0:T(8,128)(2,1)S(1)}, bf16[2,16,1536]{2,1,0:T(8,128)(2,1)S(1)}, u32[]{:S(2)}, u32[]{:S(2)}) collective-permute-start(bf16[2,16,1536]{2,1,0:T(8,128)(2,1)S(1)} %constant_dynamic-update-slice_fusion), channel_id=1, source_target_pairs={{2,0},{4,2},{6,4},{8,6},{10,8},{12,10},{14,12},{16,14},{18,16},{20... | collective-permute-start | bytes 294920 | tf_op jit(solution)/shard_map/ppermute | solution.py:167
  15.4 13.4 %collective-permute-start.3 = (bf16[2,16,1536]{2,1,0:T(8,128)(2,1)S(1)}, bf16[2,16,1536]{2,1,0:T(8,128)(2,1)S(1)}, u32[]{:S(2)}, u32[]{:S(2)}) collective-permute-start(bf16[2,16,1536]{2,1,0:T(8,128)(2,1)S(1)} %constant_dynamic-update-slice_fusion), channel_id=1, source_target_pairs={{0,28},{2,26},{4,24},{6,22},{8,20},{10,18},{12,16},{14,14},{16,12}... | collective-permute-start | bytes 294920 | tf_op jit(solution)/shard_map/ppermute | solution.py:168
  20.6 8.2 %collective-permute-start.4 = (bf16[2,16,1536]{2,1,0:T(8,128)(2,1)S(1)}, bf16[2,16,1536]{2,1,0:T(8,128)(2,1)S(1)}, u32[]{:S(2)}, u32[]{:S(2)}) collective-permute-start(bf16[2,16,1536]{2,1,0:T(8,128)(2,1)S(1)} %constant_dynamic-update-slice_fusion), channel_id=1, source_target_pairs={{0,30},{2,28},{4,26},{6,24},{8,22},{10,20},{12,18},{14,16},{16,14}... | collective-permute-start | bytes 294920 | tf_op jit(solution)/shard_map/ppermute | solution.py:169
  22.2 9.0 %collective-permute-start.5 = (bf16[2,16,1536]{2,1,0:T(8,128)(2,1)S(1)}, bf16[2,16,1536]{2,1,0:T(8,128)(2,1)S(1)}, u32[]{:S(2)}, u32[]{:S(2)}) collective-permute-start(bf16[2,16,1536]{2,1,0:T(8,128)(2,1)S(1)} %constant_dynamic-update-slice_fusion), channel_id=1, source_target_pairs={{2,30},{4,28},{6,26},{8,24},{10,22},{12,20},{14,18},{16,16},{18,14... | collective-permute-start | bytes 294920 | tf_op jit(solution)/shard_map/ppermute | solution.py:170
  34.6 0.7 %copy-start = (s32[4,1024]{1,0:T(4,128)S(1)}, s32[4,1024]{1,0:T(4,128)}, u32[]{:S(2)}) copy-start(s32[4,1024]{1,0:T(4,128)} %stretch_ref.1) | copy-start | bytes 49156

commit v12 on v11

--- a/solution.py
+++ b/solution.py
@@ -163,12 +163,21 @@
             lax.ppermute(record, "tm", [(i, (i + shift) % minutes) for i in range(minutes)])
         )
     own_block = jnp.concatenate(parts, axis=0)
-    below = lax.ppermute(own_block, "chan", [(s, s + 1) for s in range(blocks - 1)])
-    above = lax.ppermute(own_block, "chan", [(s, s - 1) for s in range(1, blocks)])
-    far_low = lax.ppermute(own_block, "chan", [(s, blocks - 2 - s) for s in range(blocks - 1)])
-    far_mid = lax.ppermute(own_block, "chan", [(s, blocks - 1 - s) for s in range(blocks)])
-    far_high = lax.ppermute(own_block, "chan", [(s, blocks - s) for s in range(1, blocks)])
-    candidates = jnp.concatenate([below, own_block, above, far_low, far_mid, far_high], axis=1)
+    mirrored = lax.ppermute(own_block, "chan", [(s, blocks - 1 - s) for s in range(blocks)])
+    bundle = jnp.concatenate([own_block, mirrored], axis=1)
+    from_below = lax.ppermute(bundle, "chan", [(s, s + 1) for s in range(blocks - 1)])
+    from_above = lax.ppermute(bundle, "chan", [(s, s - 1) for s in range(1, blocks)])
+    candidates = jnp.concatenate(
+        [
+            from_below[:, :block_rows],
+            own_block,
+            from_above[:, :block_rows],
+            from_above[:, block_rows:],
+            mirrored,
+            from_below[:, block_rows:],
+        ],
+        axis=1,
+    )
     slot_rows = candidates.shape[1]
     spectrum = jnp.dot(
         candidates.reshape(minutes * slot_rows, NT), forward_table(),

time: 53.2 us -> 50.3 us (0.945)
  starting transfers between devices: 21.2 us -> 12.8 us
  waiting for transfers between devices: 2.36 us -> 7.86 us
    ppermute x4 -> x2, starting transfers between devices: 17.6 us -> 5.56 us  [the longest x1 3.46 us: body(): lax.ppermute(bundle, 'chan', [(s, s + 1) for s in range(blocks - 1)])]
    ppermute x1, starting transfers between devices: 1.53 us -> 5.18 us  [body(): lax.ppermute(own_block, 'chan', [(s, blocks - 1 - s) for s in range(block...]
    ppermute x1, waiting for transfers between devices: 0.01 us -> 3.04 us  [body(): lax.ppermute(own_block, 'chan', [(s, blocks - 1 - s) for s in range(block...]
    ppermute x4 -> x2, waiting for transfers between devices: 2.36 us -> 4.82 us  [the longest x1 4.82 us: body(): lax.ppermute(bundle, 'chan', [(s, s - 1) for s in range(1, blocks)])]
    unnamed x14 -> x13, local copies, waits for them, and re-layouts: 1.36 us -> 1.36 us
  transfers between devices with their start and end apart: 6 -> 4, of which waited for: 1 -> 2; matrix products, arithmetic and copies ran while one was open for 14% -> 15% of each run, Pallas kernels for 0% -> 0%
where the time goes in v12:
time: 50.3 us; the launch traced here: 49.7 us
  Pallas kernels  16.7 us (33%)
  starting transfers between devices  12.8 us (25%)
  waiting for transfers between devices  7.86 us (16%)
  other arithmetic  7.82 us (16%)
  matrix products  2.21 us (4%)
  local copies, waits for them, and re-layouts  2.13 us (4%)
    pallas_call x1, Pallas kernels, coherence(): pl.pallas_call(coherence_kernel, grid_spec=pltpu.PrefetchScalarGridSpec(n...  16.7 us
    ppermute x1, starting transfers between devices, body(): lax.ppermute(own_block, 'chan', [(s, blocks - 1 - s) for s in range(block...  5.18 us
    ppermute x1, waiting for transfers between devices, body(): lax.ppermute(bundle, 'chan', [(s, s - 1) for s in range(1, blocks)])  4.82 us
    ppermute x1, starting transfers between devices, body(): lax.ppermute(bundle, 'chan', [(s, s + 1) for s in range(blocks - 1)])  3.46 us
    sin x3, other arithmetic, unit_angles(): return (jnp.cos(phase), jnp.sin(phase))  3.4 us
    ppermute x1, waiting for transfers between devices, body(): lax.ppermute(own_block, 'chan', [(s, blocks - 1 - s) for s in range(block...  3.04 us
    another operation x2, other arithmetic  2.33 us
    ppermute x1, starting transfers between devices, body(): lax.ppermute(bundle, 'chan', [(s, s - 1) for s in range(1, blocks)])  2.1 us
  transfers between devices with their start and end apart: 4, of which 2 were waited for; matrix products, arithmetic and copies ran while one was open for 15% of the time, Pallas kernels for 0%

profile of v12, /device:TPU:1, one launch (start us, length us, event | category | flops | bytes accessed | tf_op | source)
XLA Modules:
  0.0 49.7 jit_solution(17592620768930889323)
XLA Ops:
  0.0 2.0 %collective-permute-start = (bf16[1,16,1536]{2,1,0:T(8,128)(2,1)}, bf16[1,16,1536]{2,1,0:T(8,128)(2,1)S(1)}, u32[]{:S(2)}, u32[]{:S(2)}) collective-permute-start(bf16[1,16,1536]{2,1,0:T(8,128)(2,1)} %param.3), channel_id=1, source_target_pairs={{0,1},{1,0},{2,3},{3,2},{4,5},{5,4},{6,7},{7,6},{8,9},{9,8},{10,11... | collective-permute-start | bytes 147464 | tf_op jit(solution)/shard_map/ppermute | solution.py:163
  2.0 0.8 %constant_dynamic-update-slice_fusion.1 = bf16[2,16,1536]{2,1,0:T(8,128)(2,1)S(1)} fusion(bf16[1,16,1536]{2,1,0:T(8,128)(2,1)} %param.3), kind=kLoop, calls=%fused_computation.55 | loop fusion | bytes 98304
  2.9 1.6 %fusion.18 = (f32[128,768]{1,0:T(8,128)S(1)}, f32[128,768]{1,0:T(8,128)S(1)}) fusion(), kind=kLoop, calls=%fused_computation.33 | loop fusion | flops 884736 | bytes 786432 | tf_op jit(solution)/shard_map/sin | solution.py:19
  4.5 0.2 fusion.31
  4.7 0.0 copy-start.2
  4.7 1.6 %fusion.12 = (f32[768,128]{1,0:T(8,128)S(1)}, f32[768,128]{1,0:T(8,128)S(1)}) fusion(), kind=kLoop, calls=%fused_computation.23 | loop fusion | flops 884736 | bytes 786432 | tf_op jit(solution)/shard_map/sin | solution.py:19
  6.3 0.0 copy-start.1
  6.3 1.4 %subtract_convert_fusion = (bf16[12,128,768]{2,1,0:T(8,128)(2,1)S(1)}, bf16[12,128,768]{2,1,0:T(8,128)(2,1)S(1)}) fusion(f32[128,768]{1,0:T(8,128)S(1)} %get-tuple-element.15, f32[12,768]{1,0:T(8,128)S(1)} %get-tuple-element.17, f32[128,768]{1,0:T(8,128)S(1)} %get-tuple-element.16, f32[12,768]{1,0:T(8,128)S(1)} %get-tuple-element.18), kind=kLoop, calls=%fused_computation.5 | loop fusion | flops 10616832 | bytes 5578752 | tf_op jit(solution)/shard_map/convert.8
  7.8 0.0 copy-done.2
  7.8 0.0 collective-permute-done
  7.8 5.2 %collective-permute-start.1 = (bf16[2,16,1536]{2,1,0:T(8,128)(2,1)S(1)}, bf16[2,16,1536]{2,1,0:T(8,128)(2,1)S(1)}, u32[]{:S(2)}, u32[]{:S(2)}) collective-permute-start(bf16[2,16,1536]{2,1,0:T(8,128)(2,1)S(1)} %constant_dynamic-update-slice_fusion), channel_id=1, source_target_pairs={{0,30},{2,28},{4,26},{6,24},{8,22},{10,20},{12,18},{14,16},{16,14}... | collective-permute-start | bytes 294920 | tf_op jit(solution)/shard_map/ppermute | solution.py:166
  13.0 3.0 %collective-permute-done.1 = bf16[2,16,1536]{2,1,0:T(8,128)(2,1)S(1)} collective-permute-done((bf16[2,16,1536]{2,1,0:T(8,128)(2,1)S(1)}, bf16[2,16,1536]{2,1,0:T(8,128)(2,1)S(1)}, u32[]{:S(2)}, u32[]{:S(2)}) %collective-permute-start.1) | collective-permute-done | bytes 98336 | tf_op jit(solution)/shard_map/ppermute | solution.py:166
  16.1 3.5 %collective-permute-start.2 = (bf16[2,32,1536]{2,1,0:T(8,128)(2,1)S(1)}, bf16[2,32,1536]{2,1,0:T(8,128)(2,1)S(1)}, u32[]{:S(2)}, u32[]{:S(2)}) collective-permute-start(bf16[2,32,1536]{2,1,0:T(8,128)(2,1)S(1)} %pad_maximum_fusion.1), channel_id=1, source_target_pairs={{0,2},{2,4},{4,6},{6,8},{8,10},{10,12},{12,14},{14,16},{16,18},{18... | collective-permute-start | bytes 589832 | tf_op jit(solution)/shard_map/ppermute | solution.py:168
  19.5 1.6 %sine_multiply_fusion = (f32[768,8]{1,0:T(8,128)S(1)}, f32[768,8]{1,0:T(8,128)S(1)}) fusion(f32[768]{0:T(1024)S(1)} %fusion.34, s32[8]{0:T(128)S(1)} %iota_add_fusion), kind=kLoop, calls=%fused_computation.25 | loop fusion | flops 67584 | bytes 52256 | tf_op jit(solution)/shard_map/mul | solution.py:40
  21.2 2.1 %collective-permute-start.3 = (bf16[2,32,1536]{2,1,0:T(8,128)(2,1)S(1)}, bf16[2,32,1536]{2,1,0:T(8,128)(2,1)S(1)}, u32[]{:S(2)}, u32[]{:S(2)}) collective-permute-start(bf16[2,32,1536]{2,1,0:T(8,128)(2,1)S(1)} %pad_maximum_fusion.1), channel_id=1, source_target_pairs={{2,0},{4,2},{6,4},{8,6},{10,8},{12,10},{14,12},{16,14},{18,16},{20... | collective-permute-start | bytes 589832 | tf_op jit(solution)/shard_map/ppermute | solution.py:169
  23.3 0.0 collective-permute-done.2
  23.3 0.0 copy-done.1
  23.3 4.8 %collective-permute-done.3 = bf16[2,32,1536]{2,1,0:T(8,128)(2,1)S(1)} collective-permute-done((bf16[2,32,1536]{2,1,0:T(8,128)(2,1)S(1)}, bf16[2,32,1536]{2,1,0:T(8,128)(2,1)S(1)}, u32[]{:S(2)}, u32[]{:S(2)}) %collective-permute-start.3) | collective-permute-done | bytes 196640 | tf_op jit(solution)/shard_map/ppermute | solution.py:169
  28.2 1.2 %multiply_reduce_fusion = (f32[192]{0:T(256)S(1)}, f32[192,1536]{1,0:T(8,128)S(1)}) fusion(bf16[192,1536]{1,0:T(8,128)(2,1)S(1)} %bitcast.36, bf16[1536,768]{1,0:T(8,128)(2,1)S(1)} %bitcast.35, bf16[1536,768]{1,0:T(8,128)(2,1)S(1)} %bitcast.34), kind=kOutput, calls=%fused_computation.10 | convolution fusion | flops 915996480 | bytes 6488832 | tf_op jit(solution)/shard_map/dot_general | solution.py:182
  29.4 0.2 divide_convert_fusion
  29.6 1.0 %fusion.24 = f32[2,1536,512]{1,2,0:T(8,128)S(1)} fusion(bf16[2,96,1536]{2,1,0:T(8,128)(2,1)S(1)} %bitcast.33, s32[512]{0:T(512)S(1)} %bitcast.37), kind=kOutput, calls=%fused_computation.41 | convolution fusion | flops 302039040 | bytes 6883328 | tf_op jit(solution)/shard_map/pq,mqk->mpk/dot_general | solution.py:200
  30.7 0.9 %add_convert_fusion = (bf16[2,2,256,768]{3,2,1,0:T(8,128)(2,1)S(1)}, bf16[2,2,256,768]{3,2,1,0:T(8,128)(2,1)S(1)}) fusion(f32[2,2,256,1536]{3,2,1,0:T(8,128)S(1)} %bitcast.29, f32[2,2,768]{2,1,0:T(2,128)S(1)} %get-tuple-element.10, f32[2,2,768]{2,1,0:T(2,128)S(1)} %get-tuple-element.9), kind=kLoop, calls=%fused_computation.8 | loop fusion | flops 6291456 | bytes 9461760 | tf_op jit(solution)/shard_map/convert.4
  31.6 0.0 copy-start
  31.6 0.2 pad_maximum_fusion.crossed_ref
  31.9 0.5 copy-done
  32.3 16.7 %shard_map.37 = f32[512,128]{1,0:T(8,128)S(1)} custom-call(s32[1]{0:T(128)} %constant.23.clone.1.own_ref, s32[4,1024]{1,0:T(4,128)S(1)} %copy-done, bf16[2,512,1536]{2,1,0:T(8,128)(2,1)S(1)} %pad_maximum_fusion.crossed_ref, f32[768,8]{1,0:T(8,128)S(1)} %get-tuple-element.12.wcos_ref, f32[768,8]{1,0:T(8,128)S(1)} %get-tuple-element.11.wsin_ref, ...), custom_call_target="tpu_custom_call" | custom-call | tf_op jit(solution)/shard_map/pallas_call | solution.py:133
  49.0 0.7 %copy.7 = f32[1,4,2,256]{3,2,1,0:T(2,128)} copy(f32[1,4,2,256]{1,3,2,0:T(8,128)S(1)} %bitcast.28) | data formatting | bytes 16384 | tf_op jit(solution)/shard_map/reshape | solution.py:208
  (17 shorter events, 0.2 us)
Async XLA Ops:
  0.0 7.8 %collective-permute-start = (bf16[1,16,1536]{2,1,0:T(8,128)(2,1)}, bf16[1,16,1536]{2,1,0:T(8,128)(2,1)S(1)}, u32[]{:S(2)}, u32[]{:S(2)}) collective-permute-start(bf16[1,16,1536]{2,1,0:T(8,128)(2,1)} %param.3), channel_id=1, source_target_pairs={{0,1},{1,0},{2,3},{3,2},{4,5},{5,4},{6,7},{7,6},{8,9},{9,8},{10,11... | collective-permute-start | bytes 147464 | tf_op jit(solution)/shard_map/ppermute | solution.py:163
  4.7 3.0 %copy-start.2 = (s32[2,256]{1,0:T(2,128)S(1)}, s32[2,256]{1,0:T(2,128)}, u32[]{:S(2)}) copy-start(s32[2,256]{1,0:T(2,128)} %param.4) | copy-start | bytes 6148
  6.3 17.0 %copy-start.1 = (bf16[1,16,1536]{2,1,0:T(8,128)(2,1)S(1)}, bf16[1,16,1536]{2,1,0:T(8,128)(2,1)}, u32[]{:S(2)}) copy-start(bf16[1,16,1536]{2,1,0:T(8,128)(2,1)} %param.3) | copy-start | bytes 147460
  7.8 8.2 %collective-permute-start.1 = (bf16[2,16,1536]{2,1,0:T(8,128)(2,1)S(1)}, bf16[2,16,1536]{2,1,0:T(8,128)(2,1)S(1)}, u32[]{:S(2)}, u32[]{:S(2)}) collective-permute-start(bf16[2,16,1536]{2,1,0:T(8,128)(2,1)S(1)} %constant_dynamic-update-slice_fusion), channel_id=1, source_target_pairs={{0,30},{2,28},{4,26},{6,24},{8,22},{10,20},{12,18},{14,16},{16,14}... | collective-permute-start | bytes 294920 | tf_op jit(solution)/shard_map/ppermute | solution.py:166
  16.1 7.2 %collective-permute-start.2 = (bf16[2,32,1536]{2,1,0:T(8,128)(2,1)S(1)}, bf16[2,32,1536]{2,1,0:T(8,128)(2,1)S(1)}, u32[]{:S(2)}, u32[]{:S(2)}) collective-permute-start(bf16[2,32,1536]{2,1,0:T(8,128)(2,1)S(1)} %pad_maximum_fusion.1), channel_id=1, source_target_pairs={{0,2},{2,4},{4,6},{6,8},{8,10},{10,12},{12,14},{14,16},{16,18},{18... | collective-permute-start | bytes 589832 | tf_op jit(solution)/shard_map/ppermute | solution.py:168
  21.2 7.0 %collective-permute-start.3 = (bf16[2,32,1536]{2,1,0:T(8,128)(2,1)S(1)}, bf16[2,32,1536]{2,1,0:T(8,128)(2,1)S(1)}, u32[]{:S(2)}, u32[]{:S(2)}) collective-permute-start(bf16[2,32,1536]{2,1,0:T(8,128)(2,1)S(1)} %pad_maximum_fusion.1), channel_id=1, source_target_pairs={{2,0},{4,2},{6,4},{8,6},{10,8},{12,10},{14,12},{16,14},{18,16},{20... | collective-permute-start | bytes 589832 | tf_op jit(solution)/shard_map/ppermute | solution.py:169
  31.6 0.7 %copy-start = (s32[4,1024]{1,0:T(4,128)S(1)}, s32[4,1024]{1,0:T(4,128)}, u32[]{:S(2)}) copy-start(s32[4,1024]{1,0:T(4,128)} %stretch_ref.1) | copy-start | bytes 49156

commit v13 on v12

--- a/solution.py
+++ b/solution.py
@@ -58,7 +58,7 @@
     return jnp.concatenate([real_part, imag_part], axis=-1).astype(jnp.bfloat16)
 
 
-PAIR_BLOCK = 128
+PAIR_BLOCK = 256
 
 
 def coherence_kernel(
@@ -106,10 +106,11 @@
             current = jnp.where(own == minute, correlation, current)
     high = stacked.astype(jnp.bfloat16)
     low = (stacked - high.astype(jnp.float32)).astype(jnp.bfloat16)
-    picks = picks_ref[...]
-    moved = jnp.dot(high, picks, preferred_element_type=jnp.float32) + jnp.dot(
-        low, picks, preferred_element_type=jnp.float32
-    )
+    rows = stacked.shape[0]
+    moved = jnp.dot(
+        jnp.concatenate([high, low], axis=0), picks_ref[...], preferred_element_type=jnp.float32
+    )
+    moved = moved[:rows] + moved[rows:]
     scale = 1.0 / LAGS
     current_power = jnp.sum(current * current, axis=1, keepdims=True) * scale
     lanes = lax.broadcasted_iota(jnp.int32, out_ref.shape, 1)
@@ -130,16 +131,17 @@
     minutes, pair_count, width = crossed.shape
     stretch_count = stretch_index.shape[0]
     own = jnp.reshape(own_minute, (1,)).astype(jnp.int32)
+    block = min(PAIR_BLOCK, pair_count)
     out = pl.pallas_call(
         coherence_kernel,
         grid_spec=pltpu.PrefetchScalarGridSpec(
             num_scalar_prefetch=1,
-            grid=(pair_count // PAIR_BLOCK,),
+            grid=(pair_count // block,),
             in_specs=[
                 pl.BlockSpec(stretch_index.shape, lambda i, own: (0, 0)),
-                pl.BlockSpec((minutes, PAIR_BLOCK, width), lambda i, own: (0, i, 0)),
+                pl.BlockSpec((minutes, block, width), lambda i, own: (0, i, 0)),
             ] + [pl.BlockSpec(factor.shape, lambda i, own: (0, 0)) for factor in factors],
-            out_specs=pl.BlockSpec((PAIR_BLOCK, 128), lambda i, own: (i, 0)),
+            out_specs=pl.BlockSpec((block, 128), lambda i, own: (i, 0)),
             scratch_shapes=[
                 pltpu.VMEM((LAGS, (stretch_count - 1) * LAGS), jnp.bfloat16),
                 pltpu.VMEM((width, LAGS), jnp.bfloat16),

time: 50.3 us -> 49.3 us (0.980)
  Pallas kernels: 16.7 us -> 15.6 us
    pallas_call x1, Pallas kernels: 16.7 us -> 15.6 us  [coherence(): pl.pallas_call(coherence_kernel, grid_spec=pltpu.PrefetchScalarGridSpec(n...]
where the time goes in v13:
time: 49.3 us; the launch traced here: 48.6 us
  Pallas kernels  15.6 us (32%)
  starting transfers between devices  12.8 us (26%)
  waiting for transfers between devices  7.86 us (16%)
  other arithmetic  7.82 us (16%)
  matrix products  2.21 us (4%)
  local copies, waits for them, and re-layouts  2.13 us (4%)
    pallas_call x1, Pallas kernels, coherence(): pl.pallas_call(coherence_kernel, grid_spec=pltpu.PrefetchScalarGridSpec(n...  15.6 us
    ppermute x1, starting transfers between devices, body(): lax.ppermute(own_block, 'chan', [(s, blocks - 1 - s) for s in range(block...  5.18 us
    ppermute x1, waiting for transfers between devices, body(): lax.ppermute(bundle, 'chan', [(s, s - 1) for s in range(1, blocks)])  4.82 us
    ppermute x1, starting transfers between devices, body(): lax.ppermute(bundle, 'chan', [(s, s + 1) for s in range(blocks - 1)])  3.46 us
    sin x3, other arithmetic, unit_angles(): return (jnp.cos(phase), jnp.sin(phase))  3.4 us
    ppermute x1, waiting for transfers between devices, body(): lax.ppermute(own_block, 'chan', [(s, blocks - 1 - s) for s in range(block...  3.04 us
    another operation x2, other arithmetic  2.33 us
    ppermute x1, starting transfers between devices, body(): lax.ppermute(bundle, 'chan', [(s, s - 1) for s in range(1, blocks)])  2.1 us
  transfers between devices with their start and end apart: 4, of which 2 were waited for; matrix products, arithmetic and copies ran while one was open for 15% of the time, Pallas kernels for 0%

profile of v13, /device:TPU:1, one launch (start us, length us, event | category | flops | bytes accessed | tf_op | source)
XLA Modules:
  0.0 48.6 jit_solution(5190258566591161252)
XLA Ops:
  0.0 2.0 %collective-permute-start = (bf16[1,16,1536]{2,1,0:T(8,128)(2,1)}, bf16[1,16,1536]{2,1,0:T(8,128)(2,1)S(1)}, u32[]{:S(2)}, u32[]{:S(2)}) collective-permute-start(bf16[1,16,1536]{2,1,0:T(8,128)(2,1)} %param.3), channel_id=1, source_target_pairs={{0,1},{1,0},{2,3},{3,2},{4,5},{5,4},{6,7},{7,6},{8,9},{9,8},{10,11... | collective-permute-start | bytes 147464 | tf_op jit(solution)/shard_map/ppermute | solution.py:165
  2.0 0.8 %constant_dynamic-update-slice_fusion.1 = bf16[2,16,1536]{2,1,0:T(8,128)(2,1)S(1)} fusion(bf16[1,16,1536]{2,1,0:T(8,128)(2,1)} %param.3), kind=kLoop, calls=%fused_computation.55 | loop fusion | bytes 98304
  2.9 1.6 %fusion.18 = (f32[128,768]{1,0:T(8,128)S(1)}, f32[128,768]{1,0:T(8,128)S(1)}) fusion(), kind=kLoop, calls=%fused_computation.33 | loop fusion | flops 884736 | bytes 786432 | tf_op jit(solution)/shard_map/sin | solution.py:19
  4.5 0.2 fusion.31
  4.7 0.0 copy-start.2
  4.7 1.6 %fusion.12 = (f32[768,128]{1,0:T(8,128)S(1)}, f32[768,128]{1,0:T(8,128)S(1)}) fusion(), kind=kLoop, calls=%fused_computation.23 | loop fusion | flops 884736 | bytes 786432 | tf_op jit(solution)/shard_map/sin | solution.py:19
  6.3 0.0 copy-start.1
  6.3 1.4 %subtract_convert_fusion = (bf16[12,128,768]{2,1,0:T(8,128)(2,1)S(1)}, bf16[12,128,768]{2,1,0:T(8,128)(2,1)S(1)}) fusion(f32[128,768]{1,0:T(8,128)S(1)} %get-tuple-element.15, f32[12,768]{1,0:T(8,128)S(1)} %get-tuple-element.17, f32[128,768]{1,0:T(8,128)S(1)} %get-tuple-element.16, f32[12,768]{1,0:T(8,128)S(1)} %get-tuple-element.18), kind=kLoop, calls=%fused_computation.5 | loop fusion | flops 10616832 | bytes 5578752 | tf_op jit(solution)/shard_map/convert.8
  7.8 0.0 copy-done.2
  7.8 0.0 collective-permute-done
  7.8 5.2 %collective-permute-start.1 = (bf16[2,16,1536]{2,1,0:T(8,128)(2,1)S(1)}, bf16[2,16,1536]{2,1,0:T(8,128)(2,1)S(1)}, u32[]{:S(2)}, u32[]{:S(2)}) collective-permute-start(bf16[2,16,1536]{2,1,0:T(8,128)(2,1)S(1)} %constant_dynamic-update-slice_fusion), channel_id=1, source_target_pairs={{0,30},{2,28},{4,26},{6,24},{8,22},{10,20},{12,18},{14,16},{16,14}... | collective-permute-start | bytes 294920 | tf_op jit(solution)/shard_map/ppermute | solution.py:168
  13.0 3.0 %collective-permute-done.1 = bf16[2,16,1536]{2,1,0:T(8,128)(2,1)S(1)} collective-permute-done((bf16[2,16,1536]{2,1,0:T(8,128)(2,1)S(1)}, bf16[2,16,1536]{2,1,0:T(8,128)(2,1)S(1)}, u32[]{:S(2)}, u32[]{:S(2)}) %collective-permute-start.1) | collective-permute-done | bytes 98336 | tf_op jit(solution)/shard_map/ppermute | solution.py:168
  16.1 3.5 %collective-permute-start.2 = (bf16[2,32,1536]{2,1,0:T(8,128)(2,1)S(1)}, bf16[2,32,1536]{2,1,0:T(8,128)(2,1)S(1)}, u32[]{:S(2)}, u32[]{:S(2)}) collective-permute-start(bf16[2,32,1536]{2,1,0:T(8,128)(2,1)S(1)} %pad_maximum_fusion.1), channel_id=1, source_target_pairs={{0,2},{2,4},{4,6},{6,8},{8,10},{10,12},{12,14},{14,16},{16,18},{18... | collective-permute-start | bytes 589832 | tf_op jit(solution)/shard_map/ppermute | solution.py:170
  19.5 1.6 %sine_multiply_fusion = (f32[768,8]{1,0:T(8,128)S(1)}, f32[768,8]{1,0:T(8,128)S(1)}) fusion(f32[768]{0:T(1024)S(1)} %fusion.34, s32[8]{0:T(128)S(1)} %iota_add_fusion), kind=kLoop, calls=%fused_computation.25 | loop fusion | flops 67584 | bytes 52256 | tf_op jit(solution)/shard_map/mul | solution.py:40
  21.2 2.1 %collective-permute-start.3 = (bf16[2,32,1536]{2,1,0:T(8,128)(2,1)S(1)}, bf16[2,32,1536]{2,1,0:T(8,128)(2,1)S(1)}, u32[]{:S(2)}, u32[]{:S(2)}) collective-permute-start(bf16[2,32,1536]{2,1,0:T(8,128)(2,1)S(1)} %pad_maximum_fusion.1), channel_id=1, source_target_pairs={{2,0},{4,2},{6,4},{8,6},{10,8},{12,10},{14,12},{16,14},{18,16},{20... | collective-permute-start | bytes 589832 | tf_op jit(solution)/shard_map/ppermute | solution.py:171
  23.3 0.0 collective-permute-done.2
  23.3 0.0 copy-done.1
  23.3 4.8 %collective-permute-done.3 = bf16[2,32,1536]{2,1,0:T(8,128)(2,1)S(1)} collective-permute-done((bf16[2,32,1536]{2,1,0:T(8,128)(2,1)S(1)}, bf16[2,32,1536]{2,1,0:T(8,128)(2,1)S(1)}, u32[]{:S(2)}, u32[]{:S(2)}) %collective-permute-start.3) | collective-permute-done | bytes 196640 | tf_op jit(solution)/shard_map/ppermute | solution.py:171
  28.2 1.2 %multiply_reduce_fusion = (f32[192]{0:T(256)S(1)}, f32[192,1536]{1,0:T(8,128)S(1)}) fusion(bf16[192,1536]{1,0:T(8,128)(2,1)S(1)} %bitcast.36, bf16[1536,768]{1,0:T(8,128)(2,1)S(1)} %bitcast.35, bf16[1536,768]{1,0:T(8,128)(2,1)S(1)} %bitcast.34), kind=kOutput, calls=%fused_computation.10 | convolution fusion | flops 915996480 | bytes 6488832 | tf_op jit(solution)/shard_map/dot_general | solution.py:184
  29.4 0.2 divide_convert_fusion
  29.6 1.0 %fusion.24 = f32[2,1536,512]{1,2,0:T(8,128)S(1)} fusion(bf16[2,96,1536]{2,1,0:T(8,128)(2,1)S(1)} %bitcast.33, s32[512]{0:T(512)S(1)} %bitcast.37), kind=kOutput, calls=%fused_computation.41 | convolution fusion | flops 302039040 | bytes 6883328 | tf_op jit(solution)/shard_map/pq,mqk->mpk/dot_general | solution.py:202
  30.7 0.9 %add_convert_fusion = (bf16[2,2,256,768]{3,2,1,0:T(8,128)(2,1)S(1)}, bf16[2,2,256,768]{3,2,1,0:T(8,128)(2,1)S(1)}) fusion(f32[2,2,256,1536]{3,2,1,0:T(8,128)S(1)} %bitcast.29, f32[2,2,768]{2,1,0:T(2,128)S(1)} %get-tuple-element.10, f32[2,2,768]{2,1,0:T(2,128)S(1)} %get-tuple-element.9), kind=kLoop, calls=%fused_computation.8 | loop fusion | flops 6291456 | bytes 9461760 | tf_op jit(solution)/shard_map/convert.4
  31.6 0.0 copy-start
  31.6 0.2 pad_maximum_fusion.crossed_ref
  31.9 0.5 copy-done
  32.3 15.6 %shard_map.37 = f32[512,128]{1,0:T(8,128)S(1)} custom-call(s32[1]{0:T(128)} %constant.23.clone.1.own_ref, s32[4,1024]{1,0:T(4,128)S(1)} %copy-done, bf16[2,512,1536]{2,1,0:T(8,128)(2,1)S(1)} %pad_maximum_fusion.crossed_ref, f32[768,8]{1,0:T(8,128)S(1)} %get-tuple-element.12.wcos_ref, f32[768,8]{1,0:T(8,128)S(1)} %get-tuple-element.11.wsin_ref, ...), custom_call_target="tpu_custom_call" | custom-call | tf_op jit(solution)/shard_map/pallas_call | solution.py:135
  47.9 0.7 %copy.7 = f32[1,4,2,256]{3,2,1,0:T(2,128)} copy(f32[1,4,2,256]{1,3,2,0:T(8,128)S(1)} %bitcast.28) | data formatting | bytes 16384 | tf_op jit(solution)/shard_map/reshape | solution.py:210
  (17 shorter events, 0.2 us)
Async XLA Ops:
  0.0 7.8 %collective-permute-start = (bf16[1,16,1536]{2,1,0:T(8,128)(2,1)}, bf16[1,16,1536]{2,1,0:T(8,128)(2,1)S(1)}, u32[]{:S(2)}, u32[]{:S(2)}) collective-permute-start(bf16[1,16,1536]{2,1,0:T(8,128)(2,1)} %param.3), channel_id=1, source_target_pairs={{0,1},{1,0},{2,3},{3,2},{4,5},{5,4},{6,7},{7,6},{8,9},{9,8},{10,11... | collective-permute-start | bytes 147464 | tf_op jit(solution)/shard_map/ppermute | solution.py:165
  4.7 3.0 %copy-start.2 = (s32[2,256]{1,0:T(2,128)S(1)}, s32[2,256]{1,0:T(2,128)}, u32[]{:S(2)}) copy-start(s32[2,256]{1,0:T(2,128)} %param.4) | copy-start | bytes 6148
  6.3 17.0 %copy-start.1 = (bf16[1,16,1536]{2,1,0:T(8,128)(2,1)S(1)}, bf16[1,16,1536]{2,1,0:T(8,128)(2,1)}, u32[]{:S(2)}) copy-start(bf16[1,16,1536]{2,1,0:T(8,128)(2,1)} %param.3) | copy-start | bytes 147460
  7.8 8.2 %collective-permute-start.1 = (bf16[2,16,1536]{2,1,0:T(8,128)(2,1)S(1)}, bf16[2,16,1536]{2,1,0:T(8,128)(2,1)S(1)}, u32[]{:S(2)}, u32[]{:S(2)}) collective-permute-start(bf16[2,16,1536]{2,1,0:T(8,128)(2,1)S(1)} %constant_dynamic-update-slice_fusion), channel_id=1, source_target_pairs={{0,30},{2,28},{4,26},{6,24},{8,22},{10,20},{12,18},{14,16},{16,14}... | collective-permute-start | bytes 294920 | tf_op jit(solution)/shard_map/ppermute | solution.py:168
  16.1 7.2 %collective-permute-start.2 = (bf16[2,32,1536]{2,1,0:T(8,128)(2,1)S(1)}, bf16[2,32,1536]{2,1,0:T(8,128)(2,1)S(1)}, u32[]{:S(2)}, u32[]{:S(2)}) collective-permute-start(bf16[2,32,1536]{2,1,0:T(8,128)(2,1)S(1)} %pad_maximum_fusion.1), channel_id=1, source_target_pairs={{0,2},{2,4},{4,6},{6,8},{8,10},{10,12},{12,14},{14,16},{16,18},{18... | collective-permute-start | bytes 589832 | tf_op jit(solution)/shard_map/ppermute | solution.py:170
  21.2 7.0 %collective-permute-start.3 = (bf16[2,32,1536]{2,1,0:T(8,128)(2,1)S(1)}, bf16[2,32,1536]{2,1,0:T(8,128)(2,1)S(1)}, u32[]{:S(2)}, u32[]{:S(2)}) collective-permute-start(bf16[2,32,1536]{2,1,0:T(8,128)(2,1)S(1)} %pad_maximum_fusion.1), channel_id=1, source_target_pairs={{2,0},{4,2},{6,4},{8,6},{10,8},{12,10},{14,12},{16,14},{18,16},{20... | collective-permute-start | bytes 589832 | tf_op jit(solution)/shard_map/ppermute | solution.py:171
  31.6 0.7 %copy-start = (s32[4,1024]{1,0:T(4,128)S(1)}, s32[4,1024]{1,0:T(4,128)}, u32[]{:S(2)}) copy-start(s32[4,1024]{1,0:T(4,128)} %stretch_ref.1) | copy-start | bytes 49156

commit v14 on v13

--- a/solution.py
+++ b/solution.py
@@ -159,23 +159,23 @@
     block_rows = record.shape[1]
     minutes = lax.axis_size("tm")
     blocks = lax.axis_size("chan")
-    parts = [record]
+    mirrored = lax.ppermute(record, "chan", [(s, blocks - 1 - s) for s in range(blocks)])
+    pair = jnp.concatenate([record, mirrored], axis=1)
+    parts = [pair]
     for shift in range(1, minutes):
         parts.append(
-            lax.ppermute(record, "tm", [(i, (i + shift) % minutes) for i in range(minutes)])
+            lax.ppermute(pair, "tm", [(i, (i + shift) % minutes) for i in range(minutes)])
         )
-    own_block = jnp.concatenate(parts, axis=0)
-    mirrored = lax.ppermute(own_block, "chan", [(s, blocks - 1 - s) for s in range(blocks)])
-    bundle = jnp.concatenate([own_block, mirrored], axis=1)
+    bundle = jnp.concatenate(parts, axis=0)
     from_below = lax.ppermute(bundle, "chan", [(s, s + 1) for s in range(blocks - 1)])
     from_above = lax.ppermute(bundle, "chan", [(s, s - 1) for s in range(1, blocks)])
     candidates = jnp.concatenate(
         [
             from_below[:, :block_rows],
-            own_block,
+            bundle[:, :block_rows],
             from_above[:, :block_rows],
             from_above[:, block_rows:],
-            mirrored,
+            bundle[:, block_rows:],
             from_below[:, block_rows:],
         ],
         axis=1,

time: 49.3 us -> 48.2 us (0.978)
  starting transfers between devices: 12.8 us -> 11.8 us
    ppermute x1, starting transfers between devices: 3.46 us -> 2.71 us  [body(): lax.ppermute(bundle, 'chan', [(s, s + 1) for s in range(blocks - 1)])]
    unnamed x13 -> x8, local copies, waits for them, and re-layouts: 1.36 us -> 1.33 us
where the time goes in v14:
time: 48.2 us; the launch traced here: 47.9 us
  Pallas kernels  15.6 us (32%)
  starting transfers between devices  11.8 us (24%)
  waiting for transfers between devices  8.15 us (17%)
  other arithmetic  7.84 us (16%)
  matrix products  2.21 us (5%)
  local copies, waits for them, and re-layouts  2.1 us (4%)
    pallas_call x1, Pallas kernels, coherence(): pl.pallas_call(coherence_kernel, grid_spec=pltpu.PrefetchScalarGridSpec(n...  15.6 us
    ppermute x1, starting transfers between devices, body(): lax.ppermute(record, 'chan', [(s, blocks - 1 - s) for s in range(blocks)])  5.67 us
    ppermute x1, waiting for transfers between devices, body(): lax.ppermute(bundle, 'chan', [(s, s - 1) for s in range(1, blocks)])  4.84 us
    sin x3, other arithmetic, unit_angles(): return (jnp.cos(phase), jnp.sin(phase))  3.4 us
    ppermute x1, waiting for transfers between devices, body(): lax.ppermute(pair, 'tm', [(i, (i + shift) % minutes) for i in range(minut...  3.3 us
    ppermute x1, starting transfers between devices, body(): lax.ppermute(bundle, 'chan', [(s, s + 1) for s in range(blocks - 1)])  2.71 us
    another operation x2, other arithmetic  2.33 us
    ppermute x1, starting transfers between devices, body(): lax.ppermute(bundle, 'chan', [(s, s - 1) for s in range(1, blocks)])  2.1 us
  transfers between devices with their start and end apart: 4, of which 2 were waited for; matrix products, arithmetic and copies ran while one was open for 15% of the time, Pallas kernels for 0%

profile of v14, /device:TPU:1, one launch (start us, length us, event | category | flops | bytes accessed | tf_op | source)
XLA Modules:
  0.0 47.9 jit_solution(18349241363974258512)
XLA Ops:
  0.0 5.7 %collective-permute-start = (bf16[1,16,1536]{2,1,0:T(8,128)(2,1)}, bf16[1,16,1536]{2,1,0:T(8,128)(2,1)S(1)}, u32[]{:S(2)}, u32[]{:S(2)}) collective-permute-start(bf16[1,16,1536]{2,1,0:T(8,128)(2,1)} %param.3), channel_id=1, source_target_pairs={{0,30},{2,28},{4,26},{6,24},{8,22},{10,20},{12,18},{14,16},{16,14}... | collective-permute-start | bytes 147464 | tf_op jit(solution)/shard_map/ppermute | solution.py:162
  5.7 0.8 %constant_dynamic-update-slice_fusion.1 = bf16[1,32,1536]{2,1,0:T(8,128)(2,1)S(1)} fusion(bf16[1,16,1536]{2,1,0:T(8,128)(2,1)} %param.3), kind=kLoop, calls=%fused_computation.63 | loop fusion | bytes 98304
  6.5 1.6 %fusion.18 = (f32[128,768]{1,0:T(8,128)S(1)}, f32[128,768]{1,0:T(8,128)S(1)}) fusion(), kind=kLoop, calls=%fused_computation.33 | loop fusion | flops 884736 | bytes 786432 | tf_op jit(solution)/shard_map/sin | solution.py:19
  8.1 0.2 fusion.35
  8.3 0.0 copy-start.1
  8.3 1.6 %fusion.12 = (f32[768,128]{1,0:T(8,128)S(1)}, f32[768,128]{1,0:T(8,128)S(1)}) fusion(), kind=kLoop, calls=%fused_computation.23 | loop fusion | flops 884736 | bytes 786432 | tf_op jit(solution)/shard_map/sin | solution.py:19
  10.0 1.4 %subtract_convert_fusion = (bf16[12,128,768]{2,1,0:T(8,128)(2,1)S(1)}, bf16[12,128,768]{2,1,0:T(8,128)(2,1)S(1)}) fusion(f32[128,768]{1,0:T(8,128)S(1)} %get-tuple-element.15, f32[12,768]{1,0:T(8,128)S(1)} %get-tuple-element.17, f32[128,768]{1,0:T(8,128)S(1)} %get-tuple-element.16, f32[12,768]{1,0:T(8,128)S(1)} %get-tuple-element.18), kind=kLoop, calls=%fused_computation.5 | loop fusion | flops 10616832 | bytes 5578752 | tf_op jit(solution)/shard_map/convert.8
  11.4 0.0 copy-done.1
  11.4 0.0 collective-permute-done
  11.4 1.3 %collective-permute-start.1 = (bf16[1,32,1536]{2,1,0:T(8,128)(2,1)S(1)}, bf16[1,32,1536]{2,1,0:T(8,128)(2,1)S(1)}, u32[]{:S(2)}, u32[]{:S(2)}) collective-permute-start(bf16[1,32,1536]{2,1,0:T(8,128)(2,1)S(1)} %constant_dynamic-update-slice_fusion), channel_id=1, source_target_pairs={{0,1},{1,0},{2,3},{3,2},{4,5},{5,4},{6,7},{7,6},{8,9},{9,8},{10,11... | collective-permute-start | bytes 294920 | tf_op jit(solution)/shard_map/ppermute | solution.py:167
  12.7 3.3 %collective-permute-done.1 = bf16[1,32,1536]{2,1,0:T(8,128)(2,1)S(1)} collective-permute-done((bf16[1,32,1536]{2,1,0:T(8,128)(2,1)S(1)}, bf16[1,32,1536]{2,1,0:T(8,128)(2,1)S(1)}, u32[]{:S(2)}, u32[]{:S(2)}) %collective-permute-start.1) | collective-permute-done | bytes 98336 | tf_op jit(solution)/shard_map/ppermute | solution.py:167
  16.0 2.7 %collective-permute-start.2 = (bf16[2,32,1536]{2,1,0:T(8,128)(2,1)S(1)}, bf16[2,32,1536]{2,1,0:T(8,128)(2,1)S(1)}, u32[]{:S(2)}, u32[]{:S(2)}) collective-permute-start(bf16[2,32,1536]{2,1,0:T(8,128)(2,1)S(1)} %pad_maximum_fusion.1), channel_id=1, source_target_pairs={{0,2},{2,4},{4,6},{6,8},{8,10},{10,12},{12,14},{14,16},{16,18},{18... | collective-permute-start | bytes 589832 | tf_op jit(solution)/shard_map/ppermute | solution.py:170
  18.8 1.6 %sine_multiply_fusion = (f32[768,8]{1,0:T(8,128)S(1)}, f32[768,8]{1,0:T(8,128)S(1)}) fusion(f32[768]{0:T(1024)S(1)} %fusion.38, s32[8]{0:T(128)S(1)} %iota_add_fusion), kind=kLoop, calls=%fused_computation.25 | loop fusion | flops 67584 | bytes 52256 | tf_op jit(solution)/shard_map/mul | solution.py:40
  20.4 2.1 %collective-permute-start.3 = (bf16[2,32,1536]{2,1,0:T(8,128)(2,1)S(1)}, bf16[2,32,1536]{2,1,0:T(8,128)(2,1)S(1)}, u32[]{:S(2)}, u32[]{:S(2)}) collective-permute-start(bf16[2,32,1536]{2,1,0:T(8,128)(2,1)S(1)} %pad_maximum_fusion.1), channel_id=1, source_target_pairs={{2,0},{4,2},{6,4},{8,6},{10,8},{12,10},{14,12},{16,14},{18,16},{20... | collective-permute-start | bytes 589832 | tf_op jit(solution)/shard_map/ppermute | solution.py:171
  22.5 0.0 collective-permute-done.2
  22.6 4.8 %collective-permute-done.3 = bf16[2,32,1536]{2,1,0:T(8,128)(2,1)S(1)} collective-permute-done((bf16[2,32,1536]{2,1,0:T(8,128)(2,1)S(1)}, bf16[2,32,1536]{2,1,0:T(8,128)(2,1)S(1)}, u32[]{:S(2)}, u32[]{:S(2)}) %collective-permute-start.3) | collective-permute-done | bytes 196640 | tf_op jit(solution)/shard_map/ppermute | solution.py:171
  27.4 1.2 %multiply_reduce_fusion = (f32[192]{0:T(256)S(1)}, f32[192,1536]{1,0:T(8,128)S(1)}) fusion(bf16[192,1536]{1,0:T(8,128)(2,1)S(1)} %bitcast.36, bf16[1536,768]{1,0:T(8,128)(2,1)S(1)} %bitcast.35, bf16[1536,768]{1,0:T(8,128)(2,1)S(1)} %bitcast.34), kind=kOutput, calls=%fused_computation.10 | convolution fusion | flops 915996480 | bytes 6488832 | tf_op jit(solution)/shard_map/dot_general | solution.py:184
  28.6 0.2 divide_convert_fusion
  28.8 1.0 %fusion.24 = f32[2,1536,512]{1,2,0:T(8,128)S(1)} fusion(bf16[2,96,1536]{2,1,0:T(8,128)(2,1)S(1)} %bitcast.33, s32[512]{0:T(512)S(1)} %bitcast.37), kind=kOutput, calls=%fused_computation.45 | convolution fusion | flops 302039040 | bytes 6883328 | tf_op jit(solution)/shard_map/pq,mqk->mpk/dot_general | solution.py:202
  29.9 0.9 %add_convert_fusion = (bf16[2,2,256,768]{3,2,1,0:T(8,128)(2,1)S(1)}, bf16[2,2,256,768]{3,2,1,0:T(8,128)(2,1)S(1)}) fusion(f32[2,2,256,1536]{3,2,1,0:T(8,128)S(1)} %bitcast.29, f32[2,2,768]{2,1,0:T(2,128)S(1)} %get-tuple-element.10, f32[2,2,768]{2,1,0:T(2,128)S(1)} %get-tuple-element.9), kind=kLoop, calls=%fused_computation.8 | loop fusion | flops 6291456 | bytes 9461760 | tf_op jit(solution)/shard_map/convert.4
  30.8 0.0 copy-start
  30.8 0.2 pad_maximum_fusion.crossed_ref
  31.1 0.5 copy-done
  31.6 15.6 %shard_map.37 = f32[512,128]{1,0:T(8,128)S(1)} custom-call(s32[1]{0:T(128)} %constant.23.clone.1.own_ref, s32[4,1024]{1,0:T(4,128)S(1)} %copy-done, bf16[2,512,1536]{2,1,0:T(8,128)(2,1)S(1)} %pad_maximum_fusion.crossed_ref, f32[768,8]{1,0:T(8,128)S(1)} %get-tuple-element.12.wcos_ref, f32[768,8]{1,0:T(8,128)S(1)} %get-tuple-element.11.wsin_ref, ...), custom_call_target="tpu_custom_call" | custom-call | tf_op jit(solution)/shard_map/pallas_call | solution.py:135
  47.2 0.7 %copy.7 = f32[1,4,2,256]{3,2,1,0:T(2,128)} copy(f32[1,4,2,256]{1,3,2,0:T(8,128)S(1)} %bitcast.28) | data formatting | bytes 16384 | tf_op jit(solution)/shard_map/reshape | solution.py:210
  (16 shorter events, 0.2 us)
Async XLA Ops:
  0.0 11.4 %collective-permute-start = (bf16[1,16,1536]{2,1,0:T(8,128)(2,1)}, bf16[1,16,1536]{2,1,0:T(8,128)(2,1)S(1)}, u32[]{:S(2)}, u32[]{:S(2)}) collective-permute-start(bf16[1,16,1536]{2,1,0:T(8,128)(2,1)} %param.3), channel_id=1, source_target_pairs={{0,30},{2,28},{4,26},{6,24},{8,22},{10,20},{12,18},{14,16},{16,14}... | collective-permute-start | bytes 147464 | tf_op jit(solution)/shard_map/ppermute | solution.py:162
  8.3 3.0 %copy-start.1 = (s32[2,256]{1,0:T(2,128)S(1)}, s32[2,256]{1,0:T(2,128)}, u32[]{:S(2)}) copy-start(s32[2,256]{1,0:T(2,128)} %param.4) | copy-start | bytes 6148
  11.4 4.6 %collective-permute-start.1 = (bf16[1,32,1536]{2,1,0:T(8,128)(2,1)S(1)}, bf16[1,32,1536]{2,1,0:T(8,128)(2,1)S(1)}, u32[]{:S(2)}, u32[]{:S(2)}) collective-permute-start(bf16[1,32,1536]{2,1,0:T(8,128)(2,1)S(1)} %constant_dynamic-update-slice_fusion), channel_id=1, source_target_pairs={{0,1},{1,0},{2,3},{3,2},{4,5},{5,4},{6,7},{7,6},{8,9},{9,8},{10,11... | collective-permute-start | bytes 294920 | tf_op jit(solution)/shard_map/ppermute | solution.py:167
  16.0 6.5 %collective-permute-start.2 = (bf16[2,32,1536]{2,1,0:T(8,128)(2,1)S(1)}, bf16[2,32,1536]{2,1,0:T(8,128)(2,1)S(1)}, u32[]{:S(2)}, u32[]{:S(2)}) collective-permute-start(bf16[2,32,1536]{2,1,0:T(8,128)(2,1)S(1)} %pad_maximum_fusion.1), channel_id=1, source_target_pairs={{0,2},{2,4},{4,6},{6,8},{8,10},{10,12},{12,14},{14,16},{16,18},{18... | collective-permute-start | bytes 589832 | tf_op jit(solution)/shard_map/ppermute | solution.py:170
  20.4 7.0 %collective-permute-start.3 = (bf16[2,32,1536]{2,1,0:T(8,128)(2,1)S(1)}, bf16[2,32,1536]{2,1,0:T(8,128)(2,1)S(1)}, u32[]{:S(2)}, u32[]{:S(2)}) collective-permute-start(bf16[2,32,1536]{2,1,0:T(8,128)(2,1)S(1)} %pad_maximum_fusion.1), channel_id=1, source_target_pairs={{2,0},{4,2},{6,4},{8,6},{10,8},{12,10},{14,12},{16,14},{18,16},{20... | collective-permute-start | bytes 589832 | tf_op jit(solution)/shard_map/ppermute | solution.py:171
  30.8 0.7 %copy-start = (s32[4,1024]{1,0:T(4,128)S(1)}, s32[4,1024]{1,0:T(4,128)}, u32[]{:S(2)}) copy-start(s32[4,1024]{1,0:T(4,128)} %stretch_ref.1) | copy-start | bytes 49156

commit v15 on v14

--- a/solution.py
+++ b/solution.py
@@ -63,7 +63,7 @@
 
 def coherence_kernel(
     own_ref, stretch_ref, crossed_ref, wcos_ref, wsin_ref, fcos_ref, fsin_ref,
-    out_ref, picks_ref, inverse_ref,
+    out_ref, inverse_ref,
 ):
     minutes = crossed_ref.shape[0]
     moves = stretch_ref.shape[0] - 1
@@ -85,14 +85,6 @@
                 jnp.bfloat16
             )
 
-    @pl.when(pl.program_id(0) == 0)
-    def _():
-        rows = lax.broadcasted_iota(jnp.int32, (LAGS, LAGS), 0)
-        for move in range(moves):
-            picks_ref[:, move * LAGS:(move + 1) * LAGS] = (
-                rows == stretch_ref[move + 1:move + 2, :]
-            ).astype(jnp.bfloat16)
-
     inverse = inverse_ref[...]
     own = own_ref[0]
     stacked = None
@@ -107,10 +99,13 @@
     high = stacked.astype(jnp.bfloat16)
     low = (stacked - high.astype(jnp.float32)).astype(jnp.bfloat16)
     rows = stacked.shape[0]
-    moved = jnp.dot(
-        jnp.concatenate([high, low], axis=0), picks_ref[...], preferred_element_type=jnp.float32
-    )
-    moved = moved[:rows] + moved[rows:]
+    parts = jnp.concatenate([high, low], axis=0)
+    lag_rows = lax.broadcasted_iota(jnp.int32, (LAGS, LAGS), 0)
+    moved = []
+    for move in range(moves):
+        picks = (lag_rows == stretch_ref[move + 1:move + 2, :]).astype(jnp.bfloat16)
+        product = jnp.dot(parts, picks, preferred_element_type=jnp.float32)
+        moved.append(product[:rows] + product[rows:])
     scale = 1.0 / LAGS
     current_power = jnp.sum(current * current, axis=1, keepdims=True) * scale
     lanes = lax.broadcasted_iota(jnp.int32, out_ref.shape, 1)
@@ -119,7 +114,7 @@
         if stretch == 0:
             shifted = stacked
         else:
-            shifted = moved[:, (stretch - 1) * LAGS:stretch * LAGS]
+            shifted = moved[stretch - 1]
         numerator = jnp.sum(current * shifted, axis=1, keepdims=True) * scale
         shifted_power = jnp.sum(shifted * shifted, axis=1, keepdims=True) * scale
         value = numerator / jnp.sqrt((current_power + epsilon) * (shifted_power + epsilon))
@@ -143,7 +138,6 @@
             ] + [pl.BlockSpec(factor.shape, lambda i, own: (0, 0)) for factor in factors],
             out_specs=pl.BlockSpec((block, 128), lambda i, own: (i, 0)),
             scratch_shapes=[
-                pltpu.VMEM((LAGS, (stretch_count - 1) * LAGS), jnp.bfloat16),
                 pltpu.VMEM((width, LAGS), jnp.bfloat16),
             ],
         ),

time: 48.2 us -> 45.4 us (0.942)
  Pallas kernels: 15.6 us -> 12.9 us
    pallas_call x1, Pallas kernels: 15.6 us -> 12.9 us  [coherence(): pl.pallas_call(coherence_kernel, grid_spec=pltpu.PrefetchScalarGridSpec(n...]
  transfers between devices with their start and end apart: 4 -> 4, of which waited for: 2 -> 2; matrix products, arithmetic and copies ran while one was open for 15% -> 16% of each run, Pallas kernels for 0% -> 0%
where the time goes in v15:
time: 45.4 us; the launch traced here: 45.2 us
  Pallas kernels  12.9 us (28%)
  starting transfers between devices  11.8 us (26%)
  waiting for transfers between devices  8.15 us (18%)
  other arithmetic  7.84 us (17%)
  matrix products  2.21 us (5%)
  local copies, waits for them, and re-layouts  2.1 us (5%)
    pallas_call x1, Pallas kernels, coherence(): pl.pallas_call(coherence_kernel, grid_spec=pltpu.PrefetchScalarGridSpec(n...  12.9 us
    ppermute x1, starting transfers between devices, body(): lax.ppermute(record, 'chan', [(s, blocks - 1 - s) for s in range(blocks)])  5.67 us
    ppermute x1, waiting for transfers between devices, body(): lax.ppermute(bundle, 'chan', [(s, s - 1) for s in range(1, blocks)])  4.84 us
    sin x3, other arithmetic, unit_angles(): return (jnp.cos(phase), jnp.sin(phase))  3.4 us
    ppermute x1, waiting for transfers between devices, body(): lax.ppermute(pair, 'tm', [(i, (i + shift) % minutes) for i in range(minut...  3.3 us
    ppermute x1, starting transfers between devices, body(): lax.ppermute(bundle, 'chan', [(s, s + 1) for s in range(blocks - 1)])  2.71 us
    another operation x2, other arithmetic  2.33 us
    ppermute x1, starting transfers between devices, body(): lax.ppermute(bundle, 'chan', [(s, s - 1) for s in range(1, blocks)])  2.1 us
  transfers between devices with their start and end apart: 4, of which 2 were waited for; matrix products, arithmetic and copies ran while one was open for 16% of the time, Pallas kernels for 0%

profile of v15, /device:TPU:1, one launch (start us, length us, event | category | flops | bytes accessed | tf_op | source)
XLA Modules:
  0.0 45.2 jit_solution(5276652086631192296)
XLA Ops:
  0.0 5.7 %collective-permute-start = (bf16[1,16,1536]{2,1,0:T(8,128)(2,1)}, bf16[1,16,1536]{2,1,0:T(8,128)(2,1)S(1)}, u32[]{:S(2)}, u32[]{:S(2)}) collective-permute-start(bf16[1,16,1536]{2,1,0:T(8,128)(2,1)} %param.3), channel_id=1, source_target_pairs={{0,30},{2,28},{4,26},{6,24},{8,22},{10,20},{12,18},{14,16},{16,14}... | collective-permute-start | bytes 147464 | tf_op jit(solution)/shard_map/ppermute | solution.py:156
  5.7 0.8 %constant_dynamic-update-slice_fusion.1 = bf16[1,32,1536]{2,1,0:T(8,128)(2,1)S(1)} fusion(bf16[1,16,1536]{2,1,0:T(8,128)(2,1)} %param.3), kind=kLoop, calls=%fused_computation.63 | loop fusion | bytes 98304
  6.5 1.6 %fusion.18 = (f32[128,768]{1,0:T(8,128)S(1)}, f32[128,768]{1,0:T(8,128)S(1)}) fusion(), kind=kLoop, calls=%fused_computation.33 | loop fusion | flops 884736 | bytes 786432 | tf_op jit(solution)/shard_map/sin | solution.py:19
  8.1 0.2 fusion.35
  8.3 0.0 copy-start.1
  8.3 1.6 %fusion.12 = (f32[768,128]{1,0:T(8,128)S(1)}, f32[768,128]{1,0:T(8,128)S(1)}) fusion(), kind=kLoop, calls=%fused_computation.23 | loop fusion | flops 884736 | bytes 786432 | tf_op jit(solution)/shard_map/sin | solution.py:19
  10.0 1.4 %subtract_convert_fusion = (bf16[12,128,768]{2,1,0:T(8,128)(2,1)S(1)}, bf16[12,128,768]{2,1,0:T(8,128)(2,1)S(1)}) fusion(f32[128,768]{1,0:T(8,128)S(1)} %get-tuple-element.15, f32[12,768]{1,0:T(8,128)S(1)} %get-tuple-element.17, f32[128,768]{1,0:T(8,128)S(1)} %get-tuple-element.16, f32[12,768]{1,0:T(8,128)S(1)} %get-tuple-element.18), kind=kLoop, calls=%fused_computation.5 | loop fusion | flops 10616832 | bytes 5578752 | tf_op jit(solution)/shard_map/convert.8
  11.4 0.0 copy-done.1
  11.4 0.0 collective-permute-done
  11.4 1.3 %collective-permute-start.1 = (bf16[1,32,1536]{2,1,0:T(8,128)(2,1)S(1)}, bf16[1,32,1536]{2,1,0:T(8,128)(2,1)S(1)}, u32[]{:S(2)}, u32[]{:S(2)}) collective-permute-start(bf16[1,32,1536]{2,1,0:T(8,128)(2,1)S(1)} %constant_dynamic-update-slice_fusion), channel_id=1, source_target_pairs={{0,1},{1,0},{2,3},{3,2},{4,5},{5,4},{6,7},{7,6},{8,9},{9,8},{10,11... | collective-permute-start | bytes 294920 | tf_op jit(solution)/shard_map/ppermute | solution.py:161
  12.7 3.3 %collective-permute-done.1 = bf16[1,32,1536]{2,1,0:T(8,128)(2,1)S(1)} collective-permute-done((bf16[1,32,1536]{2,1,0:T(8,128)(2,1)S(1)}, bf16[1,32,1536]{2,1,0:T(8,128)(2,1)S(1)}, u32[]{:S(2)}, u32[]{:S(2)}) %collective-permute-start.1) | collective-permute-done | bytes 98336 | tf_op jit(solution)/shard_map/ppermute | solution.py:161
  16.0 2.7 %collective-permute-start.2 = (bf16[2,32,1536]{2,1,0:T(8,128)(2,1)S(1)}, bf16[2,32,1536]{2,1,0:T(8,128)(2,1)S(1)}, u32[]{:S(2)}, u32[]{:S(2)}) collective-permute-start(bf16[2,32,1536]{2,1,0:T(8,128)(2,1)S(1)} %pad_maximum_fusion.1), channel_id=1, source_target_pairs={{0,2},{2,4},{4,6},{6,8},{8,10},{10,12},{12,14},{14,16},{16,18},{18... | collective-permute-start | bytes 589832 | tf_op jit(solution)/shard_map/ppermute | solution.py:164
  18.8 1.6 %sine_multiply_fusion = (f32[768,8]{1,0:T(8,128)S(1)}, f32[768,8]{1,0:T(8,128)S(1)}) fusion(f32[768]{0:T(1024)S(1)} %fusion.38, s32[8]{0:T(128)S(1)} %iota_add_fusion), kind=kLoop, calls=%fused_computation.25 | loop fusion | flops 67584 | bytes 52256 | tf_op jit(solution)/shard_map/mul | solution.py:40
  20.4 2.1 %collective-permute-start.3 = (bf16[2,32,1536]{2,1,0:T(8,128)(2,1)S(1)}, bf16[2,32,1536]{2,1,0:T(8,128)(2,1)S(1)}, u32[]{:S(2)}, u32[]{:S(2)}) collective-permute-start(bf16[2,32,1536]{2,1,0:T(8,128)(2,1)S(1)} %pad_maximum_fusion.1), channel_id=1, source_target_pairs={{2,0},{4,2},{6,4},{8,6},{10,8},{12,10},{14,12},{16,14},{18,16},{20... | collective-permute-start | bytes 589832 | tf_op jit(solution)/shard_map/ppermute | solution.py:165
  22.5 0.0 collective-permute-done.2
  22.6 4.8 %collective-permute-done.3 = bf16[2,32,1536]{2,1,0:T(8,128)(2,1)S(1)} collective-permute-done((bf16[2,32,1536]{2,1,0:T(8,128)(2,1)S(1)}, bf16[2,32,1536]{2,1,0:T(8,128)(2,1)S(1)}, u32[]{:S(2)}, u32[]{:S(2)}) %collective-permute-start.3) | collective-permute-done | bytes 196640 | tf_op jit(solution)/shard_map/ppermute | solution.py:165
  27.4 1.2 %multiply_reduce_fusion = (f32[192]{0:T(256)S(1)}, f32[192,1536]{1,0:T(8,128)S(1)}) fusion(bf16[192,1536]{1,0:T(8,128)(2,1)S(1)} %bitcast.36, bf16[1536,768]{1,0:T(8,128)(2,1)S(1)} %bitcast.35, bf16[1536,768]{1,0:T(8,128)(2,1)S(1)} %bitcast.34), kind=kOutput, calls=%fused_computation.10 | convolution fusion | flops 915996480 | bytes 6488832 | tf_op jit(solution)/shard_map/dot_general | solution.py:178
  28.6 0.2 divide_convert_fusion
  28.8 1.0 %fusion.24 = f32[2,1536,512]{1,2,0:T(8,128)S(1)} fusion(bf16[2,96,1536]{2,1,0:T(8,128)(2,1)S(1)} %bitcast.33, s32[512]{0:T(512)S(1)} %bitcast.37), kind=kOutput, calls=%fused_computation.45 | convolution fusion | flops 302039040 | bytes 6883328 | tf_op jit(solution)/shard_map/pq,mqk->mpk/dot_general | solution.py:196
  29.9 0.9 %add_convert_fusion = (bf16[2,2,256,768]{3,2,1,0:T(8,128)(2,1)S(1)}, bf16[2,2,256,768]{3,2,1,0:T(8,128)(2,1)S(1)}) fusion(f32[2,2,256,1536]{3,2,1,0:T(8,128)S(1)} %bitcast.29, f32[2,2,768]{2,1,0:T(2,128)S(1)} %get-tuple-element.10, f32[2,2,768]{2,1,0:T(2,128)S(1)} %get-tuple-element.9), kind=kLoop, calls=%fused_computation.8 | loop fusion | flops 6291456 | bytes 9461760 | tf_op jit(solution)/shard_map/convert.4
  30.8 0.0 copy-start
  30.8 0.2 pad_maximum_fusion.crossed_ref
  31.1 0.5 %copy-done = s32[4,1024]{1,0:T(4,128)S(1)} copy-done((s32[4,1024]{1,0:T(4,128)S(1)}, s32[4,1024]{1,0:T(4,128)}, u32[]{:S(2)}) %copy-start) | copy-done | bytes 16408
  31.6 12.9 %shard_map.37 = f32[512,128]{1,0:T(8,128)S(1)} custom-call(s32[1]{0:T(128)} %constant.23.clone.1.own_ref, s32[4,1024]{1,0:T(4,128)S(1)} %copy-done, bf16[2,512,1536]{2,1,0:T(8,128)(2,1)S(1)} %pad_maximum_fusion.crossed_ref, f32[768,8]{1,0:T(8,128)S(1)} %get-tuple-element.12.wcos_ref, f32[768,8]{1,0:T(8,128)S(1)} %get-tuple-element.11.wsin_ref, ...), custom_call_target="tpu_custom_call" | custom-call | tf_op jit(solution)/shard_map/pallas_call | solution.py:130
  44.5 0.7 %copy.7 = f32[1,4,2,256]{3,2,1,0:T(2,128)} copy(f32[1,4,2,256]{1,3,2,0:T(8,128)S(1)} %bitcast.28) | data formatting | bytes 16384 | tf_op jit(solution)/shard_map/reshape | solution.py:204
  (16 shorter events, 0.2 us)
Async XLA Ops:
  0.0 11.4 %collective-permute-start = (bf16[1,16,1536]{2,1,0:T(8,128)(2,1)}, bf16[1,16,1536]{2,1,0:T(8,128)(2,1)S(1)}, u32[]{:S(2)}, u32[]{:S(2)}) collective-permute-start(bf16[1,16,1536]{2,1,0:T(8,128)(2,1)} %param.3), channel_id=1, source_target_pairs={{0,30},{2,28},{4,26},{6,24},{8,22},{10,20},{12,18},{14,16},{16,14}... | collective-permute-start | bytes 147464 | tf_op jit(solution)/shard_map/ppermute | solution.py:156
  8.3 3.0 %copy-start.1 = (s32[2,256]{1,0:T(2,128)S(1)}, s32[2,256]{1,0:T(2,128)}, u32[]{:S(2)}) copy-start(s32[2,256]{1,0:T(2,128)} %param.4) | copy-start | bytes 6148
  11.4 4.6 %collective-permute-start.1 = (bf16[1,32,1536]{2,1,0:T(8,128)(2,1)S(1)}, bf16[1,32,1536]{2,1,0:T(8,128)(2,1)S(1)}, u32[]{:S(2)}, u32[]{:S(2)}) collective-permute-start(bf16[1,32,1536]{2,1,0:T(8,128)(2,1)S(1)} %constant_dynamic-update-slice_fusion), channel_id=1, source_target_pairs={{0,1},{1,0},{2,3},{3,2},{4,5},{5,4},{6,7},{7,6},{8,9},{9,8},{10,11... | collective-permute-start | bytes 294920 | tf_op jit(solution)/shard_map/ppermute | solution.py:161
  16.0 6.5 %collective-permute-start.2 = (bf16[2,32,1536]{2,1,0:T(8,128)(2,1)S(1)}, bf16[2,32,1536]{2,1,0:T(8,128)(2,1)S(1)}, u32[]{:S(2)}, u32[]{:S(2)}) collective-permute-start(bf16[2,32,1536]{2,1,0:T(8,128)(2,1)S(1)} %pad_maximum_fusion.1), channel_id=1, source_target_pairs={{0,2},{2,4},{4,6},{6,8},{8,10},{10,12},{12,14},{14,16},{16,18},{18... | collective-permute-start | bytes 589832 | tf_op jit(solution)/shard_map/ppermute | solution.py:164
  20.4 7.0 %collective-permute-start.3 = (bf16[2,32,1536]{2,1,0:T(8,128)(2,1)S(1)}, bf16[2,32,1536]{2,1,0:T(8,128)(2,1)S(1)}, u32[]{:S(2)}, u32[]{:S(2)}) collective-permute-start(bf16[2,32,1536]{2,1,0:T(8,128)(2,1)S(1)} %pad_maximum_fusion.1), channel_id=1, source_target_pairs={{2,0},{4,2},{6,4},{8,6},{10,8},{12,10},{14,12},{16,14},{18,16},{20... | collective-permute-start | bytes 589832 | tf_op jit(solution)/shard_map/ppermute | solution.py:165
  30.8 0.7 %copy-start = (s32[4,1024]{1,0:T(4,128)S(1)}, s32[4,1024]{1,0:T(4,128)}, u32[]{:S(2)}) copy-start(s32[4,1024]{1,0:T(4,128)} %stretch_ref.1) | copy-start | bytes 49156

commit v16 on v15

--- a/solution.py
+++ b/solution.py
@@ -63,34 +63,40 @@
 
 def coherence_kernel(
     own_ref, stretch_ref, crossed_ref, wcos_ref, wsin_ref, fcos_ref, fsin_ref,
-    out_ref, inverse_ref,
+    out_ref,
 ):
     minutes = crossed_ref.shape[0]
     moves = stretch_ref.shape[0] - 1
     groups = wcos_ref.shape[1]
     fine = fcos_ref.shape[1]
 
-    @pl.when(pl.program_id(0) == 0)
-    def _():
-        fine_cos = fcos_ref[...]
-        fine_sin = fsin_ref[...]
-        for group in range(groups):
+    fine_cos = fcos_ref[...]
+    fine_sin = fsin_ref[...]
+    own = own_ref[0]
+    pieces = [[] for _ in range(minutes)]
+    for pair_group in range(groups // 2):
+        columns = []
+        for group in (2 * pair_group, 2 * pair_group + 1):
             coarse_cos = wcos_ref[:, group:group + 1]
             coarse_sin = wsin_ref[:, group:group + 1]
-            lags = slice(group * fine, (group + 1) * fine)
-            inverse_ref[:NF, lags] = (coarse_cos * fine_cos - coarse_sin * fine_sin).astype(
-                jnp.bfloat16
+            columns.append(
+                jnp.concatenate(
+                    [
+                        coarse_cos * fine_cos - coarse_sin * fine_sin,
+                        -(coarse_sin * fine_cos + coarse_cos * fine_sin),
+                    ],
+                    axis=0,
+                ).astype(jnp.bfloat16)
             )
-            inverse_ref[NF:, lags] = (-(coarse_sin * fine_cos + coarse_cos * fine_sin)).astype(
-                jnp.bfloat16
+        inverse = jnp.concatenate(columns, axis=1)
+        for minute in range(minutes):
+            pieces[minute].append(
+                jnp.dot(crossed_ref[minute], inverse, preferred_element_type=jnp.float32)
             )
-
-    inverse = inverse_ref[...]
-    own = own_ref[0]
     stacked = None
     current = None
     for minute in range(minutes):
-        correlation = jnp.dot(crossed_ref[minute], inverse, preferred_element_type=jnp.float32)
+        correlation = jnp.concatenate(pieces[minute], axis=1)
         if stacked is None:
             stacked, current = correlation, correlation
         else:
@@ -137,9 +143,6 @@
                 pl.BlockSpec((minutes, block, width), lambda i, own: (0, i, 0)),
             ] + [pl.BlockSpec(factor.shape, lambda i, own: (0, 0)) for factor in factors],
             out_specs=pl.BlockSpec((block, 128), lambda i, own: (i, 0)),
-            scratch_shapes=[
-                pltpu.VMEM((width, LAGS), jnp.bfloat16),
-            ],
         ),
         out_shape=jax.ShapeDtypeStruct((pair_count, 128), jnp.float32),
         compiler_params=pltpu.CompilerParams(

time: 45.4 us -> 45.8 us (level)
  no operation moved by 1% of the time
where the time goes in v16:
time: 45.8 us; the launch traced here: 45.6 us
  Pallas kernels  13.3 us (29%)
  starting transfers between devices  11.8 us (26%)
  waiting for transfers between devices  8.15 us (18%)
  other arithmetic  7.84 us (17%)
  matrix products  2.21 us (5%)
  local copies, waits for them, and re-layouts  2.1 us (5%)
    pallas_call x1, Pallas kernels, coherence(): pl.pallas_call(coherence_kernel, grid_spec=pltpu.PrefetchScalarGridSpec(n...  13.3 us
    ppermute x1, starting transfers between devices, body(): lax.ppermute(record, 'chan', [(s, blocks - 1 - s) for s in range(blocks)])  5.67 us
    ppermute x1, waiting for transfers between devices, body(): lax.ppermute(bundle, 'chan', [(s, s - 1) for s in range(1, blocks)])  4.84 us
    sin x3, other arithmetic, unit_angles(): return (jnp.cos(phase), jnp.sin(phase))  3.4 us
    ppermute x1, waiting for transfers between devices, body(): lax.ppermute(pair, 'tm', [(i, (i + shift) % minutes) for i in range(minut...  3.3 us
    ppermute x1, starting transfers between devices, body(): lax.ppermute(bundle, 'chan', [(s, s + 1) for s in range(blocks - 1)])  2.71 us
    another operation x2, other arithmetic  2.33 us
    ppermute x1, starting transfers between devices, body(): lax.ppermute(bundle, 'chan', [(s, s - 1) for s in range(1, blocks)])  2.1 us
  transfers between devices with their start and end apart: 4, of which 2 were waited for; matrix products, arithmetic and copies ran while one was open for 16% of the time, Pallas kernels for 0%

profile of v16, /device:TPU:1, one launch (start us, length us, event | category | flops | bytes accessed | tf_op | source)
XLA Modules:
  0.0 45.6 jit_solution(11766422197836064153)
XLA Ops:
  0.0 5.7 %collective-permute-start = (bf16[1,16,1536]{2,1,0:T(8,128)(2,1)}, bf16[1,16,1536]{2,1,0:T(8,128)(2,1)S(1)}, u32[]{:S(2)}, u32[]{:S(2)}) collective-permute-start(bf16[1,16,1536]{2,1,0:T(8,128)(2,1)} %param.3), channel_id=1, source_target_pairs={{0,30},{2,28},{4,26},{6,24},{8,22},{10,20},{12,18},{14,16},{16,14}... | collective-permute-start | bytes 147464 | tf_op jit(solution)/shard_map/ppermute | solution.py:159
  5.7 0.8 %constant_dynamic-update-slice_fusion.1 = bf16[1,32,1536]{2,1,0:T(8,128)(2,1)S(1)} fusion(bf16[1,16,1536]{2,1,0:T(8,128)(2,1)} %param.3), kind=kLoop, calls=%fused_computation.63 | loop fusion | bytes 98304
  6.5 1.6 %fusion.18 = (f32[128,768]{1,0:T(8,128)S(1)}, f32[128,768]{1,0:T(8,128)S(1)}) fusion(), kind=kLoop, calls=%fused_computation.33 | loop fusion | flops 884736 | bytes 786432 | tf_op jit(solution)/shard_map/sin | solution.py:19
  8.1 0.2 fusion.35
  8.3 0.0 copy-start.1
  8.3 1.6 %fusion.12 = (f32[768,128]{1,0:T(8,128)S(1)}, f32[768,128]{1,0:T(8,128)S(1)}) fusion(), kind=kLoop, calls=%fused_computation.23 | loop fusion | flops 884736 | bytes 786432 | tf_op jit(solution)/shard_map/sin | solution.py:19
  10.0 1.4 %subtract_convert_fusion = (bf16[12,128,768]{2,1,0:T(8,128)(2,1)S(1)}, bf16[12,128,768]{2,1,0:T(8,128)(2,1)S(1)}) fusion(f32[128,768]{1,0:T(8,128)S(1)} %get-tuple-element.15, f32[12,768]{1,0:T(8,128)S(1)} %get-tuple-element.17, f32[128,768]{1,0:T(8,128)S(1)} %get-tuple-element.16, f32[12,768]{1,0:T(8,128)S(1)} %get-tuple-element.18), kind=kLoop, calls=%fused_computation.5 | loop fusion | flops 10616832 | bytes 5578752 | tf_op jit(solution)/shard_map/convert.8
  11.4 0.0 copy-done.1
  11.4 0.0 collective-permute-done
  11.4 1.3 %collective-permute-start.1 = (bf16[1,32,1536]{2,1,0:T(8,128)(2,1)S(1)}, bf16[1,32,1536]{2,1,0:T(8,128)(2,1)S(1)}, u32[]{:S(2)}, u32[]{:S(2)}) collective-permute-start(bf16[1,32,1536]{2,1,0:T(8,128)(2,1)S(1)} %constant_dynamic-update-slice_fusion), channel_id=1, source_target_pairs={{0,1},{1,0},{2,3},{3,2},{4,5},{5,4},{6,7},{7,6},{8,9},{9,8},{10,11... | collective-permute-start | bytes 294920 | tf_op jit(solution)/shard_map/ppermute | solution.py:164
  12.7 3.3 %collective-permute-done.1 = bf16[1,32,1536]{2,1,0:T(8,128)(2,1)S(1)} collective-permute-done((bf16[1,32,1536]{2,1,0:T(8,128)(2,1)S(1)}, bf16[1,32,1536]{2,1,0:T(8,128)(2,1)S(1)}, u32[]{:S(2)}, u32[]{:S(2)}) %collective-permute-start.1) | collective-permute-done | bytes 98336 | tf_op jit(solution)/shard_map/ppermute | solution.py:164
  16.0 2.7 %collective-permute-start.2 = (bf16[2,32,1536]{2,1,0:T(8,128)(2,1)S(1)}, bf16[2,32,1536]{2,1,0:T(8,128)(2,1)S(1)}, u32[]{:S(2)}, u32[]{:S(2)}) collective-permute-start(bf16[2,32,1536]{2,1,0:T(8,128)(2,1)S(1)} %pad_maximum_fusion.1), channel_id=1, source_target_pairs={{0,2},{2,4},{4,6},{6,8},{8,10},{10,12},{12,14},{14,16},{16,18},{18... | collective-permute-start | bytes 589832 | tf_op jit(solution)/shard_map/ppermute | solution.py:167
  18.8 1.6 %sine_multiply_fusion = (f32[768,8]{1,0:T(8,128)S(1)}, f32[768,8]{1,0:T(8,128)S(1)}) fusion(f32[768]{0:T(1024)S(1)} %fusion.38, s32[8]{0:T(128)S(1)} %iota_add_fusion), kind=kLoop, calls=%fused_computation.25 | loop fusion | flops 67584 | bytes 52256 | tf_op jit(solution)/shard_map/mul | solution.py:40
  20.4 2.1 %collective-permute-start.3 = (bf16[2,32,1536]{2,1,0:T(8,128)(2,1)S(1)}, bf16[2,32,1536]{2,1,0:T(8,128)(2,1)S(1)}, u32[]{:S(2)}, u32[]{:S(2)}) collective-permute-start(bf16[2,32,1536]{2,1,0:T(8,128)(2,1)S(1)} %pad_maximum_fusion.1), channel_id=1, source_target_pairs={{2,0},{4,2},{6,4},{8,6},{10,8},{12,10},{14,12},{16,14},{18,16},{20... | collective-permute-start | bytes 589832 | tf_op jit(solution)/shard_map/ppermute | solution.py:168
  22.5 0.0 collective-permute-done.2
  22.6 4.8 %collective-permute-done.3 = bf16[2,32,1536]{2,1,0:T(8,128)(2,1)S(1)} collective-permute-done((bf16[2,32,1536]{2,1,0:T(8,128)(2,1)S(1)}, bf16[2,32,1536]{2,1,0:T(8,128)(2,1)S(1)}, u32[]{:S(2)}, u32[]{:S(2)}) %collective-permute-start.3) | collective-permute-done | bytes 196640 | tf_op jit(solution)/shard_map/ppermute | solution.py:168
  27.4 1.2 %multiply_reduce_fusion = (f32[192]{0:T(256)S(1)}, f32[192,1536]{1,0:T(8,128)S(1)}) fusion(bf16[192,1536]{1,0:T(8,128)(2,1)S(1)} %bitcast.36, bf16[1536,768]{1,0:T(8,128)(2,1)S(1)} %bitcast.35, bf16[1536,768]{1,0:T(8,128)(2,1)S(1)} %bitcast.34), kind=kOutput, calls=%fused_computation.10 | convolution fusion | flops 915996480 | bytes 6488832 | tf_op jit(solution)/shard_map/dot_general | solution.py:181
  28.6 0.2 divide_convert_fusion
  28.8 1.0 %fusion.24 = f32[2,1536,512]{1,2,0:T(8,128)S(1)} fusion(bf16[2,96,1536]{2,1,0:T(8,128)(2,1)S(1)} %bitcast.33, s32[512]{0:T(512)S(1)} %bitcast.37), kind=kOutput, calls=%fused_computation.45 | convolution fusion | flops 302039040 | bytes 6883328 | tf_op jit(solution)/shard_map/pq,mqk->mpk/dot_general | solution.py:199
  29.9 0.9 %add_convert_fusion = (bf16[2,2,256,768]{3,2,1,0:T(8,128)(2,1)S(1)}, bf16[2,2,256,768]{3,2,1,0:T(8,128)(2,1)S(1)}) fusion(f32[2,2,256,1536]{3,2,1,0:T(8,128)S(1)} %bitcast.29, f32[2,2,768]{2,1,0:T(2,128)S(1)} %get-tuple-element.10, f32[2,2,768]{2,1,0:T(2,128)S(1)} %get-tuple-element.9), kind=kLoop, calls=%fused_computation.8 | loop fusion | flops 6291456 | bytes 9461760 | tf_op jit(solution)/shard_map/convert.4
  30.8 0.0 copy-start
  30.8 0.2 pad_maximum_fusion.crossed_ref
  31.1 0.5 %copy-done = s32[4,1024]{1,0:T(4,128)S(1)} copy-done((s32[4,1024]{1,0:T(4,128)S(1)}, s32[4,1024]{1,0:T(4,128)}, u32[]{:S(2)}) %copy-start) | copy-done | bytes 16408
  31.6 13.3 %shard_map.37 = f32[512,128]{1,0:T(8,128)S(1)} custom-call(s32[1]{0:T(128)} %constant.23.clone.1.own_ref, s32[4,1024]{1,0:T(4,128)S(1)} %copy-done, bf16[2,512,1536]{2,1,0:T(8,128)(2,1)S(1)} %pad_maximum_fusion.crossed_ref, f32[768,8]{1,0:T(8,128)S(1)} %get-tuple-element.12.wcos_ref, f32[768,8]{1,0:T(8,128)S(1)} %get-tuple-element.11.wsin_ref, ...), custom_call_target="tpu_custom_call" | custom-call | tf_op jit(solution)/shard_map/pallas_call | solution.py:136
  44.9 0.7 %copy.7 = f32[1,4,2,256]{3,2,1,0:T(2,128)} copy(f32[1,4,2,256]{1,3,2,0:T(8,128)S(1)} %bitcast.28) | data formatting | bytes 16384 | tf_op jit(solution)/shard_map/reshape | solution.py:207
  (16 shorter events, 0.2 us)
Async XLA Ops:
  0.0 11.4 %collective-permute-start = (bf16[1,16,1536]{2,1,0:T(8,128)(2,1)}, bf16[1,16,1536]{2,1,0:T(8,128)(2,1)S(1)}, u32[]{:S(2)}, u32[]{:S(2)}) collective-permute-start(bf16[1,16,1536]{2,1,0:T(8,128)(2,1)} %param.3), channel_id=1, source_target_pairs={{0,30},{2,28},{4,26},{6,24},{8,22},{10,20},{12,18},{14,16},{16,14}... | collective-permute-start | bytes 147464 | tf_op jit(solution)/shard_map/ppermute | solution.py:159
  8.3 3.0 %copy-start.1 = (s32[2,256]{1,0:T(2,128)S(1)}, s32[2,256]{1,0:T(2,128)}, u32[]{:S(2)}) copy-start(s32[2,256]{1,0:T(2,128)} %param.4) | copy-start | bytes 6148
  11.4 4.6 %collective-permute-start.1 = (bf16[1,32,1536]{2,1,0:T(8,128)(2,1)S(1)}, bf16[1,32,1536]{2,1,0:T(8,128)(2,1)S(1)}, u32[]{:S(2)}, u32[]{:S(2)}) collective-permute-start(bf16[1,32,1536]{2,1,0:T(8,128)(2,1)S(1)} %constant_dynamic-update-slice_fusion), channel_id=1, source_target_pairs={{0,1},{1,0},{2,3},{3,2},{4,5},{5,4},{6,7},{7,6},{8,9},{9,8},{10,11... | collective-permute-start | bytes 294920 | tf_op jit(solution)/shard_map/ppermute | solution.py:164
  16.0 6.5 %collective-permute-start.2 = (bf16[2,32,1536]{2,1,0:T(8,128)(2,1)S(1)}, bf16[2,32,1536]{2,1,0:T(8,128)(2,1)S(1)}, u32[]{:S(2)}, u32[]{:S(2)}) collective-permute-start(bf16[2,32,1536]{2,1,0:T(8,128)(2,1)S(1)} %pad_maximum_fusion.1), channel_id=1, source_target_pairs={{0,2},{2,4},{4,6},{6,8},{8,10},{10,12},{12,14},{14,16},{16,18},{18... | collective-permute-start | bytes 589832 | tf_op jit(solution)/shard_map/ppermute | solution.py:167
  20.4 7.0 %collective-permute-start.3 = (bf16[2,32,1536]{2,1,0:T(8,128)(2,1)S(1)}, bf16[2,32,1536]{2,1,0:T(8,128)(2,1)S(1)}, u32[]{:S(2)}, u32[]{:S(2)}) collective-permute-start(bf16[2,32,1536]{2,1,0:T(8,128)(2,1)S(1)} %pad_maximum_fusion.1), channel_id=1, source_target_pairs={{2,0},{4,2},{6,4},{8,6},{10,8},{12,10},{14,12},{16,14},{18,16},{20... | collective-permute-start | bytes 589832 | tf_op jit(solution)/shard_map/ppermute | solution.py:168
  30.8 0.7 %copy-start = (s32[4,1024]{1,0:T(4,128)S(1)}, s32[4,1024]{1,0:T(4,128)}, u32[]{:S(2)}) copy-start(s32[4,1024]{1,0:T(4,128)} %stretch_ref.1) | copy-start | bytes 49156

commit v17 on v15

--- a/solution.py
+++ b/solution.py
@@ -1,3 +1,4 @@
+import functools
 import math
 
 import jax
@@ -149,17 +150,26 @@
     return out[:, :stretch_count].T
 
 
-def body(record, pairs, stretch_index):
+def body(axis_order, record, pairs, stretch_index):
     block_rows = record.shape[1]
     minutes = lax.axis_size("tm")
     blocks = lax.axis_size("chan")
-    mirrored = lax.ppermute(record, "chan", [(s, blocks - 1 - s) for s in range(blocks)])
-    pair = jnp.concatenate([record, mirrored], axis=1)
-    parts = [pair]
-    for shift in range(1, minutes):
-        parts.append(
-            lax.ppermute(pair, "tm", [(i, (i + shift) % minutes) for i in range(minutes)])
-        )
+    def linear(t, b):
+        return t * blocks + b if axis_order[0] == "tm" else b * minutes + t
+
+    parts = []
+    for shift in range(minutes):
+        if shift == 0:
+            own = record
+        else:
+            own = lax.ppermute(record, "tm", [(i, (i + shift) % minutes) for i in range(minutes)])
+        route = [
+            (linear(t, b), linear((t + shift) % minutes, blocks - 1 - b))
+            for t in range(minutes)
+            for b in range(blocks)
+        ]
+        mirrored = lax.ppermute(record, axis_order, route)
+        parts.append(jnp.concatenate([own, mirrored], axis=1))
     bundle = jnp.concatenate(parts, axis=0)
     from_below = lax.ppermute(bundle, "chan", [(s, s + 1) for s in range(blocks - 1)])
     from_above = lax.ppermute(bundle, "chan", [(s, s - 1) for s in range(1, blocks)])
@@ -205,8 +215,9 @@
 
 
 def solution(mesh):
+    axis_order = tuple(name for name in mesh.axis_names if name in ("tm", "chan"))
     return jax.shard_map(
-        body,
+        functools.partial(body, axis_order),
         mesh=mesh,
         in_specs=(P("tm", "chan", None), P("chan", None), P()),
         out_specs=P("tm", None, "chan", None),

time: 45.4 us -> 43.1 us (0.949)
  waiting for transfers between devices: 8.15 us -> 6.68 us
  local copies, waits for them, and re-layouts: 2.1 us -> 1.29 us
    ppermute x2 -> x3, waiting for transfers between devices: 3.31 us -> 2.15 us  [the longest x2 2.15 us: body(): mirrored = lax.ppermute(record, axis_order, route)]
    unnamed x8 -> x11, local copies, waits for them, and re-layouts: 1.33 us -> 0.52 us
    ppermute x1, starting transfers between devices: 2.71 us -> 2.1 us  [body(): lax.ppermute(bundle, 'chan', [(s, s + 1) for s in range(blocks - 1)])]
    ppermute x2 -> x3, starting transfers between devices: 6.94 us -> 7.13 us  [the longest x2 5.92 us: body(): mirrored = lax.ppermute(record, axis_order, route)]
  transfers between devices with their start and end apart: 4 -> 5, of which waited for: 2 -> 2; matrix products, arithmetic and copies ran while one was open for 16% -> 15% of each run, Pallas kernels for 0% -> 0%
where the time goes in v17:
time: 43.1 us; the launch traced here: 42.8 us
  Pallas kernels  12.9 us (30%)
  starting transfers between devices  11.6 us (27%)
  other arithmetic  7.82 us (18%)
  waiting for transfers between devices  6.68 us (15%)
  matrix products  2.21 us (5%)
  local copies, waits for them, and re-layouts  1.29 us (3%)
    pallas_call x1, Pallas kernels, coherence(): pl.pallas_call(coherence_kernel, grid_spec=pltpu.PrefetchScalarGridSpec(n...  12.9 us
    ppermute x2, starting transfers between devices, body(): mirrored = lax.ppermute(record, axis_order, route)  5.92 us
    ppermute x1, waiting for transfers between devices, body(): lax.ppermute(bundle, 'chan', [(s, s - 1) for s in range(1, blocks)])  4.52 us
    sin x3, other arithmetic, unit_angles(): return (jnp.cos(phase), jnp.sin(phase))  3.4 us
    ppermute x1, starting transfers between devices, body(): lax.ppermute(bundle, 'chan', [(s, s - 1) for s in range(1, blocks)])  2.41 us
    another operation x2, other arithmetic  2.33 us
    ppermute x2, waiting for transfers between devices, body(): mirrored = lax.ppermute(record, axis_order, route)  2.15 us
    ppermute x1, starting transfers between devices, body(): lax.ppermute(bundle, 'chan', [(s, s + 1) for s in range(blocks - 1)])  2.1 us
  transfers between devices with their start and end apart: 5, of which 2 were waited for; matrix products, arithmetic and copies ran while one was open for 15% of the time, Pallas kernels for 0%

profile of v17, /device:TPU:1, one launch (start us, length us, event | category | flops | bytes accessed | tf_op | source)
XLA Modules:
  0.0 42.8 jit_solution(8739064207955526940)
XLA Ops:
  0.0 5.7 %collective-permute-start = (bf16[1,16,1536]{2,1,0:T(8,128)(2,1)}, bf16[1,16,1536]{2,1,0:T(8,128)(2,1)S(1)}, u32[]{:S(2)}, u32[]{:S(2)}) collective-permute-start(bf16[1,16,1536]{2,1,0:T(8,128)(2,1)} %param.3), channel_id=1, source_target_pairs={{0,30},{2,28},{4,26},{6,24},{8,22},{10,20},{12,18},{14,16},{16,14}... | collective-permute-start | bytes 147464 | tf_op jit(solution)/shard_map/ppermute | solution.py:171
  5.7 1.2 %collective-permute-start.1 = (bf16[1,16,1536]{2,1,0:T(8,128)(2,1)}, bf16[1,16,1536]{2,1,0:T(8,128)(2,1)S(1)}, u32[]{:S(2)}, u32[]{:S(2)}) collective-permute-start(bf16[1,16,1536]{2,1,0:T(8,128)(2,1)} %param.3), channel_id=1, source_target_pairs={{0,1},{1,0},{2,3},{3,2},{4,5},{5,4},{6,7},{7,6},{8,9},{9,8},{10,11... | collective-permute-start | bytes 147464 | tf_op jit(solution)/shard_map/ppermute | solution.py:165
  6.9 0.3 collective-permute-start.2
  7.1 1.6 %fusion.18 = (f32[128,768]{1,0:T(8,128)S(1)}, f32[128,768]{1,0:T(8,128)S(1)}) fusion(), kind=kLoop, calls=%fused_computation.33 | loop fusion | flops 884736 | bytes 786432 | tf_op jit(solution)/shard_map/sin | solution.py:20
  8.7 0.2 fusion.31
  9.0 0.0 copy-start.2
  9.0 0.0 copy-start.1
  9.0 1.6 %fusion.12 = (f32[768,128]{1,0:T(8,128)S(1)}, f32[768,128]{1,0:T(8,128)S(1)}) fusion(), kind=kLoop, calls=%fused_computation.23 | loop fusion | flops 884736 | bytes 786432 | tf_op jit(solution)/shard_map/sin | solution.py:20
  10.6 1.4 %subtract_convert_fusion = (bf16[12,128,768]{2,1,0:T(8,128)(2,1)S(1)}, bf16[12,128,768]{2,1,0:T(8,128)(2,1)S(1)}) fusion(f32[128,768]{1,0:T(8,128)S(1)} %get-tuple-element.15, f32[12,768]{1,0:T(8,128)S(1)} %get-tuple-element.17, f32[128,768]{1,0:T(8,128)S(1)} %get-tuple-element.16, f32[12,768]{1,0:T(8,128)S(1)} %get-tuple-element.18), kind=kLoop, calls=%fused_computation.5 | loop fusion | flops 10616832 | bytes 5578752 | tf_op jit(solution)/shard_map/convert.8
  12.0 0.0 copy-done.2
  12.1 0.0 collective-permute-done
  12.1 0.0 collective-permute-done.1
  12.1 2.1 %collective-permute-done.2 = bf16[1,16,1536]{2,1,0:T(8,128)(2,1)S(1)} collective-permute-done((bf16[1,16,1536]{2,1,0:T(8,128)(2,1)}, bf16[1,16,1536]{2,1,0:T(8,128)(2,1)S(1)}, u32[]{:S(2)}, u32[]{:S(2)}) %collective-permute-start.2) | collective-permute-done | bytes 49184 | tf_op jit(solution)/shard_map/ppermute | solution.py:171
  14.2 0.0 copy-done.1
  14.3 2.1 %collective-permute-start.3 = (bf16[2,32,1536]{2,1,0:T(8,128)(2,1)S(1)}, bf16[2,32,1536]{2,1,0:T(8,128)(2,1)S(1)}, u32[]{:S(2)}, u32[]{:S(2)}) collective-permute-start(bf16[2,32,1536]{2,1,0:T(8,128)(2,1)S(1)} %maximum_maximum_fusion), channel_id=1, source_target_pairs={{0,2},{2,4},{4,6},{6,8},{8,10},{10,12},{12,14},{14,16},{16,18},{18... | collective-permute-start | bytes 589832 | tf_op jit(solution)/shard_map/ppermute | solution.py:174
  16.4 1.6 %sine_multiply_fusion = (f32[768,8]{1,0:T(8,128)S(1)}, f32[768,8]{1,0:T(8,128)S(1)}) fusion(f32[768]{0:T(1024)S(1)} %fusion.34, s32[8]{0:T(128)S(1)} %iota_add_fusion), kind=kLoop, calls=%fused_computation.25 | loop fusion | flops 67584 | bytes 52256 | tf_op jit(solution)/shard_map/mul | solution.py:41
  18.0 2.4 %collective-permute-start.4 = (bf16[2,32,1536]{2,1,0:T(8,128)(2,1)S(1)}, bf16[2,32,1536]{2,1,0:T(8,128)(2,1)S(1)}, u32[]{:S(2)}, u32[]{:S(2)}) collective-permute-start(bf16[2,32,1536]{2,1,0:T(8,128)(2,1)S(1)} %maximum_maximum_fusion), channel_id=1, source_target_pairs={{2,0},{4,2},{6,4},{8,6},{10,8},{12,10},{14,12},{16,14},{18,16},{20... | collective-permute-start | bytes 589832 | tf_op jit(solution)/shard_map/ppermute | solution.py:175
  20.4 0.0 collective-permute-done.3
  20.5 4.5 %collective-permute-done.4 = bf16[2,32,1536]{2,1,0:T(8,128)(2,1)S(1)} collective-permute-done((bf16[2,32,1536]{2,1,0:T(8,128)(2,1)S(1)}, bf16[2,32,1536]{2,1,0:T(8,128)(2,1)S(1)}, u32[]{:S(2)}, u32[]{:S(2)}) %collective-permute-start.4) | collective-permute-done | bytes 196640 | tf_op jit(solution)/shard_map/ppermute | solution.py:175
  25.0 1.2 %multiply_reduce_fusion = (f32[192]{0:T(256)S(1)}, f32[192,1536]{1,0:T(8,128)S(1)}) fusion(bf16[192,1536]{1,0:T(8,128)(2,1)S(1)} %bitcast.36, bf16[1536,768]{1,0:T(8,128)(2,1)S(1)} %bitcast.35, bf16[1536,768]{1,0:T(8,128)(2,1)S(1)} %bitcast.34), kind=kOutput, calls=%fused_computation.10 | convolution fusion | flops 915996480 | bytes 6488832 | tf_op jit(solution)/shard_map/dot_general | solution.py:188
  26.2 0.2 divide_convert_fusion
  26.4 1.0 %fusion.24 = f32[2,1536,512]{1,2,0:T(8,128)S(1)} fusion(bf16[2,96,1536]{2,1,0:T(8,128)(2,1)S(1)} %bitcast.33, s32[512]{0:T(512)S(1)} %bitcast.37), kind=kOutput, calls=%fused_computation.41 | convolution fusion | flops 302039040 | bytes 6883328 | tf_op jit(solution)/shard_map/pq,mqk->mpk/dot_general | solution.py:206
  27.5 0.9 %add_convert_fusion = (bf16[2,2,256,768]{3,2,1,0:T(8,128)(2,1)S(1)}, bf16[2,2,256,768]{3,2,1,0:T(8,128)(2,1)S(1)}) fusion(f32[2,2,256,1536]{3,2,1,0:T(8,128)S(1)} %bitcast.29, f32[2,2,768]{2,1,0:T(2,128)S(1)} %get-tuple-element.10, f32[2,2,768]{2,1,0:T(2,128)S(1)} %get-tuple-element.9), kind=kLoop, calls=%fused_computation.8 | loop fusion | flops 6291456 | bytes 9461760 | tf_op jit(solution)/shard_map/convert.4
  28.4 0.0 copy-start
  28.4 0.2 pad_maximum_fusion.crossed_ref
  28.7 0.5 %copy-done = s32[4,1024]{1,0:T(4,128)S(1)} copy-done((s32[4,1024]{1,0:T(4,128)S(1)}, s32[4,1024]{1,0:T(4,128)}, u32[]{:S(2)}) %copy-start) | copy-done | bytes 16408
  29.2 12.9 %shard_map.37 = f32[512,128]{1,0:T(8,128)S(1)} custom-call(s32[1]{0:T(128)} %constant.23.clone.1.own_ref, s32[4,1024]{1,0:T(4,128)S(1)} %copy-done, bf16[2,512,1536]{2,1,0:T(8,128)(2,1)S(1)} %pad_maximum_fusion.crossed_ref, f32[768,8]{1,0:T(8,128)S(1)} %get-tuple-element.12.wcos_ref, f32[768,8]{1,0:T(8,128)S(1)} %get-tuple-element.11.wsin_ref, ...), custom_call_target="tpu_custom_call" | custom-call | tf_op jit(solution)/shard_map/pallas_call | solution.py:131
  42.1 0.7 %copy.7 = f32[1,4,2,256]{3,2,1,0:T(2,128)} copy(f32[1,4,2,256]{1,3,2,0:T(8,128)S(1)} %bitcast.28) | data formatting | bytes 16384 | tf_op jit(solution)/shard_map/reshape | solution.py:214
  (15 shorter events, 0.2 us)
Async XLA Ops:
  0.0 12.1 %collective-permute-start = (bf16[1,16,1536]{2,1,0:T(8,128)(2,1)}, bf16[1,16,1536]{2,1,0:T(8,128)(2,1)S(1)}, u32[]{:S(2)}, u32[]{:S(2)}) collective-permute-start(bf16[1,16,1536]{2,1,0:T(8,128)(2,1)} %param.3), channel_id=1, source_target_pairs={{0,30},{2,28},{4,26},{6,24},{8,22},{10,20},{12,18},{14,16},{16,14}... | collective-permute-start | bytes 147464 | tf_op jit(solution)/shard_map/ppermute | solution.py:171
  5.7 6.4 %collective-permute-start.1 = (bf16[1,16,1536]{2,1,0:T(8,128)(2,1)}, bf16[1,16,1536]{2,1,0:T(8,128)(2,1)S(1)}, u32[]{:S(2)}, u32[]{:S(2)}) collective-permute-start(bf16[1,16,1536]{2,1,0:T(8,128)(2,1)} %param.3), channel_id=1, source_target_pairs={{0,1},{1,0},{2,3},{3,2},{4,5},{5,4},{6,7},{7,6},{8,9},{9,8},{10,11... | collective-permute-start | bytes 147464 | tf_op jit(solution)/shard_map/ppermute | solution.py:165
  6.9 7.4 %collective-permute-start.2 = (bf16[1,16,1536]{2,1,0:T(8,128)(2,1)}, bf16[1,16,1536]{2,1,0:T(8,128)(2,1)S(1)}, u32[]{:S(2)}, u32[]{:S(2)}) collective-permute-start(bf16[1,16,1536]{2,1,0:T(8,128)(2,1)} %param.3), channel_id=1, source_target_pairs={{0,31},{2,29},{4,27},{6,25},{8,23},{10,21},{12,19},{14,17},{16,15}... | collective-permute-start | bytes 147464 | tf_op jit(solution)/shard_map/ppermute | solution.py:171
  9.0 3.0 %copy-start.2 = (s32[2,256]{1,0:T(2,128)S(1)}, s32[2,256]{1,0:T(2,128)}, u32[]{:S(2)}) copy-start(s32[2,256]{1,0:T(2,128)} %param.4) | copy-start | bytes 6148
  9.0 5.3 %copy-start.1 = (bf16[1,16,1536]{2,1,0:T(8,128)(2,1)S(1)}, bf16[1,16,1536]{2,1,0:T(8,128)(2,1)}, u32[]{:S(2)}) copy-start(bf16[1,16,1536]{2,1,0:T(8,128)(2,1)} %param.3) | copy-start | bytes 147460
  14.3 6.2 %collective-permute-start.3 = (bf16[2,32,1536]{2,1,0:T(8,128)(2,1)S(1)}, bf16[2,32,1536]{2,1,0:T(8,128)(2,1)S(1)}, u32[]{:S(2)}, u32[]{:S(2)}) collective-permute-start(bf16[2,32,1536]{2,1,0:T(8,128)(2,1)S(1)} %maximum_maximum_fusion), channel_id=1, source_target_pairs={{0,2},{2,4},{4,6},{6,8},{8,10},{10,12},{12,14},{14,16},{16,18},{18... | collective-permute-start | bytes 589832 | tf_op jit(solution)/shard_map/ppermute | solution.py:174
  18.0 7.0 %collective-permute-start.4 = (bf16[2,32,1536]{2,1,0:T(8,128)(2,1)S(1)}, bf16[2,32,1536]{2,1,0:T(8,128)(2,1)S(1)}, u32[]{:S(2)}, u32[]{:S(2)}) collective-permute-start(bf16[2,32,1536]{2,1,0:T(8,128)(2,1)S(1)} %maximum_maximum_fusion), channel_id=1, source_target_pairs={{2,0},{4,2},{6,4},{8,6},{10,8},{12,10},{14,12},{16,14},{18,16},{20... | collective-permute-start | bytes 589832 | tf_op jit(solution)/shard_map/ppermute | solution.py:175
  28.4 0.7 %copy-start = (s32[4,1024]{1,0:T(4,128)S(1)}, s32[4,1024]{1,0:T(4,128)}, u32[]{:S(2)}) copy-start(s32[4,1024]{1,0:T(4,128)} %stretch_ref.1) | copy-start | bytes 49156

commit v18 on v17

--- a/solution.py
+++ b/solution.py
@@ -24,7 +24,10 @@
     coarse = NT // 128
     bins = jnp.arange(NF, dtype=jnp.int32)[None, :]
     cos_a, sin_a = unit_angles(jnp.arange(coarse, dtype=jnp.int32)[:, None] * bins, coarse)
-    cos_c, sin_c = unit_angles(jnp.arange(128, dtype=jnp.int32)[:, None] * bins, NT)
+    cos_1, sin_1 = unit_angles(jnp.arange(16, dtype=jnp.int32)[:, None] * bins, NT // 8)
+    cos_2, sin_2 = unit_angles(jnp.arange(8, dtype=jnp.int32)[:, None] * bins, NT)
+    cos_c = (cos_1[:, None] * cos_2[None] - sin_1[:, None] * sin_2[None]).reshape(128, NF)
+    sin_c = (sin_1[:, None] * cos_2[None] + cos_1[:, None] * sin_2[None]).reshape(128, NF)
     cos_t = cos_a[:, None, :] * cos_c[None] - sin_a[:, None, :] * sin_c[None]
     sin_t = sin_a[:, None, :] * cos_c[None] + cos_a[:, None, :] * sin_c[None]
     table = jnp.concatenate([cos_t, -sin_t], axis=-1).astype(jnp.bfloat16)

time: 43.1 us -> 43.1 us (level)
  other arithmetic: 7.82 us -> 6.65 us
  waiting for transfers between devices: 6.68 us -> 7.83 us
    sin x3 -> x4, other arithmetic: 3.4 us -> 2.15 us  [unit_angles(): return (jnp.cos(phase), jnp.sin(phase))]
    ppermute x2, waiting for transfers between devices: 2.15 us -> 3.3 us  [body(): mirrored = lax.ppermute(record, axis_order, route)]
  transfers between devices with their start and end apart: 5 -> 5, of which waited for: 2 -> 2; matrix products, arithmetic and copies ran while one was open for 15% -> 12% of each run, Pallas kernels for 0% -> 0%
where the time goes in v18:
time: 43.1 us; the launch traced here: 42.8 us
  Pallas kernels  12.9 us (30%)
  starting transfers between devices  11.6 us (27%)
  waiting for transfers between devices  7.83 us (18%)
  other arithmetic  6.65 us (15%)
  matrix products  2.21 us (5%)
  local copies, waits for them, and re-layouts  1.29 us (3%)
    pallas_call x1, Pallas kernels, coherence(): pl.pallas_call(coherence_kernel, grid_spec=pltpu.PrefetchScalarGridSpec(n...  12.9 us
    ppermute x2, starting transfers between devices, body(): mirrored = lax.ppermute(record, axis_order, route)  5.92 us
    ppermute x1, waiting for transfers between devices, body(): lax.ppermute(bundle, 'chan', [(s, s - 1) for s in range(1, blocks)])  4.52 us
    ppermute x2, waiting for transfers between devices, body(): mirrored = lax.ppermute(record, axis_order, route)  3.3 us
    ppermute x1, starting transfers between devices, body(): lax.ppermute(bundle, 'chan', [(s, s - 1) for s in range(1, blocks)])  2.41 us
    another operation x2, other arithmetic  2.33 us
    sin x4, other arithmetic, unit_angles(): return (jnp.cos(phase), jnp.sin(phase))  2.15 us
    ppermute x1, starting transfers between devices, body(): lax.ppermute(bundle, 'chan', [(s, s + 1) for s in range(blocks - 1)])  2.1 us
  transfers between devices with their start and end apart: 5, of which 2 were waited for; matrix products, arithmetic and copies ran while one was open for 12% of the time, Pallas kernels for 0%

profile of v18, /device:TPU:1, one launch (start us, length us, event | category | flops | bytes accessed | tf_op | source)
XLA Modules:
  0.0 42.8 jit_solution(5752356784541849216)
XLA Ops:
  0.0 5.7 %collective-permute-start = (bf16[1,16,1536]{2,1,0:T(8,128)(2,1)}, bf16[1,16,1536]{2,1,0:T(8,128)(2,1)S(1)}, u32[]{:S(2)}, u32[]{:S(2)}) collective-permute-start(bf16[1,16,1536]{2,1,0:T(8,128)(2,1)} %param.3), channel_id=1, source_target_pairs={{0,30},{2,28},{4,26},{6,24},{8,22},{10,20},{12,18},{14,16},{16,14}... | collective-permute-start | bytes 147464 | tf_op jit(solution)/shard_map/ppermute | solution.py:174
  5.7 1.2 %collective-permute-start.1 = (bf16[1,16,1536]{2,1,0:T(8,128)(2,1)}, bf16[1,16,1536]{2,1,0:T(8,128)(2,1)S(1)}, u32[]{:S(2)}, u32[]{:S(2)}) collective-permute-start(bf16[1,16,1536]{2,1,0:T(8,128)(2,1)} %param.3), channel_id=1, source_target_pairs={{0,1},{1,0},{2,3},{3,2},{4,5},{5,4},{6,7},{7,6},{8,9},{9,8},{10,11... | collective-permute-start | bytes 147464 | tf_op jit(solution)/shard_map/ppermute | solution.py:168
  6.9 0.3 collective-permute-start.2
  7.1 0.2 fusion.26
  7.4 0.1 fusion.38
  7.5 0.2 fusion.30
  7.7 1.6 %fusion.10 = (f32[768,128]{1,0:T(8,128)S(1)}, f32[768,128]{1,0:T(8,128)S(1)}) fusion(), kind=kLoop, calls=%fused_computation.20 | loop fusion | flops 884736 | bytes 786432 | tf_op jit(solution)/shard_map/sin | solution.py:20
  9.3 0.0 copy-start.2
  9.3 0.0 copy-start.1
  9.4 0.1 subtract_bitcast_fusion
  9.5 1.4 %subtract_convert_fusion = (bf16[12,128,768]{2,1,0:T(8,128)(2,1)S(1)}, bf16[12,128,768]{2,1,0:T(8,128)(2,1)S(1)}) fusion(f32[128,768]{1,0:T(8,128)S(1)} %get-tuple-element.10, f32[12,768]{1,0:T(8,128)S(1)} %get-tuple-element.21, f32[128,768]{1,0:T(8,128)S(1)} %get-tuple-element.9, f32[12,768]{1,0:T(8,128)S(1)} %get-tuple-element.22), kind=kLoop, calls=%fused_computation.5 | loop fusion | flops 10616832 | bytes 5578752 | tf_op jit(solution)/shard_map/convert.8
  10.9 0.0 copy-done.2
  10.9 0.0 collective-permute-done
  10.9 0.0 collective-permute-done.1
  10.9 3.3 %collective-permute-done.2 = bf16[1,16,1536]{2,1,0:T(8,128)(2,1)S(1)} collective-permute-done((bf16[1,16,1536]{2,1,0:T(8,128)(2,1)}, bf16[1,16,1536]{2,1,0:T(8,128)(2,1)S(1)}, u32[]{:S(2)}, u32[]{:S(2)}) %collective-permute-start.2) | collective-permute-done | bytes 49184 | tf_op jit(solution)/shard_map/ppermute | solution.py:174
  14.2 0.0 copy-done.1
  14.3 2.1 %collective-permute-start.3 = (bf16[2,32,1536]{2,1,0:T(8,128)(2,1)S(1)}, bf16[2,32,1536]{2,1,0:T(8,128)(2,1)S(1)}, u32[]{:S(2)}, u32[]{:S(2)}) collective-permute-start(bf16[2,32,1536]{2,1,0:T(8,128)(2,1)S(1)} %maximum_maximum_fusion), channel_id=1, source_target_pairs={{0,2},{2,4},{4,6},{6,8},{8,10},{10,12},{12,14},{14,16},{16,18},{18... | collective-permute-start | bytes 589832 | tf_op jit(solution)/shard_map/ppermute | solution.py:177
  16.4 1.6 %sine_multiply_fusion = (f32[768,8]{1,0:T(8,128)S(1)}, f32[768,8]{1,0:T(8,128)S(1)}) fusion(f32[768]{0:T(1024)S(1)} %fusion.41, s32[8]{0:T(128)S(1)} %iota_add_fusion), kind=kLoop, calls=%fused_computation.22 | loop fusion | flops 67584 | bytes 52256 | tf_op jit(solution)/shard_map/mul | solution.py:44
  18.0 2.4 %collective-permute-start.4 = (bf16[2,32,1536]{2,1,0:T(8,128)(2,1)S(1)}, bf16[2,32,1536]{2,1,0:T(8,128)(2,1)S(1)}, u32[]{:S(2)}, u32[]{:S(2)}) collective-permute-start(bf16[2,32,1536]{2,1,0:T(8,128)(2,1)S(1)} %maximum_maximum_fusion), channel_id=1, source_target_pairs={{2,0},{4,2},{6,4},{8,6},{10,8},{12,10},{14,12},{16,14},{18,16},{20... | collective-permute-start | bytes 589832 | tf_op jit(solution)/shard_map/ppermute | solution.py:178
  20.4 0.0 collective-permute-done.3
  20.5 4.5 %collective-permute-done.4 = bf16[2,32,1536]{2,1,0:T(8,128)(2,1)S(1)} collective-permute-done((bf16[2,32,1536]{2,1,0:T(8,128)(2,1)S(1)}, bf16[2,32,1536]{2,1,0:T(8,128)(2,1)S(1)}, u32[]{:S(2)}, u32[]{:S(2)}) %collective-permute-start.4) | collective-permute-done | bytes 196640 | tf_op jit(solution)/shard_map/ppermute | solution.py:178
  25.0 1.2 %multiply_reduce_fusion = (f32[192]{0:T(256)S(1)}, f32[192,1536]{1,0:T(8,128)S(1)}) fusion(bf16[192,1536]{1,0:T(8,128)(2,1)S(1)} %bitcast.40, bf16[1536,768]{1,0:T(8,128)(2,1)S(1)} %bitcast.39, bf16[1536,768]{1,0:T(8,128)(2,1)S(1)} %bitcast.38), kind=kOutput, calls=%fused_computation.10 | convolution fusion | flops 915996480 | bytes 6488832 | tf_op jit(solution)/shard_map/dot_general | solution.py:191
  26.2 0.2 divide_convert_fusion
  26.4 1.0 %fusion.17 = f32[2,1536,512]{1,2,0:T(8,128)S(1)} fusion(bf16[2,96,1536]{2,1,0:T(8,128)(2,1)S(1)} %bitcast.37, s32[512]{0:T(512)S(1)} %bitcast.41), kind=kOutput, calls=%fused_computation.34 | convolution fusion | flops 302039040 | bytes 6883328 | tf_op jit(solution)/shard_map/pq,mqk->mpk/dot_general | solution.py:209
  27.5 0.9 %add_convert_fusion = (bf16[2,2,256,768]{3,2,1,0:T(8,128)(2,1)S(1)}, bf16[2,2,256,768]{3,2,1,0:T(8,128)(2,1)S(1)}) fusion(f32[2,2,256,1536]{3,2,1,0:T(8,128)S(1)} %bitcast.33, f32[2,2,768]{2,1,0:T(2,128)S(1)} %get-tuple-element.12, f32[2,2,768]{2,1,0:T(2,128)S(1)} %get-tuple-element.11), kind=kLoop, calls=%fused_computation.8 | loop fusion | flops 6291456 | bytes 9461760 | tf_op jit(solution)/shard_map/convert.4
  28.4 0.0 copy-start
  28.4 0.2 pad_maximum_fusion.crossed_ref
  28.7 0.5 %copy-done = s32[4,1024]{1,0:T(4,128)S(1)} copy-done((s32[4,1024]{1,0:T(4,128)S(1)}, s32[4,1024]{1,0:T(4,128)}, u32[]{:S(2)}) %copy-start) | copy-done | bytes 16408
  29.2 12.9 %shard_map.37 = f32[512,128]{1,0:T(8,128)S(1)} custom-call(s32[1]{0:T(128)} %constant.35.clone.1.own_ref, s32[4,1024]{1,0:T(4,128)S(1)} %copy-done, bf16[2,512,1536]{2,1,0:T(8,128)(2,1)S(1)} %pad_maximum_fusion.crossed_ref, f32[768,8]{1,0:T(8,128)S(1)} %get-tuple-element.14.wcos_ref, f32[768,8]{1,0:T(8,128)S(1)} %get-tuple-element.13.wsin_ref, ...), custom_call_target="tpu_custom_call" | custom-call | tf_op jit(solution)/shard_map/pallas_call | solution.py:134
  42.1 0.7 %copy.7 = f32[1,4,2,256]{3,2,1,0:T(2,128)} copy(f32[1,4,2,256]{1,3,2,0:T(8,128)S(1)} %bitcast.32) | data formatting | bytes 16384 | tf_op jit(solution)/shard_map/reshape | solution.py:217
  (15 shorter events, 0.2 us)
Async XLA Ops:
  0.0 10.9 %collective-permute-start = (bf16[1,16,1536]{2,1,0:T(8,128)(2,1)}, bf16[1,16,1536]{2,1,0:T(8,128)(2,1)S(1)}, u32[]{:S(2)}, u32[]{:S(2)}) collective-permute-start(bf16[1,16,1536]{2,1,0:T(8,128)(2,1)} %param.3), channel_id=1, source_target_pairs={{0,30},{2,28},{4,26},{6,24},{8,22},{10,20},{12,18},{14,16},{16,14}... | collective-permute-start | bytes 147464 | tf_op jit(solution)/shard_map/ppermute | solution.py:174
  5.7 5.3 %collective-permute-start.1 = (bf16[1,16,1536]{2,1,0:T(8,128)(2,1)}, bf16[1,16,1536]{2,1,0:T(8,128)(2,1)S(1)}, u32[]{:S(2)}, u32[]{:S(2)}) collective-permute-start(bf16[1,16,1536]{2,1,0:T(8,128)(2,1)} %param.3), channel_id=1, source_target_pairs={{0,1},{1,0},{2,3},{3,2},{4,5},{5,4},{6,7},{7,6},{8,9},{9,8},{10,11... | collective-permute-start | bytes 147464 | tf_op jit(solution)/shard_map/ppermute | solution.py:168
  6.9 7.4 %collective-permute-start.2 = (bf16[1,16,1536]{2,1,0:T(8,128)(2,1)}, bf16[1,16,1536]{2,1,0:T(8,128)(2,1)S(1)}, u32[]{:S(2)}, u32[]{:S(2)}) collective-permute-start(bf16[1,16,1536]{2,1,0:T(8,128)(2,1)} %param.3), channel_id=1, source_target_pairs={{0,31},{2,29},{4,27},{6,25},{8,23},{10,21},{12,19},{14,17},{16,15}... | collective-permute-start | bytes 147464 | tf_op jit(solution)/shard_map/ppermute | solution.py:174
  9.3 1.5 %copy-start.2 = (s32[2,256]{1,0:T(2,128)S(1)}, s32[2,256]{1,0:T(2,128)}, u32[]{:S(2)}) copy-start(s32[2,256]{1,0:T(2,128)} %param.4) | copy-start | bytes 6148
  9.3 4.9 %copy-start.1 = (bf16[1,16,1536]{2,1,0:T(8,128)(2,1)S(1)}, bf16[1,16,1536]{2,1,0:T(8,128)(2,1)}, u32[]{:S(2)}) copy-start(bf16[1,16,1536]{2,1,0:T(8,128)(2,1)} %param.3) | copy-start | bytes 147460
  14.3 6.2 %collective-permute-start.3 = (bf16[2,32,1536]{2,1,0:T(8,128)(2,1)S(1)}, bf16[2,32,1536]{2,1,0:T(8,128)(2,1)S(1)}, u32[]{:S(2)}, u32[]{:S(2)}) collective-permute-start(bf16[2,32,1536]{2,1,0:T(8,128)(2,1)S(1)} %maximum_maximum_fusion), channel_id=1, source_target_pairs={{0,2},{2,4},{4,6},{6,8},{8,10},{10,12},{12,14},{14,16},{16,18},{18... | collective-permute-start | bytes 589832 | tf_op jit(solution)/shard_map/ppermute | solution.py:177
  18.0 7.0 %collective-permute-start.4 = (bf16[2,32,1536]{2,1,0:T(8,128)(2,1)S(1)}, bf16[2,32,1536]{2,1,0:T(8,128)(2,1)S(1)}, u32[]{:S(2)}, u32[]{:S(2)}) collective-permute-start(bf16[2,32,1536]{2,1,0:T(8,128)(2,1)S(1)} %maximum_maximum_fusion), channel_id=1, source_target_pairs={{2,0},{4,2},{6,4},{8,6},{10,8},{12,10},{14,12},{16,14},{18,16},{20... | collective-permute-start | bytes 589832 | tf_op jit(solution)/shard_map/ppermute | solution.py:178
  28.4 0.7 %copy-start = (s32[4,1024]{1,0:T(4,128)S(1)}, s32[4,1024]{1,0:T(4,128)}, u32[]{:S(2)}) copy-start(s32[4,1024]{1,0:T(4,128)} %stretch_ref.1) | copy-start | bytes 49156

commit v19 on v17

--- a/solution.py
+++ b/solution.py
@@ -173,23 +173,30 @@
     bundle = jnp.concatenate(parts, axis=0)
     from_below = lax.ppermute(bundle, "chan", [(s, s + 1) for s in range(blocks - 1)])
     from_above = lax.ppermute(bundle, "chan", [(s, s - 1) for s in range(1, blocks)])
-    candidates = jnp.concatenate(
+    forward = forward_table()
+
+    def spectra(rows):
+        count = rows.shape[1]
+        spectrum = jnp.dot(
+            rows.reshape(minutes * count, NT), forward, preferred_element_type=jnp.float32
+        )
+        return whiten(spectrum).reshape(minutes, count, 2 * NF)
+
+    local = spectra(bundle)
+    below_rows = spectra(from_below)
+    above_rows = spectra(from_above)
+    whitened = jnp.concatenate(
         [
-            from_below[:, :block_rows],
-            bundle[:, :block_rows],
-            from_above[:, :block_rows],
-            from_above[:, block_rows:],
-            bundle[:, block_rows:],
-            from_below[:, block_rows:],
+            below_rows[:, :block_rows],
+            local[:, :block_rows],
+            above_rows[:, :block_rows],
+            above_rows[:, block_rows:],
+            local[:, block_rows:],
+            below_rows[:, block_rows:],
         ],
         axis=1,
     )
-    slot_rows = candidates.shape[1]
-    spectrum = jnp.dot(
-        candidates.reshape(minutes * slot_rows, NT), forward_table(),
-        preferred_element_type=jnp.float32,
-    )
-    whitened = whiten(spectrum).reshape(minutes, slot_rows, 2 * NF)
+    slot_rows = whitened.shape[1]
 
     position = lax.axis_index("chan")
     column_index = jnp.arange(pairs.shape[1], dtype=jnp.int32)[None, :]

time: 43.1 us -> 41.7 us (0.968)
  waiting for transfers between devices: 6.68 us -> 3.01 us
  matrix products: 2.21 us -> 4.11 us
    ppermute x1, waiting for transfers between devices: 4.52 us -> 2.54 us  [body(): lax.ppermute(bundle, 'chan', [(s, s - 1) for s in range(1, blocks)])]
    dot_general x1 -> x3, matrix products: 1.19 us -> 3.08 us  [spectra(): jnp.dot(rows.reshape(minutes * count, NT), forward, preferred_element_typ...]
    ppermute x2, waiting for transfers between devices: 2.15 us -> 0.47 us  [body(): mirrored = lax.ppermute(record, axis_order, route)]
    ppermute x1, starting transfers between devices: 2.1 us -> 2.55 us  [body(): lax.ppermute(bundle, 'chan', [(s, s + 1) for s in range(blocks - 1)])]
  transfers between devices with their start and end apart: 5 -> 5, of which waited for: 2 -> 2; matrix products, arithmetic and copies ran while one was open for 15% -> 21% of each run, Pallas kernels for 0% -> 0%
where the time goes in v19:
time: 41.7 us; the launch traced here: 41.4 us
  Pallas kernels  12.9 us (31%)
  starting transfers between devices  11.9 us (29%)
  other arithmetic  7.99 us (19%)
  matrix products  4.11 us (10%)
  waiting for transfers between devices  3.01 us (7%)
  local copies, waits for them, and re-layouts  1.3 us (3%)
    pallas_call x1, Pallas kernels, coherence(): pl.pallas_call(coherence_kernel, grid_spec=pltpu.PrefetchScalarGridSpec(n...  12.9 us
    ppermute x2, starting transfers between devices, body(): mirrored = lax.ppermute(record, axis_order, route)  5.99 us
    sin x3, other arithmetic, unit_angles(): return (jnp.cos(phase), jnp.sin(phase))  3.4 us
    dot_general x3, matrix products, spectra(): jnp.dot(rows.reshape(minutes * count, NT), forward, preferred_element_typ...  3.08 us
    ppermute x1, starting transfers between devices, body(): lax.ppermute(bundle, 'chan', [(s, s + 1) for s in range(blocks - 1)])  2.55 us
    ppermute x1, waiting for transfers between devices, body(): lax.ppermute(bundle, 'chan', [(s, s - 1) for s in range(1, blocks)])  2.54 us
    another operation x2, other arithmetic  2.33 us
    ppermute x1, starting transfers between devices, body(): lax.ppermute(bundle, 'chan', [(s, s - 1) for s in range(1, blocks)])  2.1 us
  transfers between devices with their start and end apart: 5, of which 2 were waited for; matrix products, arithmetic and copies ran while one was open for 21% of the time, Pallas kernels for 0%

profile of v19, /device:TPU:1, one launch (start us, length us, event | category | flops | bytes accessed | tf_op | source)
XLA Modules:
  0.0 41.4 jit_solution(6790227383639326128)
XLA Ops:
  0.0 0.0 copy-start.1
  0.0 0.0 copy-start.2
  0.0 5.7 %collective-permute-start = (bf16[1,16,1536]{2,1,0:T(8,128)(2,1)}, bf16[1,16,1536]{2,1,0:T(8,128)(2,1)S(1)}, u32[]{:S(2)}, u32[]{:S(2)}) collective-permute-start(bf16[1,16,1536]{2,1,0:T(8,128)(2,1)} %param.3), channel_id=1, source_target_pairs={{0,30},{2,28},{4,26},{6,24},{8,22},{10,20},{12,18},{14,16},{16,14}... | collective-permute-start | bytes 147464 | tf_op jit(solution)/shard_map/ppermute | solution.py:171
  5.7 1.2 %collective-permute-start.1 = (bf16[1,16,1536]{2,1,0:T(8,128)(2,1)}, bf16[1,16,1536]{2,1,0:T(8,128)(2,1)S(1)}, u32[]{:S(2)}, u32[]{:S(2)}) collective-permute-start(bf16[1,16,1536]{2,1,0:T(8,128)(2,1)} %param.3), channel_id=1, source_target_pairs={{0,1},{1,0},{2,3},{3,2},{4,5},{5,4},{6,7},{7,6},{8,9},{9,8},{10,11... | collective-permute-start | bytes 147464 | tf_op jit(solution)/shard_map/ppermute | solution.py:165
  6.9 0.3 collective-permute-start.2
  7.2 1.6 %fusion.17 = (f32[128,768]{1,0:T(8,128)S(1)}, f32[128,768]{1,0:T(8,128)S(1)}) fusion(), kind=kLoop, calls=%fused_computation.37 | loop fusion | flops 884736 | bytes 786432 | tf_op jit(solution)/shard_map/sin | solution.py:20
  8.8 0.2 fusion.30
  9.1 1.6 %sine_multiply_fusion = (f32[768,8]{1,0:T(8,128)S(1)}, f32[768,8]{1,0:T(8,128)S(1)}) fusion(f32[768]{0:T(1024)S(1)} %fusion.33, s32[8]{0:T(128)S(1)} %iota_add_fusion), kind=kLoop, calls=%fused_computation.23 | loop fusion | flops 67584 | bytes 52256 | tf_op jit(solution)/shard_map/mul | solution.py:41
  10.7 1.4 %subtract_convert_fusion = (bf16[12,128,768]{2,1,0:T(8,128)(2,1)S(1)}, bf16[12,128,768]{2,1,0:T(8,128)(2,1)S(1)}) fusion(f32[128,768]{1,0:T(8,128)S(1)} %get-tuple-element.21, f32[12,768]{1,0:T(8,128)S(1)} %get-tuple-element.23, f32[128,768]{1,0:T(8,128)S(1)} %get-tuple-element.22, f32[12,768]{1,0:T(8,128)S(1)} %get-tuple-element.24), kind=kLoop, calls=%fused_computation.2 | loop fusion | flops 10616832 | bytes 5578752 | tf_op jit(solution)/shard_map/convert.8
  12.1 0.0 copy-done.2
  12.1 1.6 %fusion.11 = (f32[768,128]{1,0:T(8,128)S(1)}, f32[768,128]{1,0:T(8,128)S(1)}) fusion(), kind=kLoop, calls=%fused_computation.21 | loop fusion | flops 884736 | bytes 786432 | tf_op jit(solution)/shard_map/sin | solution.py:20
  13.8 0.0 collective-permute-done
  13.8 0.0 collective-permute-done.1
  13.8 0.5 %collective-permute-done.2 = bf16[1,16,1536]{2,1,0:T(8,128)(2,1)S(1)} collective-permute-done((bf16[1,16,1536]{2,1,0:T(8,128)(2,1)}, bf16[1,16,1536]{2,1,0:T(8,128)(2,1)S(1)}, u32[]{:S(2)}, u32[]{:S(2)}) %collective-permute-start.2) | collective-permute-done | bytes 49184 | tf_op jit(solution)/shard_map/ppermute | solution.py:171
  14.2 0.0 copy-done.1
  14.3 2.5 %collective-permute-start.3 = (bf16[2,32,1536]{2,1,0:T(8,128)(2,1)S(1)}, bf16[2,32,1536]{2,1,0:T(8,128)(2,1)S(1)}, u32[]{:S(2)}, u32[]{:S(2)}) collective-permute-start(bf16[2,32,1536]{2,1,0:T(8,128)(2,1)S(1)} %maximum_maximum_fusion), channel_id=1, source_target_pairs={{0,2},{2,4},{4,6},{6,8},{8,10},{10,12},{12,14},{14,16},{16,18},{18... | collective-permute-start | bytes 589832 | tf_op jit(solution)/shard_map/ppermute | solution.py:174
  16.8 2.1 %collective-permute-start.4 = (bf16[2,32,1536]{2,1,0:T(8,128)(2,1)S(1)}, bf16[2,32,1536]{2,1,0:T(8,128)(2,1)S(1)}, u32[]{:S(2)}, u32[]{:S(2)}) collective-permute-start(bf16[2,32,1536]{2,1,0:T(8,128)(2,1)S(1)} %maximum_maximum_fusion), channel_id=1, source_target_pairs={{2,0},{4,2},{6,4},{8,6},{10,8},{12,10},{14,12},{16,14},{18,16},{20... | collective-permute-start | bytes 589832 | tf_op jit(solution)/shard_map/ppermute | solution.py:175
  18.9 1.0 %multiply_reduce_fusion.2 = (f32[64]{0:T(128)S(1)}, f32[64,1536]{1,0:T(8,128)S(1)}) fusion(bf16[64,1536]{1,0:T(8,128)(2,1)S(1)} %bitcast.49, bf16[1536,768]{1,0:T(8,128)(2,1)S(1)} %bitcast.41, bf16[1536,768]{1,0:T(8,128)(2,1)S(1)} %bitcast.38), kind=kOutput, calls=%fused_computation.33 | convolution fusion | flops 311623616 | bytes 5308672 | tf_op jit(solution)/shard_map/dot_general | solution.py:180
  20.0 0.1 divide_convert_fusion.2
  20.1 0.0 collective-permute-done.3
  20.1 1.0 %multiply_reduce_fusion.1 = (f32[64]{0:T(128)S(1)}, f32[64,1536]{1,0:T(8,128)S(1)}) fusion(bf16[64,1536]{1,0:T(8,128)(2,1)S(1)} %bitcast.52, bf16[1536,768]{1,0:T(8,128)(2,1)S(1)} %bitcast.42, bf16[1536,768]{1,0:T(8,128)(2,1)S(1)} %bitcast.39), kind=kOutput, calls=%fused_computation.31 | convolution fusion | flops 311623616 | bytes 5308672 | tf_op jit(solution)/shard_map/dot_general | solution.py:180
  21.1 0.1 divide_convert_fusion.1
  21.3 2.5 %collective-permute-done.4 = bf16[2,32,1536]{2,1,0:T(8,128)(2,1)S(1)} collective-permute-done((bf16[2,32,1536]{2,1,0:T(8,128)(2,1)S(1)}, bf16[2,32,1536]{2,1,0:T(8,128)(2,1)S(1)}, u32[]{:S(2)}, u32[]{:S(2)}) %collective-permute-start.4) | collective-permute-done | bytes 196640 | tf_op jit(solution)/shard_map/ppermute | solution.py:175
  23.8 1.0 %multiply_reduce_fusion = (f32[64]{0:T(128)S(1)}, f32[64,1536]{1,0:T(8,128)S(1)}) fusion(bf16[64,1536]{1,0:T(8,128)(2,1)S(1)} %bitcast.51, bf16[1536,768]{1,0:T(8,128)(2,1)S(1)} %bitcast.43, bf16[1536,768]{1,0:T(8,128)(2,1)S(1)} %bitcast.40), kind=kOutput, calls=%fused_computation.29 | convolution fusion | flops 311623616 | bytes 5308672 | tf_op jit(solution)/shard_map/dot_general | solution.py:180
  24.9 0.1 divide_convert_fusion
  25.1 1.0 %fusion.23 = f32[2,1536,512]{1,2,0:T(8,128)S(1)} fusion(bf16[2,96,1536]{2,1,0:T(8,128)(2,1)S(1)} %slice_dynamic-update-slice_fusion, s32[512]{0:T(512)S(1)} %bitcast.50), kind=kOutput, calls=%fused_computation.45 | convolution fusion | flops 302039040 | bytes 6883328 | tf_op jit(solution)/shard_map/pq,mqk->mpk/dot_general | solution.py:213
  26.1 0.9 %add_convert_fusion = (bf16[2,2,256,768]{3,2,1,0:T(8,128)(2,1)S(1)}, bf16[2,2,256,768]{3,2,1,0:T(8,128)(2,1)S(1)}) fusion(f32[2,2,256,1536]{3,2,1,0:T(8,128)S(1)} %bitcast.35, f32[2,2,768]{2,1,0:T(2,128)S(1)} %get-tuple-element.12, f32[2,2,768]{2,1,0:T(2,128)S(1)} %get-tuple-element.11), kind=kLoop, calls=%fused_computation.5 | loop fusion | flops 6291456 | bytes 9461760 | tf_op jit(solution)/shard_map/convert.4
  27.1 0.0 copy-start
  27.1 0.2 pad_maximum_fusion.1.crossed_ref
  27.3 0.5 %copy-done = s32[4,1024]{1,0:T(4,128)S(1)} copy-done((s32[4,1024]{1,0:T(4,128)S(1)}, s32[4,1024]{1,0:T(4,128)}, u32[]{:S(2)}) %copy-start) | copy-done | bytes 16408
  27.8 12.9 %shard_map.37 = f32[512,128]{1,0:T(8,128)S(1)} custom-call(s32[1]{0:T(128)} %constant.28.clone.1.own_ref, s32[4,1024]{1,0:T(4,128)S(1)} %copy-done, bf16[2,512,1536]{2,1,0:T(8,128)(2,1)S(1)} %pad_maximum_fusion.1.crossed_ref, f32[768,8]{1,0:T(8,128)S(1)} %get-tuple-element.14.wcos_ref, f32[768,8]{1,0:T(8,128)S(1)} %get-tuple-element.13.wsin_ref, ...), custom_call_target="tpu_custom_call" | custom-call | tf_op jit(solution)/shard_map/pallas_call | solution.py:131
  40.7 0.7 %copy.7 = f32[1,4,2,256]{3,2,1,0:T(2,128)} copy(f32[1,4,2,256]{1,3,2,0:T(8,128)S(1)} %bitcast.34) | data formatting | bytes 16384 | tf_op jit(solution)/shard_map/reshape | solution.py:221
  (17 shorter events, 0.2 us)
Async XLA Ops:
  0.0 14.2 %copy-start.1 = (bf16[1,16,1536]{2,1,0:T(8,128)(2,1)S(1)}, bf16[1,16,1536]{2,1,0:T(8,128)(2,1)}, u32[]{:S(2)}) copy-start(bf16[1,16,1536]{2,1,0:T(8,128)(2,1)} %param.3) | copy-start | bytes 147460
  0.0 12.1 %copy-start.2 = (s32[2,256]{1,0:T(2,128)S(1)}, s32[2,256]{1,0:T(2,128)}, u32[]{:S(2)}) copy-start(s32[2,256]{1,0:T(2,128)} %param.4) | copy-start | bytes 6148
  0.0 13.7 %collective-permute-start = (bf16[1,16,1536]{2,1,0:T(8,128)(2,1)}, bf16[1,16,1536]{2,1,0:T(8,128)(2,1)S(1)}, u32[]{:S(2)}, u32[]{:S(2)}) collective-permute-start(bf16[1,16,1536]{2,1,0:T(8,128)(2,1)} %param.3), channel_id=1, source_target_pairs={{0,30},{2,28},{4,26},{6,24},{8,22},{10,20},{12,18},{14,16},{16,14}... | collective-permute-start | bytes 147464 | tf_op jit(solution)/shard_map/ppermute | solution.py:171
  5.7 8.1 %collective-permute-start.1 = (bf16[1,16,1536]{2,1,0:T(8,128)(2,1)}, bf16[1,16,1536]{2,1,0:T(8,128)(2,1)S(1)}, u32[]{:S(2)}, u32[]{:S(2)}) collective-permute-start(bf16[1,16,1536]{2,1,0:T(8,128)(2,1)} %param.3), channel_id=1, source_target_pairs={{0,1},{1,0},{2,3},{3,2},{4,5},{5,4},{6,7},{7,6},{8,9},{9,8},{10,11... | collective-permute-start | bytes 147464 | tf_op jit(solution)/shard_map/ppermute | solution.py:165
  6.9 7.4 %collective-permute-start.2 = (bf16[1,16,1536]{2,1,0:T(8,128)(2,1)}, bf16[1,16,1536]{2,1,0:T(8,128)(2,1)S(1)}, u32[]{:S(2)}, u32[]{:S(2)}) collective-permute-start(bf16[1,16,1536]{2,1,0:T(8,128)(2,1)} %param.3), channel_id=1, source_target_pairs={{0,31},{2,29},{4,27},{6,25},{8,23},{10,21},{12,19},{14,17},{16,15}... | collective-permute-start | bytes 147464 | tf_op jit(solution)/shard_map/ppermute | solution.py:171
  14.3 5.8 %collective-permute-start.3 = (bf16[2,32,1536]{2,1,0:T(8,128)(2,1)S(1)}, bf16[2,32,1536]{2,1,0:T(8,128)(2,1)S(1)}, u32[]{:S(2)}, u32[]{:S(2)}) collective-permute-start(bf16[2,32,1536]{2,1,0:T(8,128)(2,1)S(1)} %maximum_maximum_fusion), channel_id=1, source_target_pairs={{0,2},{2,4},{4,6},{6,8},{8,10},{10,12},{12,14},{14,16},{16,18},{18... | collective-permute-start | bytes 589832 | tf_op jit(solution)/shard_map/ppermute | solution.py:174
  16.8 7.0 %collective-permute-start.4 = (bf16[2,32,1536]{2,1,0:T(8,128)(2,1)S(1)}, bf16[2,32,1536]{2,1,0:T(8,128)(2,1)S(1)}, u32[]{:S(2)}, u32[]{:S(2)}) collective-permute-start(bf16[2,32,1536]{2,1,0:T(8,128)(2,1)S(1)} %maximum_maximum_fusion), channel_id=1, source_target_pairs={{2,0},{4,2},{6,4},{8,6},{10,8},{12,10},{14,12},{16,14},{18,16},{20... | collective-permute-start | bytes 589832 | tf_op jit(solution)/shard_map/ppermute | solution.py:175
  27.1 0.7 %copy-start = (s32[4,1024]{1,0:T(4,128)S(1)}, s32[4,1024]{1,0:T(4,128)}, u32[]{:S(2)}) copy-start(s32[4,1024]{1,0:T(4,128)} %stretch_ref.1) | copy-start | bytes 49156

commit v20 on v19

--- a/solution.py
+++ b/solution.py
@@ -59,7 +59,7 @@
     return jnp.concatenate([real_part, imag_part], axis=-1).astype(jnp.bfloat16)
 
 
-PAIR_BLOCK = 256
+PAIR_BLOCK = 512
 
 
 def coherence_kernel(

time: 41.7 us -> 40.7 us (0.976)
  Pallas kernels: 12.9 us -> 11.8 us
    pallas_call x1, Pallas kernels: 12.9 us -> 11.8 us  [coherence(): pl.pallas_call(coherence_kernel, grid_spec=pltpu.PrefetchScalarGridSpec(n...]
  transfers between devices with their start and end apart: 5 -> 5, of which waited for: 2 -> 2; matrix products, arithmetic and copies ran while one was open for 21% -> 22% of each run, Pallas kernels for 0% -> 0%
where the time goes in v20:
time: 40.7 us; the launch traced here: 40.3 us
  starting transfers between devices  11.9 us (29%)
  Pallas kernels  11.8 us (29%)
  other arithmetic  7.99 us (20%)
  matrix products  4.11 us (10%)
  waiting for transfers between devices  3.01 us (7%)
  local copies, waits for them, and re-layouts  1.3 us (3%)
    pallas_call x1, Pallas kernels, coherence(): pl.pallas_call(coherence_kernel, grid_spec=pltpu.PrefetchScalarGridSpec(n...  11.8 us
    ppermute x2, starting transfers between devices, body(): mirrored = lax.ppermute(record, axis_order, route)  5.99 us
    sin x3, other arithmetic, unit_angles(): return (jnp.cos(phase), jnp.sin(phase))  3.4 us
    dot_general x3, matrix products, spectra(): jnp.dot(rows.reshape(minutes * count, NT), forward, preferred_element_typ...  3.08 us
    ppermute x1, starting transfers between devices, body(): lax.ppermute(bundle, 'chan', [(s, s + 1) for s in range(blocks - 1)])  2.55 us
    ppermute x1, waiting for transfers between devices, body(): lax.ppermute(bundle, 'chan', [(s, s - 1) for s in range(1, blocks)])  2.54 us
    another operation x2, other arithmetic  2.33 us
    ppermute x1, starting transfers between devices, body(): lax.ppermute(bundle, 'chan', [(s, s - 1) for s in range(1, blocks)])  2.1 us
  transfers between devices with their start and end apart: 5, of which 2 were waited for; matrix products, arithmetic and copies ran while one was open for 22% of the time, Pallas kernels for 0%

profile of v20, /device:TPU:1, one launch (start us, length us, event | category | flops | bytes accessed | tf_op | source)
XLA Modules:
  0.0 40.3 jit_solution(4159062681458585091)
XLA Ops:
  0.0 0.0 copy-start.1
  0.0 0.0 copy-start.2
  0.0 5.7 %collective-permute-start = (bf16[1,16,1536]{2,1,0:T(8,128)(2,1)}, bf16[1,16,1536]{2,1,0:T(8,128)(2,1)S(1)}, u32[]{:S(2)}, u32[]{:S(2)}) collective-permute-start(bf16[1,16,1536]{2,1,0:T(8,128)(2,1)} %param.3), channel_id=1, source_target_pairs={{0,30},{2,28},{4,26},{6,24},{8,22},{10,20},{12,18},{14,16},{16,14}... | collective-permute-start | bytes 147464 | tf_op jit(solution)/shard_map/ppermute | solution.py:171
  5.7 1.2 %collective-permute-start.1 = (bf16[1,16,1536]{2,1,0:T(8,128)(2,1)}, bf16[1,16,1536]{2,1,0:T(8,128)(2,1)S(1)}, u32[]{:S(2)}, u32[]{:S(2)}) collective-permute-start(bf16[1,16,1536]{2,1,0:T(8,128)(2,1)} %param.3), channel_id=1, source_target_pairs={{0,1},{1,0},{2,3},{3,2},{4,5},{5,4},{6,7},{7,6},{8,9},{9,8},{10,11... | collective-permute-start | bytes 147464 | tf_op jit(solution)/shard_map/ppermute | solution.py:165
  6.9 0.3 collective-permute-start.2
  7.2 1.6 %fusion.17 = (f32[128,768]{1,0:T(8,128)S(1)}, f32[128,768]{1,0:T(8,128)S(1)}) fusion(), kind=kLoop, calls=%fused_computation.37 | loop fusion | flops 884736 | bytes 786432 | tf_op jit(solution)/shard_map/sin | solution.py:20
  8.8 0.2 fusion.30
  9.1 1.6 %sine_multiply_fusion = (f32[768,8]{1,0:T(8,128)S(1)}, f32[768,8]{1,0:T(8,128)S(1)}) fusion(f32[768]{0:T(1024)S(1)} %fusion.33, s32[8]{0:T(128)S(1)} %iota_add_fusion), kind=kLoop, calls=%fused_computation.23 | loop fusion | flops 67584 | bytes 52256 | tf_op jit(solution)/shard_map/mul | solution.py:41
  10.7 1.4 %subtract_convert_fusion = (bf16[12,128,768]{2,1,0:T(8,128)(2,1)S(1)}, bf16[12,128,768]{2,1,0:T(8,128)(2,1)S(1)}) fusion(f32[128,768]{1,0:T(8,128)S(1)} %get-tuple-element.21, f32[12,768]{1,0:T(8,128)S(1)} %get-tuple-element.23, f32[128,768]{1,0:T(8,128)S(1)} %get-tuple-element.22, f32[12,768]{1,0:T(8,128)S(1)} %get-tuple-element.24), kind=kLoop, calls=%fused_computation.2 | loop fusion | flops 10616832 | bytes 5578752 | tf_op jit(solution)/shard_map/convert.8
  12.1 0.0 copy-done.2
  12.1 1.6 %fusion.11 = (f32[768,128]{1,0:T(8,128)S(1)}, f32[768,128]{1,0:T(8,128)S(1)}) fusion(), kind=kLoop, calls=%fused_computation.21 | loop fusion | flops 884736 | bytes 786432 | tf_op jit(solution)/shard_map/sin | solution.py:20
  13.8 0.0 collective-permute-done
  13.8 0.0 collective-permute-done.1
  13.8 0.5 %collective-permute-done.2 = bf16[1,16,1536]{2,1,0:T(8,128)(2,1)S(1)} collective-permute-done((bf16[1,16,1536]{2,1,0:T(8,128)(2,1)}, bf16[1,16,1536]{2,1,0:T(8,128)(2,1)S(1)}, u32[]{:S(2)}, u32[]{:S(2)}) %collective-permute-start.2) | collective-permute-done | bytes 49184 | tf_op jit(solution)/shard_map/ppermute | solution.py:171
  14.2 0.0 copy-done.1
  14.3 2.5 %collective-permute-start.3 = (bf16[2,32,1536]{2,1,0:T(8,128)(2,1)S(1)}, bf16[2,32,1536]{2,1,0:T(8,128)(2,1)S(1)}, u32[]{:S(2)}, u32[]{:S(2)}) collective-permute-start(bf16[2,32,1536]{2,1,0:T(8,128)(2,1)S(1)} %maximum_maximum_fusion), channel_id=1, source_target_pairs={{0,2},{2,4},{4,6},{6,8},{8,10},{10,12},{12,14},{14,16},{16,18},{18... | collective-permute-start | bytes 589832 | tf_op jit(solution)/shard_map/ppermute | solution.py:174
  16.8 2.1 %collective-permute-start.4 = (bf16[2,32,1536]{2,1,0:T(8,128)(2,1)S(1)}, bf16[2,32,1536]{2,1,0:T(8,128)(2,1)S(1)}, u32[]{:S(2)}, u32[]{:S(2)}) collective-permute-start(bf16[2,32,1536]{2,1,0:T(8,128)(2,1)S(1)} %maximum_maximum_fusion), channel_id=1, source_target_pairs={{2,0},{4,2},{6,4},{8,6},{10,8},{12,10},{14,12},{16,14},{18,16},{20... | collective-permute-start | bytes 589832 | tf_op jit(solution)/shard_map/ppermute | solution.py:175
  18.9 1.0 %multiply_reduce_fusion.2 = (f32[64]{0:T(128)S(1)}, f32[64,1536]{1,0:T(8,128)S(1)}) fusion(bf16[64,1536]{1,0:T(8,128)(2,1)S(1)} %bitcast.49, bf16[1536,768]{1,0:T(8,128)(2,1)S(1)} %bitcast.41, bf16[1536,768]{1,0:T(8,128)(2,1)S(1)} %bitcast.38), kind=kOutput, calls=%fused_computation.33 | convolution fusion | flops 311623616 | bytes 5308672 | tf_op jit(solution)/shard_map/dot_general | solution.py:180
  20.0 0.1 divide_convert_fusion.2
  20.1 0.0 collective-permute-done.3
  20.1 1.0 %multiply_reduce_fusion.1 = (f32[64]{0:T(128)S(1)}, f32[64,1536]{1,0:T(8,128)S(1)}) fusion(bf16[64,1536]{1,0:T(8,128)(2,1)S(1)} %bitcast.52, bf16[1536,768]{1,0:T(8,128)(2,1)S(1)} %bitcast.42, bf16[1536,768]{1,0:T(8,128)(2,1)S(1)} %bitcast.39), kind=kOutput, calls=%fused_computation.31 | convolution fusion | flops 311623616 | bytes 5308672 | tf_op jit(solution)/shard_map/dot_general | solution.py:180
  21.1 0.1 divide_convert_fusion.1
  21.3 2.5 %collective-permute-done.4 = bf16[2,32,1536]{2,1,0:T(8,128)(2,1)S(1)} collective-permute-done((bf16[2,32,1536]{2,1,0:T(8,128)(2,1)S(1)}, bf16[2,32,1536]{2,1,0:T(8,128)(2,1)S(1)}, u32[]{:S(2)}, u32[]{:S(2)}) %collective-permute-start.4) | collective-permute-done | bytes 196640 | tf_op jit(solution)/shard_map/ppermute | solution.py:175
  23.8 1.0 %multiply_reduce_fusion = (f32[64]{0:T(128)S(1)}, f32[64,1536]{1,0:T(8,128)S(1)}) fusion(bf16[64,1536]{1,0:T(8,128)(2,1)S(1)} %bitcast.51, bf16[1536,768]{1,0:T(8,128)(2,1)S(1)} %bitcast.43, bf16[1536,768]{1,0:T(8,128)(2,1)S(1)} %bitcast.40), kind=kOutput, calls=%fused_computation.29 | convolution fusion | flops 311623616 | bytes 5308672 | tf_op jit(solution)/shard_map/dot_general | solution.py:180
  24.9 0.1 divide_convert_fusion
  25.1 1.0 %fusion.23 = f32[2,1536,512]{1,2,0:T(8,128)S(1)} fusion(bf16[2,96,1536]{2,1,0:T(8,128)(2,1)S(1)} %slice_dynamic-update-slice_fusion, s32[512]{0:T(512)S(1)} %bitcast.50), kind=kOutput, calls=%fused_computation.45 | convolution fusion | flops 302039040 | bytes 6883328 | tf_op jit(solution)/shard_map/pq,mqk->mpk/dot_general | solution.py:213
  26.1 0.9 %add_convert_fusion = (bf16[2,2,256,768]{3,2,1,0:T(8,128)(2,1)S(1)}, bf16[2,2,256,768]{3,2,1,0:T(8,128)(2,1)S(1)}) fusion(f32[2,2,256,1536]{3,2,1,0:T(8,128)S(1)} %bitcast.35, f32[2,2,768]{2,1,0:T(2,128)S(1)} %get-tuple-element.12, f32[2,2,768]{2,1,0:T(2,128)S(1)} %get-tuple-element.11), kind=kLoop, calls=%fused_computation.5 | loop fusion | flops 6291456 | bytes 9461760 | tf_op jit(solution)/shard_map/convert.4
  27.1 0.0 copy-start
  27.1 0.2 pad_maximum_fusion.1.crossed_ref
  27.3 0.5 %copy-done = s32[4,1024]{1,0:T(4,128)S(1)} copy-done((s32[4,1024]{1,0:T(4,128)S(1)}, s32[4,1024]{1,0:T(4,128)}, u32[]{:S(2)}) %copy-start) | copy-done | bytes 16408
  27.8 11.8 %shard_map.37 = f32[512,128]{1,0:T(8,128)S(1)} custom-call(s32[1]{0:T(128)} %constant.28.clone.1.own_ref, s32[4,1024]{1,0:T(4,128)S(1)} %copy-done, bf16[2,512,1536]{2,1,0:T(8,128)(2,1)S(1)} %pad_maximum_fusion.1.crossed_ref, f32[768,8]{1,0:T(8,128)S(1)} %get-tuple-element.14.wcos_ref, f32[768,8]{1,0:T(8,128)S(1)} %get-tuple-element.13.wsin_ref, ...), custom_call_target="tpu_custom_call" | custom-call | tf_op jit(solution)/shard_map/pallas_call | solution.py:131
  39.6 0.7 %copy.7 = f32[1,4,2,256]{3,2,1,0:T(2,128)} copy(f32[1,4,2,256]{1,3,2,0:T(8,128)S(1)} %bitcast.34) | data formatting | bytes 16384 | tf_op jit(solution)/shard_map/reshape | solution.py:221
  (17 shorter events, 0.2 us)
Async XLA Ops:
  0.0 14.2 %copy-start.1 = (bf16[1,16,1536]{2,1,0:T(8,128)(2,1)S(1)}, bf16[1,16,1536]{2,1,0:T(8,128)(2,1)}, u32[]{:S(2)}) copy-start(bf16[1,16,1536]{2,1,0:T(8,128)(2,1)} %param.3) | copy-start | bytes 147460
  0.0 12.1 %copy-start.2 = (s32[2,256]{1,0:T(2,128)S(1)}, s32[2,256]{1,0:T(2,128)}, u32[]{:S(2)}) copy-start(s32[2,256]{1,0:T(2,128)} %param.4) | copy-start | bytes 6148
  0.0 13.7 %collective-permute-start = (bf16[1,16,1536]{2,1,0:T(8,128)(2,1)}, bf16[1,16,1536]{2,1,0:T(8,128)(2,1)S(1)}, u32[]{:S(2)}, u32[]{:S(2)}) collective-permute-start(bf16[1,16,1536]{2,1,0:T(8,128)(2,1)} %param.3), channel_id=1, source_target_pairs={{0,30},{2,28},{4,26},{6,24},{8,22},{10,20},{12,18},{14,16},{16,14}... | collective-permute-start | bytes 147464 | tf_op jit(solution)/shard_map/ppermute | solution.py:171
  5.7 8.1 %collective-permute-start.1 = (bf16[1,16,1536]{2,1,0:T(8,128)(2,1)}, bf16[1,16,1536]{2,1,0:T(8,128)(2,1)S(1)}, u32[]{:S(2)}, u32[]{:S(2)}) collective-permute-start(bf16[1,16,1536]{2,1,0:T(8,128)(2,1)} %param.3), channel_id=1, source_target_pairs={{0,1},{1,0},{2,3},{3,2},{4,5},{5,4},{6,7},{7,6},{8,9},{9,8},{10,11... | collective-permute-start | bytes 147464 | tf_op jit(solution)/shard_map/ppermute | solution.py:165
  6.9 7.4 %collective-permute-start.2 = (bf16[1,16,1536]{2,1,0:T(8,128)(2,1)}, bf16[1,16,1536]{2,1,0:T(8,128)(2,1)S(1)}, u32[]{:S(2)}, u32[]{:S(2)}) collective-permute-start(bf16[1,16,1536]{2,1,0:T(8,128)(2,1)} %param.3), channel_id=1, source_target_pairs={{0,31},{2,29},{4,27},{6,25},{8,23},{10,21},{12,19},{14,17},{16,15}... | collective-permute-start | bytes 147464 | tf_op jit(solution)/shard_map/ppermute | solution.py:171
  14.3 5.8 %collective-permute-start.3 = (bf16[2,32,1536]{2,1,0:T(8,128)(2,1)S(1)}, bf16[2,32,1536]{2,1,0:T(8,128)(2,1)S(1)}, u32[]{:S(2)}, u32[]{:S(2)}) collective-permute-start(bf16[2,32,1536]{2,1,0:T(8,128)(2,1)S(1)} %maximum_maximum_fusion), channel_id=1, source_target_pairs={{0,2},{2,4},{4,6},{6,8},{8,10},{10,12},{12,14},{14,16},{16,18},{18... | collective-permute-start | bytes 589832 | tf_op jit(solution)/shard_map/ppermute | solution.py:174
  16.8 7.0 %collective-permute-start.4 = (bf16[2,32,1536]{2,1,0:T(8,128)(2,1)S(1)}, bf16[2,32,1536]{2,1,0:T(8,128)(2,1)S(1)}, u32[]{:S(2)}, u32[]{:S(2)}) collective-permute-start(bf16[2,32,1536]{2,1,0:T(8,128)(2,1)S(1)} %maximum_maximum_fusion), channel_id=1, source_target_pairs={{2,0},{4,2},{6,4},{8,6},{10,8},{12,10},{14,12},{16,14},{18,16},{20... | collective-permute-start | bytes 589832 | tf_op jit(solution)/shard_map/ppermute | solution.py:175
  27.1 0.7 %copy-start = (s32[4,1024]{1,0:T(4,128)S(1)}, s32[4,1024]{1,0:T(4,128)}, u32[]{:S(2)}) copy-start(s32[4,1024]{1,0:T(4,128)} %stretch_ref.1) | copy-start | bytes 49156

commit v21 on v20

--- a/solution.py
+++ b/solution.py
@@ -64,34 +64,40 @@
 
 def coherence_kernel(
     own_ref, stretch_ref, crossed_ref, wcos_ref, wsin_ref, fcos_ref, fsin_ref,
-    out_ref, inverse_ref,
+    out_ref,
 ):
     minutes = crossed_ref.shape[0]
     moves = stretch_ref.shape[0] - 1
     groups = wcos_ref.shape[1]
     fine = fcos_ref.shape[1]
 
-    @pl.when(pl.program_id(0) == 0)
-    def _():
-        fine_cos = fcos_ref[...]
-        fine_sin = fsin_ref[...]
-        for group in range(groups):
+    fine_cos = fcos_ref[...]
+    fine_sin = fsin_ref[...]
+    own = own_ref[0]
+    pieces = [[] for _ in range(minutes)]
+    for pair_group in range(groups // 2):
+        columns = []
+        for group in (2 * pair_group, 2 * pair_group + 1):
             coarse_cos = wcos_ref[:, group:group + 1]
             coarse_sin = wsin_ref[:, group:group + 1]
-            lags = slice(group * fine, (group + 1) * fine)
-            inverse_ref[:NF, lags] = (coarse_cos * fine_cos - coarse_sin * fine_sin).astype(
-                jnp.bfloat16
+            columns.append(
+                jnp.concatenate(
+                    [
+                        coarse_cos * fine_cos - coarse_sin * fine_sin,
+                        -(coarse_sin * fine_cos + coarse_cos * fine_sin),
+                    ],
+                    axis=0,
+                ).astype(jnp.bfloat16)
             )
-            inverse_ref[NF:, lags] = (-(coarse_sin * fine_cos + coarse_cos * fine_sin)).astype(
-                jnp.bfloat16
+        inverse = jnp.concatenate(columns, axis=1)
+        for minute in range(minutes):
+            pieces[minute].append(
+                jnp.dot(crossed_ref[minute], inverse, preferred_element_type=jnp.float32)
             )
-
-    inverse = inverse_ref[...]
-    own = own_ref[0]
     stacked = None
     current = None
     for minute in range(minutes):
-        correlation = jnp.dot(crossed_ref[minute], inverse, preferred_element_type=jnp.float32)
+        correlation = jnp.concatenate(pieces[minute], axis=1)
         if stacked is None:
             stacked, current = correlation, correlation
         else:
@@ -138,9 +144,6 @@
                 pl.BlockSpec((minutes, block, width), lambda i, own: (0, i, 0)),
             ] + [pl.BlockSpec(factor.shape, lambda i, own: (0, 0)) for factor in factors],
             out_specs=pl.BlockSpec((block, 128), lambda i, own: (i, 0)),
-            scratch_shapes=[
-                pltpu.VMEM((width, LAGS), jnp.bfloat16),
-            ],
         ),
         out_shape=jax.ShapeDtypeStruct((pair_count, 128), jnp.float32),
         compiler_params=pltpu.CompilerParams(

time: 40.7 us -> 40 us (0.983)
  Pallas kernels: 11.8 us -> 11.1 us
    pallas_call x1, Pallas kernels: 11.8 us -> 11.1 us  [coherence(): pl.pallas_call(coherence_kernel, grid_spec=pltpu.PrefetchScalarGridSpec(n...]
where the time goes in v21:
time: 40 us; the launch traced here: 39.6 us
  starting transfers between devices  11.9 us (30%)
  Pallas kernels  11.1 us (28%)
  other arithmetic  7.99 us (20%)
  matrix products  4.11 us (10%)
  waiting for transfers between devices  3.01 us (8%)
  local copies, waits for them, and re-layouts  1.3 us (3%)
    pallas_call x1, Pallas kernels, coherence(): pl.pallas_call(coherence_kernel, grid_spec=pltpu.PrefetchScalarGridSpec(n...  11.1 us
    ppermute x2, starting transfers between devices, body(): mirrored = lax.ppermute(record, axis_order, route)  5.99 us
    sin x3, other arithmetic, unit_angles(): return (jnp.cos(phase), jnp.sin(phase))  3.4 us
    dot_general x3, matrix products, spectra(): jnp.dot(rows.reshape(minutes * count, NT), forward, preferred_element_typ...  3.08 us
    ppermute x1, starting transfers between devices, body(): lax.ppermute(bundle, 'chan', [(s, s + 1) for s in range(blocks - 1)])  2.55 us
    ppermute x1, waiting for transfers between devices, body(): lax.ppermute(bundle, 'chan', [(s, s - 1) for s in range(1, blocks)])  2.54 us
    another operation x2, other arithmetic  2.33 us
    ppermute x1, starting transfers between devices, body(): lax.ppermute(bundle, 'chan', [(s, s - 1) for s in range(1, blocks)])  2.1 us
  transfers between devices with their start and end apart: 5, of which 2 were waited for; matrix products, arithmetic and copies ran while one was open for 22% of the time, Pallas kernels for 0%

profile of v21, /device:TPU:1, one launch (start us, length us, event | category | flops | bytes accessed | tf_op | source)
XLA Modules:
  0.0 39.6 jit_solution(6012245838018911840)
XLA Ops:
  0.0 0.0 copy-start.1
  0.0 0.0 copy-start.2
  0.0 5.7 %collective-permute-start = (bf16[1,16,1536]{2,1,0:T(8,128)(2,1)}, bf16[1,16,1536]{2,1,0:T(8,128)(2,1)S(1)}, u32[]{:S(2)}, u32[]{:S(2)}) collective-permute-start(bf16[1,16,1536]{2,1,0:T(8,128)(2,1)} %param.3), channel_id=1, source_target_pairs={{0,30},{2,28},{4,26},{6,24},{8,22},{10,20},{12,18},{14,16},{16,14}... | collective-permute-start | bytes 147464 | tf_op jit(solution)/shard_map/ppermute | solution.py:174
  5.7 1.2 %collective-permute-start.1 = (bf16[1,16,1536]{2,1,0:T(8,128)(2,1)}, bf16[1,16,1536]{2,1,0:T(8,128)(2,1)S(1)}, u32[]{:S(2)}, u32[]{:S(2)}) collective-permute-start(bf16[1,16,1536]{2,1,0:T(8,128)(2,1)} %param.3), channel_id=1, source_target_pairs={{0,1},{1,0},{2,3},{3,2},{4,5},{5,4},{6,7},{7,6},{8,9},{9,8},{10,11... | collective-permute-start | bytes 147464 | tf_op jit(solution)/shard_map/ppermute | solution.py:168
  6.9 0.3 collective-permute-start.2
  7.2 1.6 %fusion.17 = (f32[128,768]{1,0:T(8,128)S(1)}, f32[128,768]{1,0:T(8,128)S(1)}) fusion(), kind=kLoop, calls=%fused_computation.37 | loop fusion | flops 884736 | bytes 786432 | tf_op jit(solution)/shard_map/sin | solution.py:20
  8.8 0.2 fusion.30
  9.1 1.6 %sine_multiply_fusion = (f32[768,8]{1,0:T(8,128)S(1)}, f32[768,8]{1,0:T(8,128)S(1)}) fusion(f32[768]{0:T(1024)S(1)} %fusion.33, s32[8]{0:T(128)S(1)} %iota_add_fusion), kind=kLoop, calls=%fused_computation.23 | loop fusion | flops 67584 | bytes 52256 | tf_op jit(solution)/shard_map/mul | solution.py:41
  10.7 1.4 %subtract_convert_fusion = (bf16[12,128,768]{2,1,0:T(8,128)(2,1)S(1)}, bf16[12,128,768]{2,1,0:T(8,128)(2,1)S(1)}) fusion(f32[128,768]{1,0:T(8,128)S(1)} %get-tuple-element.21, f32[12,768]{1,0:T(8,128)S(1)} %get-tuple-element.23, f32[128,768]{1,0:T(8,128)S(1)} %get-tuple-element.22, f32[12,768]{1,0:T(8,128)S(1)} %get-tuple-element.24), kind=kLoop, calls=%fused_computation.2 | loop fusion | flops 10616832 | bytes 5578752 | tf_op jit(solution)/shard_map/convert.8
  12.1 0.0 copy-done.2
  12.1 1.6 %fusion.11 = (f32[768,128]{1,0:T(8,128)S(1)}, f32[768,128]{1,0:T(8,128)S(1)}) fusion(), kind=kLoop, calls=%fused_computation.21 | loop fusion | flops 884736 | bytes 786432 | tf_op jit(solution)/shard_map/sin | solution.py:20
  13.8 0.0 collective-permute-done
  13.8 0.0 collective-permute-done.1
  13.8 0.5 %collective-permute-done.2 = bf16[1,16,1536]{2,1,0:T(8,128)(2,1)S(1)} collective-permute-done((bf16[1,16,1536]{2,1,0:T(8,128)(2,1)}, bf16[1,16,1536]{2,1,0:T(8,128)(2,1)S(1)}, u32[]{:S(2)}, u32[]{:S(2)}) %collective-permute-start.2) | collective-permute-done | bytes 49184 | tf_op jit(solution)/shard_map/ppermute | solution.py:174
  14.2 0.0 copy-done.1
  14.3 2.5 %collective-permute-start.3 = (bf16[2,32,1536]{2,1,0:T(8,128)(2,1)S(1)}, bf16[2,32,1536]{2,1,0:T(8,128)(2,1)S(1)}, u32[]{:S(2)}, u32[]{:S(2)}) collective-permute-start(bf16[2,32,1536]{2,1,0:T(8,128)(2,1)S(1)} %maximum_maximum_fusion), channel_id=1, source_target_pairs={{0,2},{2,4},{4,6},{6,8},{8,10},{10,12},{12,14},{14,16},{16,18},{18... | collective-permute-start | bytes 589832 | tf_op jit(solution)/shard_map/ppermute | solution.py:177
  16.8 2.1 %collective-permute-start.4 = (bf16[2,32,1536]{2,1,0:T(8,128)(2,1)S(1)}, bf16[2,32,1536]{2,1,0:T(8,128)(2,1)S(1)}, u32[]{:S(2)}, u32[]{:S(2)}) collective-permute-start(bf16[2,32,1536]{2,1,0:T(8,128)(2,1)S(1)} %maximum_maximum_fusion), channel_id=1, source_target_pairs={{2,0},{4,2},{6,4},{8,6},{10,8},{12,10},{14,12},{16,14},{18,16},{20... | collective-permute-start | bytes 589832 | tf_op jit(solution)/shard_map/ppermute | solution.py:178
  18.9 1.0 %multiply_reduce_fusion.2 = (f32[64]{0:T(128)S(1)}, f32[64,1536]{1,0:T(8,128)S(1)}) fusion(bf16[64,1536]{1,0:T(8,128)(2,1)S(1)} %bitcast.49, bf16[1536,768]{1,0:T(8,128)(2,1)S(1)} %bitcast.41, bf16[1536,768]{1,0:T(8,128)(2,1)S(1)} %bitcast.38), kind=kOutput, calls=%fused_computation.33 | convolution fusion | flops 311623616 | bytes 5308672 | tf_op jit(solution)/shard_map/dot_general | solution.py:183
  20.0 0.1 divide_convert_fusion.2
  20.1 0.0 collective-permute-done.3
  20.1 1.0 %multiply_reduce_fusion.1 = (f32[64]{0:T(128)S(1)}, f32[64,1536]{1,0:T(8,128)S(1)}) fusion(bf16[64,1536]{1,0:T(8,128)(2,1)S(1)} %bitcast.52, bf16[1536,768]{1,0:T(8,128)(2,1)S(1)} %bitcast.42, bf16[1536,768]{1,0:T(8,128)(2,1)S(1)} %bitcast.39), kind=kOutput, calls=%fused_computation.31 | convolution fusion | flops 311623616 | bytes 5308672 | tf_op jit(solution)/shard_map/dot_general | solution.py:183
  21.1 0.1 divide_convert_fusion.1
  21.3 2.5 %collective-permute-done.4 = bf16[2,32,1536]{2,1,0:T(8,128)(2,1)S(1)} collective-permute-done((bf16[2,32,1536]{2,1,0:T(8,128)(2,1)S(1)}, bf16[2,32,1536]{2,1,0:T(8,128)(2,1)S(1)}, u32[]{:S(2)}, u32[]{:S(2)}) %collective-permute-start.4) | collective-permute-done | bytes 196640 | tf_op jit(solution)/shard_map/ppermute | solution.py:178
  23.8 1.0 %multiply_reduce_fusion = (f32[64]{0:T(128)S(1)}, f32[64,1536]{1,0:T(8,128)S(1)}) fusion(bf16[64,1536]{1,0:T(8,128)(2,1)S(1)} %bitcast.51, bf16[1536,768]{1,0:T(8,128)(2,1)S(1)} %bitcast.43, bf16[1536,768]{1,0:T(8,128)(2,1)S(1)} %bitcast.40), kind=kOutput, calls=%fused_computation.29 | convolution fusion | flops 311623616 | bytes 5308672 | tf_op jit(solution)/shard_map/dot_general | solution.py:183
  24.9 0.1 divide_convert_fusion
  25.1 1.0 %fusion.23 = f32[2,1536,512]{1,2,0:T(8,128)S(1)} fusion(bf16[2,96,1536]{2,1,0:T(8,128)(2,1)S(1)} %slice_dynamic-update-slice_fusion, s32[512]{0:T(512)S(1)} %bitcast.50), kind=kOutput, calls=%fused_computation.45 | convolution fusion | flops 302039040 | bytes 6883328 | tf_op jit(solution)/shard_map/pq,mqk->mpk/dot_general | solution.py:216
  26.1 0.9 %add_convert_fusion = (bf16[2,2,256,768]{3,2,1,0:T(8,128)(2,1)S(1)}, bf16[2,2,256,768]{3,2,1,0:T(8,128)(2,1)S(1)}) fusion(f32[2,2,256,1536]{3,2,1,0:T(8,128)S(1)} %bitcast.35, f32[2,2,768]{2,1,0:T(2,128)S(1)} %get-tuple-element.12, f32[2,2,768]{2,1,0:T(2,128)S(1)} %get-tuple-element.11), kind=kLoop, calls=%fused_computation.5 | loop fusion | flops 6291456 | bytes 9461760 | tf_op jit(solution)/shard_map/convert.4
  27.1 0.0 copy-start
  27.1 0.2 pad_maximum_fusion.1.crossed_ref
  27.3 0.5 %copy-done = s32[4,1024]{1,0:T(4,128)S(1)} copy-done((s32[4,1024]{1,0:T(4,128)S(1)}, s32[4,1024]{1,0:T(4,128)}, u32[]{:S(2)}) %copy-start) | copy-done | bytes 16408
  27.8 11.1 %shard_map.37 = f32[512,128]{1,0:T(8,128)S(1)} custom-call(s32[1]{0:T(128)} %constant.28.clone.1.own_ref, s32[4,1024]{1,0:T(4,128)S(1)} %copy-done, bf16[2,512,1536]{2,1,0:T(8,128)(2,1)S(1)} %pad_maximum_fusion.1.crossed_ref, f32[768,8]{1,0:T(8,128)S(1)} %get-tuple-element.14.wcos_ref, f32[768,8]{1,0:T(8,128)S(1)} %get-tuple-element.13.wsin_ref, ...), custom_call_target="tpu_custom_call" | custom-call | tf_op jit(solution)/shard_map/pallas_call | solution.py:137
  38.9 0.7 %copy.7 = f32[1,4,2,256]{3,2,1,0:T(2,128)} copy(f32[1,4,2,256]{1,3,2,0:T(8,128)S(1)} %bitcast.34) | data formatting | bytes 16384 | tf_op jit(solution)/shard_map/reshape | solution.py:224
  (17 shorter events, 0.2 us)
Async XLA Ops:
  0.0 14.2 %copy-start.1 = (bf16[1,16,1536]{2,1,0:T(8,128)(2,1)S(1)}, bf16[1,16,1536]{2,1,0:T(8,128)(2,1)}, u32[]{:S(2)}) copy-start(bf16[1,16,1536]{2,1,0:T(8,128)(2,1)} %param.3) | copy-start | bytes 147460
  0.0 12.1 %copy-start.2 = (s32[2,256]{1,0:T(2,128)S(1)}, s32[2,256]{1,0:T(2,128)}, u32[]{:S(2)}) copy-start(s32[2,256]{1,0:T(2,128)} %param.4) | copy-start | bytes 6148
  0.0 13.7 %collective-permute-start = (bf16[1,16,1536]{2,1,0:T(8,128)(2,1)}, bf16[1,16,1536]{2,1,0:T(8,128)(2,1)S(1)}, u32[]{:S(2)}, u32[]{:S(2)}) collective-permute-start(bf16[1,16,1536]{2,1,0:T(8,128)(2,1)} %param.3), channel_id=1, source_target_pairs={{0,30},{2,28},{4,26},{6,24},{8,22},{10,20},{12,18},{14,16},{16,14}... | collective-permute-start | bytes 147464 | tf_op jit(solution)/shard_map/ppermute | solution.py:174
  5.7 8.1 %collective-permute-start.1 = (bf16[1,16,1536]{2,1,0:T(8,128)(2,1)}, bf16[1,16,1536]{2,1,0:T(8,128)(2,1)S(1)}, u32[]{:S(2)}, u32[]{:S(2)}) collective-permute-start(bf16[1,16,1536]{2,1,0:T(8,128)(2,1)} %param.3), channel_id=1, source_target_pairs={{0,1},{1,0},{2,3},{3,2},{4,5},{5,4},{6,7},{7,6},{8,9},{9,8},{10,11... | collective-permute-start | bytes 147464 | tf_op jit(solution)/shard_map/ppermute | solution.py:168
  6.9 7.4 %collective-permute-start.2 = (bf16[1,16,1536]{2,1,0:T(8,128)(2,1)}, bf16[1,16,1536]{2,1,0:T(8,128)(2,1)S(1)}, u32[]{:S(2)}, u32[]{:S(2)}) collective-permute-start(bf16[1,16,1536]{2,1,0:T(8,128)(2,1)} %param.3), channel_id=1, source_target_pairs={{0,31},{2,29},{4,27},{6,25},{8,23},{10,21},{12,19},{14,17},{16,15}... | collective-permute-start | bytes 147464 | tf_op jit(solution)/shard_map/ppermute | solution.py:174
  14.3 5.8 %collective-permute-start.3 = (bf16[2,32,1536]{2,1,0:T(8,128)(2,1)S(1)}, bf16[2,32,1536]{2,1,0:T(8,128)(2,1)S(1)}, u32[]{:S(2)}, u32[]{:S(2)}) collective-permute-start(bf16[2,32,1536]{2,1,0:T(8,128)(2,1)S(1)} %maximum_maximum_fusion), channel_id=1, source_target_pairs={{0,2},{2,4},{4,6},{6,8},{8,10},{10,12},{12,14},{14,16},{16,18},{18... | collective-permute-start | bytes 589832 | tf_op jit(solution)/shard_map/ppermute | solution.py:177
  16.8 7.0 %collective-permute-start.4 = (bf16[2,32,1536]{2,1,0:T(8,128)(2,1)S(1)}, bf16[2,32,1536]{2,1,0:T(8,128)(2,1)S(1)}, u32[]{:S(2)}, u32[]{:S(2)}) collective-permute-start(bf16[2,32,1536]{2,1,0:T(8,128)(2,1)S(1)} %maximum_maximum_fusion), channel_id=1, source_target_pairs={{2,0},{4,2},{6,4},{8,6},{10,8},{12,10},{14,12},{16,14},{18,16},{20... | collective-permute-start | bytes 589832 | tf_op jit(solution)/shard_map/ppermute | solution.py:178
  27.1 0.7 %copy-start = (s32[4,1024]{1,0:T(4,128)S(1)}, s32[4,1024]{1,0:T(4,128)}, u32[]{:S(2)}) copy-start(s32[4,1024]{1,0:T(4,128)} %stretch_ref.1) | copy-start | bytes 49156

commit v22 on v21

--- a/solution.py
+++ b/solution.py
@@ -143,14 +143,14 @@
                 pl.BlockSpec(stretch_index.shape, lambda i, own: (0, 0)),
                 pl.BlockSpec((minutes, block, width), lambda i, own: (0, i, 0)),
             ] + [pl.BlockSpec(factor.shape, lambda i, own: (0, 0)) for factor in factors],
-            out_specs=pl.BlockSpec((block, 128), lambda i, own: (i, 0)),
+            out_specs=pl.BlockSpec((block, stretch_count), lambda i, own: (i, 0)),
         ),
-        out_shape=jax.ShapeDtypeStruct((pair_count, 128), jnp.float32),
+        out_shape=jax.ShapeDtypeStruct((pair_count, stretch_count), jnp.float32),
         compiler_params=pltpu.CompilerParams(
             dimension_semantics=("arbitrary",), vmem_limit_bytes=48 << 20
         ),
     )(own, stretch_index, crossed, *factors)
-    return out[:, :stretch_count].T
+    return out.T
 
 
 def body(axis_order, record, pairs, stretch_index):

time: 40 us -> 40 us (level)
  no operation moved by 1% of the time
where the time goes in v22:
time: 40 us; the launch traced here: 39.6 us
  starting transfers between devices  11.9 us (30%)
  Pallas kernels  11.1 us (28%)
  other arithmetic  7.99 us (20%)
  matrix products  4.11 us (10%)
  waiting for transfers between devices  3.01 us (8%)
  local copies, waits for them, and re-layouts  1.3 us (3%)
    pallas_call x1, Pallas kernels, coherence(): pl.pallas_call(coherence_kernel, grid_spec=pltpu.PrefetchScalarGridSpec(n...  11.1 us
    ppermute x2, starting transfers between devices, body(): mirrored = lax.ppermute(record, axis_order, route)  5.99 us
    sin x3, other arithmetic, unit_angles(): return (jnp.cos(phase), jnp.sin(phase))  3.4 us
    dot_general x3, matrix products, spectra(): jnp.dot(rows.reshape(minutes * count, NT), forward, preferred_element_typ...  3.08 us
    ppermute x1, starting transfers between devices, body(): lax.ppermute(bundle, 'chan', [(s, s + 1) for s in range(blocks - 1)])  2.55 us
    ppermute x1, waiting for transfers between devices, body(): lax.ppermute(bundle, 'chan', [(s, s - 1) for s in range(1, blocks)])  2.54 us
    another operation x2, other arithmetic  2.33 us
    ppermute x1, starting transfers between devices, body(): lax.ppermute(bundle, 'chan', [(s, s - 1) for s in range(1, blocks)])  2.1 us
  transfers between devices with their start and end apart: 5, of which 2 were waited for; matrix products, arithmetic and copies ran while one was open for 22% of the time, Pallas kernels for 0%

profile of v22, /device:TPU:1, one launch (start us, length us, event | category | flops | bytes accessed | tf_op | source)
XLA Modules:
  0.0 39.6 jit_solution(17786939851865073427)
XLA Ops:
  0.0 0.0 copy-start.1
  0.0 0.0 copy-start.2
  0.0 5.7 %collective-permute-start = (bf16[1,16,1536]{2,1,0:T(8,128)(2,1)}, bf16[1,16,1536]{2,1,0:T(8,128)(2,1)S(1)}, u32[]{:S(2)}, u32[]{:S(2)}) collective-permute-start(bf16[1,16,1536]{2,1,0:T(8,128)(2,1)} %param.3), channel_id=1, source_target_pairs={{0,30},{2,28},{4,26},{6,24},{8,22},{10,20},{12,18},{14,16},{16,14}... | collective-permute-start | bytes 147464 | tf_op jit(solution)/shard_map/ppermute | solution.py:174
  5.7 1.2 %collective-permute-start.1 = (bf16[1,16,1536]{2,1,0:T(8,128)(2,1)}, bf16[1,16,1536]{2,1,0:T(8,128)(2,1)S(1)}, u32[]{:S(2)}, u32[]{:S(2)}) collective-permute-start(bf16[1,16,1536]{2,1,0:T(8,128)(2,1)} %param.3), channel_id=1, source_target_pairs={{0,1},{1,0},{2,3},{3,2},{4,5},{5,4},{6,7},{7,6},{8,9},{9,8},{10,11... | collective-permute-start | bytes 147464 | tf_op jit(solution)/shard_map/ppermute | solution.py:168
  6.9 0.3 collective-permute-start.2
  7.2 1.6 %fusion.17 = (f32[128,768]{1,0:T(8,128)S(1)}, f32[128,768]{1,0:T(8,128)S(1)}) fusion(), kind=kLoop, calls=%fused_computation.37 | loop fusion | flops 884736 | bytes 786432 | tf_op jit(solution)/shard_map/sin | solution.py:20
  8.8 0.2 fusion.30
  9.1 1.6 %sine_multiply_fusion = (f32[768,8]{1,0:T(8,128)S(1)}, f32[768,8]{1,0:T(8,128)S(1)}) fusion(f32[768]{0:T(1024)S(1)} %fusion.33, s32[8]{0:T(128)S(1)} %iota_add_fusion), kind=kLoop, calls=%fused_computation.23 | loop fusion | flops 67584 | bytes 52256 | tf_op jit(solution)/shard_map/mul | solution.py:41
  10.7 1.4 %subtract_convert_fusion = (bf16[12,128,768]{2,1,0:T(8,128)(2,1)S(1)}, bf16[12,128,768]{2,1,0:T(8,128)(2,1)S(1)}) fusion(f32[128,768]{1,0:T(8,128)S(1)} %get-tuple-element.21, f32[12,768]{1,0:T(8,128)S(1)} %get-tuple-element.23, f32[128,768]{1,0:T(8,128)S(1)} %get-tuple-element.22, f32[12,768]{1,0:T(8,128)S(1)} %get-tuple-element.24), kind=kLoop, calls=%fused_computation.2 | loop fusion | flops 10616832 | bytes 5578752 | tf_op jit(solution)/shard_map/convert.8
  12.1 0.0 copy-done.2
  12.1 1.6 %fusion.11 = (f32[768,128]{1,0:T(8,128)S(1)}, f32[768,128]{1,0:T(8,128)S(1)}) fusion(), kind=kLoop, calls=%fused_computation.21 | loop fusion | flops 884736 | bytes 786432 | tf_op jit(solution)/shard_map/sin | solution.py:20
  13.8 0.0 collective-permute-done
  13.8 0.0 collective-permute-done.1
  13.8 0.5 %collective-permute-done.2 = bf16[1,16,1536]{2,1,0:T(8,128)(2,1)S(1)} collective-permute-done((bf16[1,16,1536]{2,1,0:T(8,128)(2,1)}, bf16[1,16,1536]{2,1,0:T(8,128)(2,1)S(1)}, u32[]{:S(2)}, u32[]{:S(2)}) %collective-permute-start.2) | collective-permute-done | bytes 49184 | tf_op jit(solution)/shard_map/ppermute | solution.py:174
  14.2 0.0 copy-done.1
  14.3 2.5 %collective-permute-start.3 = (bf16[2,32,1536]{2,1,0:T(8,128)(2,1)S(1)}, bf16[2,32,1536]{2,1,0:T(8,128)(2,1)S(1)}, u32[]{:S(2)}, u32[]{:S(2)}) collective-permute-start(bf16[2,32,1536]{2,1,0:T(8,128)(2,1)S(1)} %maximum_maximum_fusion), channel_id=1, source_target_pairs={{0,2},{2,4},{4,6},{6,8},{8,10},{10,12},{12,14},{14,16},{16,18},{18... | collective-permute-start | bytes 589832 | tf_op jit(solution)/shard_map/ppermute | solution.py:177
  16.8 2.1 %collective-permute-start.4 = (bf16[2,32,1536]{2,1,0:T(8,128)(2,1)S(1)}, bf16[2,32,1536]{2,1,0:T(8,128)(2,1)S(1)}, u32[]{:S(2)}, u32[]{:S(2)}) collective-permute-start(bf16[2,32,1536]{2,1,0:T(8,128)(2,1)S(1)} %maximum_maximum_fusion), channel_id=1, source_target_pairs={{2,0},{4,2},{6,4},{8,6},{10,8},{12,10},{14,12},{16,14},{18,16},{20... | collective-permute-start | bytes 589832 | tf_op jit(solution)/shard_map/ppermute | solution.py:178
  18.9 1.0 %multiply_reduce_fusion.2 = (f32[64]{0:T(128)S(1)}, f32[64,1536]{1,0:T(8,128)S(1)}) fusion(bf16[64,1536]{1,0:T(8,128)(2,1)S(1)} %bitcast.48, bf16[1536,768]{1,0:T(8,128)(2,1)S(1)} %bitcast.40, bf16[1536,768]{1,0:T(8,128)(2,1)S(1)} %bitcast.37), kind=kOutput, calls=%fused_computation.33 | convolution fusion | flops 311623616 | bytes 5308672 | tf_op jit(solution)/shard_map/dot_general | solution.py:183
  20.0 0.1 divide_convert_fusion.2
  20.1 0.0 collective-permute-done.3
  20.1 1.0 %multiply_reduce_fusion.1 = (f32[64]{0:T(128)S(1)}, f32[64,1536]{1,0:T(8,128)S(1)}) fusion(bf16[64,1536]{1,0:T(8,128)(2,1)S(1)} %bitcast.51, bf16[1536,768]{1,0:T(8,128)(2,1)S(1)} %bitcast.41, bf16[1536,768]{1,0:T(8,128)(2,1)S(1)} %bitcast.38), kind=kOutput, calls=%fused_computation.31 | convolution fusion | flops 311623616 | bytes 5308672 | tf_op jit(solution)/shard_map/dot_general | solution.py:183
  21.1 0.1 divide_convert_fusion.1
  21.3 2.5 %collective-permute-done.4 = bf16[2,32,1536]{2,1,0:T(8,128)(2,1)S(1)} collective-permute-done((bf16[2,32,1536]{2,1,0:T(8,128)(2,1)S(1)}, bf16[2,32,1536]{2,1,0:T(8,128)(2,1)S(1)}, u32[]{:S(2)}, u32[]{:S(2)}) %collective-permute-start.4) | collective-permute-done | bytes 196640 | tf_op jit(solution)/shard_map/ppermute | solution.py:178
  23.8 1.0 %multiply_reduce_fusion = (f32[64]{0:T(128)S(1)}, f32[64,1536]{1,0:T(8,128)S(1)}) fusion(bf16[64,1536]{1,0:T(8,128)(2,1)S(1)} %bitcast.50, bf16[1536,768]{1,0:T(8,128)(2,1)S(1)} %bitcast.42, bf16[1536,768]{1,0:T(8,128)(2,1)S(1)} %bitcast.39), kind=kOutput, calls=%fused_computation.29 | convolution fusion | flops 311623616 | bytes 5308672 | tf_op jit(solution)/shard_map/dot_general | solution.py:183
  24.9 0.1 divide_convert_fusion
  25.1 1.0 %fusion.23 = f32[2,1536,512]{1,2,0:T(8,128)S(1)} fusion(bf16[2,96,1536]{2,1,0:T(8,128)(2,1)S(1)} %slice_dynamic-update-slice_fusion, s32[512]{0:T(512)S(1)} %bitcast.49), kind=kOutput, calls=%fused_computation.45 | convolution fusion | flops 302039040 | bytes 6883328 | tf_op jit(solution)/shard_map/pq,mqk->mpk/dot_general | solution.py:216
  26.1 0.9 %add_convert_fusion = (bf16[2,2,256,768]{3,2,1,0:T(8,128)(2,1)S(1)}, bf16[2,2,256,768]{3,2,1,0:T(8,128)(2,1)S(1)}) fusion(f32[2,2,256,1536]{3,2,1,0:T(8,128)S(1)} %bitcast.34, f32[2,2,768]{2,1,0:T(2,128)S(1)} %get-tuple-element.12, f32[2,2,768]{2,1,0:T(2,128)S(1)} %get-tuple-element.11), kind=kLoop, calls=%fused_computation.5 | loop fusion | flops 6291456 | bytes 9461760 | tf_op jit(solution)/shard_map/convert.4
  27.1 0.0 copy-start
  27.1 0.2 pad_maximum_fusion.1.crossed_ref
  27.3 0.5 %copy-done = s32[4,1024]{1,0:T(4,128)S(1)} copy-done((s32[4,1024]{1,0:T(4,128)S(1)}, s32[4,1024]{1,0:T(4,128)}, u32[]{:S(2)}) %copy-start) | copy-done | bytes 16408
  27.8 11.1 %shard_map.37 = f32[512,4]{1,0:T(8,128)S(1)} custom-call(s32[1]{0:T(128)} %constant.28.clone.1.own_ref, s32[4,1024]{1,0:T(4,128)S(1)} %copy-done, bf16[2,512,1536]{2,1,0:T(8,128)(2,1)S(1)} %pad_maximum_fusion.1.crossed_ref, f32[768,8]{1,0:T(8,128)S(1)} %get-tuple-element.14.wcos_ref, f32[768,8]{1,0:T(8,128)S(1)} %get-tuple-element.13.wsin_ref, ...), custom_call_target="tpu_custom_call" | custom-call | tf_op jit(solution)/shard_map/pallas_call | solution.py:137
  38.9 0.7 %copy.7 = f32[1,4,2,256]{3,2,1,0:T(2,128)} copy(f32[1,4,2,256]{1,3,2,0:T(8,128)S(1)} %bitcast.33) | data formatting | bytes 16384 | tf_op jit(solution)/shard_map/reshape | solution.py:224
  (17 shorter events, 0.2 us)
Async XLA Ops:
  0.0 14.2 %copy-start.1 = (bf16[1,16,1536]{2,1,0:T(8,128)(2,1)S(1)}, bf16[1,16,1536]{2,1,0:T(8,128)(2,1)}, u32[]{:S(2)}) copy-start(bf16[1,16,1536]{2,1,0:T(8,128)(2,1)} %param.3) | copy-start | bytes 147460
  0.0 12.1 %copy-start.2 = (s32[2,256]{1,0:T(2,128)S(1)}, s32[2,256]{1,0:T(2,128)}, u32[]{:S(2)}) copy-start(s32[2,256]{1,0:T(2,128)} %param.4) | copy-start | bytes 6148
  0.0 13.7 %collective-permute-start = (bf16[1,16,1536]{2,1,0:T(8,128)(2,1)}, bf16[1,16,1536]{2,1,0:T(8,128)(2,1)S(1)}, u32[]{:S(2)}, u32[]{:S(2)}) collective-permute-start(bf16[1,16,1536]{2,1,0:T(8,128)(2,1)} %param.3), channel_id=1, source_target_pairs={{0,30},{2,28},{4,26},{6,24},{8,22},{10,20},{12,18},{14,16},{16,14}... | collective-permute-start | bytes 147464 | tf_op jit(solution)/shard_map/ppermute | solution.py:174
  5.7 8.1 %collective-permute-start.1 = (bf16[1,16,1536]{2,1,0:T(8,128)(2,1)}, bf16[1,16,1536]{2,1,0:T(8,128)(2,1)S(1)}, u32[]{:S(2)}, u32[]{:S(2)}) collective-permute-start(bf16[1,16,1536]{2,1,0:T(8,128)(2,1)} %param.3), channel_id=1, source_target_pairs={{0,1},{1,0},{2,3},{3,2},{4,5},{5,4},{6,7},{7,6},{8,9},{9,8},{10,11... | collective-permute-start | bytes 147464 | tf_op jit(solution)/shard_map/ppermute | solution.py:168
  6.9 7.4 %collective-permute-start.2 = (bf16[1,16,1536]{2,1,0:T(8,128)(2,1)}, bf16[1,16,1536]{2,1,0:T(8,128)(2,1)S(1)}, u32[]{:S(2)}, u32[]{:S(2)}) collective-permute-start(bf16[1,16,1536]{2,1,0:T(8,128)(2,1)} %param.3), channel_id=1, source_target_pairs={{0,31},{2,29},{4,27},{6,25},{8,23},{10,21},{12,19},{14,17},{16,15}... | collective-permute-start | bytes 147464 | tf_op jit(solution)/shard_map/ppermute | solution.py:174
  14.3 5.8 %collective-permute-start.3 = (bf16[2,32,1536]{2,1,0:T(8,128)(2,1)S(1)}, bf16[2,32,1536]{2,1,0:T(8,128)(2,1)S(1)}, u32[]{:S(2)}, u32[]{:S(2)}) collective-permute-start(bf16[2,32,1536]{2,1,0:T(8,128)(2,1)S(1)} %maximum_maximum_fusion), channel_id=1, source_target_pairs={{0,2},{2,4},{4,6},{6,8},{8,10},{10,12},{12,14},{14,16},{16,18},{18... | collective-permute-start | bytes 589832 | tf_op jit(solution)/shard_map/ppermute | solution.py:177
  16.8 7.0 %collective-permute-start.4 = (bf16[2,32,1536]{2,1,0:T(8,128)(2,1)S(1)}, bf16[2,32,1536]{2,1,0:T(8,128)(2,1)S(1)}, u32[]{:S(2)}, u32[]{:S(2)}) collective-permute-start(bf16[2,32,1536]{2,1,0:T(8,128)(2,1)S(1)} %maximum_maximum_fusion), channel_id=1, source_target_pairs={{2,0},{4,2},{6,4},{8,6},{10,8},{12,10},{14,12},{16,14},{18,16},{20... | collective-permute-start | bytes 589832 | tf_op jit(solution)/shard_map/ppermute | solution.py:178
  27.1 0.7 %copy-start = (s32[4,1024]{1,0:T(4,128)S(1)}, s32[4,1024]{1,0:T(4,128)}, u32[]{:S(2)}) copy-start(s32[4,1024]{1,0:T(4,128)} %stretch_ref.1) | copy-start | bytes 49156

commit v23 on v22

--- a/solution.py
+++ b/solution.py
@@ -75,6 +75,8 @@
     fine_sin = fsin_ref[...]
     own = own_ref[0]
     pieces = [[] for _ in range(minutes)]
+    block = crossed_ref.shape[1]
+    all_rows = crossed_ref[...].reshape(minutes * block, crossed_ref.shape[2])
     for pair_group in range(groups // 2):
         columns = []
         for group in (2 * pair_group, 2 * pair_group + 1):
@@ -90,10 +92,9 @@
                 ).astype(jnp.bfloat16)
             )
         inverse = jnp.concatenate(columns, axis=1)
+        product = jnp.dot(all_rows, inverse, preferred_element_type=jnp.float32)
         for minute in range(minutes):
-            pieces[minute].append(
-                jnp.dot(crossed_ref[minute], inverse, preferred_element_type=jnp.float32)
-            )
+            pieces[minute].append(product[minute * block:(minute + 1) * block])
     stacked = None
     current = None
     for minute in range(minutes):

time: 40 us -> 40.1 us (level)
  no operation moved by 1% of the time
where the time goes in v23:
time: 40.1 us; the launch traced here: 39.7 us
  starting transfers between devices  11.9 us (30%)
  Pallas kernels  11.2 us (28%)
  other arithmetic  7.99 us (20%)
  matrix products  4.11 us (10%)
  waiting for transfers between devices  3.01 us (8%)
  local copies, waits for them, and re-layouts  1.3 us (3%)
    pallas_call x1, Pallas kernels, coherence(): pl.pallas_call(coherence_kernel, grid_spec=pltpu.PrefetchScalarGridSpec(n...  11.2 us
    ppermute x2, starting transfers between devices, body(): mirrored = lax.ppermute(record, axis_order, route)  5.99 us
    sin x3, other arithmetic, unit_angles(): return (jnp.cos(phase), jnp.sin(phase))  3.4 us
    dot_general x3, matrix products, spectra(): jnp.dot(rows.reshape(minutes * count, NT), forward, preferred_element_typ...  3.08 us
    ppermute x1, starting transfers between devices, body(): lax.ppermute(bundle, 'chan', [(s, s + 1) for s in range(blocks - 1)])  2.55 us
    ppermute x1, waiting for transfers between devices, body(): lax.ppermute(bundle, 'chan', [(s, s - 1) for s in range(1, blocks)])  2.54 us
    another operation x2, other arithmetic  2.33 us
    ppermute x1, starting transfers between devices, body(): lax.ppermute(bundle, 'chan', [(s, s - 1) for s in range(1, blocks)])  2.1 us
  transfers between devices with their start and end apart: 5, of which 2 were waited for; matrix products, arithmetic and copies ran while one was open for 22% of the time, Pallas kernels for 0%

profile of v23, /device:TPU:1, one launch (start us, length us, event | category | flops | bytes accessed | tf_op | source)
XLA Modules:
  0.0 39.7 jit_solution(8968261850863302406)
XLA Ops:
  0.0 0.0 copy-start.1
  0.0 0.0 copy-start.2
  0.0 5.7 %collective-permute-start = (bf16[1,16,1536]{2,1,0:T(8,128)(2,1)}, bf16[1,16,1536]{2,1,0:T(8,128)(2,1)S(1)}, u32[]{:S(2)}, u32[]{:S(2)}) collective-permute-start(bf16[1,16,1536]{2,1,0:T(8,128)(2,1)} %param.3), channel_id=1, source_target_pairs={{0,30},{2,28},{4,26},{6,24},{8,22},{10,20},{12,18},{14,16},{16,14}... | collective-permute-start | bytes 147464 | tf_op jit(solution)/shard_map/ppermute | solution.py:175
  5.7 1.2 %collective-permute-start.1 = (bf16[1,16,1536]{2,1,0:T(8,128)(2,1)}, bf16[1,16,1536]{2,1,0:T(8,128)(2,1)S(1)}, u32[]{:S(2)}, u32[]{:S(2)}) collective-permute-start(bf16[1,16,1536]{2,1,0:T(8,128)(2,1)} %param.3), channel_id=1, source_target_pairs={{0,1},{1,0},{2,3},{3,2},{4,5},{5,4},{6,7},{7,6},{8,9},{9,8},{10,11... | collective-permute-start | bytes 147464 | tf_op jit(solution)/shard_map/ppermute | solution.py:169
  6.9 0.3 collective-permute-start.2
  7.2 1.6 %fusion.17 = (f32[128,768]{1,0:T(8,128)S(1)}, f32[128,768]{1,0:T(8,128)S(1)}) fusion(), kind=kLoop, calls=%fused_computation.37 | loop fusion | flops 884736 | bytes 786432 | tf_op jit(solution)/shard_map/sin | solution.py:20
  8.8 0.2 fusion.30
  9.1 1.6 %sine_multiply_fusion = (f32[768,8]{1,0:T(8,128)S(1)}, f32[768,8]{1,0:T(8,128)S(1)}) fusion(f32[768]{0:T(1024)S(1)} %fusion.33, s32[8]{0:T(128)S(1)} %iota_add_fusion), kind=kLoop, calls=%fused_computation.23 | loop fusion | flops 67584 | bytes 52256 | tf_op jit(solution)/shard_map/mul | solution.py:41
  10.7 1.4 %subtract_convert_fusion = (bf16[12,128,768]{2,1,0:T(8,128)(2,1)S(1)}, bf16[12,128,768]{2,1,0:T(8,128)(2,1)S(1)}) fusion(f32[128,768]{1,0:T(8,128)S(1)} %get-tuple-element.21, f32[12,768]{1,0:T(8,128)S(1)} %get-tuple-element.23, f32[128,768]{1,0:T(8,128)S(1)} %get-tuple-element.22, f32[12,768]{1,0:T(8,128)S(1)} %get-tuple-element.24), kind=kLoop, calls=%fused_computation.2 | loop fusion | flops 10616832 | bytes 5578752 | tf_op jit(solution)/shard_map/convert.8
  12.1 0.0 copy-done.2
  12.1 1.6 %fusion.11 = (f32[768,128]{1,0:T(8,128)S(1)}, f32[768,128]{1,0:T(8,128)S(1)}) fusion(), kind=kLoop, calls=%fused_computation.21 | loop fusion | flops 884736 | bytes 786432 | tf_op jit(solution)/shard_map/sin | solution.py:20
  13.8 0.0 collective-permute-done
  13.8 0.0 collective-permute-done.1
  13.8 0.5 %collective-permute-done.2 = bf16[1,16,1536]{2,1,0:T(8,128)(2,1)S(1)} collective-permute-done((bf16[1,16,1536]{2,1,0:T(8,128)(2,1)}, bf16[1,16,1536]{2,1,0:T(8,128)(2,1)S(1)}, u32[]{:S(2)}, u32[]{:S(2)}) %collective-permute-start.2) | collective-permute-done | bytes 49184 | tf_op jit(solution)/shard_map/ppermute | solution.py:175
  14.2 0.0 copy-done.1
  14.3 2.5 %collective-permute-start.3 = (bf16[2,32,1536]{2,1,0:T(8,128)(2,1)S(1)}, bf16[2,32,1536]{2,1,0:T(8,128)(2,1)S(1)}, u32[]{:S(2)}, u32[]{:S(2)}) collective-permute-start(bf16[2,32,1536]{2,1,0:T(8,128)(2,1)S(1)} %maximum_maximum_fusion), channel_id=1, source_target_pairs={{0,2},{2,4},{4,6},{6,8},{8,10},{10,12},{12,14},{14,16},{16,18},{18... | collective-permute-start | bytes 589832 | tf_op jit(solution)/shard_map/ppermute | solution.py:178
  16.8 2.1 %collective-permute-start.4 = (bf16[2,32,1536]{2,1,0:T(8,128)(2,1)S(1)}, bf16[2,32,1536]{2,1,0:T(8,128)(2,1)S(1)}, u32[]{:S(2)}, u32[]{:S(2)}) collective-permute-start(bf16[2,32,1536]{2,1,0:T(8,128)(2,1)S(1)} %maximum_maximum_fusion), channel_id=1, source_target_pairs={{2,0},{4,2},{6,4},{8,6},{10,8},{12,10},{14,12},{16,14},{18,16},{20... | collective-permute-start | bytes 589832 | tf_op jit(solution)/shard_map/ppermute | solution.py:179
  18.9 1.0 %multiply_reduce_fusion.2 = (f32[64]{0:T(128)S(1)}, f32[64,1536]{1,0:T(8,128)S(1)}) fusion(bf16[64,1536]{1,0:T(8,128)(2,1)S(1)} %bitcast.48, bf16[1536,768]{1,0:T(8,128)(2,1)S(1)} %bitcast.40, bf16[1536,768]{1,0:T(8,128)(2,1)S(1)} %bitcast.37), kind=kOutput, calls=%fused_computation.33 | convolution fusion | flops 311623616 | bytes 5308672 | tf_op jit(solution)/shard_map/dot_general | solution.py:184
  20.0 0.1 divide_convert_fusion.2
  20.1 0.0 collective-permute-done.3
  20.1 1.0 %multiply_reduce_fusion.1 = (f32[64]{0:T(128)S(1)}, f32[64,1536]{1,0:T(8,128)S(1)}) fusion(bf16[64,1536]{1,0:T(8,128)(2,1)S(1)} %bitcast.51, bf16[1536,768]{1,0:T(8,128)(2,1)S(1)} %bitcast.41, bf16[1536,768]{1,0:T(8,128)(2,1)S(1)} %bitcast.38), kind=kOutput, calls=%fused_computation.31 | convolution fusion | flops 311623616 | bytes 5308672 | tf_op jit(solution)/shard_map/dot_general | solution.py:184
  21.1 0.1 divide_convert_fusion.1
  21.3 2.5 %collective-permute-done.4 = bf16[2,32,1536]{2,1,0:T(8,128)(2,1)S(1)} collective-permute-done((bf16[2,32,1536]{2,1,0:T(8,128)(2,1)S(1)}, bf16[2,32,1536]{2,1,0:T(8,128)(2,1)S(1)}, u32[]{:S(2)}, u32[]{:S(2)}) %collective-permute-start.4) | collective-permute-done | bytes 196640 | tf_op jit(solution)/shard_map/ppermute | solution.py:179
  23.8 1.0 %multiply_reduce_fusion = (f32[64]{0:T(128)S(1)}, f32[64,1536]{1,0:T(8,128)S(1)}) fusion(bf16[64,1536]{1,0:T(8,128)(2,1)S(1)} %bitcast.50, bf16[1536,768]{1,0:T(8,128)(2,1)S(1)} %bitcast.42, bf16[1536,768]{1,0:T(8,128)(2,1)S(1)} %bitcast.39), kind=kOutput, calls=%fused_computation.29 | convolution fusion | flops 311623616 | bytes 5308672 | tf_op jit(solution)/shard_map/dot_general | solution.py:184
  24.9 0.1 divide_convert_fusion
  25.1 1.0 %fusion.23 = f32[2,1536,512]{1,2,0:T(8,128)S(1)} fusion(bf16[2,96,1536]{2,1,0:T(8,128)(2,1)S(1)} %slice_dynamic-update-slice_fusion, s32[512]{0:T(512)S(1)} %bitcast.49), kind=kOutput, calls=%fused_computation.45 | convolution fusion | flops 302039040 | bytes 6883328 | tf_op jit(solution)/shard_map/pq,mqk->mpk/dot_general | solution.py:217
  26.1 0.9 %add_convert_fusion = (bf16[2,2,256,768]{3,2,1,0:T(8,128)(2,1)S(1)}, bf16[2,2,256,768]{3,2,1,0:T(8,128)(2,1)S(1)}) fusion(f32[2,2,256,1536]{3,2,1,0:T(8,128)S(1)} %bitcast.34, f32[2,2,768]{2,1,0:T(2,128)S(1)} %get-tuple-element.12, f32[2,2,768]{2,1,0:T(2,128)S(1)} %get-tuple-element.11), kind=kLoop, calls=%fused_computation.5 | loop fusion | flops 6291456 | bytes 9461760 | tf_op jit(solution)/shard_map/convert.4
  27.1 0.0 copy-start
  27.1 0.2 pad_maximum_fusion.1.crossed_ref
  27.3 0.5 %copy-done = s32[4,1024]{1,0:T(4,128)S(1)} copy-done((s32[4,1024]{1,0:T(4,128)S(1)}, s32[4,1024]{1,0:T(4,128)}, u32[]{:S(2)}) %copy-start) | copy-done | bytes 16408
  27.8 11.2 %shard_map.37 = f32[512,4]{1,0:T(8,128)S(1)} custom-call(s32[1]{0:T(128)} %constant.28.clone.1.own_ref, s32[4,1024]{1,0:T(4,128)S(1)} %copy-done, bf16[2,512,1536]{2,1,0:T(8,128)(2,1)S(1)} %pad_maximum_fusion.1.crossed_ref, f32[768,8]{1,0:T(8,128)S(1)} %get-tuple-element.14.wcos_ref, f32[768,8]{1,0:T(8,128)S(1)} %get-tuple-element.13.wsin_ref, ...), custom_call_target="tpu_custom_call" | custom-call | tf_op jit(solution)/shard_map/pallas_call | solution.py:138
  39.0 0.7 %copy.7 = f32[1,4,2,256]{3,2,1,0:T(2,128)} copy(f32[1,4,2,256]{1,3,2,0:T(8,128)S(1)} %bitcast.33) | data formatting | bytes 16384 | tf_op jit(solution)/shard_map/reshape | solution.py:225
  (17 shorter events, 0.2 us)
Async XLA Ops:
  0.0 14.2 %copy-start.1 = (bf16[1,16,1536]{2,1,0:T(8,128)(2,1)S(1)}, bf16[1,16,1536]{2,1,0:T(8,128)(2,1)}, u32[]{:S(2)}) copy-start(bf16[1,16,1536]{2,1,0:T(8,128)(2,1)} %param.3) | copy-start | bytes 147460
  0.0 12.1 %copy-start.2 = (s32[2,256]{1,0:T(2,128)S(1)}, s32[2,256]{1,0:T(2,128)}, u32[]{:S(2)}) copy-start(s32[2,256]{1,0:T(2,128)} %param.4) | copy-start | bytes 6148
  0.0 13.7 %collective-permute-start = (bf16[1,16,1536]{2,1,0:T(8,128)(2,1)}, bf16[1,16,1536]{2,1,0:T(8,128)(2,1)S(1)}, u32[]{:S(2)}, u32[]{:S(2)}) collective-permute-start(bf16[1,16,1536]{2,1,0:T(8,128)(2,1)} %param.3), channel_id=1, source_target_pairs={{0,30},{2,28},{4,26},{6,24},{8,22},{10,20},{12,18},{14,16},{16,14}... | collective-permute-start | bytes 147464 | tf_op jit(solution)/shard_map/ppermute | solution.py:175
  5.7 8.1 %collective-permute-start.1 = (bf16[1,16,1536]{2,1,0:T(8,128)(2,1)}, bf16[1,16,1536]{2,1,0:T(8,128)(2,1)S(1)}, u32[]{:S(2)}, u32[]{:S(2)}) collective-permute-start(bf16[1,16,1536]{2,1,0:T(8,128)(2,1)} %param.3), channel_id=1, source_target_pairs={{0,1},{1,0},{2,3},{3,2},{4,5},{5,4},{6,7},{7,6},{8,9},{9,8},{10,11... | collective-permute-start | bytes 147464 | tf_op jit(solution)/shard_map/ppermute | solution.py:169
  6.9 7.4 %collective-permute-start.2 = (bf16[1,16,1536]{2,1,0:T(8,128)(2,1)}, bf16[1,16,1536]{2,1,0:T(8,128)(2,1)S(1)}, u32[]{:S(2)}, u32[]{:S(2)}) collective-permute-start(bf16[1,16,1536]{2,1,0:T(8,128)(2,1)} %param.3), channel_id=1, source_target_pairs={{0,31},{2,29},{4,27},{6,25},{8,23},{10,21},{12,19},{14,17},{16,15}... | collective-permute-start | bytes 147464 | tf_op jit(solution)/shard_map/ppermute | solution.py:175
  14.3 5.8 %collective-permute-start.3 = (bf16[2,32,1536]{2,1,0:T(8,128)(2,1)S(1)}, bf16[2,32,1536]{2,1,0:T(8,128)(2,1)S(1)}, u32[]{:S(2)}, u32[]{:S(2)}) collective-permute-start(bf16[2,32,1536]{2,1,0:T(8,128)(2,1)S(1)} %maximum_maximum_fusion), channel_id=1, source_target_pairs={{0,2},{2,4},{4,6},{6,8},{8,10},{10,12},{12,14},{14,16},{16,18},{18... | collective-permute-start | bytes 589832 | tf_op jit(solution)/shard_map/ppermute | solution.py:178
  16.8 7.0 %collective-permute-start.4 = (bf16[2,32,1536]{2,1,0:T(8,128)(2,1)S(1)}, bf16[2,32,1536]{2,1,0:T(8,128)(2,1)S(1)}, u32[]{:S(2)}, u32[]{:S(2)}) collective-permute-start(bf16[2,32,1536]{2,1,0:T(8,128)(2,1)S(1)} %maximum_maximum_fusion), channel_id=1, source_target_pairs={{2,0},{4,2},{6,4},{8,6},{10,8},{12,10},{14,12},{16,14},{18,16},{20... | collective-permute-start | bytes 589832 | tf_op jit(solution)/shard_map/ppermute | solution.py:179
  27.1 0.7 %copy-start = (s32[4,1024]{1,0:T(4,128)S(1)}, s32[4,1024]{1,0:T(4,128)}, u32[]{:S(2)}) copy-start(s32[4,1024]{1,0:T(4,128)} %stretch_ref.1) | copy-start | bytes 49156

commit v24 on v22

--- a/solution.py
+++ b/solution.py
@@ -214,7 +214,7 @@
         slot_index.reshape(pair_count, 1) == jnp.arange(slot_rows, dtype=jnp.int32)[None, :]
     ).astype(jnp.bfloat16)
     receivers = jnp.einsum(
-        "pq,mqk->mpk", selector, whitened, preferred_element_type=jnp.float32
+        "pq,mqk->mpk", selector, whitened, preferred_element_type=jnp.bfloat16
     )
     receivers = receivers.reshape(minutes, source_count, recv_count, 2 * NF)
     crossed = cross_spectrum(sources[:, :, None, :], receivers)

time: 40 us -> 40 us (level)
  no operation moved by 1% of the time
where the time goes in v24:
time: 40 us; the launch traced here: 39.6 us
  starting transfers between devices  11.9 us (30%)
  Pallas kernels  11.1 us (28%)
  other arithmetic  7.99 us (20%)
  matrix products  4.11 us (10%)
  waiting for transfers between devices  3.01 us (8%)
  local copies, waits for them, and re-layouts  1.3 us (3%)
    pallas_call x1, Pallas kernels, coherence(): pl.pallas_call(coherence_kernel, grid_spec=pltpu.PrefetchScalarGridSpec(n...  11.1 us
    ppermute x2, starting transfers between devices, body(): mirrored = lax.ppermute(record, axis_order, route)  5.99 us
    sin x3, other arithmetic, unit_angles(): return (jnp.cos(phase), jnp.sin(phase))  3.4 us
    dot_general x3, matrix products, spectra(): jnp.dot(rows.reshape(minutes * count, NT), forward, preferred_element_typ...  3.08 us
    ppermute x1, starting transfers between devices, body(): lax.ppermute(bundle, 'chan', [(s, s + 1) for s in range(blocks - 1)])  2.55 us
    ppermute x1, waiting for transfers between devices, body(): lax.ppermute(bundle, 'chan', [(s, s - 1) for s in range(1, blocks)])  2.54 us
    another operation x2, other arithmetic  2.33 us
    ppermute x1, starting transfers between devices, body(): lax.ppermute(bundle, 'chan', [(s, s - 1) for s in range(1, blocks)])  2.1 us
  transfers between devices with their start and end apart: 5, of which 2 were waited for; matrix products, arithmetic and copies ran while one was open for 22% of the time, Pallas kernels for 0%

profile of v24, /device:TPU:1, one launch (start us, length us, event | category | flops | bytes accessed | tf_op | source)
XLA Modules:
  0.0 39.6 jit_solution(17786939851865073427)
XLA Ops:
  0.0 0.0 copy-start.1
  0.0 0.0 copy-start.2
  0.0 5.7 %collective-permute-start = (bf16[1,16,1536]{2,1,0:T(8,128)(2,1)}, bf16[1,16,1536]{2,1,0:T(8,128)(2,1)S(1)}, u32[]{:S(2)}, u32[]{:S(2)}) collective-permute-start(bf16[1,16,1536]{2,1,0:T(8,128)(2,1)} %param.3), channel_id=1, source_target_pairs={{0,30},{2,28},{4,26},{6,24},{8,22},{10,20},{12,18},{14,16},{16,14}... | collective-permute-start | bytes 147464 | tf_op jit(solution)/shard_map/ppermute | solution.py:174
  5.7 1.2 %collective-permute-start.1 = (bf16[1,16,1536]{2,1,0:T(8,128)(2,1)}, bf16[1,16,1536]{2,1,0:T(8,128)(2,1)S(1)}, u32[]{:S(2)}, u32[]{:S(2)}) collective-permute-start(bf16[1,16,1536]{2,1,0:T(8,128)(2,1)} %param.3), channel_id=1, source_target_pairs={{0,1},{1,0},{2,3},{3,2},{4,5},{5,4},{6,7},{7,6},{8,9},{9,8},{10,11... | collective-permute-start | bytes 147464 | tf_op jit(solution)/shard_map/ppermute | solution.py:168
  6.9 0.3 collective-permute-start.2
  7.2 1.6 %fusion.17 = (f32[128,768]{1,0:T(8,128)S(1)}, f32[128,768]{1,0:T(8,128)S(1)}) fusion(), kind=kLoop, calls=%fused_computation.38 | loop fusion | flops 884736 | bytes 786432 | tf_op jit(solution)/shard_map/sin | solution.py:20
  8.8 0.2 fusion.29
  9.1 1.6 %sine_multiply_fusion = (f32[768,8]{1,0:T(8,128)S(1)}, f32[768,8]{1,0:T(8,128)S(1)}) fusion(f32[768]{0:T(1024)S(1)} %fusion.32, s32[8]{0:T(128)S(1)} %iota_add_fusion), kind=kLoop, calls=%fused_computation.24 | loop fusion | flops 67584 | bytes 52256 | tf_op jit(solution)/shard_map/mul | solution.py:41
  10.7 1.4 %subtract_convert_fusion = (bf16[12,128,768]{2,1,0:T(8,128)(2,1)S(1)}, bf16[12,128,768]{2,1,0:T(8,128)(2,1)S(1)}) fusion(f32[128,768]{1,0:T(8,128)S(1)} %get-tuple-element.21, f32[12,768]{1,0:T(8,128)S(1)} %get-tuple-element.23, f32[128,768]{1,0:T(8,128)S(1)} %get-tuple-element.22, f32[12,768]{1,0:T(8,128)S(1)} %get-tuple-element.24), kind=kLoop, calls=%fused_computation.2 | loop fusion | flops 10616832 | bytes 5578752 | tf_op jit(solution)/shard_map/convert.10
  12.1 0.0 copy-done.2
  12.1 1.6 %fusion.11 = (f32[768,128]{1,0:T(8,128)S(1)}, f32[768,128]{1,0:T(8,128)S(1)}) fusion(), kind=kLoop, calls=%fused_computation.22 | loop fusion | flops 884736 | bytes 786432 | tf_op jit(solution)/shard_map/sin | solution.py:20
  13.8 0.0 collective-permute-done
  13.8 0.0 collective-permute-done.1
  13.8 0.5 %collective-permute-done.2 = bf16[1,16,1536]{2,1,0:T(8,128)(2,1)S(1)} collective-permute-done((bf16[1,16,1536]{2,1,0:T(8,128)(2,1)}, bf16[1,16,1536]{2,1,0:T(8,128)(2,1)S(1)}, u32[]{:S(2)}, u32[]{:S(2)}) %collective-permute-start.2) | collective-permute-done | bytes 49184 | tf_op jit(solution)/shard_map/ppermute | solution.py:174
  14.2 0.0 copy-done.1
  14.3 2.5 %collective-permute-start.3 = (bf16[2,32,1536]{2,1,0:T(8,128)(2,1)S(1)}, bf16[2,32,1536]{2,1,0:T(8,128)(2,1)S(1)}, u32[]{:S(2)}, u32[]{:S(2)}) collective-permute-start(bf16[2,32,1536]{2,1,0:T(8,128)(2,1)S(1)} %maximum_maximum_fusion), channel_id=1, source_target_pairs={{0,2},{2,4},{4,6},{6,8},{8,10},{10,12},{12,14},{14,16},{16,18},{18... | collective-permute-start | bytes 589832 | tf_op jit(solution)/shard_map/ppermute | solution.py:177
  16.8 2.1 %collective-permute-start.4 = (bf16[2,32,1536]{2,1,0:T(8,128)(2,1)S(1)}, bf16[2,32,1536]{2,1,0:T(8,128)(2,1)S(1)}, u32[]{:S(2)}, u32[]{:S(2)}) collective-permute-start(bf16[2,32,1536]{2,1,0:T(8,128)(2,1)S(1)} %maximum_maximum_fusion), channel_id=1, source_target_pairs={{2,0},{4,2},{6,4},{8,6},{10,8},{12,10},{14,12},{16,14},{18,16},{20... | collective-permute-start | bytes 589832 | tf_op jit(solution)/shard_map/ppermute | solution.py:178
  18.9 1.0 %multiply_reduce_fusion.2 = (f32[64]{0:T(128)S(1)}, f32[64,1536]{1,0:T(8,128)S(1)}) fusion(bf16[64,1536]{1,0:T(8,128)(2,1)S(1)} %bitcast.48, bf16[1536,768]{1,0:T(8,128)(2,1)S(1)} %bitcast.40, bf16[1536,768]{1,0:T(8,128)(2,1)S(1)} %bitcast.37), kind=kOutput, calls=%fused_computation.34 | convolution fusion | flops 311623616 | bytes 5308672 | tf_op jit(solution)/shard_map/dot_general | solution.py:183
  20.0 0.1 divide_convert_fusion.2
  20.1 0.0 collective-permute-done.3
  20.1 1.0 %multiply_reduce_fusion.1 = (f32[64]{0:T(128)S(1)}, f32[64,1536]{1,0:T(8,128)S(1)}) fusion(bf16[64,1536]{1,0:T(8,128)(2,1)S(1)} %bitcast.51, bf16[1536,768]{1,0:T(8,128)(2,1)S(1)} %bitcast.41, bf16[1536,768]{1,0:T(8,128)(2,1)S(1)} %bitcast.38), kind=kOutput, calls=%fused_computation.32 | convolution fusion | flops 311623616 | bytes 5308672 | tf_op jit(solution)/shard_map/dot_general | solution.py:183
  21.1 0.1 divide_convert_fusion.1
  21.3 2.5 %collective-permute-done.4 = bf16[2,32,1536]{2,1,0:T(8,128)(2,1)S(1)} collective-permute-done((bf16[2,32,1536]{2,1,0:T(8,128)(2,1)S(1)}, bf16[2,32,1536]{2,1,0:T(8,128)(2,1)S(1)}, u32[]{:S(2)}, u32[]{:S(2)}) %collective-permute-start.4) | collective-permute-done | bytes 196640 | tf_op jit(solution)/shard_map/ppermute | solution.py:178
  23.8 1.0 %multiply_reduce_fusion = (f32[64]{0:T(128)S(1)}, f32[64,1536]{1,0:T(8,128)S(1)}) fusion(bf16[64,1536]{1,0:T(8,128)(2,1)S(1)} %bitcast.50, bf16[1536,768]{1,0:T(8,128)(2,1)S(1)} %bitcast.42, bf16[1536,768]{1,0:T(8,128)(2,1)S(1)} %bitcast.39), kind=kOutput, calls=%fused_computation.30 | convolution fusion | flops 311623616 | bytes 5308672 | tf_op jit(solution)/shard_map/dot_general | solution.py:183
  24.9 0.1 divide_convert_fusion
  25.1 1.0 %convolution_convert_fusion = f32[2,1536,512]{1,2,0:T(8,128)S(1)} fusion(bf16[2,96,1536]{2,1,0:T(8,128)(2,1)S(1)} %slice_dynamic-update-slice_fusion, s32[512]{0:T(512)S(1)} %bitcast.49), kind=kOutput, calls=%fused_computation.3 | convolution fusion | flops 303611904 | bytes 6883328 | tf_op jit(solution)/shard_map/pq,mqk->mpk/dot_general | solution.py:216
  26.1 0.9 %add_convert_fusion = (bf16[2,2,256,768]{3,2,1,0:T(8,128)(2,1)S(1)}, bf16[2,2,256,768]{3,2,1,0:T(8,128)(2,1)S(1)}) fusion(f32[2,2,256,1536]{3,2,1,0:T(8,128)S(1)} %bitcast.34, f32[2,2,768]{2,1,0:T(2,128)S(1)} %get-tuple-element.12, f32[2,2,768]{2,1,0:T(2,128)S(1)} %get-tuple-element.11), kind=kLoop, calls=%fused_computation.6 | loop fusion | flops 6291456 | bytes 9461760 | tf_op jit(solution)/shard_map/convert.6
  27.1 0.0 copy-start
  27.1 0.2 pad_maximum_fusion.1.crossed_ref
  27.3 0.5 %copy-done = s32[4,1024]{1,0:T(4,128)S(1)} copy-done((s32[4,1024]{1,0:T(4,128)S(1)}, s32[4,1024]{1,0:T(4,128)}, u32[]{:S(2)}) %copy-start) | copy-done | bytes 16408
  27.8 11.1 %shard_map.37 = f32[512,4]{1,0:T(8,128)S(1)} custom-call(s32[1]{0:T(128)} %constant.28.clone.1.own_ref, s32[4,1024]{1,0:T(4,128)S(1)} %copy-done, bf16[2,512,1536]{2,1,0:T(8,128)(2,1)S(1)} %pad_maximum_fusion.1.crossed_ref, f32[768,8]{1,0:T(8,128)S(1)} %get-tuple-element.14.wcos_ref, f32[768,8]{1,0:T(8,128)S(1)} %get-tuple-element.13.wsin_ref, ...), custom_call_target="tpu_custom_call" | custom-call | tf_op jit(solution)/shard_map/pallas_call | solution.py:137
  38.9 0.7 %copy.7 = f32[1,4,2,256]{3,2,1,0:T(2,128)} copy(f32[1,4,2,256]{1,3,2,0:T(8,128)S(1)} %bitcast.33) | data formatting | bytes 16384 | tf_op jit(solution)/shard_map/reshape | solution.py:224
  (17 shorter events, 0.2 us)
Async XLA Ops:
  0.0 14.2 %copy-start.1 = (bf16[1,16,1536]{2,1,0:T(8,128)(2,1)S(1)}, bf16[1,16,1536]{2,1,0:T(8,128)(2,1)}, u32[]{:S(2)}) copy-start(bf16[1,16,1536]{2,1,0:T(8,128)(2,1)} %param.3) | copy-start | bytes 147460
  0.0 12.1 %copy-start.2 = (s32[2,256]{1,0:T(2,128)S(1)}, s32[2,256]{1,0:T(2,128)}, u32[]{:S(2)}) copy-start(s32[2,256]{1,0:T(2,128)} %param.4) | copy-start | bytes 6148
  0.0 13.7 %collective-permute-start = (bf16[1,16,1536]{2,1,0:T(8,128)(2,1)}, bf16[1,16,1536]{2,1,0:T(8,128)(2,1)S(1)}, u32[]{:S(2)}, u32[]{:S(2)}) collective-permute-start(bf16[1,16,1536]{2,1,0:T(8,128)(2,1)} %param.3), channel_id=1, source_target_pairs={{0,30},{2,28},{4,26},{6,24},{8,22},{10,20},{12,18},{14,16},{16,14}... | collective-permute-start | bytes 147464 | tf_op jit(solution)/shard_map/ppermute | solution.py:174
  5.7 8.1 %collective-permute-start.1 = (bf16[1,16,1536]{2,1,0:T(8,128)(2,1)}, bf16[1,16,1536]{2,1,0:T(8,128)(2,1)S(1)}, u32[]{:S(2)}, u32[]{:S(2)}) collective-permute-start(bf16[1,16,1536]{2,1,0:T(8,128)(2,1)} %param.3), channel_id=1, source_target_pairs={{0,1},{1,0},{2,3},{3,2},{4,5},{5,4},{6,7},{7,6},{8,9},{9,8},{10,11... | collective-permute-start | bytes 147464 | tf_op jit(solution)/shard_map/ppermute | solution.py:168
  6.9 7.4 %collective-permute-start.2 = (bf16[1,16,1536]{2,1,0:T(8,128)(2,1)}, bf16[1,16,1536]{2,1,0:T(8,128)(2,1)S(1)}, u32[]{:S(2)}, u32[]{:S(2)}) collective-permute-start(bf16[1,16,1536]{2,1,0:T(8,128)(2,1)} %param.3), channel_id=1, source_target_pairs={{0,31},{2,29},{4,27},{6,25},{8,23},{10,21},{12,19},{14,17},{16,15}... | collective-permute-start | bytes 147464 | tf_op jit(solution)/shard_map/ppermute | solution.py:174
  14.3 5.8 %collective-permute-start.3 = (bf16[2,32,1536]{2,1,0:T(8,128)(2,1)S(1)}, bf16[2,32,1536]{2,1,0:T(8,128)(2,1)S(1)}, u32[]{:S(2)}, u32[]{:S(2)}) collective-permute-start(bf16[2,32,1536]{2,1,0:T(8,128)(2,1)S(1)} %maximum_maximum_fusion), channel_id=1, source_target_pairs={{0,2},{2,4},{4,6},{6,8},{8,10},{10,12},{12,14},{14,16},{16,18},{18... | collective-permute-start | bytes 589832 | tf_op jit(solution)/shard_map/ppermute | solution.py:177
  16.8 7.0 %collective-permute-start.4 = (bf16[2,32,1536]{2,1,0:T(8,128)(2,1)S(1)}, bf16[2,32,1536]{2,1,0:T(8,128)(2,1)S(1)}, u32[]{:S(2)}, u32[]{:S(2)}) collective-permute-start(bf16[2,32,1536]{2,1,0:T(8,128)(2,1)S(1)} %maximum_maximum_fusion), channel_id=1, source_target_pairs={{2,0},{4,2},{6,4},{8,6},{10,8},{12,10},{14,12},{16,14},{18,16},{20... | collective-permute-start | bytes 589832 | tf_op jit(solution)/shard_map/ppermute | solution.py:178
  27.1 0.7 %copy-start = (s32[4,1024]{1,0:T(4,128)S(1)}, s32[4,1024]{1,0:T(4,128)}, u32[]{:S(2)}) copy-start(s32[4,1024]{1,0:T(4,128)} %stretch_ref.1) | copy-start | bytes 49156

commit v25 on v22

--- a/solution.py
+++ b/solution.py
@@ -73,7 +73,6 @@
 
     fine_cos = fcos_ref[...]
     fine_sin = fsin_ref[...]
-    own = own_ref[0]
     pieces = [[] for _ in range(minutes)]
     for pair_group in range(groups // 2):
         columns = []
@@ -102,7 +101,6 @@
             stacked, current = correlation, correlation
         else:
             stacked = stacked + correlation
-            current = jnp.where(own == minute, correlation, current)
     high = stacked.astype(jnp.bfloat16)
     low = (stacked - high.astype(jnp.float32)).astype(jnp.bfloat16)
     rows = stacked.shape[0]

time: 40 us -> 39.9 us (level)
  no operation moved by 1% of the time
where the time goes in v25:
time: 39.9 us; the launch traced here: 39.6 us
  starting transfers between devices  11.9 us (30%)
  Pallas kernels  11.1 us (28%)
  other arithmetic  7.99 us (20%)
  matrix products  4.11 us (10%)
  waiting for transfers between devices  3.01 us (8%)
  local copies, waits for them, and re-layouts  1.3 us (3%)
    pallas_call x1, Pallas kernels, coherence(): pl.pallas_call(coherence_kernel, grid_spec=pltpu.PrefetchScalarGridSpec(n...  11.1 us
    ppermute x2, starting transfers between devices, body(): mirrored = lax.ppermute(record, axis_order, route)  5.99 us
    sin x3, other arithmetic, unit_angles(): return (jnp.cos(phase), jnp.sin(phase))  3.4 us
    dot_general x3, matrix products, spectra(): jnp.dot(rows.reshape(minutes * count, NT), forward, preferred_element_typ...  3.08 us
    ppermute x1, starting transfers between devices, body(): lax.ppermute(bundle, 'chan', [(s, s + 1) for s in range(blocks - 1)])  2.55 us
    ppermute x1, waiting for transfers between devices, body(): lax.ppermute(bundle, 'chan', [(s, s - 1) for s in range(1, blocks)])  2.54 us
    another operation x2, other arithmetic  2.33 us
    ppermute x1, starting transfers between devices, body(): lax.ppermute(bundle, 'chan', [(s, s - 1) for s in range(1, blocks)])  2.1 us
  transfers between devices with their start and end apart: 5, of which 2 were waited for; matrix products, arithmetic and copies ran while one was open for 22% of the time, Pallas kernels for 0%

profile of v25, /device:TPU:1, one launch (start us, length us, event | category | flops | bytes accessed | tf_op | source)
XLA Modules:
  0.0 39.6 jit_solution(10921954590072617155)
XLA Ops:
  0.0 0.0 copy-start.1
  0.0 0.0 copy-start.2
  0.0 5.7 %collective-permute-start = (bf16[1,16,1536]{2,1,0:T(8,128)(2,1)}, bf16[1,16,1536]{2,1,0:T(8,128)(2,1)S(1)}, u32[]{:S(2)}, u32[]{:S(2)}) collective-permute-start(bf16[1,16,1536]{2,1,0:T(8,128)(2,1)} %param.3), channel_id=1, source_target_pairs={{0,30},{2,28},{4,26},{6,24},{8,22},{10,20},{12,18},{14,16},{16,14}... | collective-permute-start | bytes 147464 | tf_op jit(solution)/shard_map/ppermute | solution.py:172
  5.7 1.2 %collective-permute-start.1 = (bf16[1,16,1536]{2,1,0:T(8,128)(2,1)}, bf16[1,16,1536]{2,1,0:T(8,128)(2,1)S(1)}, u32[]{:S(2)}, u32[]{:S(2)}) collective-permute-start(bf16[1,16,1536]{2,1,0:T(8,128)(2,1)} %param.3), channel_id=1, source_target_pairs={{0,1},{1,0},{2,3},{3,2},{4,5},{5,4},{6,7},{7,6},{8,9},{9,8},{10,11... | collective-permute-start | bytes 147464 | tf_op jit(solution)/shard_map/ppermute | solution.py:166
  6.9 0.3 collective-permute-start.2
  7.2 1.6 %fusion.17 = (f32[128,768]{1,0:T(8,128)S(1)}, f32[128,768]{1,0:T(8,128)S(1)}) fusion(), kind=kLoop, calls=%fused_computation.37 | loop fusion | flops 884736 | bytes 786432 | tf_op jit(solution)/shard_map/sin | solution.py:20
  8.8 0.2 fusion.30
  9.1 1.6 %sine_multiply_fusion = (f32[768,8]{1,0:T(8,128)S(1)}, f32[768,8]{1,0:T(8,128)S(1)}) fusion(f32[768]{0:T(1024)S(1)} %fusion.33, s32[8]{0:T(128)S(1)} %iota_add_fusion), kind=kLoop, calls=%fused_computation.23 | loop fusion | flops 67584 | bytes 52256 | tf_op jit(solution)/shard_map/mul | solution.py:41
  10.7 1.4 %subtract_convert_fusion = (bf16[12,128,768]{2,1,0:T(8,128)(2,1)S(1)}, bf16[12,128,768]{2,1,0:T(8,128)(2,1)S(1)}) fusion(f32[128,768]{1,0:T(8,128)S(1)} %get-tuple-element.21, f32[12,768]{1,0:T(8,128)S(1)} %get-tuple-element.23, f32[128,768]{1,0:T(8,128)S(1)} %get-tuple-element.22, f32[12,768]{1,0:T(8,128)S(1)} %get-tuple-element.24), kind=kLoop, calls=%fused_computation.2 | loop fusion | flops 10616832 | bytes 5578752 | tf_op jit(solution)/shard_map/convert.8
  12.1 0.0 copy-done.2
  12.1 1.6 %fusion.11 = (f32[768,128]{1,0:T(8,128)S(1)}, f32[768,128]{1,0:T(8,128)S(1)}) fusion(), kind=kLoop, calls=%fused_computation.21 | loop fusion | flops 884736 | bytes 786432 | tf_op jit(solution)/shard_map/sin | solution.py:20
  13.8 0.0 collective-permute-done
  13.8 0.0 collective-permute-done.1
  13.8 0.5 %collective-permute-done.2 = bf16[1,16,1536]{2,1,0:T(8,128)(2,1)S(1)} collective-permute-done((bf16[1,16,1536]{2,1,0:T(8,128)(2,1)}, bf16[1,16,1536]{2,1,0:T(8,128)(2,1)S(1)}, u32[]{:S(2)}, u32[]{:S(2)}) %collective-permute-start.2) | collective-permute-done | bytes 49184 | tf_op jit(solution)/shard_map/ppermute | solution.py:172
  14.2 0.0 copy-done.1
  14.3 2.5 %collective-permute-start.3 = (bf16[2,32,1536]{2,1,0:T(8,128)(2,1)S(1)}, bf16[2,32,1536]{2,1,0:T(8,128)(2,1)S(1)}, u32[]{:S(2)}, u32[]{:S(2)}) collective-permute-start(bf16[2,32,1536]{2,1,0:T(8,128)(2,1)S(1)} %maximum_maximum_fusion), channel_id=1, source_target_pairs={{0,2},{2,4},{4,6},{6,8},{8,10},{10,12},{12,14},{14,16},{16,18},{18... | collective-permute-start | bytes 589832 | tf_op jit(solution)/shard_map/ppermute | solution.py:175
  16.8 2.1 %collective-permute-start.4 = (bf16[2,32,1536]{2,1,0:T(8,128)(2,1)S(1)}, bf16[2,32,1536]{2,1,0:T(8,128)(2,1)S(1)}, u32[]{:S(2)}, u32[]{:S(2)}) collective-permute-start(bf16[2,32,1536]{2,1,0:T(8,128)(2,1)S(1)} %maximum_maximum_fusion), channel_id=1, source_target_pairs={{2,0},{4,2},{6,4},{8,6},{10,8},{12,10},{14,12},{16,14},{18,16},{20... | collective-permute-start | bytes 589832 | tf_op jit(solution)/shard_map/ppermute | solution.py:176
  18.9 1.0 %multiply_reduce_fusion.2 = (f32[64]{0:T(128)S(1)}, f32[64,1536]{1,0:T(8,128)S(1)}) fusion(bf16[64,1536]{1,0:T(8,128)(2,1)S(1)} %bitcast.48, bf16[1536,768]{1,0:T(8,128)(2,1)S(1)} %bitcast.40, bf16[1536,768]{1,0:T(8,128)(2,1)S(1)} %bitcast.37), kind=kOutput, calls=%fused_computation.33 | convolution fusion | flops 311623616 | bytes 5308672 | tf_op jit(solution)/shard_map/dot_general | solution.py:181
  20.0 0.1 divide_convert_fusion.2
  20.1 0.0 collective-permute-done.3
  20.1 1.0 %multiply_reduce_fusion.1 = (f32[64]{0:T(128)S(1)}, f32[64,1536]{1,0:T(8,128)S(1)}) fusion(bf16[64,1536]{1,0:T(8,128)(2,1)S(1)} %bitcast.51, bf16[1536,768]{1,0:T(8,128)(2,1)S(1)} %bitcast.41, bf16[1536,768]{1,0:T(8,128)(2,1)S(1)} %bitcast.38), kind=kOutput, calls=%fused_computation.31 | convolution fusion | flops 311623616 | bytes 5308672 | tf_op jit(solution)/shard_map/dot_general | solution.py:181
  21.1 0.1 divide_convert_fusion.1
  21.3 2.5 %collective-permute-done.4 = bf16[2,32,1536]{2,1,0:T(8,128)(2,1)S(1)} collective-permute-done((bf16[2,32,1536]{2,1,0:T(8,128)(2,1)S(1)}, bf16[2,32,1536]{2,1,0:T(8,128)(2,1)S(1)}, u32[]{:S(2)}, u32[]{:S(2)}) %collective-permute-start.4) | collective-permute-done | bytes 196640 | tf_op jit(solution)/shard_map/ppermute | solution.py:176
  23.8 1.0 %multiply_reduce_fusion = (f32[64]{0:T(128)S(1)}, f32[64,1536]{1,0:T(8,128)S(1)}) fusion(bf16[64,1536]{1,0:T(8,128)(2,1)S(1)} %bitcast.50, bf16[1536,768]{1,0:T(8,128)(2,1)S(1)} %bitcast.42, bf16[1536,768]{1,0:T(8,128)(2,1)S(1)} %bitcast.39), kind=kOutput, calls=%fused_computation.29 | convolution fusion | flops 311623616 | bytes 5308672 | tf_op jit(solution)/shard_map/dot_general | solution.py:181
  24.9 0.1 divide_convert_fusion
  25.1 1.0 %fusion.23 = f32[2,1536,512]{1,2,0:T(8,128)S(1)} fusion(bf16[2,96,1536]{2,1,0:T(8,128)(2,1)S(1)} %slice_dynamic-update-slice_fusion, s32[512]{0:T(512)S(1)} %bitcast.49), kind=kOutput, calls=%fused_computation.45 | convolution fusion | flops 302039040 | bytes 6883328 | tf_op jit(solution)/shard_map/pq,mqk->mpk/dot_general | solution.py:214
  26.1 0.9 %add_convert_fusion = (bf16[2,2,256,768]{3,2,1,0:T(8,128)(2,1)S(1)}, bf16[2,2,256,768]{3,2,1,0:T(8,128)(2,1)S(1)}) fusion(f32[2,2,256,1536]{3,2,1,0:T(8,128)S(1)} %bitcast.34, f32[2,2,768]{2,1,0:T(2,128)S(1)} %get-tuple-element.12, f32[2,2,768]{2,1,0:T(2,128)S(1)} %get-tuple-element.11), kind=kLoop, calls=%fused_computation.5 | loop fusion | flops 6291456 | bytes 9461760 | tf_op jit(solution)/shard_map/convert.4
  27.1 0.0 copy-start
  27.1 0.2 pad_maximum_fusion.1.crossed_ref
  27.3 0.5 %copy-done = s32[4,1024]{1,0:T(4,128)S(1)} copy-done((s32[4,1024]{1,0:T(4,128)S(1)}, s32[4,1024]{1,0:T(4,128)}, u32[]{:S(2)}) %copy-start) | copy-done | bytes 16408
  27.8 11.1 %shard_map.37 = f32[512,4]{1,0:T(8,128)S(1)} custom-call(s32[1]{0:T(128)} %constant.28.clone.1.own_ref, s32[4,1024]{1,0:T(4,128)S(1)} %copy-done, bf16[2,512,1536]{2,1,0:T(8,128)(2,1)S(1)} %pad_maximum_fusion.1.crossed_ref, f32[768,8]{1,0:T(8,128)S(1)} %get-tuple-element.14.wcos_ref, f32[768,8]{1,0:T(8,128)S(1)} %get-tuple-element.13.wsin_ref, ...), custom_call_target="tpu_custom_call" | custom-call | tf_op jit(solution)/shard_map/pallas_call | solution.py:135
  38.9 0.7 %copy.7 = f32[1,4,2,256]{3,2,1,0:T(2,128)} copy(f32[1,4,2,256]{1,3,2,0:T(8,128)S(1)} %bitcast.33) | data formatting | bytes 16384 | tf_op jit(solution)/shard_map/reshape | solution.py:222
  (17 shorter events, 0.2 us)
Async XLA Ops:
  0.0 14.2 %copy-start.1 = (bf16[1,16,1536]{2,1,0:T(8,128)(2,1)S(1)}, bf16[1,16,1536]{2,1,0:T(8,128)(2,1)}, u32[]{:S(2)}) copy-start(bf16[1,16,1536]{2,1,0:T(8,128)(2,1)} %param.3) | copy-start | bytes 147460
  0.0 12.1 %copy-start.2 = (s32[2,256]{1,0:T(2,128)S(1)}, s32[2,256]{1,0:T(2,128)}, u32[]{:S(2)}) copy-start(s32[2,256]{1,0:T(2,128)} %param.4) | copy-start | bytes 6148
  0.0 13.7 %collective-permute-start = (bf16[1,16,1536]{2,1,0:T(8,128)(2,1)}, bf16[1,16,1536]{2,1,0:T(8,128)(2,1)S(1)}, u32[]{:S(2)}, u32[]{:S(2)}) collective-permute-start(bf16[1,16,1536]{2,1,0:T(8,128)(2,1)} %param.3), channel_id=1, source_target_pairs={{0,30},{2,28},{4,26},{6,24},{8,22},{10,20},{12,18},{14,16},{16,14}... | collective-permute-start | bytes 147464 | tf_op jit(solution)/shard_map/ppermute | solution.py:172
  5.7 8.1 %collective-permute-start.1 = (bf16[1,16,1536]{2,1,0:T(8,128)(2,1)}, bf16[1,16,1536]{2,1,0:T(8,128)(2,1)S(1)}, u32[]{:S(2)}, u32[]{:S(2)}) collective-permute-start(bf16[1,16,1536]{2,1,0:T(8,128)(2,1)} %param.3), channel_id=1, source_target_pairs={{0,1},{1,0},{2,3},{3,2},{4,5},{5,4},{6,7},{7,6},{8,9},{9,8},{10,11... | collective-permute-start | bytes 147464 | tf_op jit(solution)/shard_map/ppermute | solution.py:166
  6.9 7.4 %collective-permute-start.2 = (bf16[1,16,1536]{2,1,0:T(8,128)(2,1)}, bf16[1,16,1536]{2,1,0:T(8,128)(2,1)S(1)}, u32[]{:S(2)}, u32[]{:S(2)}) collective-permute-start(bf16[1,16,1536]{2,1,0:T(8,128)(2,1)} %param.3), channel_id=1, source_target_pairs={{0,31},{2,29},{4,27},{6,25},{8,23},{10,21},{12,19},{14,17},{16,15}... | collective-permute-start | bytes 147464 | tf_op jit(solution)/shard_map/ppermute | solution.py:172
  14.3 5.8 %collective-permute-start.3 = (bf16[2,32,1536]{2,1,0:T(8,128)(2,1)S(1)}, bf16[2,32,1536]{2,1,0:T(8,128)(2,1)S(1)}, u32[]{:S(2)}, u32[]{:S(2)}) collective-permute-start(bf16[2,32,1536]{2,1,0:T(8,128)(2,1)S(1)} %maximum_maximum_fusion), channel_id=1, source_target_pairs={{0,2},{2,4},{4,6},{6,8},{8,10},{10,12},{12,14},{14,16},{16,18},{18... | collective-permute-start | bytes 589832 | tf_op jit(solution)/shard_map/ppermute | solution.py:175
  16.8 7.0 %collective-permute-start.4 = (bf16[2,32,1536]{2,1,0:T(8,128)(2,1)S(1)}, bf16[2,32,1536]{2,1,0:T(8,128)(2,1)S(1)}, u32[]{:S(2)}, u32[]{:S(2)}) collective-permute-start(bf16[2,32,1536]{2,1,0:T(8,128)(2,1)S(1)} %maximum_maximum_fusion), channel_id=1, source_target_pairs={{2,0},{4,2},{6,4},{8,6},{10,8},{12,10},{14,12},{16,14},{18,16},{20... | collective-permute-start | bytes 589832 | tf_op jit(solution)/shard_map/ppermute | solution.py:176
  27.1 0.7 %copy-start = (s32[4,1024]{1,0:T(4,128)S(1)}, s32[4,1024]{1,0:T(4,128)}, u32[]{:S(2)}) copy-start(s32[4,1024]{1,0:T(4,128)} %stretch_ref.1) | copy-start | bytes 49156

commit v26 on v25

--- a/solution.py
+++ b/solution.py
@@ -113,8 +113,9 @@
         moved.append(product[:rows] + product[rows:])
     scale = 1.0 / LAGS
     current_power = jnp.sum(current * current, axis=1, keepdims=True) * scale
-    lanes = lax.broadcasted_iota(jnp.int32, out_ref.shape, 1)
-    result = jnp.zeros(out_ref.shape, jnp.float32)
+    slab = (rows, 128)
+    lanes = lax.broadcasted_iota(jnp.int32, slab, 1)
+    result = jnp.zeros(slab, jnp.float32)
     for stretch in range(moves + 1):
         if stretch == 0:
             shifted = stacked
@@ -124,7 +125,7 @@
         shifted_power = jnp.sum(shifted * shifted, axis=1, keepdims=True) * scale
         value = numerator / jnp.sqrt((current_power + epsilon) * (shifted_power + epsilon))
         result = jnp.where(lanes == stretch, value, result)
-    out_ref[...] = result
+    out_ref[...] = result.T[:out_ref.shape[0]]
 
 
 def coherence(own_minute, stretch_index, crossed, factors):
@@ -141,14 +142,14 @@
                 pl.BlockSpec(stretch_index.shape, lambda i, own: (0, 0)),
                 pl.BlockSpec((minutes, block, width), lambda i, own: (0, i, 0)),
             ] + [pl.BlockSpec(factor.shape, lambda i, own: (0, 0)) for factor in factors],
-            out_specs=pl.BlockSpec((block, stretch_count), lambda i, own: (i, 0)),
+            out_specs=pl.BlockSpec((stretch_count, block), lambda i, own: (0, i)),
         ),
-        out_shape=jax.ShapeDtypeStruct((pair_count, stretch_count), jnp.float32),
+        out_shape=jax.ShapeDtypeStruct((stretch_count, pair_count), jnp.float32),
         compiler_params=pltpu.CompilerParams(
             dimension_semantics=("arbitrary",), vmem_limit_bytes=48 << 20
         ),
     )(own, stretch_index, crossed, *factors)
-    return out.T
+    return out
 
 
 def body(axis_order, record, pairs, stretch_index):

time: 39.9 us -> 39.9 us (level)
  no operation moved by 1% of the time
where the time goes in v26:
time: 39.9 us; the launch traced here: 39.6 us
  starting transfers between devices  11.9 us (30%)
  Pallas kernels  11.1 us (28%)
  other arithmetic  7.99 us (20%)
  matrix products  4.11 us (10%)
  waiting for transfers between devices  3.01 us (8%)
  local copies, waits for them, and re-layouts  1.23 us (3%)
    pallas_call x1, Pallas kernels, coherence(): pl.pallas_call(coherence_kernel, grid_spec=pltpu.PrefetchScalarGridSpec(n...  11.1 us
    ppermute x2, starting transfers between devices, body(): mirrored = lax.ppermute(record, axis_order, route)  5.99 us
    sin x3, other arithmetic, unit_angles(): return (jnp.cos(phase), jnp.sin(phase))  3.4 us
    dot_general x3, matrix products, spectra(): jnp.dot(rows.reshape(minutes * count, NT), forward, preferred_element_typ...  3.08 us
    ppermute x1, starting transfers between devices, body(): lax.ppermute(bundle, 'chan', [(s, s + 1) for s in range(blocks - 1)])  2.55 us
    ppermute x1, waiting for transfers between devices, body(): lax.ppermute(bundle, 'chan', [(s, s - 1) for s in range(1, blocks)])  2.54 us
    another operation x2, other arithmetic  2.33 us
    ppermute x1, starting transfers between devices, body(): lax.ppermute(bundle, 'chan', [(s, s - 1) for s in range(1, blocks)])  2.1 us
  transfers between devices with their start and end apart: 5, of which 2 were waited for; matrix products, arithmetic and copies ran while one was open for 22% of the time, Pallas kernels for 0%

profile of v26, /device:TPU:1, one launch (start us, length us, event | category | flops | bytes accessed | tf_op | source)
XLA Modules:
  0.0 39.6 jit_solution(2966379434812618151)
XLA Ops:
  0.0 0.0 copy-start.1
  0.0 0.0 copy-start.2
  0.0 5.7 %collective-permute-start = (bf16[1,16,1536]{2,1,0:T(8,128)(2,1)}, bf16[1,16,1536]{2,1,0:T(8,128)(2,1)S(1)}, u32[]{:S(2)}, u32[]{:S(2)}) collective-permute-start(bf16[1,16,1536]{2,1,0:T(8,128)(2,1)} %param.3), channel_id=1, source_target_pairs={{0,30},{2,28},{4,26},{6,24},{8,22},{10,20},{12,18},{14,16},{16,14}... | collective-permute-start | bytes 147464 | tf_op jit(solution)/shard_map/ppermute | solution.py:173
  5.7 1.2 %collective-permute-start.1 = (bf16[1,16,1536]{2,1,0:T(8,128)(2,1)}, bf16[1,16,1536]{2,1,0:T(8,128)(2,1)S(1)}, u32[]{:S(2)}, u32[]{:S(2)}) collective-permute-start(bf16[1,16,1536]{2,1,0:T(8,128)(2,1)} %param.3), channel_id=1, source_target_pairs={{0,1},{1,0},{2,3},{3,2},{4,5},{5,4},{6,7},{7,6},{8,9},{9,8},{10,11... | collective-permute-start | bytes 147464 | tf_op jit(solution)/shard_map/ppermute | solution.py:167
  6.9 0.3 collective-permute-start.2
  7.2 1.6 %fusion.17 = (f32[128,768]{1,0:T(8,128)S(1)}, f32[128,768]{1,0:T(8,128)S(1)}) fusion(), kind=kLoop, calls=%fused_computation.37 | loop fusion | flops 884736 | bytes 786432 | tf_op jit(solution)/shard_map/sin | solution.py:20
  8.8 0.2 fusion.30
  9.1 1.6 %sine_multiply_fusion = (f32[768,8]{1,0:T(8,128)S(1)}, f32[768,8]{1,0:T(8,128)S(1)}) fusion(f32[768]{0:T(1024)S(1)} %fusion.33, s32[8]{0:T(128)S(1)} %iota_add_fusion), kind=kLoop, calls=%fused_computation.23 | loop fusion | flops 67584 | bytes 52256 | tf_op jit(solution)/shard_map/mul | solution.py:41
  10.7 1.4 %subtract_convert_fusion = (bf16[12,128,768]{2,1,0:T(8,128)(2,1)S(1)}, bf16[12,128,768]{2,1,0:T(8,128)(2,1)S(1)}) fusion(f32[128,768]{1,0:T(8,128)S(1)} %get-tuple-element.21, f32[12,768]{1,0:T(8,128)S(1)} %get-tuple-element.23, f32[128,768]{1,0:T(8,128)S(1)} %get-tuple-element.22, f32[12,768]{1,0:T(8,128)S(1)} %get-tuple-element.24), kind=kLoop, calls=%fused_computation.2 | loop fusion | flops 10616832 | bytes 5578752 | tf_op jit(solution)/shard_map/convert.8
  12.1 0.0 copy-done.2
  12.1 1.6 %fusion.11 = (f32[768,128]{1,0:T(8,128)S(1)}, f32[768,128]{1,0:T(8,128)S(1)}) fusion(), kind=kLoop, calls=%fused_computation.21 | loop fusion | flops 884736 | bytes 786432 | tf_op jit(solution)/shard_map/sin | solution.py:20
  13.8 0.0 collective-permute-done
  13.8 0.0 collective-permute-done.1
  13.8 0.5 %collective-permute-done.2 = bf16[1,16,1536]{2,1,0:T(8,128)(2,1)S(1)} collective-permute-done((bf16[1,16,1536]{2,1,0:T(8,128)(2,1)}, bf16[1,16,1536]{2,1,0:T(8,128)(2,1)S(1)}, u32[]{:S(2)}, u32[]{:S(2)}) %collective-permute-start.2) | collective-permute-done | bytes 49184 | tf_op jit(solution)/shard_map/ppermute | solution.py:173
  14.2 0.0 copy-done.1
  14.3 2.5 %collective-permute-start.3 = (bf16[2,32,1536]{2,1,0:T(8,128)(2,1)S(1)}, bf16[2,32,1536]{2,1,0:T(8,128)(2,1)S(1)}, u32[]{:S(2)}, u32[]{:S(2)}) collective-permute-start(bf16[2,32,1536]{2,1,0:T(8,128)(2,1)S(1)} %maximum_maximum_fusion), channel_id=1, source_target_pairs={{0,2},{2,4},{4,6},{6,8},{8,10},{10,12},{12,14},{14,16},{16,18},{18... | collective-permute-start | bytes 589832 | tf_op jit(solution)/shard_map/ppermute | solution.py:176
  16.8 2.1 %collective-permute-start.4 = (bf16[2,32,1536]{2,1,0:T(8,128)(2,1)S(1)}, bf16[2,32,1536]{2,1,0:T(8,128)(2,1)S(1)}, u32[]{:S(2)}, u32[]{:S(2)}) collective-permute-start(bf16[2,32,1536]{2,1,0:T(8,128)(2,1)S(1)} %maximum_maximum_fusion), channel_id=1, source_target_pairs={{2,0},{4,2},{6,4},{8,6},{10,8},{12,10},{14,12},{16,14},{18,16},{20... | collective-permute-start | bytes 589832 | tf_op jit(solution)/shard_map/ppermute | solution.py:177
  18.9 1.0 %multiply_reduce_fusion.2 = (f32[64]{0:T(128)S(1)}, f32[64,1536]{1,0:T(8,128)S(1)}) fusion(bf16[64,1536]{1,0:T(8,128)(2,1)S(1)} %bitcast.44, bf16[1536,768]{1,0:T(8,128)(2,1)S(1)} %bitcast.36, bf16[1536,768]{1,0:T(8,128)(2,1)S(1)} %bitcast.33), kind=kOutput, calls=%fused_computation.33 | convolution fusion | flops 311623616 | bytes 5308672 | tf_op jit(solution)/shard_map/dot_general | solution.py:182
  20.0 0.1 divide_convert_fusion.2
  20.1 0.0 collective-permute-done.3
  20.1 1.0 %multiply_reduce_fusion.1 = (f32[64]{0:T(128)S(1)}, f32[64,1536]{1,0:T(8,128)S(1)}) fusion(bf16[64,1536]{1,0:T(8,128)(2,1)S(1)} %bitcast.47, bf16[1536,768]{1,0:T(8,128)(2,1)S(1)} %bitcast.37, bf16[1536,768]{1,0:T(8,128)(2,1)S(1)} %bitcast.34), kind=kOutput, calls=%fused_computation.31 | convolution fusion | flops 311623616 | bytes 5308672 | tf_op jit(solution)/shard_map/dot_general | solution.py:182
  21.1 0.1 divide_convert_fusion.1
  21.3 2.5 %collective-permute-done.4 = bf16[2,32,1536]{2,1,0:T(8,128)(2,1)S(1)} collective-permute-done((bf16[2,32,1536]{2,1,0:T(8,128)(2,1)S(1)}, bf16[2,32,1536]{2,1,0:T(8,128)(2,1)S(1)}, u32[]{:S(2)}, u32[]{:S(2)}) %collective-permute-start.4) | collective-permute-done | bytes 196640 | tf_op jit(solution)/shard_map/ppermute | solution.py:177
  23.8 1.0 %multiply_reduce_fusion = (f32[64]{0:T(128)S(1)}, f32[64,1536]{1,0:T(8,128)S(1)}) fusion(bf16[64,1536]{1,0:T(8,128)(2,1)S(1)} %bitcast.46, bf16[1536,768]{1,0:T(8,128)(2,1)S(1)} %bitcast.38, bf16[1536,768]{1,0:T(8,128)(2,1)S(1)} %bitcast.35), kind=kOutput, calls=%fused_computation.29 | convolution fusion | flops 311623616 | bytes 5308672 | tf_op jit(solution)/shard_map/dot_general | solution.py:182
  24.9 0.1 divide_convert_fusion
  25.1 1.0 %fusion.23 = f32[2,1536,512]{1,2,0:T(8,128)S(1)} fusion(bf16[2,96,1536]{2,1,0:T(8,128)(2,1)S(1)} %slice_dynamic-update-slice_fusion, s32[512]{0:T(512)S(1)} %bitcast.45), kind=kOutput, calls=%fused_computation.45 | convolution fusion | flops 302039040 | bytes 6883328 | tf_op jit(solution)/shard_map/pq,mqk->mpk/dot_general | solution.py:215
  26.1 0.9 %add_convert_fusion = (bf16[2,2,256,768]{3,2,1,0:T(8,128)(2,1)S(1)}, bf16[2,2,256,768]{3,2,1,0:T(8,128)(2,1)S(1)}) fusion(f32[2,2,256,1536]{3,2,1,0:T(8,128)S(1)} %bitcast.30, f32[2,2,768]{2,1,0:T(2,128)S(1)} %get-tuple-element.12, f32[2,2,768]{2,1,0:T(2,128)S(1)} %get-tuple-element.11), kind=kLoop, calls=%fused_computation.5 | loop fusion | flops 6291456 | bytes 9461760 | tf_op jit(solution)/shard_map/convert.4
  27.1 0.0 copy-start
  27.1 0.2 pad_maximum_fusion.1.crossed_ref
  27.3 0.5 %copy-done = s32[4,1024]{1,0:T(4,128)S(1)} copy-done((s32[4,1024]{1,0:T(4,128)S(1)}, s32[4,1024]{1,0:T(4,128)}, u32[]{:S(2)}) %copy-start) | copy-done | bytes 16408
  27.8 11.1 %shard_map.37 = f32[4,512]{1,0:T(4,128)S(1)} custom-call(s32[1]{0:T(128)} %constant.28.clone.1.own_ref, s32[4,1024]{1,0:T(4,128)S(1)} %copy-done, bf16[2,512,1536]{2,1,0:T(8,128)(2,1)S(1)} %pad_maximum_fusion.1.crossed_ref, f32[768,8]{1,0:T(8,128)S(1)} %get-tuple-element.14.wcos_ref, f32[768,8]{1,0:T(8,128)S(1)} %get-tuple-element.13.wsin_ref, ...), custom_call_target="tpu_custom_call" | custom-call | tf_op jit(solution)/shard_map/pallas_call | solution.py:136
  38.9 0.6 %reshape.161 = f32[1,4,2,256]{3,2,1,0:T(2,128)} reshape(f32[4,512]{1,0:T(4,128)S(1)} %shard_map.37) | data formatting | bytes 16384 | tf_op jit(solution)/shard_map/reshape | solution.py:223
  (17 shorter events, 0.2 us)
Async XLA Ops:
  0.0 14.2 %copy-start.1 = (bf16[1,16,1536]{2,1,0:T(8,128)(2,1)S(1)}, bf16[1,16,1536]{2,1,0:T(8,128)(2,1)}, u32[]{:S(2)}) copy-start(bf16[1,16,1536]{2,1,0:T(8,128)(2,1)} %param.3) | copy-start | bytes 147460
  0.0 12.1 %copy-start.2 = (s32[2,256]{1,0:T(2,128)S(1)}, s32[2,256]{1,0:T(2,128)}, u32[]{:S(2)}) copy-start(s32[2,256]{1,0:T(2,128)} %param.4) | copy-start | bytes 6148
  0.0 13.7 %collective-permute-start = (bf16[1,16,1536]{2,1,0:T(8,128)(2,1)}, bf16[1,16,1536]{2,1,0:T(8,128)(2,1)S(1)}, u32[]{:S(2)}, u32[]{:S(2)}) collective-permute-start(bf16[1,16,1536]{2,1,0:T(8,128)(2,1)} %param.3), channel_id=1, source_target_pairs={{0,30},{2,28},{4,26},{6,24},{8,22},{10,20},{12,18},{14,16},{16,14}... | collective-permute-start | bytes 147464 | tf_op jit(solution)/shard_map/ppermute | solution.py:173
  5.7 8.1 %collective-permute-start.1 = (bf16[1,16,1536]{2,1,0:T(8,128)(2,1)}, bf16[1,16,1536]{2,1,0:T(8,128)(2,1)S(1)}, u32[]{:S(2)}, u32[]{:S(2)}) collective-permute-start(bf16[1,16,1536]{2,1,0:T(8,128)(2,1)} %param.3), channel_id=1, source_target_pairs={{0,1},{1,0},{2,3},{3,2},{4,5},{5,4},{6,7},{7,6},{8,9},{9,8},{10,11... | collective-permute-start | bytes 147464 | tf_op jit(solution)/shard_map/ppermute | solution.py:167
  6.9 7.4 %collective-permute-start.2 = (bf16[1,16,1536]{2,1,0:T(8,128)(2,1)}, bf16[1,16,1536]{2,1,0:T(8,128)(2,1)S(1)}, u32[]{:S(2)}, u32[]{:S(2)}) collective-permute-start(bf16[1,16,1536]{2,1,0:T(8,128)(2,1)} %param.3), channel_id=1, source_target_pairs={{0,31},{2,29},{4,27},{6,25},{8,23},{10,21},{12,19},{14,17},{16,15}... | collective-permute-start | bytes 147464 | tf_op jit(solution)/shard_map/ppermute | solution.py:173
  14.3 5.8 %collective-permute-start.3 = (bf16[2,32,1536]{2,1,0:T(8,128)(2,1)S(1)}, bf16[2,32,1536]{2,1,0:T(8,128)(2,1)S(1)}, u32[]{:S(2)}, u32[]{:S(2)}) collective-permute-start(bf16[2,32,1536]{2,1,0:T(8,128)(2,1)S(1)} %maximum_maximum_fusion), channel_id=1, source_target_pairs={{0,2},{2,4},{4,6},{6,8},{8,10},{10,12},{12,14},{14,16},{16,18},{18... | collective-permute-start | bytes 589832 | tf_op jit(solution)/shard_map/ppermute | solution.py:176
  16.8 7.0 %collective-permute-start.4 = (bf16[2,32,1536]{2,1,0:T(8,128)(2,1)S(1)}, bf16[2,32,1536]{2,1,0:T(8,128)(2,1)S(1)}, u32[]{:S(2)}, u32[]{:S(2)}) collective-permute-start(bf16[2,32,1536]{2,1,0:T(8,128)(2,1)S(1)} %maximum_maximum_fusion), channel_id=1, source_target_pairs={{2,0},{4,2},{6,4},{8,6},{10,8},{12,10},{14,12},{16,14},{18,16},{20... | collective-permute-start | bytes 589832 | tf_op jit(solution)/shard_map/ppermute | solution.py:177
  27.1 0.7 %copy-start = (s32[4,1024]{1,0:T(4,128)S(1)}, s32[4,1024]{1,0:T(4,128)}, u32[]{:S(2)}) copy-start(s32[4,1024]{1,0:T(4,128)} %stretch_ref.1) | copy-start | bytes 49156
